TPU v7x, 512 devices: a whole 4x8x8 slice. The times are simulated.
512 devices in a mesh: dp: 4 (over y_lo, core), seq: 4 (over x), fsdp: 32 (over y_hi, z).
Axes of the slice: x: 4, y: 8 (y_hi: 4, y_lo: 2; y = y_hi * 2 + y_lo), z: 8, core: 2. Of those that a mesh axis runs over, the one named last changes fastest.
Arguments:
- patches: bfloat16 [128, 768, 6144], P(('dp', 'fsdp'), 'seq'), may hold values from -100 to 100
- segments: int32 [128, 768], P(('dp', 'fsdp'), 'seq'), may hold values from 0 to 7, never falling along the last dimension, each value on 1 to 384 neighbouring positions
- qkv_weight: bfloat16 [6144, 384], P('fsdp'), may hold values from -0.078125 to 0.078125
- cotangent: bfloat16 [128, 768, 128], P(('dp', 'fsdp'), 'seq'), may hold values from -6 to 6
Outputs:
- input_grad: bfloat16 [128, 768, 6144], P(('dp', 'fsdp'), 'seq')
- weight_grad: float32 [6144, 384], P('fsdp')
Inputs may be any that keep to these rules, and one draw needn't show every extreme that they name: `segments`: within a sequence the image number never falls; each of the 8 images has 1 to 384 patches and one has exactly 384.
All inputs are finite; a program needn't handle non-finite values.
Results may differ from a plain program's by a relative error of at most 0.034.
The roundings to bfloat16 on the way count: a program that leaves them out, or rounds other values in their place, can miss the bound.
Values may be sent and summed in bfloat16 or wider, within the bound.
No kernel may reach another device: no remote copies, remote signals or barrier semaphores. Data moves between devices by JAX's collectives and lax.ppermute only.
A program may use at most 64 MiB of HBM per device.

v0:
```python
import jax
import jax.numpy as jnp
from jax import lax
from jax.sharding import PartitionSpec as P


def contract_first(left, right):
    return lax.dot_general(
        left, right, (((0,), (0,)), ((), ())), preferred_element_type=jnp.float32
    )


def contract_last(left, right):
    return lax.dot_general(
        left, right, (((1,), (1,)), ((), ())), preferred_element_type=jnp.float32
    )


def shards(patches, segments, qkv_weight, cotangent):
    features = patches[0]
    image_ids = segments[0]
    grad_out = cotangent[0]
    width_head = cotangent.shape[2]
    scale = width_head ** (-0.5)
    full_weight = lax.all_gather(qkv_weight, "fsdp", axis=0, tiled=True)
    projected = jnp.dot(features, full_weight, preferred_element_type=jnp.float32)
    heads = projected.astype(jnp.bfloat16)
    query = heads[:, :width_head]
    own_pairs = heads[:, width_head:]
    pairs_all, images_all = (
        lax.all_gather(own_pairs, "seq", axis=0, tiled=True),
        lax.all_gather(image_ids, "seq", axis=0, tiled=True),
    )
    keys_all = pairs_all[:, :width_head]
    values_all = pairs_all[:, width_head:]
    scores = contract_last(query, keys_all) * scale
    allowed = image_ids[:, None] == images_all[None, :]
    highest = jnp.max(jnp.where(allowed, scores, -jnp.inf), axis=1)
    summed = jnp.sum(jnp.where(allowed, jnp.exp(scores - highest[:, None]), 0.0), axis=1)
    log_total = highest + jnp.log(summed)
    attention = jnp.where(allowed, jnp.exp(scores - log_total[:, None]), 0.0)
    attention_low = attention.astype(jnp.bfloat16)
    output = jnp.dot(attention_low, values_all, preferred_element_type=jnp.float32)
    delta_rows = jnp.sum(grad_out.astype(jnp.float32) * output, axis=1)
    grad_attention = contract_last(grad_out, values_all)
    grad_scores = (attention * (grad_attention - delta_rows[:, None]) * scale).astype(jnp.bfloat16)
    grad_query = jnp.dot(grad_scores, keys_all, preferred_element_type=jnp.float32).astype(
        jnp.bfloat16
    )
    partial_pairs = jnp.concatenate(
        [contract_first(grad_scores, query), contract_first(attention_low, grad_out)], axis=1
    )
    grad_pairs = lax.psum_scatter(
        partial_pairs.astype(jnp.bfloat16), "seq", scatter_dimension=0, tiled=True
    )
    grad_heads = jnp.concatenate([grad_query, grad_pairs], axis=1)
    columns = lax.all_to_all(features, "fsdp", split_axis=1, concat_axis=0, tiled=True)
    partial_grad = contract_first(columns, lax.all_gather(grad_heads, "fsdp", axis=0, tiled=True))
    input_grad = contract_last(grad_heads, full_weight).astype(jnp.bfloat16)
    weight_grad = lax.psum(partial_grad.astype(jnp.bfloat16), ("dp", "seq")).astype(jnp.float32)
    return (input_grad[None], weight_grad)


def solution(mesh):
    placed = (
        P(("dp", "fsdp"), "seq", None),
        P(("dp", "fsdp"), "seq"),
        P("fsdp", None),
        P(("dp", "fsdp"), "seq", None),
    )
    return jax.shard_map(
        shards,
        mesh=mesh,
        in_specs=placed,
        out_specs=(P(("dp", "fsdp"), "seq", None), P("fsdp", None)),
        check_vma=False,
    )
```

profile of v0, /device:TPU:1, one launch (start us, length us, event | category | flops | bytes accessed | tf_op | source)
XLA Modules:
  0.0 472.2 jit_solution(8760330779892001765)
XLA Ops:
  7.2 0.7 all-gather.4.cloned.1.call-update
  7.9 1.3 dynamic-slice
  9.9 0.9 dynamic-update-slice
  10.8 7.7 %all-reduce = s32[768]{0:T(1024)S(1)} all-reduce(s32[768]{0:T(1024)S(1)} %dynamic-update-slice), channel_id=2, replica_groups=mesh['dp'=4,'seq'=4,'fsdp'=32] {'seq'}, use_global_device_ids=true, to_apply=%add | all-reduce | flops 768 | bytes 6144
  18.5 103.9 %all-gather.4.cloned.1.call-done = bf16[6144,384]{1,0:T(8,128)(2,1)} async-done(((bf16[192,384]{1,0:T(8,128)(2,1)}), bf16[6144,384]{1,0:T(8,128)(2,1)}) %all-gather.4.cloned.1.call-update) | async-done | bytes 4718608 | tf_op jit(solution)/shard_map/all_gather | solution.py:25
  122.4 4.4 fusion.7
  126.8 9.9 %all_gather.14 = bf16[768,256]{1,0:T(8,128)(2,1)S(1)} all-gather(bf16[192,256]{1,0:T(8,128)(2,1)S(1)} %slice.17), channel_id=1, replica_groups=mesh['dp'=4,'seq'=4,'fsdp'=32] {'seq'}, dimensions={0}, use_global_device_ids=true | all-gather | bytes 491520 | tf_op jit(solution)/shard_map/all_gather | solution.py:31
  136.8 0.3 fusion.12
  137.1 0.3 fusion.13
  137.9 0.3 fusion.11
  138.2 0.3 fusion.6
  138.8 0.9 copy.13
  140.1 23.7 %reduce-scatter.4.cloned.1.call-done = bf16[192,256]{1,0:T(8,128)(2,1)} async-done(((bf16[768,256]{1,0:T(8,128)(2,1)}), bf16[192,256]{1,0:T(8,128)(2,1)}) %reduce-scatter.4.cloned.1.call-update) | async-done | bytes 98320
  163.9 1.0 copy.14
  164.9 0.8 copy.10
  165.8 3.0 copy.11
  168.8 104.7 %all_to_all.19 = bf16[192,32,192]{0,2,1:T(8,128)(2,1)S(1)} all-to-all(bf16[192,32,192]{0,2,1:T(8,128)(2,1)S(1)} %bitcast.39), channel_id=1, replica_groups=mesh['dp'=4,'seq'=4,'fsdp'=32] {'fsdp'}, dimensions={1} | all-to-all | bytes 4718592 | tf_op jit(solution)/shard_map/all_to_all | solution.py:57
  273.5 1.8 copy.12
  275.2 4.2 all_to_all.17
  279.5 57.0 %all-gather.6.cloned.1.call-done = bf16[6144,384]{1,0:T(8,128)(2,1)} async-done(((bf16[192,384]{1,0:T(8,128)(2,1)}), bf16[6144,384]{1,0:T(8,128)(2,1)}) %all-gather.6.cloned.1.call-update) | async-done | bytes 4718608 | tf_op jit(solution)/shard_map/all_gather | solution.py:58
  336.4 5.1 %fusion.10 = bf16[192,384]{1,0:T(8,128)(2,1)} fusion(bf16[6144,192]{0,1:T(8,128)(2,1)} %all_to_all.17, bf16[6144,384]{1,0:T(8,128)(2,1)} %all-gather.6.cloned.1.call-done), kind=kOutput, calls=%fused_computation.14 | convolution fusion | flops 906043392 | bytes 7225344 | tf_op jit(solution)/shard_map/dot_general | solution.py:8
  341.5 5.6 %fusion = bf16[1,192,6144]{2,1,0:T(8,128)(2,1)} fusion(bf16[6144,384]{1,0:T(8,128)(2,1)} %all-gather.4.cloned.1.call-done, bf16[192,256]{0,1:T(8,128)(2,1)S(1)} %copy.14, bf16[192,128]{0,1:T(8,128)(2,1)S(1)} %copy.9), kind=kOutput, calls=%fused_computation.1 | convolution fusion | flops 907444224 | bytes 7225344 | tf_op jit(solution)/shard_map/dot_general | solution.py:14
  347.2 116.8 %all-reduce.3.cloned.1.call-done = bf16[192,384]{1,0:T(8,128)(2,1)} async-done(((bf16[192,384]{1,0:T(8,128)(2,1)}), bf16[192,384]{1,0:T(8,128)(2,1)}) %all-reduce.3.cloned.1.call-update) | async-done | bytes 147472 | tf_op jit(solution)/shard_map/psum | solution.py:60
  464.0 1.6 convert_element_type.36
  (21 shorter events, 1.3 us)
Async XLA Ops:
  7.2 115.2 %all-gather.4.cloned.1.call-start = ((), (), s32[]{:S(2)}) async-start(), calls=%async_computation.2 | async-start | bytes 4866048 | tf_op jit(solution)/shard_map/all_gather | solution.py:25
  7.9 156.0 %reduce-scatter.4.cloned.1.call-start = ((), (), s32[]{:S(2)}) async-start(), calls=%async_computation.5 | async-start | bytes 491520
  18.5 118.3 %copy-start.1 = (s32[1,192]{1,0:T(1,128)S(1)}, s32[1,192]{1,0:T(1,128)}, u32[]{:S(2)}) copy-start(s32[1,192]{1,0:T(1,128)} %param.5) | copy-start | bytes 2308
  126.8 10.8 %copy-start = (bf16[1,192,128]{2,1,0:T(8,128)(2,1)S(1)}, bf16[1,192,128]{2,1,0:T(8,128)(2,1)}, u32[]{:S(2)}) copy-start(bf16[1,192,128]{2,1,0:T(8,128)(2,1)} %param.7) | copy-start | bytes 147460
  139.7 196.7 %all-gather.6.cloned.1.call-start = ((), (), s32[]{:S(2)}) async-start(), calls=%async_computation.3 | async-start | bytes 4866048 | tf_op jit(solution)/shard_map/all_gather | solution.py:58
  165.7 298.3 %all-reduce.3.cloned.1.call-start = ((), (), s32[]{:S(2)}) async-start(), calls=%async_computation.4 | async-start | bytes 294912 | tf_op jit(solution)/shard_map/psum | solution.py:60
Sparse Core Ops, SparseCore 0:
  11.2 111.1 all-gather.3
  139.9 23.9 reduce-scatter.3
  168.1 168.2 all-gather.5
  341.7 122.2 all-reduce.2
where the time goes:
time: 473 us; the launch traced here: 472 us
  waiting for transfers between devices  302 us (64%)
  blocking collectives  122 us (26%)
  matrix products  16.9 us (4%)
  between operations  14.5 us (3%)
  local copies, waits for them, and re-layouts  14 us (3%)
    psum x1, waiting for transfers between devices, shards(): lax.psum(partial_grad.astype(jnp.bfloat16), ('dp', 'seq'))  117 us
    all_to_all x1, blocking collectives, shards(): lax.all_to_all(features, 'fsdp', split_axis=1, concat_axis=0, tiled=True)  105 us
    all_gather x1, waiting for transfers between devices, shards(): full_weight = lax.all_gather(qkv_weight, 'fsdp', axis=0, tiled=True)  104 us
    all_gather x1, waiting for transfers between devices, shards(): lax.all_gather(grad_heads, 'fsdp', axis=0, tiled=True)  57 us
    unnamed x5, waiting for transfers between devices  24.5 us
    all_gather x1, blocking collectives, shards(): lax.all_gather(own_pairs, 'seq', axis=0, tiled=True)  9.94 us
  transfers between devices with their start and end apart: 4, of which 4 were waited for; matrix products, arithmetic and copies ran while one was open for 3% of the time, Pallas kernels for 0%

commit v1 on v0

--- a/solution.py
+++ b/solution.py
@@ -16,14 +16,33 @@
     )
 
 
+def chip_partner(x):
+    pairs = [(i, i ^ 1) for i in range(lax.axis_size("dp"))]
+    return lax.ppermute(x, "dp", perm=pairs)
+
+
 def shards(patches, segments, qkv_weight, cotangent):
     features = patches[0]
     image_ids = segments[0]
     grad_out = cotangent[0]
     width_head = cotangent.shape[2]
+    width_all = qkv_weight.shape[1]
+    half = width_all // 2
     scale = width_head ** (-0.5)
-    full_weight = lax.all_gather(qkv_weight, "fsdp", axis=0, tiled=True)
-    projected = jnp.dot(features, full_weight, preferred_element_type=jnp.float32)
+    core = lax.axis_index("dp") % 2
+    first = core == 0
+
+    w_mine = lax.dynamic_slice_in_dim(qkv_weight, core * half, half, axis=1)
+    w_mine_all = lax.all_gather(w_mine, "fsdp", axis=0, tiled=True)
+    w_other_all = chip_partner(w_mine_all)
+
+    h_mine = jnp.dot(features, w_mine_all, preferred_element_type=jnp.float32)
+    h_other = jnp.dot(features, w_other_all, preferred_element_type=jnp.float32)
+    projected = jnp.where(
+        first,
+        jnp.concatenate([h_mine, h_other], axis=1),
+        jnp.concatenate([h_other, h_mine], axis=1),
+    )
     heads = projected.astype(jnp.bfloat16)
     query = heads[:, :width_head]
     own_pairs = heads[:, width_head:]
@@ -54,10 +73,27 @@
         partial_pairs.astype(jnp.bfloat16), "seq", scatter_dimension=0, tiled=True
     )
     grad_heads = jnp.concatenate([grad_query, grad_pairs], axis=1)
-    columns = lax.all_to_all(features, "fsdp", split_axis=1, concat_axis=0, tiled=True)
-    partial_grad = contract_first(columns, lax.all_gather(grad_heads, "fsdp", axis=0, tiled=True))
-    input_grad = contract_last(grad_heads, full_weight).astype(jnp.bfloat16)
-    weight_grad = lax.psum(partial_grad.astype(jnp.bfloat16), ("dp", "seq")).astype(jnp.float32)
+
+    g_lo = grad_heads[:, :half]
+    g_hi = grad_heads[:, half:]
+    g_mine = jnp.where(first, g_lo, g_hi)
+    g_other = jnp.where(first, g_hi, g_lo)
+
+    input_grad = (
+        contract_last(g_mine, w_mine_all) + contract_last(g_other, w_other_all)
+    ).astype(jnp.bfloat16)
+
+    wg_mine = contract_first(features, g_mine)
+    wg_other = contract_first(features, g_other)
+    wg_from_partner = chip_partner(wg_other.astype(jnp.bfloat16))
+    wg_chip = (wg_mine + wg_from_partner.astype(jnp.float32)).astype(jnp.bfloat16)
+    wg_rows = lax.psum_scatter(wg_chip, "fsdp", scatter_dimension=0, tiled=True)
+    gathered = lax.all_gather(wg_rows, ("dp", "seq"), axis=0, tiled=False).astype(jnp.float32)
+    n_dp = lax.axis_size("dp")
+    by_dp = gathered.reshape(n_dp, gathered.shape[0] // n_dp, *wg_rows.shape)
+    lo = jnp.sum(by_dp[0::2], axis=(0, 1))
+    hi = jnp.sum(by_dp[1::2], axis=(0, 1))
+    weight_grad = jnp.concatenate([lo, hi], axis=1)
     return (input_grad[None], weight_grad)
 
 

time: 473 us -> 476 us (level)
  blocking collectives: 122 us -> 17.5 us
  waiting for transfers between devices: 302 us -> 399 us
  starting transfers between devices: 0.16 us -> 9.08 us
    reduce_scatter x0 -> x1, waiting for transfers between devices: none -> 226 us  [shards(): wg_rows = lax.psum_scatter(wg_chip, 'fsdp', scatter_dimension=0, tiled=True)]
    psum x1 -> x0, waiting for transfers between devices: 117 us -> none  [shards(): lax.psum(partial_grad.astype(jnp.bfloat16), ('dp', 'seq'))]
    all_to_all x1 -> x0, blocking collectives: 105 us -> none  [shards(): lax.all_to_all(features, 'fsdp', split_axis=1, concat_axis=0, tiled=True)]
    all_gather x2, waiting for transfers between devices: 161 us -> 148 us  [the longest x1 100 us: shards(): w_mine_all = lax.all_gather(w_mine, 'fsdp', axis=0, tiled=True)]
    ppermute x0 -> x2, starting transfers between devices: none -> 8.91 us  [chip_partner(): return lax.ppermute(x, 'dp', perm=pairs)]
    all_to_all x2 -> x0, local copies, waits for them, and re-layouts: 5.99 us -> none  [shards(): lax.all_to_all(features, 'fsdp', split_axis=1, concat_axis=0, tiled=True)]
  transfers between devices with their start and end apart: 4 -> 6, of which waited for: 4 -> 5; matrix products, arithmetic and copies ran while one was open for 3% -> 2% of each run, Pallas kernels for 0% -> 0%
where the time goes in v1:
time: 476 us
  waiting for transfers between devices  399 us (84%)
  blocking collectives  17.5 us (4%)
  matrix products  16.9 us (4%)
  local copies, waits for them, and re-layouts  15.4 us (3%)
  between operations  14.7 us (3%)
  starting transfers between devices  9.08 us (2%)
    reduce_scatter x1, waiting for transfers between devices, shards(): wg_rows = lax.psum_scatter(wg_chip, 'fsdp', scatter_dimension=0, tiled=True)  226 us
    all_gather x1, waiting for transfers between devices, shards(): w_mine_all = lax.all_gather(w_mine, 'fsdp', axis=0, tiled=True)  100 us
    all_gather x1, waiting for transfers between devices, shards(): lax.all_gather(wg_rows, ('dp', 'seq'), axis=0, tiled=False)  47.6 us
    unnamed x5, waiting for transfers between devices  21.6 us
    all_gather x1, blocking collectives, shards(): lax.all_gather(own_pairs, 'seq', axis=0, tiled=True)  10.7 us
  transfers between devices with their start and end apart: 6, of which 5 were waited for; matrix products, arithmetic and copies ran while one was open for 2% of the time, Pallas kernels for 0%

profile of v1, /device:TPU:1, one launch (start us, length us, event | category | flops | bytes accessed | tf_op | source)
XLA Modules:
  0.0 475.5 jit_solution(8980155124904882049)
XLA Ops:
  7.2 1.8 constant_dynamic-slice_fusion
  9.1 100.3 %all-gather.5.cloned.1.call-done = bf16[6144,192]{1,0:T(8,128)(2,1)} async-done(((bf16[192,192]{1,0:T(8,128)(2,1)}), bf16[6144,192]{1,0:T(8,128)(2,1)}) %all-gather.5.cloned.1.call-update) | async-done | bytes 2359312 | tf_op jit(solution)/shard_map/all_gather | solution.py:36
  109.4 4.5 copy.13
  113.9 4.3 collective-permute-start
  118.2 1.3 dynamic-slice
  120.4 6.8 %all-reduce = s32[768]{0:T(1024)S(1)} all-reduce(s32[768]{0:T(1024)S(1)} %dynamic-update-slice), channel_id=2, replica_groups=mesh['dp'=4,'seq'=4,'fsdp'=32] {'seq'}, use_global_device_ids=true, to_apply=%add | all-reduce | flops 768 | bytes 6144
  127.2 2.7 fusion.18
  129.9 2.5 fusion.15
  132.5 10.7 %all_gather.17 = bf16[768,256]{1,0:T(8,128)(2,1)S(1)} all-gather(bf16[192,256]{1,0:T(8,128)(2,1)S(1)} %slice.33), channel_id=1, replica_groups=mesh['dp'=4,'seq'=4,'fsdp'=32] {'seq'}, dimensions={0}, use_global_device_ids=true | all-gather | bytes 491520 | tf_op jit(solution)/shard_map/all_gather | solution.py:50
  143.2 0.3 fusion.22
  145.3 0.9 copy.19
  146.6 21.6 %reduce-scatter.7.cloned.1.call-done = bf16[192,256]{1,0:T(8,128)(2,1)} async-done(((bf16[768,256]{1,0:T(8,128)(2,1)}), bf16[192,256]{1,0:T(8,128)(2,1)}) %reduce-scatter.7.cloned.1.call-update) | async-done | bytes 98320
  168.1 1.0 copy.20
  169.2 0.8 fusion.2
  169.9 4.6 collective-permute-start.1
  174.6 4.1 collective-permute-done.1
  178.7 2.2 add_convert_fusion
  180.9 4.5 copy.21
  185.5 225.6 %reduce-scatter.9.cloned.1.call-done = bf16[192,192]{1,0:T(8,128)(2,1)} async-done(((bf16[6144,192]{1,0:T(8,128)(2,1)}), bf16[192,192]{1,0:T(8,128)(2,1)}) %reduce-scatter.9.cloned.1.call-update) | async-done | bytes 73744 | tf_op jit(solution)/shard_map/reduce_scatter | solution.py:90
  411.1 3.1 fusion.34
  414.3 4.0 fusion.1
  418.2 47.6 %all-gather.7.cloned.1.call-done = bf16[3072,192]{1,0:T(8,128)(2,1)} async-done(((bf16[192,192]{1,0:T(8,128)(2,1)}), bf16[3072,192]{1,0:T(8,128)(2,1)}) %all-gather.7.cloned.1.call-update) | async-done | bytes 1179664 | tf_op jit(solution)/shard_map/all_gather | solution.py:91
  465.9 1.7 convert.9
  468.1 0.9 copy.18
  (34 shorter events, 3.1 us)
Async XLA Ops:
  7.2 120.0 %copy-start = (bf16[1,192,6144]{2,1,0:T(8,128)(2,1)S(1)}, bf16[1,192,6144]{2,1,0:T(8,128)(2,1)}, u32[]{:S(2)}) copy-start(bf16[1,192,6144]{2,1,0:T(8,128)(2,1)} %param.4) | copy-start | bytes 7077892
  7.2 102.2 %all-gather.5.cloned.1.call-start = ((), (), s32[]{:S(2)}) async-start(), calls=%async_computation.2 | async-start | bytes 3244032 | tf_op jit(solution)/shard_map/all_gather | solution.py:36
  9.1 111.1 %copy-start.2 = (s32[1,192]{1,0:T(1,128)S(1)}, s32[1,192]{1,0:T(1,128)}, u32[]{:S(2)}) copy-start(s32[1,192]{1,0:T(1,128)} %param.5) | copy-start | bytes 2308
  9.1 159.1 %reduce-scatter.7.cloned.1.call-start = ((), (), s32[]{:S(2)}) async-start(), calls=%async_computation.4 | async-start | bytes 491520
  113.9 16.0 %collective-permute-start = (bf16[6144,192]{0,1:T(8,128)(2,1)}, bf16[6144,192]{0,1:T(8,128)(2,1)}, u32[]{:S(2)}, u32[]{:S(2)}) collective-permute-start(bf16[6144,192]{0,1:T(8,128)(2,1)} %copy.13), channel_id=1, source_target_pairs={{0,128},{128,0},{256,384},{384,256},{1,129},{129,1},{257,385},{385... | collective-permute-start | bytes 7077896 | tf_op jit(solution)/shard_map/ppermute | solution.py:21
  132.3 11.7 %copy-start.1 = (bf16[1,192,128]{2,1,0:T(8,128)(2,1)S(1)}, bf16[1,192,128]{2,1,0:T(8,128)(2,1)}, u32[]{:S(2)}) copy-start(bf16[1,192,128]{2,1,0:T(8,128)(2,1)} %param.7) | copy-start | bytes 147460
  146.2 264.9 %reduce-scatter.9.cloned.1.call-start = ((), (), s32[]{:S(2)}) async-start(), calls=%async_computation.5 | async-start | bytes 3244032 | tf_op jit(solution)/shard_map/reduce_scatter | solution.py:90
  169.9 8.8 %collective-permute-start.1 = (bf16[6144,192]{0,1:T(8,128)(2,1)S(1)}, bf16[6144,192]{0,1:T(8,128)(2,1)S(1)}, u32[]{:S(2)}, u32[]{:S(2)}) collective-permute-start(bf16[6144,192]{0,1:T(8,128)(2,1)S(1)} %fusion.2), channel_id=1, source_target_pairs={{0,128},{128,0},{256,384},{384,256},{1,129},{129,1},{257,385},{385... | collective-permute-start | bytes 7077896 | tf_op jit(solution)/shard_map/ppermute | solution.py:21
  185.5 280.4 %all-gather.7.cloned.1.call-start = ((), (), s32[]{:S(2)}) async-start(), calls=%async_computation.3 | async-start | bytes 1671168 | tf_op jit(solution)/shard_map/all_gather | solution.py:91
Sparse Core Ops, SparseCore 0:
  11.7 97.6 all-gather.4
  146.3 21.7 reduce-scatter.6
  185.6 225.4 reduce-scatter.8
  413.1 52.7 all-gather.6

commit v2 on v1

--- a/solution.py
+++ b/solution.py
@@ -1,3 +1,5 @@
+import functools
+
 import jax
 import jax.numpy as jnp
 from jax import lax
@@ -16,25 +18,98 @@
     )
 
 
-def chip_partner(x):
-    pairs = [(i, i ^ 1) for i in range(lax.axis_size("dp"))]
+def dp_partner(x, bit):
+    pairs = [(i, i ^ bit) for i in range(lax.axis_size("dp"))]
     return lax.ppermute(x, "dp", perm=pairs)
 
 
-def shards(patches, segments, qkv_weight, cotangent):
+class Ring:
+    def __init__(self, axis, size, inner):
+        self.axis, self.size, self.inner = axis, size, inner
+
+    def total(self):
+        return lax.axis_size(self.axis)
+
+    def position(self):
+        return (lax.axis_index(self.axis) // self.inner) % self.size
+
+    def shift(self, x, step):
+        n, inner, total = self.size, self.inner, self.total()
+        pairs = []
+        for i in range(total):
+            pos = (i // inner) % n
+            base = i - pos * inner
+            pairs.append((i, base + ((pos + step) % n) * inner))
+        return lax.ppermute(x, self.axis, perm=pairs)
+
+
+def ring_gather(x, ring):
+    n = ring.size
+    got, slot = [x], {0: 0}
+    cw, ccw = x, x
+    for t in range(1, n):
+        if t % 2 == 1:
+            cw = ring.shift(cw, 1)
+            slot[(n - (t + 1) // 2) % n] = len(got)
+            got.append(cw)
+        else:
+            ccw = ring.shift(ccw, -1)
+            slot[t // 2] = len(got)
+            got.append(ccw)
+    return jnp.stack(got), [slot[k] for k in range(n)]
+
+
+def ring_reduce_scatter(blocks, ring):
+    n = ring.size
+    if n == 1:
+        return blocks[0]
+    me = ring.position()
+    rows = blocks.shape[1]
+    upper, lower = blocks[:, : rows // 2], blocks[:, rows // 2 :]
+
+    def pick(part, index):
+        return lax.dynamic_index_in_dim(part, index % n, axis=0, keepdims=False)
+
+    acc_cw = pick(upper, me - 1)
+    acc_ccw = pick(lower, me + 1)
+    for t in range(1, n):
+        acc_cw = ring.shift(acc_cw.astype(jnp.bfloat16), 1).astype(jnp.float32) + pick(
+            upper, me - 1 - t
+        )
+        acc_ccw = ring.shift(acc_ccw.astype(jnp.bfloat16), -1).astype(jnp.float32) + pick(
+            lower, me + 1 + t
+        )
+    return jnp.concatenate([acc_cw, acc_ccw], axis=0)
+
+
+def shards(patches, segments, qkv_weight, cotangent, inner_fsdp):
     features = patches[0]
     image_ids = segments[0]
     grad_out = cotangent[0]
     width_head = cotangent.shape[2]
     width_all = qkv_weight.shape[1]
+    rows_w = qkv_weight.shape[0]
     half = width_all // 2
     scale = width_head ** (-0.5)
     core = lax.axis_index("dp") % 2
     first = core == 0
+    n_fsdp = lax.axis_size("fsdp")
+    outer_fsdp = n_fsdp // inner_fsdp
+    ring_y = Ring("fsdp", outer_fsdp, inner_fsdp)
+    ring_z = Ring("fsdp", inner_fsdp, 1)
+    ring_x = Ring("seq", lax.axis_size("seq"), 1)
 
     w_mine = lax.dynamic_slice_in_dim(qkv_weight, core * half, half, axis=1)
-    w_mine_all = lax.all_gather(w_mine, "fsdp", axis=0, tiled=True)
-    w_other_all = chip_partner(w_mine_all)
+    stack_y, slot_y = ring_gather(w_mine, ring_y)
+    stack_zy, slot_z = ring_gather(stack_y, ring_z)
+    flat = stack_zy.reshape(-1, rows_w, half)
+    me_y, me_z = ring_y.position(), ring_z.position()
+    absolute = jnp.arange(n_fsdp, dtype=jnp.int32)
+    rel_y = (absolute // inner_fsdp - me_y) % outer_fsdp
+    rel_z = (absolute % inner_fsdp - me_z) % inner_fsdp
+    order = jnp.asarray(slot_z, jnp.int32)[rel_z] * outer_fsdp + jnp.asarray(slot_y, jnp.int32)[rel_y]
+    w_mine_all = jnp.take(flat, order, axis=0).reshape(n_fsdp * rows_w, half)
+    w_other_all = dp_partner(w_mine_all, 1)
 
     h_mine = jnp.dot(features, w_mine_all, preferred_element_type=jnp.float32)
     h_other = jnp.dot(features, w_other_all, preferred_element_type=jnp.float32)
@@ -85,16 +160,41 @@
 
     wg_mine = contract_first(features, g_mine)
     wg_other = contract_first(features, g_other)
-    wg_from_partner = chip_partner(wg_other.astype(jnp.bfloat16))
-    wg_chip = (wg_mine + wg_from_partner.astype(jnp.float32)).astype(jnp.bfloat16)
-    wg_rows = lax.psum_scatter(wg_chip, "fsdp", scatter_dimension=0, tiled=True)
-    gathered = lax.all_gather(wg_rows, ("dp", "seq"), axis=0, tiled=False).astype(jnp.float32)
-    n_dp = lax.axis_size("dp")
-    by_dp = gathered.reshape(n_dp, gathered.shape[0] // n_dp, *wg_rows.shape)
-    lo = jnp.sum(by_dp[0::2], axis=(0, 1))
-    hi = jnp.sum(by_dp[1::2], axis=(0, 1))
-    weight_grad = jnp.concatenate([lo, hi], axis=1)
+    wg_from_partner = dp_partner(wg_other.astype(jnp.bfloat16), 1)
+    wg_chip = wg_mine + wg_from_partner.astype(jnp.float32)
+    blocks = wg_chip.reshape(outer_fsdp, inner_fsdp, rows_w, half)
+    over_z = ring_reduce_scatter(jnp.moveaxis(blocks, 1, 0), ring_z)
+    over_fsdp = ring_reduce_scatter(over_z, ring_y)
+
+    stack_x, slot_x = ring_gather(over_fsdp, ring_x)
+    me_x = ring_x.position()
+    n_x = ring_x.size
+    rel_x = (jnp.arange(n_x, dtype=jnp.int32) - me_x) % n_x
+    in_order = jnp.take(stack_x, jnp.asarray(slot_x, jnp.int32)[rel_x], axis=0)
+    over_seq = in_order[0]
+    for s in range(1, n_x):
+        over_seq = over_seq + in_order[s]
+    if lax.axis_size("dp") > 2:
+        over_seq = over_seq + dp_partner(over_seq, 2)
+    other_half = dp_partner(over_seq, 1)
+    weight_grad = jnp.where(
+        first,
+        jnp.concatenate([over_seq, other_half], axis=1),
+        jnp.concatenate([other_half, over_seq], axis=1),
+    )
     return (input_grad[None], weight_grad)
+
+
+def inner_ring_size(mesh):
+    axis = mesh.axis_names.index("fsdp")
+    line = mesh.devices[tuple(0 if a != axis else slice(None) for a in range(mesh.devices.ndim))]
+    line = list(line)
+    if not hasattr(line[0], "coords"):
+        return len(line)
+    count = 1
+    while count < len(line) and line[count].coords[1] == line[0].coords[1]:
+        count += 1
+    return count
 
 
 def solution(mesh):
@@ -105,7 +205,7 @@
         P(("dp", "fsdp"), "seq", None),
     )
     return jax.shard_map(
-        shards,
+        functools.partial(shards, inner_fsdp=inner_ring_size(mesh)),
         mesh=mesh,
         in_specs=placed,
         out_specs=(P(("dp", "fsdp"), "seq", None), P("fsdp", None)),

time: 476 us -> 334 us (0.70)
  waiting for transfers between devices: 399 us -> 65.3 us
  starting transfers between devices: 9.08 us -> 150 us
  local copies, waits for them, and re-layouts: 15.4 us -> 45.7 us
  other arithmetic: 2.66 us -> 19.5 us
    reduce_scatter x1 -> x0, waiting for transfers between devices: 226 us -> none  [shards(): wg_rows = lax.psum_scatter(wg_chip, 'fsdp', scatter_dimension=0, tiled=True)]
    all_gather x2 -> x0, waiting for transfers between devices: 148 us -> none  [the longest x1 100 us: shards(): w_mine_all = lax.all_gather(w_mine, 'fsdp', axis=0, tiled=True)]
    ppermute x2 -> x37, starting transfers between devices: 8.91 us -> 150 us  [the longest x33 120 us: shift(): return lax.ppermute(x, self.axis, perm=pairs)]
    ppermute x2 -> x37, waiting for transfers between devices: 4.14 us -> 40 us  [the longest x33 33.5 us: shift(): return lax.ppermute(x, self.axis, perm=pairs)]
    reshape x0 -> x2, local copies, waits for them, and re-layouts: none -> 14.9 us  [shards(): blocks = wg_chip.reshape(outer_fsdp, inner_fsdp, rows_w, half)]
    gather x0 -> x5, local copies, waits for them, and re-layouts: none -> 11.3 us  [the longest x2 8.73 us: shards(): w_mine_all = jnp.take(flat, order, axis=0).reshape(n_fsdp * rows_w, half)]
    convert_element_type x0 -> x17, other arithmetic: none -> 8.74 us  [the longest x8 6.29 us: ring_reduce_scatter(): acc_cw.astype(jnp.bfloat16)]
    select_n x0 -> x8, other arithmetic: none -> 7.14 us  [the longest x3 6.09 us: shards(): w_mine_all = jnp.take(flat, order, axis=0).reshape(n_fsdp * rows_w, half)]
  transfers between devices with their start and end apart: 6 -> 38, of which waited for: 5 -> 20; matrix products, arithmetic and copies ran while one was open for 2% -> 10% of each run, Pallas kernels for 0% -> 0%
where the time goes in v2:
time: 334 us; the launch traced here: 332 us
  starting transfers between devices  150 us (45%)
  waiting for transfers between devices  65.3 us (20%)
  local copies, waits for them, and re-layouts  45.7 us (14%)
  other arithmetic  19.5 us (6%)
  matrix products  18.2 us (5%)
  blocking collectives  17.5 us (5%)
  between operations  16.1 us (5%)
    ppermute x33, starting transfers between devices, shift(): return lax.ppermute(x, self.axis, perm=pairs)  120 us
    ppermute x33, waiting for transfers between devices, shift(): return lax.ppermute(x, self.axis, perm=pairs)  33.5 us
    ppermute x4, starting transfers between devices, dp_partner(): return lax.ppermute(x, 'dp', perm=pairs)  29.8 us
    unnamed x2, waiting for transfers between devices  25.4 us
    reshape x2, local copies, waits for them, and re-layouts, shards(): blocks = wg_chip.reshape(outer_fsdp, inner_fsdp, rows_w, half)  14.9 us
    all_gather x1, blocking collectives, shards(): lax.all_gather(own_pairs, 'seq', axis=0, tiled=True)  10.7 us
    unnamed x29, local copies, waits for them, and re-layouts  9.88 us
    gather x2, local copies, waits for them, and re-layouts, shards(): w_mine_all = jnp.take(flat, order, axis=0).reshape(n_fsdp * rows_w, half)  8.73 us
  transfers between devices with their start and end apart: 38, of which 20 were waited for; matrix products, arithmetic and copies ran while one was open for 10% of the time, Pallas kernels for 0%

profile of v2, /device:TPU:1, one launch (start us, length us, event | category | flops | bytes accessed | tf_op | source)
XLA Modules:
  0.0 332.0 jit_solution(15427400321697803334)
XLA Ops:
  8.4 5.0 %collective-permute-start = (bf16[192,192]{1,0:T(8,128)(2,1)S(1)}, bf16[192,192]{1,0:T(8,128)(2,1)S(1)}, u32[]{:S(2)}, u32[]{:S(2)}) collective-permute-start(bf16[192,192]{1,0:T(8,128)(2,1)S(1)} %constant_dynamic-slice_fusion), channel_id=1, source_target_pairs={{0,8},{1,9},{2,10},{3,11},{4,12},{5,13},{6,14},{7,15},{8,16},{9,17... | collective-permute-start | bytes 221192 | tf_op jit(solution)/shard_map/ppermute | solution.py:43
  31.5 8.6 %collective-permute-start.4 = (bf16[4,192,192]{2,1,0:T(8,128)(2,1)S(1)}, bf16[4,192,192]{2,1,0:T(8,128)(2,1)S(1)}, u32[]{:S(2)}, u32[]{:S(2)}) collective-permute-start(bf16[4,192,192]{2,1,0:T(8,128)(2,1)S(1)} %pad_maximum_fusion.1), channel_id=1, source_target_pairs={{0,7},{1,0},{2,1},{3,2},{4,3},{5,4},{6,5},{7,6},{8,15},{9,8},{10,9... | collective-permute-start | bytes 884744 | tf_op jit(solution)/shard_map/ppermute | solution.py:43
  46.4 4.9 %collective-permute-start.6 = (bf16[4,192,192]{2,1,0:T(8,128)(2,1)S(1)}, bf16[4,192,192]{2,1,0:T(8,128)(2,1)S(1)}, u32[]{:S(2)}, u32[]{:S(2)}) collective-permute-start(bf16[4,192,192]{2,1,0:T(8,128)(2,1)S(1)} %collective-permute-done.4), channel_id=1, source_target_pairs={{0,7},{1,0},{2,1},{3,2},{4,3},{5,4},{6,5},{7,6},{8,15},{9,8},{10,9... | collective-permute-start | bytes 884744 | tf_op jit(solution)/shard_map/ppermute | solution.py:43
  57.0 4.6 %collective-permute-start.8 = (bf16[4,192,192]{2,1,0:T(8,128)(2,1)S(1)}, bf16[4,192,192]{2,1,0:T(8,128)(2,1)S(1)}, u32[]{:S(2)}, u32[]{:S(2)}) collective-permute-start(bf16[4,192,192]{2,1,0:T(8,128)(2,1)S(1)} %collective-permute-done.6), channel_id=1, source_target_pairs={{0,7},{1,0},{2,1},{3,2},{4,3},{5,4},{6,5},{7,6},{8,15},{9,8},{10,9... | collective-permute-start | bytes 884744 | tf_op jit(solution)/shard_map/ppermute | solution.py:43
  67.5 6.2 %collective-permute-done.9 = bf16[4,192,192]{2,1,0:T(8,128)(2,1)S(1)} collective-permute-done((bf16[4,192,192]{2,1,0:T(8,128)(2,1)S(1)}, bf16[4,192,192]{2,1,0:T(8,128)(2,1)S(1)}, u32[]{:S(2)}, u32[]{:S(2)}) %collective-permute-start.9) | collective-permute-done | bytes 294944 | tf_op jit(solution)/shard_map/ppermute | solution.py:43
  86.6 8.3 %collective-permute-start.10 = (bf16[6144,192]{0,1:T(8,128)(2,1)}, bf16[6144,192]{0,1:T(8,128)(2,1)}, u32[]{:S(2)}, u32[]{:S(2)}) collective-permute-start(bf16[6144,192]{0,1:T(8,128)(2,1)} %broadcast_select_fusion.1), channel_id=1, source_target_pairs={{0,128},{128,0},{256,384},{384,256},{1,129},{129,1},{257,385},{385... | collective-permute-start | bytes 7077896 | tf_op jit(solution)/shard_map/ppermute | solution.py:23
  97.0 6.9 %all-reduce = s32[768]{0:T(1024)S(1)} all-reduce(s32[768]{0:T(1024)S(1)} %dynamic-update-slice), channel_id=2, replica_groups=mesh['dp'=4,'seq'=4,'fsdp'=32] {'seq'}, use_global_device_ids=true, to_apply=%add | all-reduce | flops 768 | bytes 6144
  109.6 10.7 %all_gather.7 = bf16[768,256]{1,0:T(8,128)(2,1)S(1)} all-gather(bf16[192,256]{1,0:T(8,128)(2,1)S(1)} %slice.70), channel_id=1, replica_groups=mesh['dp'=4,'seq'=4,'fsdp'=32] {'seq'}, dimensions={0}, use_global_device_ids=true | all-gather | bytes 491520 | tf_op jit(solution)/shard_map/all_gather | solution.py:125
  123.6 25.3 %reduce-scatter.4.cloned.1.call-done = bf16[192,256]{1,0:T(8,128)(2,1)} async-done(((bf16[768,256]{1,0:T(8,128)(2,1)}), bf16[192,256]{1,0:T(8,128)(2,1)}) %reduce-scatter.4.cloned.1.call-update) | async-done | bytes 98320
  152.1 4.6 %collective-permute-start.11 = (bf16[6144,192]{0,1:T(8,128)(2,1)}, bf16[6144,192]{0,1:T(8,128)(2,1)}, u32[]{:S(2)}, u32[]{:S(2)}) collective-permute-start(bf16[6144,192]{0,1:T(8,128)(2,1)} %fusion.2), channel_id=1, source_target_pairs={{0,128},{128,0},{256,384},{384,256},{1,129},{129,1},{257,385},{385... | collective-permute-start | bytes 7077896 | tf_op jit(solution)/shard_map/ppermute | solution.py:23
  161.3 4.7 %convert_add_fusion = f32[6144,192]{0,1:T(8,128)} fusion(bf16[6144,192]{0,1:T(8,128)(2,1)} %collective-permute-done.11, bf16[1,192,6144]{2,1,0:T(8,128)(2,1)S(1)} %copy-done, bf16[192,192]{0,1:T(8,128)(2,1)S(1)} %pad_maximum_fusion.4, pred[]{:T(512)S(6)} %eq.55, bf16[192,256]{0,1:T(8,128)(2,1)S(1)} %copy.20), kind=kOutput, calls=%fused_computation.10 | convolution fusion | flops 455380992 | bytes 9633793 | tf_op jit(solution)/shard_map/dot_general | solution.py:10
  165.9 7.6 %reshape.300 = f32[4,8,192,192]{2,1,0,3:T(8,128)} reshape(f32[6144,192]{0,1:T(8,128)} %convert_add_fusion) | data formatting | bytes 9437184 | tf_op jit(solution)/shard_map/reshape | solution.py:165
  173.5 7.3 %copy.18 = f32[4,8,192,192]{3,2,0,1:T(8,128)} copy(f32[4,8,192,192]{2,1,0,3:T(8,128)} %reshape.300) | data formatting | bytes 9437184 | tf_op jit(solution)/shard_map/reshape | solution.py:165
  180.8 5.2 %fusion.81 = (f32[8,2,192,192]{3,2,1,0:T(8,128)}, f32[8,2,192,192]{3,2,1,0:T(8,128)S(1)}) fusion(f32[8,4,192,192]{3,2,1,0:T(8,128)} %bitcast.192), kind=kLoop, calls=%fused_computation.176 | loop fusion | bytes 9437184 | tf_op jit(solution)/shard_map/slice | solution.py:68
  202.5 5.3 %collective-permute-start.20 = (bf16[2,192,192]{2,1,0:T(8,128)(2,1)S(1)}, bf16[2,192,192]{2,1,0:T(8,128)(2,1)S(1)}, u32[]{:S(2)}, u32[]{:S(2)}) collective-permute-start(bf16[2,192,192]{2,1,0:T(8,128)(2,1)S(1)} %fusion.31), channel_id=1, source_target_pairs={{0,7},{1,0},{2,1},{3,2},{4,3},{5,4},{6,5},{7,6},{8,15},{9,8},{10,9... | collective-permute-start | bytes 442376 | tf_op jit(solution)/shard_map/ppermute | solution.py:43
  212.2 5.0 %collective-permute-start.21 = (bf16[2,192,192]{2,1,0:T(8,128)(2,1)S(1)}, bf16[2,192,192]{2,1,0:T(8,128)(2,1)S(1)}, u32[]{:S(2)}, u32[]{:S(2)}) collective-permute-start(bf16[2,192,192]{2,1,0:T(8,128)(2,1)S(1)} %fusion.30), channel_id=1, source_target_pairs={{0,7},{1,0},{2,1},{3,2},{4,3},{5,4},{6,5},{7,6},{8,15},{9,8},{10,9... | collective-permute-start | bytes 442376 | tf_op jit(solution)/shard_map/ppermute | solution.py:43
  220.3 4.6 %collective-permute-start.22 = (bf16[2,192,192]{2,1,0:T(8,128)(2,1)S(1)}, bf16[2,192,192]{2,1,0:T(8,128)(2,1)S(1)}, u32[]{:S(2)}, u32[]{:S(2)}) collective-permute-start(bf16[2,192,192]{2,1,0:T(8,128)(2,1)S(1)} %fusion.29), channel_id=1, source_target_pairs={{0,7},{1,0},{2,1},{3,2},{4,3},{5,4},{6,5},{7,6},{8,15},{9,8},{10,9... | collective-permute-start | bytes 442376 | tf_op jit(solution)/shard_map/ppermute | solution.py:43
  237.6 4.6 %collective-permute-start.24 = (bf16[2,192,192]{2,1,0:T(8,128)(2,1)S(1)}, bf16[2,192,192]{2,1,0:T(8,128)(2,1)S(1)}, u32[]{:S(2)}, u32[]{:S(2)}) collective-permute-start(bf16[2,192,192]{2,1,0:T(8,128)(2,1)S(1)} %fusion.27), channel_id=1, source_target_pairs={{0,7},{1,0},{2,1},{3,2},{4,3},{5,4},{6,5},{7,6},{8,15},{9,8},{10,9... | collective-permute-start | bytes 442376 | tf_op jit(solution)/shard_map/ppermute | solution.py:43
  253.6 5.3 %collective-permute-start.29 = (bf16[96,192]{1,0:T(8,128)(2,1)S(1)}, bf16[96,192]{1,0:T(8,128)(2,1)S(1)}, u32[]{:S(2)}, u32[]{:S(2)}) collective-permute-start(bf16[96,192]{1,0:T(8,128)(2,1)S(1)} %fusion.64), channel_id=1, source_target_pairs={{0,24},{1,25},{2,26},{3,27},{4,28},{5,29},{6,30},{7,31},{8,0},{9,1... | collective-permute-start | bytes 110600 | tf_op jit(solution)/shard_map/ppermute | solution.py:43
  260.9 5.5 %collective-permute-start.30 = (bf16[96,192]{1,0:T(8,128)(2,1)S(1)}, bf16[96,192]{1,0:T(8,128)(2,1)S(1)}, u32[]{:S(2)}, u32[]{:S(2)}) collective-permute-start(bf16[96,192]{1,0:T(8,128)(2,1)S(1)} %fusion.54), channel_id=1, source_target_pairs={{0,24},{1,25},{2,26},{3,27},{4,28},{5,29},{6,30},{7,31},{8,0},{9,1... | collective-permute-start | bytes 110600 | tf_op jit(solution)/shard_map/ppermute | solution.py:43
  269.0 6.1 %collective-permute-start.31 = (bf16[96,192]{1,0:T(8,128)(2,1)S(1)}, bf16[96,192]{1,0:T(8,128)(2,1)S(1)}, u32[]{:S(2)}, u32[]{:S(2)}) collective-permute-start(bf16[96,192]{1,0:T(8,128)(2,1)S(1)} %fusion.58), channel_id=1, source_target_pairs={{0,24},{1,25},{2,26},{3,27},{4,28},{5,29},{6,30},{7,31},{8,0},{9,1... | collective-permute-start | bytes 110600 | tf_op jit(solution)/shard_map/ppermute | solution.py:43
  277.1 5.6 %collective-permute-done.28 = bf16[96,192]{1,0:T(8,128)(2,1)S(1)} collective-permute-done((bf16[96,192]{1,0:T(8,128)(2,1)S(1)}, bf16[96,192]{1,0:T(8,128)(2,1)S(1)}, u32[]{:S(2)}, u32[]{:S(2)}) %collective-permute-start.28) | collective-permute-done | bytes 36896 | tf_op jit(solution)/shard_map/ppermute | solution.py:43
  292.3 5.7 %collective-permute-done.34 = f32[192,192]{1,0:T(8,128)S(1)} collective-permute-done((f32[192,192]{1,0:T(8,128)S(1)}, f32[192,192]{1,0:T(8,128)S(1)}, u32[]{:S(2)}, u32[]{:S(2)}) %collective-permute-start.34) | collective-permute-done | bytes 147488 | tf_op jit(solution)/shard_map/ppermute | solution.py:43
  305.3 15.0 %collective-permute-start.36 = (f32[192,192]{1,0:T(8,128)S(1)}, f32[192,192]{1,0:T(8,128)S(1)}, u32[]{:S(2)}, u32[]{:S(2)}) collective-permute-start(f32[192,192]{1,0:T(8,128)S(1)} %fusion.90), channel_id=1, source_target_pairs={{0,128},{128,0},{256,384},{384,256},{1,129},{129,1},{257,385},{385... | collective-permute-start | bytes 442376 | tf_op jit(solution)/shard_map/ppermute | solution.py:23
  (162 shorter events, 143.5 us)
Async XLA Ops:
  7.2 141.7 %reduce-scatter.4.cloned.1.call-start = ((), (), s32[]{:S(2)}) async-start(), calls=%async_computation.1 | async-start | bytes 491520
  8.4 10.1 %collective-permute-start = (bf16[192,192]{1,0:T(8,128)(2,1)S(1)}, bf16[192,192]{1,0:T(8,128)(2,1)S(1)}, u32[]{:S(2)}, u32[]{:S(2)}) collective-permute-start(bf16[192,192]{1,0:T(8,128)(2,1)S(1)} %constant_dynamic-slice_fusion), channel_id=1, source_target_pairs={{0,8},{1,9},{2,10},{3,11},{4,12},{5,13},{6,14},{7,15},{8,16},{9,17... | collective-permute-start | bytes 221192 | tf_op jit(solution)/shard_map/ppermute | solution.py:43
  13.4 10.6 %collective-permute-start.1 = (bf16[192,192]{1,0:T(8,128)(2,1)S(1)}, bf16[192,192]{1,0:T(8,128)(2,1)S(1)}, u32[]{:S(2)}, u32[]{:S(2)}) collective-permute-start(bf16[192,192]{1,0:T(8,128)(2,1)S(1)} %constant_dynamic-slice_fusion), channel_id=1, source_target_pairs={{0,24},{1,25},{2,26},{3,27},{4,28},{5,29},{6,30},{7,31},{8,0},{9,1... | collective-permute-start | bytes 221192 | tf_op jit(solution)/shard_map/ppermute | solution.py:43
  26.2 17.5 %collective-permute-start.3 = (bf16[4,192,192]{2,1,0:T(8,128)(2,1)S(1)}, bf16[4,192,192]{2,1,0:T(8,128)(2,1)S(1)}, u32[]{:S(2)}, u32[]{:S(2)}) collective-permute-start(bf16[4,192,192]{2,1,0:T(8,128)(2,1)S(1)} %pad_maximum_fusion.1), channel_id=1, source_target_pairs={{0,1},{1,2},{2,3},{3,4},{4,5},{5,6},{6,7},{7,0},{8,9},{9,10},{10,1... | collective-permute-start | bytes 884744 | tf_op jit(solution)/shard_map/ppermute | solution.py:43
  31.5 14.9 %collective-permute-start.4 = (bf16[4,192,192]{2,1,0:T(8,128)(2,1)S(1)}, bf16[4,192,192]{2,1,0:T(8,128)(2,1)S(1)}, u32[]{:S(2)}, u32[]{:S(2)}) collective-permute-start(bf16[4,192,192]{2,1,0:T(8,128)(2,1)S(1)} %pad_maximum_fusion.1), channel_id=1, source_target_pairs={{0,7},{1,0},{2,1},{3,2},{4,3},{5,4},{6,5},{7,6},{8,15},{9,8},{10,9... | collective-permute-start | bytes 884744 | tf_op jit(solution)/shard_map/ppermute | solution.py:43
  43.7 10.6 %collective-permute-start.5 = (bf16[4,192,192]{2,1,0:T(8,128)(2,1)S(1)}, bf16[4,192,192]{2,1,0:T(8,128)(2,1)S(1)}, u32[]{:S(2)}, u32[]{:S(2)}) collective-permute-start(bf16[4,192,192]{2,1,0:T(8,128)(2,1)S(1)} %collective-permute-done.3), channel_id=1, source_target_pairs={{0,1},{1,2},{2,3},{3,4},{4,5},{5,6},{6,7},{7,0},{8,9},{9,10},{10,1... | collective-permute-start | bytes 884744 | tf_op jit(solution)/shard_map/ppermute | solution.py:43
  46.4 10.6 %collective-permute-start.6 = (bf16[4,192,192]{2,1,0:T(8,128)(2,1)S(1)}, bf16[4,192,192]{2,1,0:T(8,128)(2,1)S(1)}, u32[]{:S(2)}, u32[]{:S(2)}) collective-permute-start(bf16[4,192,192]{2,1,0:T(8,128)(2,1)S(1)} %collective-permute-done.4), channel_id=1, source_target_pairs={{0,7},{1,0},{2,1},{3,2},{4,3},{5,4},{6,5},{7,6},{8,15},{9,8},{10,9... | collective-permute-start | bytes 884744 | tf_op jit(solution)/shard_map/ppermute | solution.py:43
  54.3 9.7 %collective-permute-start.7 = (bf16[4,192,192]{2,1,0:T(8,128)(2,1)S(1)}, bf16[4,192,192]{2,1,0:T(8,128)(2,1)S(1)}, u32[]{:S(2)}, u32[]{:S(2)}) collective-permute-start(bf16[4,192,192]{2,1,0:T(8,128)(2,1)S(1)} %collective-permute-done.5), channel_id=1, source_target_pairs={{0,1},{1,2},{2,3},{3,4},{4,5},{5,6},{6,7},{7,0},{8,9},{9,10},{10,1... | collective-permute-start | bytes 884744 | tf_op jit(solution)/shard_map/ppermute | solution.py:43
  57.0 9.7 %collective-permute-start.8 = (bf16[4,192,192]{2,1,0:T(8,128)(2,1)S(1)}, bf16[4,192,192]{2,1,0:T(8,128)(2,1)S(1)}, u32[]{:S(2)}, u32[]{:S(2)}) collective-permute-start(bf16[4,192,192]{2,1,0:T(8,128)(2,1)S(1)} %collective-permute-done.6), channel_id=1, source_target_pairs={{0,7},{1,0},{2,1},{3,2},{4,3},{5,4},{6,5},{7,6},{8,15},{9,8},{10,9... | collective-permute-start | bytes 884744 | tf_op jit(solution)/shard_map/ppermute | solution.py:43
  64.0 9.7 %collective-permute-start.9 = (bf16[4,192,192]{2,1,0:T(8,128)(2,1)S(1)}, bf16[4,192,192]{2,1,0:T(8,128)(2,1)S(1)}, u32[]{:S(2)}, u32[]{:S(2)}) collective-permute-start(bf16[4,192,192]{2,1,0:T(8,128)(2,1)S(1)} %collective-permute-done.7), channel_id=1, source_target_pairs={{0,1},{1,2},{2,3},{3,4},{4,5},{5,6},{6,7},{7,0},{8,9},{9,10},{10,1... | collective-permute-start | bytes 884744 | tf_op jit(solution)/shard_map/ppermute | solution.py:43
  86.6 20.4 %collective-permute-start.10 = (bf16[6144,192]{0,1:T(8,128)(2,1)}, bf16[6144,192]{0,1:T(8,128)(2,1)}, u32[]{:S(2)}, u32[]{:S(2)}) collective-permute-start(bf16[6144,192]{0,1:T(8,128)(2,1)} %broadcast_select_fusion.1), channel_id=1, source_target_pairs={{0,128},{128,0},{256,384},{384,256},{1,129},{129,1},{257,385},{385... | collective-permute-start | bytes 7077896 | tf_op jit(solution)/shard_map/ppermute | solution.py:23
  152.1 9.1 %collective-permute-start.11 = (bf16[6144,192]{0,1:T(8,128)(2,1)}, bf16[6144,192]{0,1:T(8,128)(2,1)}, u32[]{:S(2)}, u32[]{:S(2)}) collective-permute-start(bf16[6144,192]{0,1:T(8,128)(2,1)} %fusion.2), channel_id=1, source_target_pairs={{0,128},{128,0},{256,384},{384,256},{1,129},{129,1},{257,385},{385... | collective-permute-start | bytes 7077896 | tf_op jit(solution)/shard_map/ppermute | solution.py:23
  187.7 10.6 %collective-permute-start.12 = (bf16[2,192,192]{2,1,0:T(8,128)(2,1)S(1)}, bf16[2,192,192]{2,1,0:T(8,128)(2,1)S(1)}, u32[]{:S(2)}, u32[]{:S(2)}) collective-permute-start(bf16[2,192,192]{2,1,0:T(8,128)(2,1)S(1)} %fusion.39), channel_id=1, source_target_pairs={{0,1},{1,2},{2,3},{3,4},{4,5},{5,6},{6,7},{7,0},{8,9},{9,10},{10,1... | collective-permute-start | bytes 442376 | tf_op jit(solution)/shard_map/ppermute | solution.py:43
  193.4 8.1 %collective-permute-start.19 = (bf16[2,192,192]{2,1,0:T(8,128)(2,1)S(1)}, bf16[2,192,192]{2,1,0:T(8,128)(2,1)S(1)}, u32[]{:S(2)}, u32[]{:S(2)}) collective-permute-start(bf16[2,192,192]{2,1,0:T(8,128)(2,1)S(1)} %fusion.40), channel_id=1, source_target_pairs={{0,7},{1,0},{2,1},{3,2},{4,3},{5,4},{6,5},{7,6},{8,15},{9,8},{10,9... | collective-permute-start | bytes 442376 | tf_op jit(solution)/shard_map/ppermute | solution.py:43
  199.3 8.6 %collective-permute-start.13 = (bf16[2,192,192]{2,1,0:T(8,128)(2,1)S(1)}, bf16[2,192,192]{2,1,0:T(8,128)(2,1)S(1)}, u32[]{:S(2)}, u32[]{:S(2)}) collective-permute-start(bf16[2,192,192]{2,1,0:T(8,128)(2,1)S(1)} %fusion.37), channel_id=1, source_target_pairs={{0,1},{1,2},{2,3},{3,4},{4,5},{5,6},{6,7},{7,0},{8,9},{9,10},{10,1... | collective-permute-start | bytes 442376 | tf_op jit(solution)/shard_map/ppermute | solution.py:43
  202.5 8.6 %collective-permute-start.20 = (bf16[2,192,192]{2,1,0:T(8,128)(2,1)S(1)}, bf16[2,192,192]{2,1,0:T(8,128)(2,1)S(1)}, u32[]{:S(2)}, u32[]{:S(2)}) collective-permute-start(bf16[2,192,192]{2,1,0:T(8,128)(2,1)S(1)} %fusion.31), channel_id=1, source_target_pairs={{0,7},{1,0},{2,1},{3,2},{4,3},{5,4},{6,5},{7,6},{8,15},{9,8},{10,9... | collective-permute-start | bytes 442376 | tf_op jit(solution)/shard_map/ppermute | solution.py:43
  209.0 8.2 %collective-permute-start.14 = (bf16[2,192,192]{2,1,0:T(8,128)(2,1)S(1)}, bf16[2,192,192]{2,1,0:T(8,128)(2,1)S(1)}, u32[]{:S(2)}, u32[]{:S(2)}) collective-permute-start(bf16[2,192,192]{2,1,0:T(8,128)(2,1)S(1)} %fusion.36), channel_id=1, source_target_pairs={{0,1},{1,2},{2,3},{3,4},{4,5},{5,6},{6,7},{7,0},{8,9},{9,10},{10,1... | collective-permute-start | bytes 442376 | tf_op jit(solution)/shard_map/ppermute | solution.py:43
  220.3 8.6 %collective-permute-start.22 = (bf16[2,192,192]{2,1,0:T(8,128)(2,1)S(1)}, bf16[2,192,192]{2,1,0:T(8,128)(2,1)S(1)}, u32[]{:S(2)}, u32[]{:S(2)}) collective-permute-start(bf16[2,192,192]{2,1,0:T(8,128)(2,1)S(1)} %fusion.29), channel_id=1, source_target_pairs={{0,7},{1,0},{2,1},{3,2},{4,3},{5,4},{6,5},{7,6},{8,15},{9,8},{10,9... | collective-permute-start | bytes 442376 | tf_op jit(solution)/shard_map/ppermute | solution.py:43
  228.9 8.6 %collective-permute-start.23 = (bf16[2,192,192]{2,1,0:T(8,128)(2,1)S(1)}, bf16[2,192,192]{2,1,0:T(8,128)(2,1)S(1)}, u32[]{:S(2)}, u32[]{:S(2)}) collective-permute-start(bf16[2,192,192]{2,1,0:T(8,128)(2,1)S(1)} %fusion.28), channel_id=1, source_target_pairs={{0,7},{1,0},{2,1},{3,2},{4,3},{5,4},{6,5},{7,6},{8,15},{9,8},{10,9... | collective-permute-start | bytes 442376 | tf_op jit(solution)/shard_map/ppermute | solution.py:43
  237.6 8.6 %collective-permute-start.24 = (bf16[2,192,192]{2,1,0:T(8,128)(2,1)S(1)}, bf16[2,192,192]{2,1,0:T(8,128)(2,1)S(1)}, u32[]{:S(2)}, u32[]{:S(2)}) collective-permute-start(bf16[2,192,192]{2,1,0:T(8,128)(2,1)S(1)} %fusion.27), channel_id=1, source_target_pairs={{0,7},{1,0},{2,1},{3,2},{4,3},{5,4},{6,5},{7,6},{8,15},{9,8},{10,9... | collective-permute-start | bytes 442376 | tf_op jit(solution)/shard_map/ppermute | solution.py:43
  260.9 8.1 %collective-permute-start.30 = (bf16[96,192]{1,0:T(8,128)(2,1)S(1)}, bf16[96,192]{1,0:T(8,128)(2,1)S(1)}, u32[]{:S(2)}, u32[]{:S(2)}) collective-permute-start(bf16[96,192]{1,0:T(8,128)(2,1)S(1)} %fusion.54), channel_id=1, source_target_pairs={{0,24},{1,25},{2,26},{3,27},{4,28},{5,29},{6,30},{7,31},{8,0},{9,1... | collective-permute-start | bytes 110600 | tf_op jit(solution)/shard_map/ppermute | solution.py:43
  266.4 8.7 %collective-permute-start.27 = (bf16[96,192]{1,0:T(8,128)(2,1)S(1)}, bf16[96,192]{1,0:T(8,128)(2,1)S(1)}, u32[]{:S(2)}, u32[]{:S(2)}) collective-permute-start(bf16[96,192]{1,0:T(8,128)(2,1)S(1)} %fusion.60), channel_id=1, source_target_pairs={{0,8},{1,9},{2,10},{3,11},{4,12},{5,13},{6,14},{7,15},{8,16},{9,17... | collective-permute-start | bytes 110600 | tf_op jit(solution)/shard_map/ppermute | solution.py:43
  269.0 8.1 %collective-permute-start.31 = (bf16[96,192]{1,0:T(8,128)(2,1)S(1)}, bf16[96,192]{1,0:T(8,128)(2,1)S(1)}, u32[]{:S(2)}, u32[]{:S(2)}) collective-permute-start(bf16[96,192]{1,0:T(8,128)(2,1)S(1)} %fusion.58), channel_id=1, source_target_pairs={{0,24},{1,25},{2,26},{3,27},{4,28},{5,29},{6,30},{7,31},{8,0},{9,1... | collective-permute-start | bytes 110600 | tf_op jit(solution)/shard_map/ppermute | solution.py:43
  305.3 18.9 %collective-permute-start.36 = (f32[192,192]{1,0:T(8,128)S(1)}, f32[192,192]{1,0:T(8,128)S(1)}, u32[]{:S(2)}, u32[]{:S(2)}) collective-permute-start(f32[192,192]{1,0:T(8,128)S(1)} %fusion.90), channel_id=1, source_target_pairs={{0,128},{128,0},{256,384},{384,256},{1,129},{129,1},{257,385},{385... | collective-permute-start | bytes 442376 | tf_op jit(solution)/shard_map/ppermute | solution.py:23
  (23 other events, 324.5 us)
Sparse Core Ops, SparseCore 0:
  123.4 25.5 reduce-scatter.3

commit v3 on v2

--- a/solution.py
+++ b/solution.py
@@ -59,16 +59,18 @@
     return jnp.stack(got), [slot[k] for k in range(n)]
 
 
-def ring_reduce_scatter(blocks, ring):
+def ring_reduce_scatter(blocks, ring, axis=0):
     n = ring.size
     if n == 1:
-        return blocks[0]
+        return lax.index_in_dim(blocks, 0, axis=axis, keepdims=False)
     me = ring.position()
-    rows = blocks.shape[1]
-    upper, lower = blocks[:, : rows // 2], blocks[:, rows // 2 :]
+    split = 1 if axis == 0 else 0
+    rows = blocks.shape[split]
+    upper = lax.slice_in_dim(blocks, 0, rows // 2, axis=split)
+    lower = lax.slice_in_dim(blocks, rows // 2, rows, axis=split)
 
     def pick(part, index):
-        return lax.dynamic_index_in_dim(part, index % n, axis=0, keepdims=False)
+        return lax.dynamic_index_in_dim(part, index % n, axis=axis, keepdims=False)
 
     acc_cw = pick(upper, me - 1)
     acc_ccw = pick(lower, me + 1)
@@ -79,7 +81,8 @@
         acc_ccw = ring.shift(acc_ccw.astype(jnp.bfloat16), -1).astype(jnp.float32) + pick(
             lower, me + 1 + t
         )
-    return jnp.concatenate([acc_cw, acc_ccw], axis=0)
+    out_split = split - 1 if split > axis else split
+    return jnp.concatenate([acc_cw, acc_ccw], axis=out_split)
 
 
 def shards(patches, segments, qkv_weight, cotangent, inner_fsdp):
@@ -108,7 +111,7 @@
     rel_y = (absolute // inner_fsdp - me_y) % outer_fsdp
     rel_z = (absolute % inner_fsdp - me_z) % inner_fsdp
     order = jnp.asarray(slot_z, jnp.int32)[rel_z] * outer_fsdp + jnp.asarray(slot_y, jnp.int32)[rel_y]
-    w_mine_all = jnp.take(flat, order, axis=0).reshape(n_fsdp * rows_w, half)
+    w_mine_all = jnp.take(flat, order, axis=0, mode="clip").reshape(n_fsdp * rows_w, half)
     w_other_all = dp_partner(w_mine_all, 1)
 
     h_mine = jnp.dot(features, w_mine_all, preferred_element_type=jnp.float32)
@@ -119,35 +122,36 @@
         jnp.concatenate([h_other, h_mine], axis=1),
     )
     heads = projected.astype(jnp.bfloat16)
-    query = heads[:, :width_head]
-    own_pairs = heads[:, width_head:]
-    pairs_all, images_all = (
-        lax.all_gather(own_pairs, "seq", axis=0, tiled=True),
-        lax.all_gather(image_ids, "seq", axis=0, tiled=True),
-    )
-    keys_all = pairs_all[:, :width_head]
-    values_all = pairs_all[:, width_head:]
-    scores = contract_last(query, keys_all) * scale
-    allowed = image_ids[:, None] == images_all[None, :]
+    n_rows = features.shape[0]
+    n_x = ring_x.size
+    me_x = ring_x.position()
+    ids_col = jnp.broadcast_to(image_ids.astype(jnp.bfloat16)[:, None], (n_rows, width_head))
+    packed = jnp.concatenate([heads, grad_out, ids_col], axis=1)
+    packed_all = lax.all_gather(packed, "seq", axis=0, tiled=True)
+    query_all = packed_all[:, :width_head]
+    keys_all = packed_all[:, width_head : 2 * width_head]
+    values_all = packed_all[:, 2 * width_head : 3 * width_head]
+    grad_out_all = packed_all[:, 3 * width_head : 4 * width_head]
+    images_all = packed_all[:, 4 * width_head]
+    scores = contract_last(query_all, keys_all) * scale
+    allowed = images_all[:, None] == images_all[None, :]
     highest = jnp.max(jnp.where(allowed, scores, -jnp.inf), axis=1)
     summed = jnp.sum(jnp.where(allowed, jnp.exp(scores - highest[:, None]), 0.0), axis=1)
     log_total = highest + jnp.log(summed)
     attention = jnp.where(allowed, jnp.exp(scores - log_total[:, None]), 0.0)
     attention_low = attention.astype(jnp.bfloat16)
     output = jnp.dot(attention_low, values_all, preferred_element_type=jnp.float32)
-    delta_rows = jnp.sum(grad_out.astype(jnp.float32) * output, axis=1)
-    grad_attention = contract_last(grad_out, values_all)
+    delta_rows = jnp.sum(grad_out_all.astype(jnp.float32) * output, axis=1)
+    grad_attention = contract_last(grad_out_all, values_all)
     grad_scores = (attention * (grad_attention - delta_rows[:, None]) * scale).astype(jnp.bfloat16)
-    grad_query = jnp.dot(grad_scores, keys_all, preferred_element_type=jnp.float32).astype(
-        jnp.bfloat16
-    )
-    partial_pairs = jnp.concatenate(
-        [contract_first(grad_scores, query), contract_first(attention_low, grad_out)], axis=1
-    )
-    grad_pairs = lax.psum_scatter(
-        partial_pairs.astype(jnp.bfloat16), "seq", scatter_dimension=0, tiled=True
-    )
-    grad_heads = jnp.concatenate([grad_query, grad_pairs], axis=1)
+    start = me_x * n_rows
+    own_rows = lax.dynamic_slice_in_dim(grad_scores, start, n_rows, axis=0)
+    own_cols = lax.dynamic_slice_in_dim(grad_scores, start, n_rows, axis=1)
+    own_attention = lax.dynamic_slice_in_dim(attention_low, start, n_rows, axis=1)
+    grad_query = jnp.dot(own_rows, keys_all, preferred_element_type=jnp.float32)
+    grad_key = contract_first(own_cols, query_all)
+    grad_value = contract_first(own_attention, grad_out_all)
+    grad_heads = jnp.concatenate([grad_query, grad_key, grad_value], axis=1).astype(jnp.bfloat16)
 
     g_lo = grad_heads[:, :half]
     g_hi = grad_heads[:, half:]
@@ -158,19 +162,18 @@
         contract_last(g_mine, w_mine_all) + contract_last(g_other, w_other_all)
     ).astype(jnp.bfloat16)
 
-    wg_mine = contract_first(features, g_mine)
-    wg_other = contract_first(features, g_other)
+    blocked = features.reshape(n_rows, n_fsdp, rows_w)
+    wg_mine = jnp.einsum("pjd,pc->jdc", blocked, g_mine, preferred_element_type=jnp.float32)
+    wg_other = jnp.einsum("pjd,pc->jdc", blocked, g_other, preferred_element_type=jnp.float32)
     wg_from_partner = dp_partner(wg_other.astype(jnp.bfloat16), 1)
     wg_chip = wg_mine + wg_from_partner.astype(jnp.float32)
     blocks = wg_chip.reshape(outer_fsdp, inner_fsdp, rows_w, half)
-    over_z = ring_reduce_scatter(jnp.moveaxis(blocks, 1, 0), ring_z)
+    over_z = ring_reduce_scatter(blocks, ring_z, axis=1)
     over_fsdp = ring_reduce_scatter(over_z, ring_y)
 
     stack_x, slot_x = ring_gather(over_fsdp, ring_x)
-    me_x = ring_x.position()
-    n_x = ring_x.size
     rel_x = (jnp.arange(n_x, dtype=jnp.int32) - me_x) % n_x
-    in_order = jnp.take(stack_x, jnp.asarray(slot_x, jnp.int32)[rel_x], axis=0)
+    in_order = jnp.take(stack_x, jnp.asarray(slot_x, jnp.int32)[rel_x], axis=0, mode="clip")
     over_seq = in_order[0]
     for s in range(1, n_x):
         over_seq = over_seq + in_order[s]

time: 334 us -> 274 us (0.82)
  local copies, waits for them, and re-layouts: 45.7 us -> 22.8 us
  waiting for transfers between devices: 65.3 us -> 44.2 us
  between operations: 16.1 us -> 2.05 us
  blocking collectives: 17.5 us -> 13.5 us
    unnamed x2 -> x0, waiting for transfers between devices: 25.4 us -> none
    reshape x2 -> x1, local copies, waits for them, and re-layouts: 14.9 us -> 2.59 us  [shards(): jnp.take(flat, order, axis=0, mode='clip').reshape(n_fsdp * rows_w, half)]
    dot_general x4 -> x2, matrix products: 7.39 us -> 0.44 us  [contract_first(): lax.dot_general(left, right, (((0,), (0,)), ((), ())), preferred_element_...]
    unnamed x1 -> x0, blocking collectives: 6.86 us -> none
    select_n x6 -> x1, other arithmetic: 6.23 us -> 0.01 us  [shards(): jnp.asarray(slot_x, jnp.int32)[rel_x]]
    unnamed x29 -> x28, local copies, waits for them, and re-layouts: 9.88 us -> 4.55 us
    ppermute x33, waiting for transfers between devices: 33.5 us -> 38.4 us  [shift(): return lax.ppermute(x, self.axis, perm=pairs)]
    another operation x0 -> x1, local copies, waits for them, and re-layouts: none -> 4.49 us  [shards(): blocked = features.reshape(n_rows, n_fsdp, rows_w)]
  transfers between devices with their start and end apart: 38 -> 37, of which waited for: 20 -> 18; matrix products, arithmetic and copies ran while one was open for 10% -> 11% of each run, Pallas kernels for 0% -> 0%
where the time goes in v3:
time: 274 us; the launch traced here: 273 us
  starting transfers between devices  152 us (55%)
  waiting for transfers between devices  44.2 us (16%)
  local copies, waits for them, and re-layouts  22.8 us (8%)
  other arithmetic  19.5 us (7%)
  matrix products  18.8 us (7%)
  blocking collectives  13.5 us (5%)
    ppermute x33, starting transfers between devices, shift(): return lax.ppermute(x, self.axis, perm=pairs)  121 us
    ppermute x33, waiting for transfers between devices, shift(): return lax.ppermute(x, self.axis, perm=pairs)  38.4 us
    ppermute x4, starting transfers between devices, dp_partner(): return lax.ppermute(x, 'dp', perm=pairs)  30.3 us
    all_gather x1, blocking collectives, shards(): packed_all = lax.all_gather(packed, 'seq', axis=0, tiled=True)  13.5 us
    dot_general x4, matrix products, contract_last(): lax.dot_general(left, right, (((1,), (1,)), ((), ())), preferred_element_...  6.52 us
    convert_element_type x8, other arithmetic, ring_reduce_scatter(): acc_cw.astype(jnp.bfloat16)  6.36 us
    ppermute x4, waiting for transfers between devices, dp_partner(): return lax.ppermute(x, 'dp', perm=pairs)  5.82 us
  transfers between devices with their start and end apart: 37, of which 18 were waited for; matrix products, arithmetic and copies ran while one was open for 11% of the time, Pallas kernels for 0%

profile of v3, /device:TPU:1, one launch (start us, length us, event | category | flops | bytes accessed | tf_op | source)
XLA Modules:
  0.0 272.5 jit_solution(6914159818152350490)
XLA Ops:
  1.7 5.0 %collective-permute-start = (bf16[192,192]{1,0:T(8,128)(2,1)S(1)}, bf16[192,192]{1,0:T(8,128)(2,1)S(1)}, u32[]{:S(2)}, u32[]{:S(2)}) collective-permute-start(bf16[192,192]{1,0:T(8,128)(2,1)S(1)} %constant_dynamic-slice_fusion), channel_id=1, source_target_pairs={{0,8},{1,9},{2,10},{3,11},{4,12},{5,13},{6,14},{7,15},{8,16},{9,17... | collective-permute-start | bytes 221192 | tf_op jit(solution)/shard_map/ppermute | solution.py:43
  11.7 4.6 %collective-permute-start.2 = (bf16[192,192]{1,0:T(8,128)(2,1)S(1)}, bf16[192,192]{1,0:T(8,128)(2,1)S(1)}, u32[]{:S(2)}, u32[]{:S(2)}) collective-permute-start(bf16[192,192]{1,0:T(8,128)(2,1)S(1)} %collective-permute-done), channel_id=1, source_target_pairs={{0,8},{1,9},{2,10},{3,11},{4,12},{5,13},{6,14},{7,15},{8,16},{9,17... | collective-permute-start | bytes 221192 | tf_op jit(solution)/shard_map/ppermute | solution.py:43
  19.4 3.9 %collective-permute-start.3 = (bf16[4,192,192]{2,1,0:T(8,128)(2,1)S(1)}, bf16[4,192,192]{2,1,0:T(8,128)(2,1)S(1)}, u32[]{:S(2)}, u32[]{:S(2)}) collective-permute-start(bf16[4,192,192]{2,1,0:T(8,128)(2,1)S(1)} %pad_maximum_fusion.1), channel_id=1, source_target_pairs={{0,1},{1,2},{2,3},{3,4},{4,5},{5,6},{6,7},{7,0},{8,9},{9,10},{10,1... | collective-permute-start | bytes 884744 | tf_op jit(solution)/shard_map/ppermute | solution.py:43
  23.3 8.6 %collective-permute-start.4 = (bf16[4,192,192]{2,1,0:T(8,128)(2,1)S(1)}, bf16[4,192,192]{2,1,0:T(8,128)(2,1)S(1)}, u32[]{:S(2)}, u32[]{:S(2)}) collective-permute-start(bf16[4,192,192]{2,1,0:T(8,128)(2,1)S(1)} %pad_maximum_fusion.1), channel_id=1, source_target_pairs={{0,7},{1,0},{2,1},{3,2},{4,3},{5,4},{6,5},{7,6},{8,15},{9,8},{10,9... | collective-permute-start | bytes 884744 | tf_op jit(solution)/shard_map/ppermute | solution.py:43
  32.0 4.4 %collective-permute-done.3 = bf16[4,192,192]{2,1,0:T(8,128)(2,1)S(1)} collective-permute-done((bf16[4,192,192]{2,1,0:T(8,128)(2,1)S(1)}, bf16[4,192,192]{2,1,0:T(8,128)(2,1)S(1)}, u32[]{:S(2)}, u32[]{:S(2)}) %collective-permute-start.3) | collective-permute-done | bytes 294944 | tf_op jit(solution)/shard_map/ppermute | solution.py:43
  38.4 4.6 %collective-permute-start.6 = (bf16[4,192,192]{2,1,0:T(8,128)(2,1)S(1)}, bf16[4,192,192]{2,1,0:T(8,128)(2,1)S(1)}, u32[]{:S(2)}, u32[]{:S(2)}) collective-permute-start(bf16[4,192,192]{2,1,0:T(8,128)(2,1)S(1)} %collective-permute-done.4), channel_id=1, source_target_pairs={{0,7},{1,0},{2,1},{3,2},{4,3},{5,4},{6,5},{7,6},{8,15},{9,8},{10,9... | collective-permute-start | bytes 884744 | tf_op jit(solution)/shard_map/ppermute | solution.py:43
  48.4 4.6 %collective-permute-start.8 = (bf16[4,192,192]{2,1,0:T(8,128)(2,1)S(1)}, bf16[4,192,192]{2,1,0:T(8,128)(2,1)S(1)}, u32[]{:S(2)}, u32[]{:S(2)}) collective-permute-start(bf16[4,192,192]{2,1,0:T(8,128)(2,1)S(1)} %collective-permute-done.6), channel_id=1, source_target_pairs={{0,7},{1,0},{2,1},{3,2},{4,3},{5,4},{6,5},{7,6},{8,15},{9,8},{10,9... | collective-permute-start | bytes 884744 | tf_op jit(solution)/shard_map/ppermute | solution.py:43
  58.2 7.7 %collective-permute-done.9 = bf16[4,192,192]{2,1,0:T(8,128)(2,1)S(1)} collective-permute-done((bf16[4,192,192]{2,1,0:T(8,128)(2,1)S(1)}, bf16[4,192,192]{2,1,0:T(8,128)(2,1)S(1)}, u32[]{:S(2)}, u32[]{:S(2)}) %collective-permute-start.9) | collective-permute-done | bytes 294944 | tf_op jit(solution)/shard_map/ppermute | solution.py:43
  72.8 8.9 %collective-permute-start.10 = (bf16[6144,192]{0,1:T(8,128)(2,1)}, bf16[6144,192]{0,1:T(8,128)(2,1)}, u32[]{:S(2)}, u32[]{:S(2)}) collective-permute-start(bf16[6144,192]{0,1:T(8,128)(2,1)} %copy.30), channel_id=1, source_target_pairs={{0,128},{128,0},{256,384},{384,256},{1,129},{129,1},{257,385},{385... | collective-permute-start | bytes 7077896 | tf_op jit(solution)/shard_map/ppermute | solution.py:23
  81.7 4.5 %copy.44 = bf16[1,192,6144]{1,2,0:T(8,128)(2,1)} copy(bf16[1,192,6144]{2,1,0:T(8,128)(2,1)} %param.7) | data formatting | bytes 4718592 | tf_op jit(solution)/shard_map/reshape;squeeze | solution.py:165
  91.6 13.5 %all_gather.3 = bf16[768,640]{1,0:T(8,128)(2,1)S(1)} all-gather(bf16[192,640]{1,0:T(8,128)(2,1)S(1)} %pad_maximum_fusion.2), channel_id=1, replica_groups=mesh['dp'=4,'seq'=4,'fsdp'=32] {'seq'}, dimensions={0}, use_global_device_ids=true | all-gather | bytes 1228800 | tf_op jit(solution)/shard_map/all_gather | solution.py:130
  131.7 4.6 %collective-permute-start.19 = (bf16[2,192,192]{2,1,0:T(8,128)(2,1)S(1)}, bf16[2,192,192]{2,1,0:T(8,128)(2,1)S(1)}, u32[]{:S(2)}, u32[]{:S(2)}) collective-permute-start(bf16[2,192,192]{2,1,0:T(8,128)(2,1)S(1)} %fusion.35), channel_id=1, source_target_pairs={{0,7},{1,0},{2,1},{3,2},{4,3},{5,4},{6,5},{7,6},{8,15},{9,8},{10,9... | collective-permute-start | bytes 442376 | tf_op jit(solution)/shard_map/ppermute | solution.py:43
  141.7 4.6 %collective-permute-start.20 = (bf16[2,192,192]{2,1,0:T(8,128)(2,1)S(1)}, bf16[2,192,192]{2,1,0:T(8,128)(2,1)S(1)}, u32[]{:S(2)}, u32[]{:S(2)}) collective-permute-start(bf16[2,192,192]{2,1,0:T(8,128)(2,1)S(1)} %fusion.24), channel_id=1, source_target_pairs={{0,7},{1,0},{2,1},{3,2},{4,3},{5,4},{6,5},{7,6},{8,15},{9,8},{10,9... | collective-permute-start | bytes 442376 | tf_op jit(solution)/shard_map/ppermute | solution.py:43
  150.9 4.6 %collective-permute-start.21 = (bf16[2,192,192]{2,1,0:T(8,128)(2,1)S(1)}, bf16[2,192,192]{2,1,0:T(8,128)(2,1)S(1)}, u32[]{:S(2)}, u32[]{:S(2)}) collective-permute-start(bf16[2,192,192]{2,1,0:T(8,128)(2,1)S(1)} %fusion.23), channel_id=1, source_target_pairs={{0,7},{1,0},{2,1},{3,2},{4,3},{5,4},{6,5},{7,6},{8,15},{9,8},{10,9... | collective-permute-start | bytes 442376 | tf_op jit(solution)/shard_map/ppermute | solution.py:43
  158.6 4.6 %collective-permute-start.22 = (bf16[2,192,192]{2,1,0:T(8,128)(2,1)S(1)}, bf16[2,192,192]{2,1,0:T(8,128)(2,1)S(1)}, u32[]{:S(2)}, u32[]{:S(2)}) collective-permute-start(bf16[2,192,192]{2,1,0:T(8,128)(2,1)S(1)} %fusion.22), channel_id=1, source_target_pairs={{0,7},{1,0},{2,1},{3,2},{4,3},{5,4},{6,5},{7,6},{8,15},{9,8},{10,9... | collective-permute-start | bytes 442376 | tf_op jit(solution)/shard_map/ppermute | solution.py:43
  167.3 4.6 %collective-permute-start.23 = (bf16[2,192,192]{2,1,0:T(8,128)(2,1)S(1)}, bf16[2,192,192]{2,1,0:T(8,128)(2,1)S(1)}, u32[]{:S(2)}, u32[]{:S(2)}) collective-permute-start(bf16[2,192,192]{2,1,0:T(8,128)(2,1)S(1)} %fusion.21), channel_id=1, source_target_pairs={{0,7},{1,0},{2,1},{3,2},{4,3},{5,4},{6,5},{7,6},{8,15},{9,8},{10,9... | collective-permute-start | bytes 442376 | tf_op jit(solution)/shard_map/ppermute | solution.py:43
  175.9 4.6 %collective-permute-start.24 = (bf16[2,192,192]{2,1,0:T(8,128)(2,1)S(1)}, bf16[2,192,192]{2,1,0:T(8,128)(2,1)S(1)}, u32[]{:S(2)}, u32[]{:S(2)}) collective-permute-start(bf16[2,192,192]{2,1,0:T(8,128)(2,1)S(1)} %fusion.20), channel_id=1, source_target_pairs={{0,7},{1,0},{2,1},{3,2},{4,3},{5,4},{6,5},{7,6},{8,15},{9,8},{10,9... | collective-permute-start | bytes 442376 | tf_op jit(solution)/shard_map/ppermute | solution.py:43
  184.6 4.6 %collective-permute-start.25 = (bf16[2,192,192]{2,1,0:T(8,128)(2,1)S(1)}, bf16[2,192,192]{2,1,0:T(8,128)(2,1)S(1)}, u32[]{:S(2)}, u32[]{:S(2)}) collective-permute-start(bf16[2,192,192]{2,1,0:T(8,128)(2,1)S(1)} %fusion.19), channel_id=1, source_target_pairs={{0,7},{1,0},{2,1},{3,2},{4,3},{5,4},{6,5},{7,6},{8,15},{9,8},{10,9... | collective-permute-start | bytes 442376 | tf_op jit(solution)/shard_map/ppermute | solution.py:43
  191.9 4.4 %collective-permute-start.29 = (bf16[96,192]{1,0:T(8,128)(2,1)S(1)}, bf16[96,192]{1,0:T(8,128)(2,1)S(1)}, u32[]{:S(2)}, u32[]{:S(2)}) collective-permute-start(bf16[96,192]{1,0:T(8,128)(2,1)S(1)} %fusion.64), channel_id=1, source_target_pairs={{0,24},{1,25},{2,26},{3,27},{4,28},{5,29},{6,30},{7,31},{8,0},{9,1... | collective-permute-start | bytes 110600 | tf_op jit(solution)/shard_map/ppermute | solution.py:43
  198.5 9.6 %collective-permute-start.30 = (bf16[96,192]{1,0:T(8,128)(2,1)S(1)}, bf16[96,192]{1,0:T(8,128)(2,1)S(1)}, u32[]{:S(2)}, u32[]{:S(2)}) collective-permute-start(bf16[96,192]{1,0:T(8,128)(2,1)S(1)} %fusion.55), channel_id=1, source_target_pairs={{0,24},{1,25},{2,26},{3,27},{4,28},{5,29},{6,30},{7,31},{8,0},{9,1... | collective-permute-start | bytes 110600 | tf_op jit(solution)/shard_map/ppermute | solution.py:43
  210.1 5.6 %collective-permute-start.31 = (bf16[96,192]{1,0:T(8,128)(2,1)S(1)}, bf16[96,192]{1,0:T(8,128)(2,1)S(1)}, u32[]{:S(2)}, u32[]{:S(2)}) collective-permute-start(bf16[96,192]{1,0:T(8,128)(2,1)S(1)} %fusion.59), channel_id=1, source_target_pairs={{0,24},{1,25},{2,26},{3,27},{4,28},{5,29},{6,30},{7,31},{8,0},{9,1... | collective-permute-start | bytes 110600 | tf_op jit(solution)/shard_map/ppermute | solution.py:43
  234.1 5.1 %collective-permute-done.34 = f32[192,192]{1,0:T(8,128)} collective-permute-done((f32[192,192]{1,0:T(8,128)}, f32[192,192]{1,0:T(8,128)}, u32[]{:S(2)}, u32[]{:S(2)}) %collective-permute-start.34) | collective-permute-done | bytes 147488 | tf_op jit(solution)/shard_map/ppermute | solution.py:43
  251.8 15.9 %collective-permute-start.36 = (f32[192,192]{1,0:T(8,128)S(1)}, f32[192,192]{1,0:T(8,128)S(1)}, u32[]{:S(2)}, u32[]{:S(2)}) collective-permute-start(f32[192,192]{1,0:T(8,128)S(1)} %fusion.86), channel_id=1, source_target_pairs={{0,128},{128,0},{256,384},{384,256},{1,129},{129,1},{257,385},{385... | collective-permute-start | bytes 442376 | tf_op jit(solution)/shard_map/ppermute | solution.py:23
  267.7 4.0 %fusion.1 = bf16[1,192,6144]{2,1,0:T(8,128)(2,1)} fusion(f32[192,6144]{1,0:T(8,128)S(1)} %fusion.77, bf16[6144,192]{0,1:T(8,128)(2,1)} %collective-permute-done.10, pred[]{:T(512)S(6)} %eq.55, bf16[192,128]{1,0:T(8,128)(2,1)S(1)} %convolution_convert_fusion.1, bf16[192,128]{1,0:T(8,128)(2,1)S(1)} %convolution_convert_fusion.2, ...), kind=kOutput, calls=%fused_computation.6 | convolution fusion | flops 455675904 | bytes 9584641 | tf_op jit(solution)/shard_map/dot_general | solution.py:16
  (149 shorter events, 123.7 us)
Async XLA Ops:
  1.7 10.1 %collective-permute-start = (bf16[192,192]{1,0:T(8,128)(2,1)S(1)}, bf16[192,192]{1,0:T(8,128)(2,1)S(1)}, u32[]{:S(2)}, u32[]{:S(2)}) collective-permute-start(bf16[192,192]{1,0:T(8,128)(2,1)S(1)} %constant_dynamic-slice_fusion), channel_id=1, source_target_pairs={{0,8},{1,9},{2,10},{3,11},{4,12},{5,13},{6,14},{7,15},{8,16},{9,17... | collective-permute-start | bytes 221192 | tf_op jit(solution)/shard_map/ppermute | solution.py:43
  6.7 9.9 %collective-permute-start.1 = (bf16[192,192]{1,0:T(8,128)(2,1)S(1)}, bf16[192,192]{1,0:T(8,128)(2,1)S(1)}, u32[]{:S(2)}, u32[]{:S(2)}) collective-permute-start(bf16[192,192]{1,0:T(8,128)(2,1)S(1)} %constant_dynamic-slice_fusion), channel_id=1, source_target_pairs={{0,24},{1,25},{2,26},{3,27},{4,28},{5,29},{6,30},{7,31},{8,0},{9,1... | collective-permute-start | bytes 221192 | tf_op jit(solution)/shard_map/ppermute | solution.py:43
  19.4 17.0 %collective-permute-start.3 = (bf16[4,192,192]{2,1,0:T(8,128)(2,1)S(1)}, bf16[4,192,192]{2,1,0:T(8,128)(2,1)S(1)}, u32[]{:S(2)}, u32[]{:S(2)}) collective-permute-start(bf16[4,192,192]{2,1,0:T(8,128)(2,1)S(1)} %pad_maximum_fusion.1), channel_id=1, source_target_pairs={{0,1},{1,2},{2,3},{3,4},{4,5},{5,6},{6,7},{7,0},{8,9},{9,10},{10,1... | collective-permute-start | bytes 884744 | tf_op jit(solution)/shard_map/ppermute | solution.py:43
  23.3 15.0 %collective-permute-start.4 = (bf16[4,192,192]{2,1,0:T(8,128)(2,1)S(1)}, bf16[4,192,192]{2,1,0:T(8,128)(2,1)S(1)}, u32[]{:S(2)}, u32[]{:S(2)}) collective-permute-start(bf16[4,192,192]{2,1,0:T(8,128)(2,1)S(1)} %pad_maximum_fusion.1), channel_id=1, source_target_pairs={{0,7},{1,0},{2,1},{3,2},{4,3},{5,4},{6,5},{7,6},{8,15},{9,8},{10,9... | collective-permute-start | bytes 884744 | tf_op jit(solution)/shard_map/ppermute | solution.py:43
  36.4 10.1 %collective-permute-start.5 = (bf16[4,192,192]{2,1,0:T(8,128)(2,1)S(1)}, bf16[4,192,192]{2,1,0:T(8,128)(2,1)S(1)}, u32[]{:S(2)}, u32[]{:S(2)}) collective-permute-start(bf16[4,192,192]{2,1,0:T(8,128)(2,1)S(1)} %collective-permute-done.3), channel_id=1, source_target_pairs={{0,1},{1,2},{2,3},{3,4},{4,5},{5,6},{6,7},{7,0},{8,9},{9,10},{10,1... | collective-permute-start | bytes 884744 | tf_op jit(solution)/shard_map/ppermute | solution.py:43
  38.4 10.1 %collective-permute-start.6 = (bf16[4,192,192]{2,1,0:T(8,128)(2,1)S(1)}, bf16[4,192,192]{2,1,0:T(8,128)(2,1)S(1)}, u32[]{:S(2)}, u32[]{:S(2)}) collective-permute-start(bf16[4,192,192]{2,1,0:T(8,128)(2,1)S(1)} %collective-permute-done.4), channel_id=1, source_target_pairs={{0,7},{1,0},{2,1},{3,2},{4,3},{5,4},{6,5},{7,6},{8,15},{9,8},{10,9... | collective-permute-start | bytes 884744 | tf_op jit(solution)/shard_map/ppermute | solution.py:43
  46.5 9.7 %collective-permute-start.7 = (bf16[4,192,192]{2,1,0:T(8,128)(2,1)S(1)}, bf16[4,192,192]{2,1,0:T(8,128)(2,1)S(1)}, u32[]{:S(2)}, u32[]{:S(2)}) collective-permute-start(bf16[4,192,192]{2,1,0:T(8,128)(2,1)S(1)} %collective-permute-done.5), channel_id=1, source_target_pairs={{0,1},{1,2},{2,3},{3,4},{4,5},{5,6},{6,7},{7,0},{8,9},{9,10},{10,1... | collective-permute-start | bytes 884744 | tf_op jit(solution)/shard_map/ppermute | solution.py:43
  48.4 9.7 %collective-permute-start.8 = (bf16[4,192,192]{2,1,0:T(8,128)(2,1)S(1)}, bf16[4,192,192]{2,1,0:T(8,128)(2,1)S(1)}, u32[]{:S(2)}, u32[]{:S(2)}) collective-permute-start(bf16[4,192,192]{2,1,0:T(8,128)(2,1)S(1)} %collective-permute-done.6), channel_id=1, source_target_pairs={{0,7},{1,0},{2,1},{3,2},{4,3},{5,4},{6,5},{7,6},{8,15},{9,8},{10,9... | collective-permute-start | bytes 884744 | tf_op jit(solution)/shard_map/ppermute | solution.py:43
  56.2 9.7 %collective-permute-start.9 = (bf16[4,192,192]{2,1,0:T(8,128)(2,1)S(1)}, bf16[4,192,192]{2,1,0:T(8,128)(2,1)S(1)}, u32[]{:S(2)}, u32[]{:S(2)}) collective-permute-start(bf16[4,192,192]{2,1,0:T(8,128)(2,1)S(1)} %collective-permute-done.7), channel_id=1, source_target_pairs={{0,1},{1,2},{2,3},{3,4},{4,5},{5,6},{6,7},{7,0},{8,9},{9,10},{10,1... | collective-permute-start | bytes 884744 | tf_op jit(solution)/shard_map/ppermute | solution.py:43
  72.8 16.1 %collective-permute-start.10 = (bf16[6144,192]{0,1:T(8,128)(2,1)}, bf16[6144,192]{0,1:T(8,128)(2,1)}, u32[]{:S(2)}, u32[]{:S(2)}) collective-permute-start(bf16[6144,192]{0,1:T(8,128)(2,1)} %copy.30), channel_id=1, source_target_pairs={{0,128},{128,0},{256,384},{384,256},{1,129},{129,1},{257,385},{385... | collective-permute-start | bytes 7077896 | tf_op jit(solution)/shard_map/ppermute | solution.py:23
  112.1 9.0 %collective-permute-start.11 = (bf16[32,192,192]{2,1,0:T(8,128)(2,1)}, bf16[32,192,192]{2,1,0:T(8,128)(2,1)}, u32[]{:S(2)}, u32[]{:S(2)}) collective-permute-start(bf16[32,192,192]{2,1,0:T(8,128)(2,1)} %convert_bitcast_fusion), channel_id=1, source_target_pairs={{0,128},{128,0},{256,384},{384,256},{1,129},{129,1},{257,385},{385... | collective-permute-start | bytes 7077896 | tf_op jit(solution)/shard_map/ppermute | solution.py:23
  128.1 9.3 %collective-permute-start.12 = (bf16[2,192,192]{2,1,0:T(8,128)(2,1)S(1)}, bf16[2,192,192]{2,1,0:T(8,128)(2,1)}, u32[]{:S(2)}, u32[]{:S(2)}) collective-permute-start(bf16[2,192,192]{2,1,0:T(8,128)(2,1)S(1)} %fusion.36), channel_id=1, source_target_pairs={{0,1},{1,2},{2,3},{3,4},{4,5},{5,6},{6,7},{7,0},{8,9},{9,10},{10,1... | collective-permute-start | bytes 442376 | tf_op jit(solution)/shard_map/ppermute | solution.py:43
  131.7 8.9 %collective-permute-start.19 = (bf16[2,192,192]{2,1,0:T(8,128)(2,1)S(1)}, bf16[2,192,192]{2,1,0:T(8,128)(2,1)S(1)}, u32[]{:S(2)}, u32[]{:S(2)}) collective-permute-start(bf16[2,192,192]{2,1,0:T(8,128)(2,1)S(1)} %fusion.35), channel_id=1, source_target_pairs={{0,7},{1,0},{2,1},{3,2},{4,3},{5,4},{6,5},{7,6},{8,15},{9,8},{10,9... | collective-permute-start | bytes 442376 | tf_op jit(solution)/shard_map/ppermute | solution.py:43
  138.6 8.3 %collective-permute-start.13 = (bf16[2,192,192]{2,1,0:T(8,128)(2,1)S(1)}, bf16[2,192,192]{2,1,0:T(8,128)(2,1)S(1)}, u32[]{:S(2)}, u32[]{:S(2)}) collective-permute-start(bf16[2,192,192]{2,1,0:T(8,128)(2,1)S(1)} %fusion.30), channel_id=1, source_target_pairs={{0,1},{1,2},{2,3},{3,4},{4,5},{5,6},{6,7},{7,0},{8,9},{9,10},{10,1... | collective-permute-start | bytes 442376 | tf_op jit(solution)/shard_map/ppermute | solution.py:43
  141.7 8.1 %collective-permute-start.20 = (bf16[2,192,192]{2,1,0:T(8,128)(2,1)S(1)}, bf16[2,192,192]{2,1,0:T(8,128)(2,1)S(1)}, u32[]{:S(2)}, u32[]{:S(2)}) collective-permute-start(bf16[2,192,192]{2,1,0:T(8,128)(2,1)S(1)} %fusion.24), channel_id=1, source_target_pairs={{0,7},{1,0},{2,1},{3,2},{4,3},{5,4},{6,5},{7,6},{8,15},{9,8},{10,9... | collective-permute-start | bytes 442376 | tf_op jit(solution)/shard_map/ppermute | solution.py:43
  158.6 8.6 %collective-permute-start.22 = (bf16[2,192,192]{2,1,0:T(8,128)(2,1)S(1)}, bf16[2,192,192]{2,1,0:T(8,128)(2,1)S(1)}, u32[]{:S(2)}, u32[]{:S(2)}) collective-permute-start(bf16[2,192,192]{2,1,0:T(8,128)(2,1)S(1)} %fusion.22), channel_id=1, source_target_pairs={{0,7},{1,0},{2,1},{3,2},{4,3},{5,4},{6,5},{7,6},{8,15},{9,8},{10,9... | collective-permute-start | bytes 442376 | tf_op jit(solution)/shard_map/ppermute | solution.py:43
  167.3 8.6 %collective-permute-start.23 = (bf16[2,192,192]{2,1,0:T(8,128)(2,1)S(1)}, bf16[2,192,192]{2,1,0:T(8,128)(2,1)S(1)}, u32[]{:S(2)}, u32[]{:S(2)}) collective-permute-start(bf16[2,192,192]{2,1,0:T(8,128)(2,1)S(1)} %fusion.21), channel_id=1, source_target_pairs={{0,7},{1,0},{2,1},{3,2},{4,3},{5,4},{6,5},{7,6},{8,15},{9,8},{10,9... | collective-permute-start | bytes 442376 | tf_op jit(solution)/shard_map/ppermute | solution.py:43
  175.9 8.6 %collective-permute-start.24 = (bf16[2,192,192]{2,1,0:T(8,128)(2,1)S(1)}, bf16[2,192,192]{2,1,0:T(8,128)(2,1)S(1)}, u32[]{:S(2)}, u32[]{:S(2)}) collective-permute-start(bf16[2,192,192]{2,1,0:T(8,128)(2,1)S(1)} %fusion.20), channel_id=1, source_target_pairs={{0,7},{1,0},{2,1},{3,2},{4,3},{5,4},{6,5},{7,6},{8,15},{9,8},{10,9... | collective-permute-start | bytes 442376 | tf_op jit(solution)/shard_map/ppermute | solution.py:43
  196.4 11.7 %collective-permute-start.26 = (bf16[96,192]{1,0:T(8,128)(2,1)S(1)}, bf16[96,192]{1,0:T(8,128)(2,1)S(1)}, u32[]{:S(2)}, u32[]{:S(2)}) collective-permute-start(bf16[96,192]{1,0:T(8,128)(2,1)S(1)} %fusion.63), channel_id=1, source_target_pairs={{0,8},{1,9},{2,10},{3,11},{4,12},{5,13},{6,14},{7,15},{8,16},{9,17... | collective-permute-start | bytes 110600 | tf_op jit(solution)/shard_map/ppermute | solution.py:43
  198.5 11.5 %collective-permute-start.30 = (bf16[96,192]{1,0:T(8,128)(2,1)S(1)}, bf16[96,192]{1,0:T(8,128)(2,1)S(1)}, u32[]{:S(2)}, u32[]{:S(2)}) collective-permute-start(bf16[96,192]{1,0:T(8,128)(2,1)S(1)} %fusion.55), channel_id=1, source_target_pairs={{0,24},{1,25},{2,26},{3,27},{4,28},{5,29},{6,30},{7,31},{8,0},{9,1... | collective-permute-start | bytes 110600 | tf_op jit(solution)/shard_map/ppermute | solution.py:43
  210.1 8.6 %collective-permute-start.31 = (bf16[96,192]{1,0:T(8,128)(2,1)S(1)}, bf16[96,192]{1,0:T(8,128)(2,1)S(1)}, u32[]{:S(2)}, u32[]{:S(2)}) collective-permute-start(bf16[96,192]{1,0:T(8,128)(2,1)S(1)} %fusion.59), channel_id=1, source_target_pairs={{0,24},{1,25},{2,26},{3,27},{4,28},{5,29},{6,30},{7,31},{8,0},{9,1... | collective-permute-start | bytes 110600 | tf_op jit(solution)/shard_map/ppermute | solution.py:43
  223.3 7.9 %collective-permute-start.32 = (f32[192,192]{1,0:T(8,128)}, f32[192,192]{1,0:T(8,128)}, u32[]{:S(2)}, u32[]{:S(2)}) collective-permute-start(f32[192,192]{1,0:T(8,128)} %get-tuple-element.5), channel_id=1, source_target_pairs={{0,32},{32,64},{64,96},{96,0},{1,33},{33,65},{65,97},{97,1},{2,34}... | collective-permute-start | bytes 442376 | tf_op jit(solution)/shard_map/ppermute | solution.py:43
  231.3 7.9 %collective-permute-start.34 = (f32[192,192]{1,0:T(8,128)}, f32[192,192]{1,0:T(8,128)}, u32[]{:S(2)}, u32[]{:S(2)}) collective-permute-start(f32[192,192]{1,0:T(8,128)} %collective-permute-done.32), channel_id=1, source_target_pairs={{0,32},{32,64},{64,96},{96,0},{1,33},{33,65},{65,97},{97,1},{2,34}... | collective-permute-start | bytes 442376 | tf_op jit(solution)/shard_map/ppermute | solution.py:43
  251.8 19.9 %collective-permute-start.36 = (f32[192,192]{1,0:T(8,128)S(1)}, f32[192,192]{1,0:T(8,128)S(1)}, u32[]{:S(2)}, u32[]{:S(2)}) collective-permute-start(f32[192,192]{1,0:T(8,128)S(1)} %fusion.86), channel_id=1, source_target_pairs={{0,128},{128,0},{256,384},{384,256},{1,129},{129,1},{257,385},{385... | collective-permute-start | bytes 442376 | tf_op jit(solution)/shard_map/ppermute | solution.py:23
  (24 other events, 217.3 us)

commit v4 on v3

--- a/solution.py
+++ b/solution.py
@@ -61,28 +61,29 @@
 
 def ring_reduce_scatter(blocks, ring, axis=0):
     n = ring.size
+    me = ring.position()
+
+    def pick(index):
+        return lax.dynamic_index_in_dim(blocks, index % n, axis=axis, keepdims=False)
+
+    total = pick(me)
     if n == 1:
-        return lax.index_in_dim(blocks, 0, axis=axis, keepdims=False)
-    me = ring.position()
-    split = 1 if axis == 0 else 0
-    rows = blocks.shape[split]
-    upper = lax.slice_in_dim(blocks, 0, rows // 2, axis=split)
-    lower = lax.slice_in_dim(blocks, rows // 2, rows, axis=split)
-
-    def pick(part, index):
-        return lax.dynamic_index_in_dim(part, index % n, axis=axis, keepdims=False)
-
-    acc_cw = pick(upper, me - 1)
-    acc_ccw = pick(lower, me + 1)
-    for t in range(1, n):
-        acc_cw = ring.shift(acc_cw.astype(jnp.bfloat16), 1).astype(jnp.float32) + pick(
-            upper, me - 1 - t
-        )
-        acc_ccw = ring.shift(acc_ccw.astype(jnp.bfloat16), -1).astype(jnp.float32) + pick(
-            lower, me + 1 + t
-        )
-    out_split = split - 1 if split > axis else split
-    return jnp.concatenate([acc_cw, acc_ccw], axis=out_split)
+        return total
+    up, down = n // 2, (n - 1) // 2
+    acc = pick(me + up)
+    for t in range(1, up + 1):
+        acc = ring.shift(acc.astype(jnp.bfloat16), 1).astype(jnp.float32)
+        if t < up:
+            acc = acc + pick(me + up - t)
+    total = total + acc
+    if down:
+        acc = pick(me - down)
+        for t in range(1, down + 1):
+            acc = ring.shift(acc.astype(jnp.bfloat16), -1).astype(jnp.float32)
+            if t < down:
+                acc = acc + pick(me - down + t)
+        total = total + acc
+    return total
 
 
 def shards(patches, segments, qkv_weight, cotangent, inner_fsdp):
@@ -171,20 +172,18 @@
     over_z = ring_reduce_scatter(blocks, ring_z, axis=1)
     over_fsdp = ring_reduce_scatter(over_z, ring_y)
 
-    stack_x, slot_x = ring_gather(over_fsdp, ring_x)
-    rel_x = (jnp.arange(n_x, dtype=jnp.int32) - me_x) % n_x
-    in_order = jnp.take(stack_x, jnp.asarray(slot_x, jnp.int32)[rel_x], axis=0, mode="clip")
-    over_seq = in_order[0]
-    for s in range(1, n_x):
-        over_seq = over_seq + in_order[s]
-    if lax.axis_size("dp") > 2:
-        over_seq = over_seq + dp_partner(over_seq, 2)
-    other_half = dp_partner(over_seq, 1)
-    weight_grad = jnp.where(
-        first,
-        jnp.concatenate([over_seq, other_half], axis=1),
-        jnp.concatenate([other_half, over_seq], axis=1),
-    )
+    by_seq = lax.all_gather(over_fsdp, "seq", axis=0, tiled=False)
+    over_seq = by_seq[0]
+    for s_i in range(1, by_seq.shape[0]):
+        over_seq = over_seq + by_seq[s_i]
+    by_dp = lax.all_gather(over_seq, "dp", axis=0, tiled=False)
+    halves = []
+    for c in range(2):
+        part = by_dp[c]
+        for d in range(c + 2, by_dp.shape[0], 2):
+            part = part + by_dp[d]
+        halves.append(part)
+    weight_grad = jnp.concatenate(halves, axis=1)
     return (input_grad[None], weight_grad)
 
 

time: 274 us -> 248 us (0.905)
  starting transfers between devices: 152 us -> 90.3 us
  blocking collectives: 13.5 us -> 41.1 us
  local copies, waits for them, and re-layouts: 22.8 us -> 42.6 us
  waiting for transfers between devices: 44.2 us -> 34.4 us
  other arithmetic: 19.5 us -> 14.3 us
  matrix products: 18.8 us -> 22.6 us
    ppermute x33 -> x20, starting transfers between devices: 121 us -> 78 us  [shift(): return lax.ppermute(x, self.axis, perm=pairs)]
    all_gather x0 -> x2, blocking collectives: none -> 27.6 us  [the longest x1 16.2 us: shards(): by_dp = lax.all_gather(over_seq, 'dp', axis=0, tiled=False)]
    dynamic_slice x0 -> x8, local copies, waits for them, and re-layouts: none -> 19.7 us  [pick(): lax.dynamic_index_in_dim(blocks, index % n, axis=axis, keepdims=False)]
    ppermute x4 -> x2, starting transfers between devices: 30.3 us -> 12.3 us  [dp_partner(): return lax.ppermute(x, 'dp', perm=pairs)]
    ppermute x33 -> x20, waiting for transfers between devices: 38.4 us -> 29 us  [shift(): return lax.ppermute(x, self.axis, perm=pairs)]
    dot_general x0 -> x1, matrix products: none -> 5.36 us  [shards(): jnp.einsum('pjd,pc->jdc', blocked, g_mine, preferred_element_type=jnp.flo...]
    unnamed x28 -> x22, local copies, waits for them, and re-layouts: 4.55 us -> 9.45 us
    add x7 -> x4, other arithmetic: 5.48 us -> 1.59 us  [the longest x2 1.49 us: ring_reduce_scatter(): total = total + acc]
  transfers between devices with their start and end apart: 37 -> 22, of which waited for: 18 -> 9; matrix products, arithmetic and copies ran while one was open for 11% -> 19% of each run, Pallas kernels for 0% -> 0%
where the time goes in v4:
time: 248 us; the launch traced here: 247 us
  starting transfers between devices  90.3 us (36%)
  local copies, waits for them, and re-layouts  42.6 us (17%)
  blocking collectives  41.1 us (17%)
  waiting for transfers between devices  34.4 us (14%)
  matrix products  22.6 us (9%)
  other arithmetic  14.3 us (6%)
    ppermute x20, starting transfers between devices, shift(): return lax.ppermute(x, self.axis, perm=pairs)  78 us
    ppermute x20, waiting for transfers between devices, shift(): return lax.ppermute(x, self.axis, perm=pairs)  29 us
    dynamic_slice x8, local copies, waits for them, and re-layouts, pick(): lax.dynamic_index_in_dim(blocks, index % n, axis=axis, keepdims=False)  19.7 us
    all_gather x1, blocking collectives, shards(): by_dp = lax.all_gather(over_seq, 'dp', axis=0, tiled=False)  16.2 us
    all_gather x1, blocking collectives, shards(): packed_all = lax.all_gather(packed, 'seq', axis=0, tiled=True)  13.5 us
    ppermute x2, starting transfers between devices, dp_partner(): return lax.ppermute(x, 'dp', perm=pairs)  12.3 us
    all_gather x1, blocking collectives, shards(): by_seq = lax.all_gather(over_fsdp, 'seq', axis=0, tiled=False)  11.4 us
    unnamed x22, local copies, waits for them, and re-layouts  9.45 us
  transfers between devices with their start and end apart: 22, of which 9 were waited for; matrix products, arithmetic and copies ran while one was open for 19% of the time, Pallas kernels for 0%

profile of v4, /device:TPU:1, one launch (start us, length us, event | category | flops | bytes accessed | tf_op | source)
XLA Modules:
  0.0 246.8 jit_solution(2830698702119070671)
XLA Ops:
  1.6 5.0 %collective-permute-start = (bf16[192,192]{1,0:T(8,128)(2,1)S(1)}, bf16[192,192]{1,0:T(8,128)(2,1)S(1)}, u32[]{:S(2)}, u32[]{:S(2)}) collective-permute-start(bf16[192,192]{1,0:T(8,128)(2,1)S(1)} %constant_dynamic-slice_fusion.8), channel_id=1, source_target_pairs={{0,8},{1,9},{2,10},{3,11},{4,12},{5,13},{6,14},{7,15},{8,16},{9,17... | collective-permute-start | bytes 221192 | tf_op jit(solution)/shard_map/ppermute | solution.py:43
  11.7 4.6 %collective-permute-start.2 = (bf16[192,192]{1,0:T(8,128)(2,1)S(1)}, bf16[192,192]{1,0:T(8,128)(2,1)S(1)}, u32[]{:S(2)}, u32[]{:S(2)}) collective-permute-start(bf16[192,192]{1,0:T(8,128)(2,1)S(1)} %collective-permute-done), channel_id=1, source_target_pairs={{0,8},{1,9},{2,10},{3,11},{4,12},{5,13},{6,14},{7,15},{8,16},{9,17... | collective-permute-start | bytes 221192 | tf_op jit(solution)/shard_map/ppermute | solution.py:43
  19.4 3.9 %collective-permute-start.3 = (bf16[4,192,192]{2,1,0:T(8,128)(2,1)S(1)}, bf16[4,192,192]{2,1,0:T(8,128)(2,1)S(1)}, u32[]{:S(2)}, u32[]{:S(2)}) collective-permute-start(bf16[4,192,192]{2,1,0:T(8,128)(2,1)S(1)} %pad_maximum_fusion), channel_id=1, source_target_pairs={{0,1},{1,2},{2,3},{3,4},{4,5},{5,6},{6,7},{7,0},{8,9},{9,10},{10,1... | collective-permute-start | bytes 884744 | tf_op jit(solution)/shard_map/ppermute | solution.py:43
  23.3 8.6 %collective-permute-start.4 = (bf16[4,192,192]{2,1,0:T(8,128)(2,1)S(1)}, bf16[4,192,192]{2,1,0:T(8,128)(2,1)S(1)}, u32[]{:S(2)}, u32[]{:S(2)}) collective-permute-start(bf16[4,192,192]{2,1,0:T(8,128)(2,1)S(1)} %pad_maximum_fusion), channel_id=1, source_target_pairs={{0,7},{1,0},{2,1},{3,2},{4,3},{5,4},{6,5},{7,6},{8,15},{9,8},{10,9... | collective-permute-start | bytes 884744 | tf_op jit(solution)/shard_map/ppermute | solution.py:43
  32.0 4.4 %collective-permute-done.3 = bf16[4,192,192]{2,1,0:T(8,128)(2,1)S(1)} collective-permute-done((bf16[4,192,192]{2,1,0:T(8,128)(2,1)S(1)}, bf16[4,192,192]{2,1,0:T(8,128)(2,1)S(1)}, u32[]{:S(2)}, u32[]{:S(2)}) %collective-permute-start.3) | collective-permute-done | bytes 294944 | tf_op jit(solution)/shard_map/ppermute | solution.py:43
  38.4 4.6 %collective-permute-start.6 = (bf16[4,192,192]{2,1,0:T(8,128)(2,1)S(1)}, bf16[4,192,192]{2,1,0:T(8,128)(2,1)S(1)}, u32[]{:S(2)}, u32[]{:S(2)}) collective-permute-start(bf16[4,192,192]{2,1,0:T(8,128)(2,1)S(1)} %collective-permute-done.4), channel_id=1, source_target_pairs={{0,7},{1,0},{2,1},{3,2},{4,3},{5,4},{6,5},{7,6},{8,15},{9,8},{10,9... | collective-permute-start | bytes 884744 | tf_op jit(solution)/shard_map/ppermute | solution.py:43
  48.4 4.6 %collective-permute-start.8 = (bf16[4,192,192]{2,1,0:T(8,128)(2,1)S(1)}, bf16[4,192,192]{2,1,0:T(8,128)(2,1)S(1)}, u32[]{:S(2)}, u32[]{:S(2)}) collective-permute-start(bf16[4,192,192]{2,1,0:T(8,128)(2,1)S(1)} %collective-permute-done.6), channel_id=1, source_target_pairs={{0,7},{1,0},{2,1},{3,2},{4,3},{5,4},{6,5},{7,6},{8,15},{9,8},{10,9... | collective-permute-start | bytes 884744 | tf_op jit(solution)/shard_map/ppermute | solution.py:43
  58.2 7.7 %collective-permute-done.9 = bf16[4,192,192]{2,1,0:T(8,128)(2,1)S(1)} collective-permute-done((bf16[4,192,192]{2,1,0:T(8,128)(2,1)S(1)}, bf16[4,192,192]{2,1,0:T(8,128)(2,1)S(1)}, u32[]{:S(2)}, u32[]{:S(2)}) %collective-permute-start.9) | collective-permute-done | bytes 294944 | tf_op jit(solution)/shard_map/ppermute | solution.py:43
  72.8 8.8 %collective-permute-start.10 = (bf16[6144,192]{0,1:T(8,128)(2,1)}, bf16[6144,192]{0,1:T(8,128)(2,1)}, u32[]{:S(2)}, u32[]{:S(2)}) collective-permute-start(bf16[6144,192]{0,1:T(8,128)(2,1)} %copy.50), channel_id=1, source_target_pairs={{0,128},{128,0},{256,384},{384,256},{1,129},{129,1},{257,385},{385... | collective-permute-start | bytes 7077896 | tf_op jit(solution)/shard_map/ppermute | solution.py:23
  81.6 6.4 %reshape_squeeze.3 = bf16[192,32,192]{2,1,0:T(8,128)(2,1)} reshape(bf16[1,192,6144]{2,1,0:T(8,128)(2,1)} %param.6) | data formatting | bytes 4718592 | tf_op jit(solution)/shard_map/reshape;squeeze | solution.py:166
  93.5 13.5 %all_gather.13 = bf16[768,640]{1,0:T(8,128)(2,1)S(1)} all-gather(bf16[192,640]{1,0:T(8,128)(2,1)S(1)} %pad_maximum_fusion.2), channel_id=1, replica_groups=mesh['dp'=4,'seq'=4,'fsdp'=32] {'seq'}, dimensions={0}, use_global_device_ids=true | all-gather | bytes 1228800 | tf_op jit(solution)/shard_map/all_gather | solution.py:131
  111.2 4.2 %convert_bitcast_fusion = bf16[32,192,192]{1,2,0:T(8,128)(2,1)} fusion(bf16[192,32,192]{2,1,0:T(8,128)(2,1)S(1)} %copy-done.1, pred[]{:T(512)S(6)} %eq.41, bf16[192,128]{1,0:T(8,128)(2,1)S(1)} %convolution_convert_fusion.1, bf16[192,128]{1,0:T(8,128)(2,1)S(1)} %convolution_convert_fusion.2, bf16[192,128]{1,0:T(8,128)(2,1)S(1)} %convolution_convert_fusion), kind=kOutput, calls=%fused_computation.9 | convolution fusion | flops 454496256 | bytes 4866049 | tf_op jit(solution)/shard_map/pjd,pc->jdc/dot_general | solution.py:168
  119.0 5.4 %collective-permute-done.11 = bf16[32,192,192]{1,2,0:T(8,128)(2,1)} collective-permute-done((bf16[32,192,192]{1,2,0:T(8,128)(2,1)}, bf16[32,192,192]{1,2,0:T(8,128)(2,1)}, u32[]{:S(2)}, u32[]{:S(2)}) %collective-permute-start.11) | collective-permute-done | bytes 2359328 | tf_op jit(solution)/shard_map/ppermute | solution.py:23
  124.4 5.4 %bitcast_add_fusion = f32[32,192,192]{1,2,0:T(8,128)S(1)} fusion(bf16[32,192,192]{1,2,0:T(8,128)(2,1)} %collective-permute-done.11, bf16[192,32,192]{2,1,0:T(8,128)(2,1)} %reshape_squeeze.3, pred[]{:T(512)S(6)} %eq.41, bf16[192,128]{1,0:T(8,128)(2,1)S(1)} %convolution_convert_fusion.1, bf16[192,128]{1,0:T(8,128)(2,1)S(1)} %convolution_convert_fusion.2, ...), kind=kOutput, calls=%fused_computation.5 | convolution fusion | flops 455675904 | bytes 9584641 | tf_op jit(solution)/shard_map/pjd,pc->jdc/dot_general | solution.py:167
  139.3 4.6 %collective-permute-start.16 = (bf16[4,192,192]{2,1,0:T(8,128)(2,1)}, bf16[4,192,192]{2,1,0:T(8,128)(2,1)}, u32[]{:S(2)}, u32[]{:S(2)}) collective-permute-start(bf16[4,192,192]{2,1,0:T(8,128)(2,1)} %bitcast.122), channel_id=1, source_target_pairs={{0,7},{1,0},{2,1},{3,2},{4,3},{5,4},{6,5},{7,6},{8,15},{9,8},{10,9... | collective-permute-start | bytes 884744 | tf_op jit(solution)/shard_map/ppermute | solution.py:43
  143.9 4.6 %constant_dynamic-slice_fusion.5 = (f32[4,1,192,192]{2,3,1,0:T(8,128)}, f32[4,1,192,192]{2,3,1,0:T(8,128)}, f32[4,1,192,192]{2,3,1,0:T(8,128)}, f32[4,1,192,192]...) fusion(f32[4,8,192,192]{2,3,1,0:T(8,128)} %bitcast.113, s32[]{:T(128)S(6)} %select_n.248, ...), kind=kLoop, calls=%fused_computation.99 | loop fusion | bytes 7077912 | tf_op jit(solution)/shard_map/jit(dynamic_index_in_dim)/dynamic_slice | solution.py:67
  161.7 4.6 %collective-permute-start.17 = (bf16[4,192,192]{2,1,0:T(8,128)(2,1)}, bf16[4,192,192]{2,1,0:T(8,128)(2,1)}, u32[]{:S(2)}, u32[]{:S(2)}) collective-permute-start(bf16[4,192,192]{2,1,0:T(8,128)(2,1)} %fusion.25), channel_id=1, source_target_pairs={{0,7},{1,0},{2,1},{3,2},{4,3},{5,4},{6,5},{7,6},{8,15},{9,8},{10,9... | collective-permute-start | bytes 884744 | tf_op jit(solution)/shard_map/ppermute | solution.py:43
  177.0 4.6 %collective-permute-start.18 = (bf16[4,192,192]{2,1,0:T(8,128)(2,1)}, bf16[4,192,192]{2,1,0:T(8,128)(2,1)}, u32[]{:S(2)}, u32[]{:S(2)}) collective-permute-start(bf16[4,192,192]{2,1,0:T(8,128)(2,1)} %fusion.24), channel_id=1, source_target_pairs={{0,7},{1,0},{2,1},{3,2},{4,3},{5,4},{6,5},{7,6},{8,15},{9,8},{10,9... | collective-permute-start | bytes 884744 | tf_op jit(solution)/shard_map/ppermute | solution.py:43
  188.4 7.1 %collective-permute-done.15 = bf16[4,192,192]{2,1,0:T(8,128)(2,1)} collective-permute-done((bf16[4,192,192]{2,1,0:T(8,128)(2,1)}, bf16[4,192,192]{2,1,0:T(8,128)(2,1)}, u32[]{:S(2)}, u32[]{:S(2)}) %collective-permute-start.15) | collective-permute-done | bytes 294944 | tf_op jit(solution)/shard_map/ppermute | solution.py:43
  197.0 4.6 %collective-permute-start.19 = (bf16[192,192]{1,0:T(8,128)(2,1)S(1)}, bf16[192,192]{1,0:T(8,128)(2,1)S(1)}, u32[]{:S(2)}, u32[]{:S(2)}) collective-permute-start(bf16[192,192]{1,0:T(8,128)(2,1)S(1)} %get-tuple-element.12), channel_id=1, source_target_pairs={{0,8},{1,9},{2,10},{3,11},{4,12},{5,13},{6,14},{7,15},{8,16},{9,17... | collective-permute-start | bytes 221192 | tf_op jit(solution)/shard_map/ppermute | solution.py:43
  205.6 8.7 %collective-permute-start.20 = (bf16[192,192]{1,0:T(8,128)(2,1)S(1)}, bf16[192,192]{1,0:T(8,128)(2,1)S(1)}, u32[]{:S(2)}, u32[]{:S(2)}) collective-permute-start(bf16[192,192]{1,0:T(8,128)(2,1)S(1)} %fusion.37), channel_id=1, source_target_pairs={{0,8},{1,9},{2,10},{3,11},{4,12},{5,13},{6,14},{7,15},{8,16},{9,17... | collective-permute-start | bytes 221192 | tf_op jit(solution)/shard_map/ppermute | solution.py:43
  214.3 4.0 %fusion.1 = bf16[1,192,6144]{2,1,0:T(8,128)(2,1)} fusion(f32[192,6144]{1,0:T(8,128)S(1)} %fusion.62, bf16[6144,192]{0,1:T(8,128)(2,1)} %collective-permute-done.10, pred[]{:T(512)S(6)} %eq.41, bf16[192,128]{1,0:T(8,128)(2,1)S(1)} %convolution_convert_fusion.1, bf16[192,128]{1,0:T(8,128)(2,1)S(1)} %convolution_convert_fusion.2, ...), kind=kOutput, calls=%fused_computation.4 | convolution fusion | flops 455675904 | bytes 9584641 | tf_op jit(solution)/shard_map/dot_general | solution.py:16
  218.3 11.4 %all-gather = f32[768,192]{1,0:T(8,128)S(1)} all-gather(f32[192,192]{1,0:T(8,128)S(1)} %fusion.38), channel_id=2, replica_groups=mesh['dp'=4,'seq'=4,'fsdp'=32] {'seq'}, dimensions={0}, use_global_device_ids=true | all-gather | bytes 737280 | tf_op jit(solution)/shard_map/all_gather | solution.py:175
  229.7 16.2 %all_gather.16 = f32[4,192,192]{2,1,0:T(8,128)S(1)} all-gather(f32[1,192,192]{2,1,0:T(8,128)S(1)} %fusion.36), channel_id=1, replica_groups=mesh['dp'=4,'seq'=4,'fsdp'=32] {'dp'}, dimensions={0}, use_global_device_ids=true | all-gather | bytes 737280 | tf_op jit(solution)/shard_map/all_gather | solution.py:179
  (98 shorter events, 88.1 us)
Async XLA Ops:
  1.6 10.1 %collective-permute-start = (bf16[192,192]{1,0:T(8,128)(2,1)S(1)}, bf16[192,192]{1,0:T(8,128)(2,1)S(1)}, u32[]{:S(2)}, u32[]{:S(2)}) collective-permute-start(bf16[192,192]{1,0:T(8,128)(2,1)S(1)} %constant_dynamic-slice_fusion.8), channel_id=1, source_target_pairs={{0,8},{1,9},{2,10},{3,11},{4,12},{5,13},{6,14},{7,15},{8,16},{9,17... | collective-permute-start | bytes 221192 | tf_op jit(solution)/shard_map/ppermute | solution.py:43
  6.7 9.9 %collective-permute-start.1 = (bf16[192,192]{1,0:T(8,128)(2,1)S(1)}, bf16[192,192]{1,0:T(8,128)(2,1)S(1)}, u32[]{:S(2)}, u32[]{:S(2)}) collective-permute-start(bf16[192,192]{1,0:T(8,128)(2,1)S(1)} %constant_dynamic-slice_fusion.8), channel_id=1, source_target_pairs={{0,24},{1,25},{2,26},{3,27},{4,28},{5,29},{6,30},{7,31},{8,0},{9,1... | collective-permute-start | bytes 221192 | tf_op jit(solution)/shard_map/ppermute | solution.py:43
  11.7 7.5 %collective-permute-start.2 = (bf16[192,192]{1,0:T(8,128)(2,1)S(1)}, bf16[192,192]{1,0:T(8,128)(2,1)S(1)}, u32[]{:S(2)}, u32[]{:S(2)}) collective-permute-start(bf16[192,192]{1,0:T(8,128)(2,1)S(1)} %collective-permute-done), channel_id=1, source_target_pairs={{0,8},{1,9},{2,10},{3,11},{4,12},{5,13},{6,14},{7,15},{8,16},{9,17... | collective-permute-start | bytes 221192 | tf_op jit(solution)/shard_map/ppermute | solution.py:43
  19.4 17.0 %collective-permute-start.3 = (bf16[4,192,192]{2,1,0:T(8,128)(2,1)S(1)}, bf16[4,192,192]{2,1,0:T(8,128)(2,1)S(1)}, u32[]{:S(2)}, u32[]{:S(2)}) collective-permute-start(bf16[4,192,192]{2,1,0:T(8,128)(2,1)S(1)} %pad_maximum_fusion), channel_id=1, source_target_pairs={{0,1},{1,2},{2,3},{3,4},{4,5},{5,6},{6,7},{7,0},{8,9},{9,10},{10,1... | collective-permute-start | bytes 884744 | tf_op jit(solution)/shard_map/ppermute | solution.py:43
  23.3 15.0 %collective-permute-start.4 = (bf16[4,192,192]{2,1,0:T(8,128)(2,1)S(1)}, bf16[4,192,192]{2,1,0:T(8,128)(2,1)S(1)}, u32[]{:S(2)}, u32[]{:S(2)}) collective-permute-start(bf16[4,192,192]{2,1,0:T(8,128)(2,1)S(1)} %pad_maximum_fusion), channel_id=1, source_target_pairs={{0,7},{1,0},{2,1},{3,2},{4,3},{5,4},{6,5},{7,6},{8,15},{9,8},{10,9... | collective-permute-start | bytes 884744 | tf_op jit(solution)/shard_map/ppermute | solution.py:43
  36.4 10.1 %collective-permute-start.5 = (bf16[4,192,192]{2,1,0:T(8,128)(2,1)S(1)}, bf16[4,192,192]{2,1,0:T(8,128)(2,1)S(1)}, u32[]{:S(2)}, u32[]{:S(2)}) collective-permute-start(bf16[4,192,192]{2,1,0:T(8,128)(2,1)S(1)} %collective-permute-done.3), channel_id=1, source_target_pairs={{0,1},{1,2},{2,3},{3,4},{4,5},{5,6},{6,7},{7,0},{8,9},{9,10},{10,1... | collective-permute-start | bytes 884744 | tf_op jit(solution)/shard_map/ppermute | solution.py:43
  38.4 10.1 %collective-permute-start.6 = (bf16[4,192,192]{2,1,0:T(8,128)(2,1)S(1)}, bf16[4,192,192]{2,1,0:T(8,128)(2,1)S(1)}, u32[]{:S(2)}, u32[]{:S(2)}) collective-permute-start(bf16[4,192,192]{2,1,0:T(8,128)(2,1)S(1)} %collective-permute-done.4), channel_id=1, source_target_pairs={{0,7},{1,0},{2,1},{3,2},{4,3},{5,4},{6,5},{7,6},{8,15},{9,8},{10,9... | collective-permute-start | bytes 884744 | tf_op jit(solution)/shard_map/ppermute | solution.py:43
  46.5 9.7 %collective-permute-start.7 = (bf16[4,192,192]{2,1,0:T(8,128)(2,1)S(1)}, bf16[4,192,192]{2,1,0:T(8,128)(2,1)S(1)}, u32[]{:S(2)}, u32[]{:S(2)}) collective-permute-start(bf16[4,192,192]{2,1,0:T(8,128)(2,1)S(1)} %collective-permute-done.5), channel_id=1, source_target_pairs={{0,1},{1,2},{2,3},{3,4},{4,5},{5,6},{6,7},{7,0},{8,9},{9,10},{10,1... | collective-permute-start | bytes 884744 | tf_op jit(solution)/shard_map/ppermute | solution.py:43
  48.4 9.7 %collective-permute-start.8 = (bf16[4,192,192]{2,1,0:T(8,128)(2,1)S(1)}, bf16[4,192,192]{2,1,0:T(8,128)(2,1)S(1)}, u32[]{:S(2)}, u32[]{:S(2)}) collective-permute-start(bf16[4,192,192]{2,1,0:T(8,128)(2,1)S(1)} %collective-permute-done.6), channel_id=1, source_target_pairs={{0,7},{1,0},{2,1},{3,2},{4,3},{5,4},{6,5},{7,6},{8,15},{9,8},{10,9... | collective-permute-start | bytes 884744 | tf_op jit(solution)/shard_map/ppermute | solution.py:43
  56.2 9.7 %collective-permute-start.9 = (bf16[4,192,192]{2,1,0:T(8,128)(2,1)S(1)}, bf16[4,192,192]{2,1,0:T(8,128)(2,1)S(1)}, u32[]{:S(2)}, u32[]{:S(2)}) collective-permute-start(bf16[4,192,192]{2,1,0:T(8,128)(2,1)S(1)} %collective-permute-done.7), channel_id=1, source_target_pairs={{0,1},{1,2},{2,3},{3,4},{4,5},{5,6},{6,7},{7,0},{8,9},{9,10},{10,1... | collective-permute-start | bytes 884744 | tf_op jit(solution)/shard_map/ppermute | solution.py:43
  72.8 17.9 %collective-permute-start.10 = (bf16[6144,192]{0,1:T(8,128)(2,1)}, bf16[6144,192]{0,1:T(8,128)(2,1)}, u32[]{:S(2)}, u32[]{:S(2)}) collective-permute-start(bf16[6144,192]{0,1:T(8,128)(2,1)} %copy.50), channel_id=1, source_target_pairs={{0,128},{128,0},{256,384},{384,256},{1,129},{129,1},{257,385},{385... | collective-permute-start | bytes 7077896 | tf_op jit(solution)/shard_map/ppermute | solution.py:23
  81.6 6.5 %copy-start.6 = (s32[1,192]{1,0:T(1,128)S(1)}, s32[1,192]{1,0:T(1,128)}, u32[]{:S(2)}) copy-start(s32[1,192]{1,0:T(1,128)} %param.7) | copy-start | bytes 2308
  90.7 2.7 %copy-start.5 = (bf16[1,192,128]{2,1,0:T(8,128)(2,1)S(1)}, bf16[1,192,128]{2,1,0:T(8,128)(2,1)}, u32[]{:S(2)}) copy-start(bf16[1,192,128]{2,1,0:T(8,128)(2,1)} %param.9) | copy-start | bytes 147460
  115.4 9.0 %collective-permute-start.11 = (bf16[32,192,192]{1,2,0:T(8,128)(2,1)}, bf16[32,192,192]{1,2,0:T(8,128)(2,1)}, u32[]{:S(2)}, u32[]{:S(2)}) collective-permute-start(bf16[32,192,192]{1,2,0:T(8,128)(2,1)} %convert_bitcast_fusion), channel_id=1, source_target_pairs={{0,128},{128,0},{256,384},{384,256},{1,129},{129,1},{257,385},{385... | collective-permute-start | bytes 7077896 | tf_op jit(solution)/shard_map/ppermute | solution.py:23
  135.3 15.5 %collective-permute-start.12 = (bf16[4,192,192]{2,1,0:T(8,128)(2,1)}, bf16[4,192,192]{2,1,0:T(8,128)(2,1)}, u32[]{:S(2)}, u32[]{:S(2)}) collective-permute-start(bf16[4,192,192]{2,1,0:T(8,128)(2,1)} %bitcast.121), channel_id=1, source_target_pairs={{0,1},{1,2},{2,3},{3,4},{4,5},{5,6},{6,7},{7,0},{8,9},{9,10},{10,1... | collective-permute-start | bytes 884744 | tf_op jit(solution)/shard_map/ppermute | solution.py:43
  139.3 20.2 %collective-permute-start.16 = (bf16[4,192,192]{2,1,0:T(8,128)(2,1)}, bf16[4,192,192]{2,1,0:T(8,128)(2,1)}, u32[]{:S(2)}, u32[]{:S(2)}) collective-permute-start(bf16[4,192,192]{2,1,0:T(8,128)(2,1)} %bitcast.122), channel_id=1, source_target_pairs={{0,7},{1,0},{2,1},{3,2},{4,3},{5,4},{6,5},{7,6},{8,15},{9,8},{10,9... | collective-permute-start | bytes 884744 | tf_op jit(solution)/shard_map/ppermute | solution.py:43
  153.0 13.3 %collective-permute-start.13 = (bf16[4,192,192]{2,1,0:T(8,128)(2,1)}, bf16[4,192,192]{2,1,0:T(8,128)(2,1)}, u32[]{:S(2)}, u32[]{:S(2)}) collective-permute-start(bf16[4,192,192]{2,1,0:T(8,128)(2,1)} %fusion.28), channel_id=1, source_target_pairs={{0,1},{1,2},{2,3},{3,4},{4,5},{5,6},{6,7},{7,0},{8,9},{9,10},{10,1... | collective-permute-start | bytes 884744 | tf_op jit(solution)/shard_map/ppermute | solution.py:43
  161.7 13.3 %collective-permute-start.17 = (bf16[4,192,192]{2,1,0:T(8,128)(2,1)}, bf16[4,192,192]{2,1,0:T(8,128)(2,1)}, u32[]{:S(2)}, u32[]{:S(2)}) collective-permute-start(bf16[4,192,192]{2,1,0:T(8,128)(2,1)} %fusion.25), channel_id=1, source_target_pairs={{0,7},{1,0},{2,1},{3,2},{4,3},{5,4},{6,5},{7,6},{8,15},{9,8},{10,9... | collective-permute-start | bytes 884744 | tf_op jit(solution)/shard_map/ppermute | solution.py:43
  168.3 13.3 %collective-permute-start.14 = (bf16[4,192,192]{2,1,0:T(8,128)(2,1)}, bf16[4,192,192]{2,1,0:T(8,128)(2,1)}, u32[]{:S(2)}, u32[]{:S(2)}) collective-permute-start(bf16[4,192,192]{2,1,0:T(8,128)(2,1)} %fusion.27), channel_id=1, source_target_pairs={{0,1},{1,2},{2,3},{3,4},{4,5},{5,6},{6,7},{7,0},{8,9},{9,10},{10,1... | collective-permute-start | bytes 884744 | tf_op jit(solution)/shard_map/ppermute | solution.py:43
  177.0 11.3 %collective-permute-start.18 = (bf16[4,192,192]{2,1,0:T(8,128)(2,1)}, bf16[4,192,192]{2,1,0:T(8,128)(2,1)}, u32[]{:S(2)}, u32[]{:S(2)}) collective-permute-start(bf16[4,192,192]{2,1,0:T(8,128)(2,1)} %fusion.24), channel_id=1, source_target_pairs={{0,7},{1,0},{2,1},{3,2},{4,3},{5,4},{6,5},{7,6},{8,15},{9,8},{10,9... | collective-permute-start | bytes 884744 | tf_op jit(solution)/shard_map/ppermute | solution.py:43
  183.7 11.8 %collective-permute-start.15 = (bf16[4,192,192]{2,1,0:T(8,128)(2,1)}, bf16[4,192,192]{2,1,0:T(8,128)(2,1)}, u32[]{:S(2)}, u32[]{:S(2)}) collective-permute-start(bf16[4,192,192]{2,1,0:T(8,128)(2,1)} %fusion.26), channel_id=1, source_target_pairs={{0,1},{1,2},{2,3},{3,4},{4,5},{5,6},{6,7},{7,0},{8,9},{9,10},{10,1... | collective-permute-start | bytes 884744 | tf_op jit(solution)/shard_map/ppermute | solution.py:43
  197.0 8.6 %collective-permute-start.19 = (bf16[192,192]{1,0:T(8,128)(2,1)S(1)}, bf16[192,192]{1,0:T(8,128)(2,1)S(1)}, u32[]{:S(2)}, u32[]{:S(2)}) collective-permute-start(bf16[192,192]{1,0:T(8,128)(2,1)S(1)} %get-tuple-element.12), channel_id=1, source_target_pairs={{0,8},{1,9},{2,10},{3,11},{4,12},{5,13},{6,14},{7,15},{8,16},{9,17... | collective-permute-start | bytes 221192 | tf_op jit(solution)/shard_map/ppermute | solution.py:43
  202.8 15.5 %collective-permute-start.21 = (bf16[192,192]{1,0:T(8,128)(2,1)S(1)}, bf16[192,192]{1,0:T(8,128)(2,1)S(1)}, u32[]{:S(2)}, u32[]{:S(2)}) collective-permute-start(bf16[192,192]{1,0:T(8,128)(2,1)S(1)} %get-tuple-element.13), channel_id=1, source_target_pairs={{0,24},{1,25},{2,26},{3,27},{4,28},{5,29},{6,30},{7,31},{8,0},{9,1... | collective-permute-start | bytes 221192 | tf_op jit(solution)/shard_map/ppermute | solution.py:43
  205.6 12.7 %collective-permute-start.20 = (bf16[192,192]{1,0:T(8,128)(2,1)S(1)}, bf16[192,192]{1,0:T(8,128)(2,1)S(1)}, u32[]{:S(2)}, u32[]{:S(2)}) collective-permute-start(bf16[192,192]{1,0:T(8,128)(2,1)S(1)} %fusion.37), channel_id=1, source_target_pairs={{0,8},{1,9},{2,10},{3,11},{4,12},{5,13},{6,14},{7,15},{8,16},{9,17... | collective-permute-start | bytes 221192 | tf_op jit(solution)/shard_map/ppermute | solution.py:43
  (5 other events, 9.8 us)

commit v5 on v4

--- a/solution.py
+++ b/solution.py
@@ -163,13 +163,12 @@
         contract_last(g_mine, w_mine_all) + contract_last(g_other, w_other_all)
     ).astype(jnp.bfloat16)
 
-    blocked = features.reshape(n_rows, n_fsdp, rows_w)
-    wg_mine = jnp.einsum("pjd,pc->jdc", blocked, g_mine, preferred_element_type=jnp.float32)
-    wg_other = jnp.einsum("pjd,pc->jdc", blocked, g_other, preferred_element_type=jnp.float32)
+    blocked = features.reshape(n_rows, outer_fsdp, inner_fsdp, rows_w)
+    wg_mine = jnp.einsum("pyzd,pc->zydc", blocked, g_mine, preferred_element_type=jnp.float32)
+    wg_other = jnp.einsum("pyzd,pc->zydc", blocked, g_other, preferred_element_type=jnp.float32)
     wg_from_partner = dp_partner(wg_other.astype(jnp.bfloat16), 1)
-    wg_chip = wg_mine + wg_from_partner.astype(jnp.float32)
-    blocks = wg_chip.reshape(outer_fsdp, inner_fsdp, rows_w, half)
-    over_z = ring_reduce_scatter(blocks, ring_z, axis=1)
+    blocks = wg_mine + wg_from_partner.astype(jnp.float32)
+    over_z = ring_reduce_scatter(blocks, ring_z, axis=0)
     over_fsdp = ring_reduce_scatter(over_z, ring_y)
 
     by_seq = lax.all_gather(over_fsdp, "seq", axis=0, tiled=False)

time: 248 us -> 249 us (level)
  waiting for transfers between devices: 34.4 us -> 59.6 us
  local copies, waits for them, and re-layouts: 42.6 us -> 20.1 us
  other arithmetic: 14.3 us -> 11.3 us
    ppermute x20, waiting for transfers between devices: 29 us -> 54.3 us  [shift(): return lax.ppermute(x, self.axis, perm=pairs)]
    dynamic_slice x8 -> x0, local copies, waits for them, and re-layouts: 19.7 us -> none  [pick(): lax.dynamic_index_in_dim(blocks, index % n, axis=axis, keepdims=False)]
    convert_element_type x2 -> x0, other arithmetic: 4.17 us -> none  [ring_reduce_scatter(): acc = ring.shift(acc.astype(jnp.bfloat16), -1).astype(jnp.float32)]
    unnamed x22 -> x20, local copies, waits for them, and re-layouts: 9.45 us -> 5.52 us
  transfers between devices with their start and end apart: 22 -> 22, of which waited for: 9 -> 13; matrix products, arithmetic and copies ran while one was open for 19% -> 7% of each run, Pallas kernels for 0% -> 0%
where the time goes in v5:
time: 249 us; the launch traced here: 248 us
  starting transfers between devices  91.1 us (37%)
  waiting for transfers between devices  59.6 us (24%)
  blocking collectives  41.4 us (17%)
  matrix products  22.6 us (9%)
  local copies, waits for them, and re-layouts  20.1 us (8%)
  other arithmetic  11.3 us (5%)
    ppermute x20, starting transfers between devices, shift(): return lax.ppermute(x, self.axis, perm=pairs)  78.8 us
    ppermute x20, waiting for transfers between devices, shift(): return lax.ppermute(x, self.axis, perm=pairs)  54.3 us
    all_gather x1, blocking collectives, shards(): by_dp = lax.all_gather(over_seq, 'dp', axis=0, tiled=False)  16.6 us
    all_gather x1, blocking collectives, shards(): packed_all = lax.all_gather(packed, 'seq', axis=0, tiled=True)  13.5 us
    ppermute x2, starting transfers between devices, dp_partner(): return lax.ppermute(x, 'dp', perm=pairs)  12.3 us
    all_gather x1, blocking collectives, shards(): by_seq = lax.all_gather(over_fsdp, 'seq', axis=0, tiled=False)  11.4 us
    convert_element_type x4, other arithmetic, ring_reduce_scatter(): acc = ring.shift(acc.astype(jnp.bfloat16), 1).astype(jnp.float32)  7.41 us
    dot_general x4, matrix products, contract_last(): lax.dot_general(left, right, (((1,), (1,)), ((), ())), preferred_element_...  6.53 us
  transfers between devices with their start and end apart: 22, of which 13 were waited for; matrix products, arithmetic and copies ran while one was open for 7% of the time, Pallas kernels for 0%

profile of v5, /device:TPU:1, one launch (start us, length us, event | category | flops | bytes accessed | tf_op | source)
XLA Modules:
  0.0 247.8 jit_solution(10567625881245204246)
XLA Ops:
  1.6 5.0 %collective-permute-start = (bf16[192,192]{1,0:T(8,128)(2,1)S(1)}, bf16[192,192]{1,0:T(8,128)(2,1)S(1)}, u32[]{:S(2)}, u32[]{:S(2)}) collective-permute-start(bf16[192,192]{1,0:T(8,128)(2,1)S(1)} %constant_dynamic-slice_fusion), channel_id=1, source_target_pairs={{0,8},{1,9},{2,10},{3,11},{4,12},{5,13},{6,14},{7,15},{8,16},{9,17... | collective-permute-start | bytes 221192 | tf_op jit(solution)/shard_map/ppermute | solution.py:43
  11.7 4.6 %collective-permute-start.2 = (bf16[192,192]{1,0:T(8,128)(2,1)S(1)}, bf16[192,192]{1,0:T(8,128)(2,1)S(1)}, u32[]{:S(2)}, u32[]{:S(2)}) collective-permute-start(bf16[192,192]{1,0:T(8,128)(2,1)S(1)} %collective-permute-done), channel_id=1, source_target_pairs={{0,8},{1,9},{2,10},{3,11},{4,12},{5,13},{6,14},{7,15},{8,16},{9,17... | collective-permute-start | bytes 221192 | tf_op jit(solution)/shard_map/ppermute | solution.py:43
  23.3 8.6 %collective-permute-start.4 = (bf16[4,192,192]{2,1,0:T(8,128)(2,1)S(1)}, bf16[4,192,192]{2,1,0:T(8,128)(2,1)S(1)}, u32[]{:S(2)}, u32[]{:S(2)}) collective-permute-start(bf16[4,192,192]{2,1,0:T(8,128)(2,1)S(1)} %pad_maximum_fusion), channel_id=1, source_target_pairs={{0,7},{1,0},{2,1},{3,2},{4,3},{5,4},{6,5},{7,6},{8,15},{9,8},{10,9... | collective-permute-start | bytes 884744 | tf_op jit(solution)/shard_map/ppermute | solution.py:43
  32.0 4.4 %collective-permute-done.3 = bf16[4,192,192]{2,1,0:T(8,128)(2,1)S(1)} collective-permute-done((bf16[4,192,192]{2,1,0:T(8,128)(2,1)S(1)}, bf16[4,192,192]{2,1,0:T(8,128)(2,1)S(1)}, u32[]{:S(2)}, u32[]{:S(2)}) %collective-permute-start.3) | collective-permute-done | bytes 294944 | tf_op jit(solution)/shard_map/ppermute | solution.py:43
  38.4 4.6 %collective-permute-start.6 = (bf16[4,192,192]{2,1,0:T(8,128)(2,1)S(1)}, bf16[4,192,192]{2,1,0:T(8,128)(2,1)S(1)}, u32[]{:S(2)}, u32[]{:S(2)}) collective-permute-start(bf16[4,192,192]{2,1,0:T(8,128)(2,1)S(1)} %collective-permute-done.4), channel_id=1, source_target_pairs={{0,7},{1,0},{2,1},{3,2},{4,3},{5,4},{6,5},{7,6},{8,15},{9,8},{10,9... | collective-permute-start | bytes 884744 | tf_op jit(solution)/shard_map/ppermute | solution.py:43
  48.4 4.6 %collective-permute-start.8 = (bf16[4,192,192]{2,1,0:T(8,128)(2,1)S(1)}, bf16[4,192,192]{2,1,0:T(8,128)(2,1)S(1)}, u32[]{:S(2)}, u32[]{:S(2)}) collective-permute-start(bf16[4,192,192]{2,1,0:T(8,128)(2,1)S(1)} %collective-permute-done.6), channel_id=1, source_target_pairs={{0,7},{1,0},{2,1},{3,2},{4,3},{5,4},{6,5},{7,6},{8,15},{9,8},{10,9... | collective-permute-start | bytes 884744 | tf_op jit(solution)/shard_map/ppermute | solution.py:43
  58.2 7.7 %collective-permute-done.9 = bf16[4,192,192]{2,1,0:T(8,128)(2,1)S(1)} collective-permute-done((bf16[4,192,192]{2,1,0:T(8,128)(2,1)S(1)}, bf16[4,192,192]{2,1,0:T(8,128)(2,1)S(1)}, u32[]{:S(2)}, u32[]{:S(2)}) %collective-permute-start.9) | collective-permute-done | bytes 294944 | tf_op jit(solution)/shard_map/ppermute | solution.py:43
  72.8 8.8 %collective-permute-start.10 = (bf16[6144,192]{0,1:T(8,128)(2,1)}, bf16[6144,192]{0,1:T(8,128)(2,1)}, u32[]{:S(2)}, u32[]{:S(2)}) collective-permute-start(bf16[6144,192]{0,1:T(8,128)(2,1)} %copy.32), channel_id=1, source_target_pairs={{0,128},{128,0},{256,384},{384,256},{1,129},{129,1},{257,385},{385... | collective-permute-start | bytes 7077896 | tf_op jit(solution)/shard_map/ppermute | solution.py:23
  81.6 6.4 %reshape_squeeze.3 = bf16[192,4,8,192]{3,2,1,0:T(8,128)(2,1)} reshape(bf16[1,192,6144]{2,1,0:T(8,128)(2,1)} %param.6) | data formatting | bytes 4718592 | tf_op jit(solution)/shard_map/reshape;squeeze | solution.py:166
  93.5 13.5 %all_gather.13 = bf16[768,640]{1,0:T(8,128)(2,1)S(1)} all-gather(bf16[192,640]{1,0:T(8,128)(2,1)S(1)} %pad_maximum_fusion.2), channel_id=1, replica_groups=mesh['dp'=4,'seq'=4,'fsdp'=32] {'seq'}, dimensions={0}, use_global_device_ids=true | all-gather | bytes 1228800 | tf_op jit(solution)/shard_map/all_gather | solution.py:131
  111.2 4.2 %convert_bitcast_fusion = bf16[8,4,192,192]{2,3,0,1:T(8,128)(2,1)} fusion(bf16[192,4,8,192]{3,2,1,0:T(8,128)(2,1)S(1)} %copy-done.1, pred[]{:T(512)S(6)} %eq.41, bf16[192,128]{1,0:T(8,128)(2,1)S(1)} %convolution_convert_fusion.1, bf16[192,128]{1,0:T(8,128)(2,1)S(1)} %convolution_convert_fusion.2, bf16[192,128]{1,0:T(8,128)(2,1)S(1)} %convolution_convert_fusion), kind=kOutput, calls=%fused_computation.9 | convolution fusion | flops 454496256 | bytes 4866049 | tf_op jit(solution)/shard_map/pyzd,pc->zydc/dot_general | solution.py:168
  119.0 5.4 %collective-permute-done.11 = bf16[8,4,192,192]{2,3,0,1:T(8,128)(2,1)} collective-permute-done((bf16[8,4,192,192]{2,3,0,1:T(8,128)(2,1)}, bf16[8,4,192,192]{2,3,0,1:T(8,128)(2,1)}, u32[]{:S(2)}, u32[]{:S(2)}) %collective-permute-start.11) | collective-permute-done | bytes 2359328 | tf_op jit(solution)/shard_map/ppermute | solution.py:23
  124.4 5.4 %bitcast_add_fusion = f32[8,4,192,192]{2,3,0,1:T(8,128)S(1)} fusion(bf16[8,4,192,192]{2,3,0,1:T(8,128)(2,1)} %collective-permute-done.11, bf16[192,4,8,192]{3,2,1,0:T(8,128)(2,1)} %reshape_squeeze.3, pred[]{:T(512)S(6)} %eq.41, bf16[192,128]{1,0:T(8,128)(2,1)S(1)} %convolution_convert_fusion.1, bf16[192,128]{1,0:T(8,128)(2,1)S(1)} %convolution_convert_fusion.2, ...), kind=kOutput, calls=%fused_computation.5 | convolution fusion | flops 455675904 | bytes 9584641 | tf_op jit(solution)/shard_map/pyzd,pc->zydc/dot_general | solution.py:167
  135.3 4.6 %collective-permute-start.16 = (bf16[4,192,192]{1,2,0:T(8,128)(2,1)}, bf16[4,192,192]{1,2,0:T(8,128)(2,1)}, u32[]{:S(2)}, u32[]{:S(2)}) collective-permute-start(bf16[4,192,192]{1,2,0:T(8,128)(2,1)} %get-tuple-element.11), channel_id=1, source_target_pairs={{0,7},{1,0},{2,1},{3,2},{4,3},{5,4},{6,5},{7,6},{8,15},{9,8},{10,9... | collective-permute-start | bytes 884744 | tf_op jit(solution)/shard_map/ppermute | solution.py:43
  139.9 7.2 %collective-permute-done.12 = bf16[4,192,192]{1,2,0:T(8,128)(2,1)} collective-permute-done((bf16[4,192,192]{1,2,0:T(8,128)(2,1)}, bf16[4,192,192]{1,2,0:T(8,128)(2,1)}, u32[]{:S(2)}, u32[]{:S(2)}) %collective-permute-start.12) | collective-permute-done | bytes 294944 | tf_op jit(solution)/shard_map/ppermute | solution.py:43
  151.2 10.8 %collective-permute-done.13 = bf16[4,192,192]{1,2,0:T(8,128)(2,1)} collective-permute-done((bf16[4,192,192]{1,2,0:T(8,128)(2,1)}, bf16[4,192,192]{1,2,0:T(8,128)(2,1)}, u32[]{:S(2)}, u32[]{:S(2)}) %collective-permute-start.13) | collective-permute-done | bytes 294944 | tf_op jit(solution)/shard_map/ppermute | solution.py:43
  166.6 4.6 %collective-permute-start.17 = (bf16[4,192,192]{1,2,0:T(8,128)(2,1)}, bf16[4,192,192]{1,2,0:T(8,128)(2,1)}, u32[]{:S(2)}, u32[]{:S(2)}) collective-permute-start(bf16[4,192,192]{1,2,0:T(8,128)(2,1)} %get-tuple-element.9), channel_id=1, source_target_pairs={{0,7},{1,0},{2,1},{3,2},{4,3},{5,4},{6,5},{7,6},{8,15},{9,8},{10,9... | collective-permute-start | bytes 884744 | tf_op jit(solution)/shard_map/ppermute | solution.py:43
  171.2 5.3 %collective-permute-done.14 = bf16[4,192,192]{1,2,0:T(8,128)(2,1)} collective-permute-done((bf16[4,192,192]{1,2,0:T(8,128)(2,1)}, bf16[4,192,192]{1,2,0:T(8,128)(2,1)}, u32[]{:S(2)}, u32[]{:S(2)}) %collective-permute-start.14) | collective-permute-done | bytes 294944 | tf_op jit(solution)/shard_map/ppermute | solution.py:43
  180.1 5.3 %collective-permute-start.18 = (bf16[4,192,192]{1,2,0:T(8,128)(2,1)}, bf16[4,192,192]{1,2,0:T(8,128)(2,1)}, u32[]{:S(2)}, u32[]{:S(2)}) collective-permute-start(bf16[4,192,192]{1,2,0:T(8,128)(2,1)} %get-tuple-element.7), channel_id=1, source_target_pairs={{0,7},{1,0},{2,1},{3,2},{4,3},{5,4},{6,5},{7,6},{8,15},{9,8},{10,9... | collective-permute-start | bytes 884744 | tf_op jit(solution)/shard_map/ppermute | solution.py:43
  190.8 5.0 %collective-permute-done.15 = bf16[4,192,192]{1,2,0:T(8,128)(2,1)} collective-permute-done((bf16[4,192,192]{1,2,0:T(8,128)(2,1)}, bf16[4,192,192]{1,2,0:T(8,128)(2,1)}, u32[]{:S(2)}, u32[]{:S(2)}) %collective-permute-start.15) | collective-permute-done | bytes 294944 | tf_op jit(solution)/shard_map/ppermute | solution.py:43
  197.4 4.6 %collective-permute-start.19 = (bf16[192,192]{0,1:T(8,128)(2,1)S(1)}, bf16[192,192]{0,1:T(8,128)(2,1)S(1)}, u32[]{:S(2)}, u32[]{:S(2)}) collective-permute-start(bf16[192,192]{0,1:T(8,128)(2,1)S(1)} %get-tuple-element.14), channel_id=1, source_target_pairs={{0,8},{1,9},{2,10},{3,11},{4,12},{5,13},{6,14},{7,15},{8,16},{9,17... | collective-permute-start | bytes 221192 | tf_op jit(solution)/shard_map/ppermute | solution.py:43
  206.0 8.7 %collective-permute-start.20 = (bf16[192,192]{0,1:T(8,128)(2,1)S(1)}, bf16[192,192]{0,1:T(8,128)(2,1)S(1)}, u32[]{:S(2)}, u32[]{:S(2)}) collective-permute-start(bf16[192,192]{0,1:T(8,128)(2,1)S(1)} %fusion.39), channel_id=1, source_target_pairs={{0,8},{1,9},{2,10},{3,11},{4,12},{5,13},{6,14},{7,15},{8,16},{9,17... | collective-permute-start | bytes 221192 | tf_op jit(solution)/shard_map/ppermute | solution.py:43
  218.9 11.4 %all-gather = f32[768,192]{1,0:T(8,128)S(1)} all-gather(f32[192,192]{1,0:T(8,128)S(1)} %copy.40), channel_id=2, replica_groups=mesh['dp'=4,'seq'=4,'fsdp'=32] {'seq'}, dimensions={0}, use_global_device_ids=true | all-gather | bytes 737280 | tf_op jit(solution)/shard_map/all_gather | solution.py:174
  230.3 16.6 %all_gather.16 = f32[4,192,192]{2,1,0:T(8,128)S(1)} all-gather(f32[1,192,192]{2,1,0:T(8,128)S(1)} %fusion.38), channel_id=1, replica_groups=mesh['dp'=4,'seq'=4,'fsdp'=32] {'dp'}, dimensions={0}, use_global_device_ids=true | all-gather | bytes 737280 | tf_op jit(solution)/shard_map/all_gather | solution.py:178
  (88 shorter events, 79.1 us)
Async XLA Ops:
  1.6 10.1 %collective-permute-start = (bf16[192,192]{1,0:T(8,128)(2,1)S(1)}, bf16[192,192]{1,0:T(8,128)(2,1)S(1)}, u32[]{:S(2)}, u32[]{:S(2)}) collective-permute-start(bf16[192,192]{1,0:T(8,128)(2,1)S(1)} %constant_dynamic-slice_fusion), channel_id=1, source_target_pairs={{0,8},{1,9},{2,10},{3,11},{4,12},{5,13},{6,14},{7,15},{8,16},{9,17... | collective-permute-start | bytes 221192 | tf_op jit(solution)/shard_map/ppermute | solution.py:43
  6.7 9.9 %collective-permute-start.1 = (bf16[192,192]{1,0:T(8,128)(2,1)S(1)}, bf16[192,192]{1,0:T(8,128)(2,1)S(1)}, u32[]{:S(2)}, u32[]{:S(2)}) collective-permute-start(bf16[192,192]{1,0:T(8,128)(2,1)S(1)} %constant_dynamic-slice_fusion), channel_id=1, source_target_pairs={{0,24},{1,25},{2,26},{3,27},{4,28},{5,29},{6,30},{7,31},{8,0},{9,1... | collective-permute-start | bytes 221192 | tf_op jit(solution)/shard_map/ppermute | solution.py:43
  11.7 7.5 %collective-permute-start.2 = (bf16[192,192]{1,0:T(8,128)(2,1)S(1)}, bf16[192,192]{1,0:T(8,128)(2,1)S(1)}, u32[]{:S(2)}, u32[]{:S(2)}) collective-permute-start(bf16[192,192]{1,0:T(8,128)(2,1)S(1)} %collective-permute-done), channel_id=1, source_target_pairs={{0,8},{1,9},{2,10},{3,11},{4,12},{5,13},{6,14},{7,15},{8,16},{9,17... | collective-permute-start | bytes 221192 | tf_op jit(solution)/shard_map/ppermute | solution.py:43
  19.4 17.0 %collective-permute-start.3 = (bf16[4,192,192]{2,1,0:T(8,128)(2,1)S(1)}, bf16[4,192,192]{2,1,0:T(8,128)(2,1)S(1)}, u32[]{:S(2)}, u32[]{:S(2)}) collective-permute-start(bf16[4,192,192]{2,1,0:T(8,128)(2,1)S(1)} %pad_maximum_fusion), channel_id=1, source_target_pairs={{0,1},{1,2},{2,3},{3,4},{4,5},{5,6},{6,7},{7,0},{8,9},{9,10},{10,1... | collective-permute-start | bytes 884744 | tf_op jit(solution)/shard_map/ppermute | solution.py:43
  23.3 15.0 %collective-permute-start.4 = (bf16[4,192,192]{2,1,0:T(8,128)(2,1)S(1)}, bf16[4,192,192]{2,1,0:T(8,128)(2,1)S(1)}, u32[]{:S(2)}, u32[]{:S(2)}) collective-permute-start(bf16[4,192,192]{2,1,0:T(8,128)(2,1)S(1)} %pad_maximum_fusion), channel_id=1, source_target_pairs={{0,7},{1,0},{2,1},{3,2},{4,3},{5,4},{6,5},{7,6},{8,15},{9,8},{10,9... | collective-permute-start | bytes 884744 | tf_op jit(solution)/shard_map/ppermute | solution.py:43
  36.4 10.1 %collective-permute-start.5 = (bf16[4,192,192]{2,1,0:T(8,128)(2,1)S(1)}, bf16[4,192,192]{2,1,0:T(8,128)(2,1)S(1)}, u32[]{:S(2)}, u32[]{:S(2)}) collective-permute-start(bf16[4,192,192]{2,1,0:T(8,128)(2,1)S(1)} %collective-permute-done.3), channel_id=1, source_target_pairs={{0,1},{1,2},{2,3},{3,4},{4,5},{5,6},{6,7},{7,0},{8,9},{9,10},{10,1... | collective-permute-start | bytes 884744 | tf_op jit(solution)/shard_map/ppermute | solution.py:43
  38.4 10.1 %collective-permute-start.6 = (bf16[4,192,192]{2,1,0:T(8,128)(2,1)S(1)}, bf16[4,192,192]{2,1,0:T(8,128)(2,1)S(1)}, u32[]{:S(2)}, u32[]{:S(2)}) collective-permute-start(bf16[4,192,192]{2,1,0:T(8,128)(2,1)S(1)} %collective-permute-done.4), channel_id=1, source_target_pairs={{0,7},{1,0},{2,1},{3,2},{4,3},{5,4},{6,5},{7,6},{8,15},{9,8},{10,9... | collective-permute-start | bytes 884744 | tf_op jit(solution)/shard_map/ppermute | solution.py:43
  46.5 9.7 %collective-permute-start.7 = (bf16[4,192,192]{2,1,0:T(8,128)(2,1)S(1)}, bf16[4,192,192]{2,1,0:T(8,128)(2,1)S(1)}, u32[]{:S(2)}, u32[]{:S(2)}) collective-permute-start(bf16[4,192,192]{2,1,0:T(8,128)(2,1)S(1)} %collective-permute-done.5), channel_id=1, source_target_pairs={{0,1},{1,2},{2,3},{3,4},{4,5},{5,6},{6,7},{7,0},{8,9},{9,10},{10,1... | collective-permute-start | bytes 884744 | tf_op jit(solution)/shard_map/ppermute | solution.py:43
  48.4 9.7 %collective-permute-start.8 = (bf16[4,192,192]{2,1,0:T(8,128)(2,1)S(1)}, bf16[4,192,192]{2,1,0:T(8,128)(2,1)S(1)}, u32[]{:S(2)}, u32[]{:S(2)}) collective-permute-start(bf16[4,192,192]{2,1,0:T(8,128)(2,1)S(1)} %collective-permute-done.6), channel_id=1, source_target_pairs={{0,7},{1,0},{2,1},{3,2},{4,3},{5,4},{6,5},{7,6},{8,15},{9,8},{10,9... | collective-permute-start | bytes 884744 | tf_op jit(solution)/shard_map/ppermute | solution.py:43
  56.2 9.7 %collective-permute-start.9 = (bf16[4,192,192]{2,1,0:T(8,128)(2,1)S(1)}, bf16[4,192,192]{2,1,0:T(8,128)(2,1)S(1)}, u32[]{:S(2)}, u32[]{:S(2)}) collective-permute-start(bf16[4,192,192]{2,1,0:T(8,128)(2,1)S(1)} %collective-permute-done.7), channel_id=1, source_target_pairs={{0,1},{1,2},{2,3},{3,4},{4,5},{5,6},{6,7},{7,0},{8,9},{9,10},{10,1... | collective-permute-start | bytes 884744 | tf_op jit(solution)/shard_map/ppermute | solution.py:43
  72.8 17.9 %collective-permute-start.10 = (bf16[6144,192]{0,1:T(8,128)(2,1)}, bf16[6144,192]{0,1:T(8,128)(2,1)}, u32[]{:S(2)}, u32[]{:S(2)}) collective-permute-start(bf16[6144,192]{0,1:T(8,128)(2,1)} %copy.32), channel_id=1, source_target_pairs={{0,128},{128,0},{256,384},{384,256},{1,129},{129,1},{257,385},{385... | collective-permute-start | bytes 7077896 | tf_op jit(solution)/shard_map/ppermute | solution.py:23
  81.6 6.5 %copy-start.6 = (s32[1,192]{1,0:T(1,128)S(1)}, s32[1,192]{1,0:T(1,128)}, u32[]{:S(2)}) copy-start(s32[1,192]{1,0:T(1,128)} %param.7) | copy-start | bytes 2308
  90.7 2.7 %copy-start.5 = (bf16[1,192,128]{2,1,0:T(8,128)(2,1)S(1)}, bf16[1,192,128]{2,1,0:T(8,128)(2,1)}, u32[]{:S(2)}) copy-start(bf16[1,192,128]{2,1,0:T(8,128)(2,1)} %param.9) | copy-start | bytes 147460
  115.4 9.0 %collective-permute-start.11 = (bf16[8,4,192,192]{2,3,0,1:T(8,128)(2,1)}, bf16[8,4,192,192]{2,3,0,1:T(8,128)(2,1)}, u32[]{:S(2)}, u32[]{:S(2)}) collective-permute-start(bf16[8,4,192,192]{2,3,0,1:T(8,128)(2,1)} %convert_bitcast_fusion), channel_id=1, source_target_pairs={{0,128},{128,0},{256,384},{384,256},{1,129},{129,1},{257,385},{385... | collective-permute-start | bytes 7077896 | tf_op jit(solution)/shard_map/ppermute | solution.py:23
  133.4 13.7 %collective-permute-start.12 = (bf16[4,192,192]{1,2,0:T(8,128)(2,1)}, bf16[4,192,192]{1,2,0:T(8,128)(2,1)}, u32[]{:S(2)}, u32[]{:S(2)}) collective-permute-start(bf16[4,192,192]{1,2,0:T(8,128)(2,1)} %get-tuple-element.10), channel_id=1, source_target_pairs={{0,1},{1,2},{2,3},{3,4},{4,5},{5,6},{6,7},{7,0},{8,9},{9,10},{10,1... | collective-permute-start | bytes 884744 | tf_op jit(solution)/shard_map/ppermute | solution.py:43
  135.3 15.8 %collective-permute-start.16 = (bf16[4,192,192]{1,2,0:T(8,128)(2,1)}, bf16[4,192,192]{1,2,0:T(8,128)(2,1)}, u32[]{:S(2)}, u32[]{:S(2)}) collective-permute-start(bf16[4,192,192]{1,2,0:T(8,128)(2,1)} %get-tuple-element.11), channel_id=1, source_target_pairs={{0,7},{1,0},{2,1},{3,2},{4,3},{5,4},{6,5},{7,6},{8,15},{9,8},{10,9... | collective-permute-start | bytes 884744 | tf_op jit(solution)/shard_map/ppermute | solution.py:43
  149.2 12.8 %collective-permute-start.13 = (bf16[4,192,192]{1,2,0:T(8,128)(2,1)}, bf16[4,192,192]{1,2,0:T(8,128)(2,1)}, u32[]{:S(2)}, u32[]{:S(2)}) collective-permute-start(bf16[4,192,192]{1,2,0:T(8,128)(2,1)} %fusion.28), channel_id=1, source_target_pairs={{0,1},{1,2},{2,3},{3,4},{4,5},{5,6},{6,7},{7,0},{8,9},{9,10},{10,1... | collective-permute-start | bytes 884744 | tf_op jit(solution)/shard_map/ppermute | solution.py:43
  164.7 11.9 %collective-permute-start.14 = (bf16[4,192,192]{1,2,0:T(8,128)(2,1)}, bf16[4,192,192]{1,2,0:T(8,128)(2,1)}, u32[]{:S(2)}, u32[]{:S(2)}) collective-permute-start(bf16[4,192,192]{1,2,0:T(8,128)(2,1)} %get-tuple-element.8), channel_id=1, source_target_pairs={{0,1},{1,2},{2,3},{3,4},{4,5},{5,6},{6,7},{7,0},{8,9},{9,10},{10,1... | collective-permute-start | bytes 884744 | tf_op jit(solution)/shard_map/ppermute | solution.py:43
  166.6 10.9 %collective-permute-start.17 = (bf16[4,192,192]{1,2,0:T(8,128)(2,1)}, bf16[4,192,192]{1,2,0:T(8,128)(2,1)}, u32[]{:S(2)}, u32[]{:S(2)}) collective-permute-start(bf16[4,192,192]{1,2,0:T(8,128)(2,1)} %get-tuple-element.9), channel_id=1, source_target_pairs={{0,7},{1,0},{2,1},{3,2},{4,3},{5,4},{6,5},{7,6},{8,15},{9,8},{10,9... | collective-permute-start | bytes 884744 | tf_op jit(solution)/shard_map/ppermute | solution.py:43
  180.1 10.7 %collective-permute-start.18 = (bf16[4,192,192]{1,2,0:T(8,128)(2,1)}, bf16[4,192,192]{1,2,0:T(8,128)(2,1)}, u32[]{:S(2)}, u32[]{:S(2)}) collective-permute-start(bf16[4,192,192]{1,2,0:T(8,128)(2,1)} %get-tuple-element.7), channel_id=1, source_target_pairs={{0,7},{1,0},{2,1},{3,2},{4,3},{5,4},{6,5},{7,6},{8,15},{9,8},{10,9... | collective-permute-start | bytes 884744 | tf_op jit(solution)/shard_map/ppermute | solution.py:43
  185.4 10.4 %collective-permute-start.15 = (bf16[4,192,192]{1,2,0:T(8,128)(2,1)}, bf16[4,192,192]{1,2,0:T(8,128)(2,1)}, u32[]{:S(2)}, u32[]{:S(2)}) collective-permute-start(bf16[4,192,192]{1,2,0:T(8,128)(2,1)} %get-tuple-element.6), channel_id=1, source_target_pairs={{0,1},{1,2},{2,3},{3,4},{4,5},{5,6},{6,7},{7,0},{8,9},{9,10},{10,1... | collective-permute-start | bytes 884744 | tf_op jit(solution)/shard_map/ppermute | solution.py:43
  197.4 8.6 %collective-permute-start.19 = (bf16[192,192]{0,1:T(8,128)(2,1)S(1)}, bf16[192,192]{0,1:T(8,128)(2,1)S(1)}, u32[]{:S(2)}, u32[]{:S(2)}) collective-permute-start(bf16[192,192]{0,1:T(8,128)(2,1)S(1)} %get-tuple-element.14), channel_id=1, source_target_pairs={{0,8},{1,9},{2,10},{3,11},{4,12},{5,13},{6,14},{7,15},{8,16},{9,17... | collective-permute-start | bytes 221192 | tf_op jit(solution)/shard_map/ppermute | solution.py:43
  203.1 15.6 %collective-permute-start.21 = (bf16[192,192]{0,1:T(8,128)(2,1)S(1)}, bf16[192,192]{0,1:T(8,128)(2,1)S(1)}, u32[]{:S(2)}, u32[]{:S(2)}) collective-permute-start(bf16[192,192]{0,1:T(8,128)(2,1)S(1)} %get-tuple-element.15), channel_id=1, source_target_pairs={{0,24},{1,25},{2,26},{3,27},{4,28},{5,29},{6,30},{7,31},{8,0},{9,1... | collective-permute-start | bytes 221192 | tf_op jit(solution)/shard_map/ppermute | solution.py:43
  206.0 12.7 %collective-permute-start.20 = (bf16[192,192]{0,1:T(8,128)(2,1)S(1)}, bf16[192,192]{0,1:T(8,128)(2,1)S(1)}, u32[]{:S(2)}, u32[]{:S(2)}) collective-permute-start(bf16[192,192]{0,1:T(8,128)(2,1)S(1)} %fusion.39), channel_id=1, source_target_pairs={{0,8},{1,9},{2,10},{3,11},{4,12},{5,13},{6,14},{7,15},{8,16},{9,17... | collective-permute-start | bytes 221192 | tf_op jit(solution)/shard_map/ppermute | solution.py:43
  (5 other events, 9.8 us)

commit v6 on v5

--- a/solution.py
+++ b/solution.py
@@ -43,23 +43,25 @@
         return lax.ppermute(x, self.axis, perm=pairs)
 
 
-def ring_gather(x, ring):
+def ring_gather(x, ring, beside=None):
     n = ring.size
     got, slot = [x], {0: 0}
     cw, ccw = x, x
     for t in range(1, n):
         if t % 2 == 1:
             cw = ring.shift(cw, 1)
+            if t == 1 and beside is not None:
+                cw, beside = lax.optimization_barrier((cw, beside))
             slot[(n - (t + 1) // 2) % n] = len(got)
             got.append(cw)
         else:
             ccw = ring.shift(ccw, -1)
             slot[t // 2] = len(got)
             got.append(ccw)
-    return jnp.stack(got), [slot[k] for k in range(n)]
-
-
-def ring_reduce_scatter(blocks, ring, axis=0):
+    return jnp.stack(got), [slot[k] for k in range(n)], beside
+
+
+def ring_reduce_scatter(blocks, ring, axis=0, beside=None):
     n = ring.size
     me = ring.position()
 
@@ -68,11 +70,14 @@
 
     total = pick(me)
     if n == 1:
-        return total
+        return total, beside
     up, down = n // 2, (n - 1) // 2
     acc = pick(me + up)
     for t in range(1, up + 1):
-        acc = ring.shift(acc.astype(jnp.bfloat16), 1).astype(jnp.float32)
+        acc = ring.shift(acc.astype(jnp.bfloat16), 1)
+        if t == 1 and beside is not None:
+            acc, beside = lax.optimization_barrier((acc, beside))
+        acc = acc.astype(jnp.float32)
         if t < up:
             acc = acc + pick(me + up - t)
     total = total + acc
@@ -83,7 +88,7 @@
             if t < down:
                 acc = acc + pick(me - down + t)
         total = total + acc
-    return total
+    return total, beside
 
 
 def shards(patches, segments, qkv_weight, cotangent, inner_fsdp):
@@ -104,8 +109,9 @@
     ring_x = Ring("seq", lax.axis_size("seq"), 1)
 
     w_mine = lax.dynamic_slice_in_dim(qkv_weight, core * half, half, axis=1)
-    stack_y, slot_y = ring_gather(w_mine, ring_y)
-    stack_zy, slot_z = ring_gather(stack_y, ring_z)
+    stack_y, slot_y, _ = ring_gather(w_mine, ring_y)
+    blocked = features.reshape(features.shape[0], outer_fsdp, inner_fsdp, rows_w)
+    stack_zy, slot_z, blocked = ring_gather(stack_y, ring_z, beside=blocked)
     flat = stack_zy.reshape(-1, rows_w, half)
     me_y, me_z = ring_y.position(), ring_z.position()
     absolute = jnp.arange(n_fsdp, dtype=jnp.int32)
@@ -163,13 +169,13 @@
         contract_last(g_mine, w_mine_all) + contract_last(g_other, w_other_all)
     ).astype(jnp.bfloat16)
 
-    blocked = features.reshape(n_rows, outer_fsdp, inner_fsdp, rows_w)
-    wg_mine = jnp.einsum("pyzd,pc->zydc", blocked, g_mine, preferred_element_type=jnp.float32)
     wg_other = jnp.einsum("pyzd,pc->zydc", blocked, g_other, preferred_element_type=jnp.float32)
     wg_from_partner = dp_partner(wg_other.astype(jnp.bfloat16), 1)
+    wg_mine = jnp.einsum("pyzd,pc->zydc", blocked, g_mine, preferred_element_type=jnp.float32)
+    wg_mine, wg_from_partner = lax.optimization_barrier((wg_mine, wg_from_partner))
     blocks = wg_mine + wg_from_partner.astype(jnp.float32)
-    over_z = ring_reduce_scatter(blocks, ring_z, axis=0)
-    over_fsdp = ring_reduce_scatter(over_z, ring_y)
+    over_z, input_grad = ring_reduce_scatter(blocks, ring_z, axis=0, beside=input_grad)
+    over_fsdp, _ = ring_reduce_scatter(over_z, ring_y)
 
     by_seq = lax.all_gather(over_fsdp, "seq", axis=0, tiled=False)
     over_seq = by_seq[0]

time: 249 us -> 232 us (0.932)
  waiting for transfers between devices: 59.6 us -> 47.3 us
  matrix products: 22.6 us -> 19.6 us
  blocking collectives: 41.4 us -> 44.4 us
  local copies, waits for them, and re-layouts: 20.1 us -> 17.5 us
    ppermute x20, waiting for transfers between devices: 54.3 us -> 44.4 us  [shift(): return lax.ppermute(x, self.axis, perm=pairs)]
    convert_element_type x4, other arithmetic: 7.41 us -> 3.22 us  [ring_reduce_scatter(): acc = ring.shift(acc.astype(jnp.bfloat16), 1)]
    all_gather x1, blocking collectives: 16.6 us -> 19.9 us  [shards(): by_dp = lax.all_gather(over_seq, 'dp', axis=0, tiled=False)]
    add x0 -> x1, other arithmetic: none -> 3.03 us  [shards(): blocks = wg_mine + wg_from_partner.astype(jnp.float32)]
    dot_general x1, matrix products: 5.36 us -> 2.4 us  [shards(): jnp.einsum('pyzd,pc->zydc', blocked, g_mine, preferred_element_type=jnp.f...]
    ppermute x2, waiting for transfers between devices: 5.39 us -> 2.87 us  [dp_partner(): return lax.ppermute(x, 'dp', perm=pairs)]
    unnamed x20 -> x22, local copies, waits for them, and re-layouts: 5.52 us -> 3.79 us
  transfers between devices with their start and end apart: 22 -> 22, of which waited for: 13 -> 18; matrix products, arithmetic and copies ran while one was open for 7% -> 8% of each run, Pallas kernels for 0% -> 0%
where the time goes in v6:
time: 232 us; the launch traced here: 231 us
  starting transfers between devices  90.7 us (39%)
  waiting for transfers between devices  47.3 us (20%)
  blocking collectives  44.4 us (19%)
  matrix products  19.6 us (8%)
  local copies, waits for them, and re-layouts  17.5 us (8%)
  other arithmetic  9.94 us (4%)
    ppermute x20, starting transfers between devices, shift(): return lax.ppermute(x, self.axis, perm=pairs)  78.1 us
    ppermute x20, waiting for transfers between devices, shift(): return lax.ppermute(x, self.axis, perm=pairs)  44.4 us
    all_gather x1, blocking collectives, shards(): by_dp = lax.all_gather(over_seq, 'dp', axis=0, tiled=False)  19.9 us
    all_gather x1, blocking collectives, shards(): packed_all = lax.all_gather(packed, 'seq', axis=0, tiled=True)  12.9 us
    ppermute x2, starting transfers between devices, dp_partner(): return lax.ppermute(x, 'dp', perm=pairs)  12.6 us
    all_gather x1, blocking collectives, shards(): by_seq = lax.all_gather(over_fsdp, 'seq', axis=0, tiled=False)  11.5 us
    dot_general x4, matrix products, contract_last(): lax.dot_general(left, right, (((1,), (1,)), ((), ())), preferred_element_...  6.51 us
    another operation x1, local copies, waits for them, and re-layouts, shards(): features.reshape(features.shape[0], outer_fsdp, inner_fsdp, rows_w)  6.44 us
  transfers between devices with their start and end apart: 22, of which 18 were waited for; matrix products, arithmetic and copies ran while one was open for 8% of the time, Pallas kernels for 0%

profile of v6, /device:TPU:1, one launch (start us, length us, event | category | flops | bytes accessed | tf_op | source)
XLA Modules:
  0.0 230.8 jit_solution(15228257013158225127)
XLA Ops:
  1.6 5.0 %collective-permute-start = (bf16[192,192]{1,0:T(8,128)(2,1)S(1)}, bf16[192,192]{1,0:T(8,128)(2,1)S(1)}, u32[]{:S(2)}, u32[]{:S(2)}) collective-permute-start(bf16[192,192]{1,0:T(8,128)(2,1)S(1)} %constant_dynamic-slice_fusion), channel_id=1, source_target_pairs={{0,8},{1,9},{2,10},{3,11},{4,12},{5,13},{6,14},{7,15},{8,16},{9,17... | collective-permute-start | bytes 221192 | tf_op jit(solution)/shard_map/ppermute | solution.py:43
  6.7 3.6 %collective-permute-start.1 = (bf16[192,192]{1,0:T(8,128)(2,1)S(1)}, bf16[192,192]{1,0:T(8,128)(2,1)S(1)}, u32[]{:S(2)}, u32[]{:S(2)}) collective-permute-start(bf16[192,192]{1,0:T(8,128)(2,1)S(1)} %constant_dynamic-slice_fusion), channel_id=1, source_target_pairs={{0,24},{1,25},{2,26},{3,27},{4,28},{5,29},{6,30},{7,31},{8,0},{9,1... | collective-permute-start | bytes 221192 | tf_op jit(solution)/shard_map/ppermute | solution.py:43
  11.7 4.6 %collective-permute-start.2 = (bf16[192,192]{1,0:T(8,128)(2,1)S(1)}, bf16[192,192]{1,0:T(8,128)(2,1)S(1)}, u32[]{:S(2)}, u32[]{:S(2)}) collective-permute-start(bf16[192,192]{1,0:T(8,128)(2,1)S(1)} %collective-permute-done), channel_id=1, source_target_pairs={{0,8},{1,9},{2,10},{3,11},{4,12},{5,13},{6,14},{7,15},{8,16},{9,17... | collective-permute-start | bytes 221192 | tf_op jit(solution)/shard_map/ppermute | solution.py:43
  19.4 3.9 %collective-permute-start.3 = (bf16[4,192,192]{2,1,0:T(8,128)(2,1)S(1)}, bf16[4,192,192]{2,1,0:T(8,128)(2,1)S(1)}, u32[]{:S(2)}, u32[]{:S(2)}) collective-permute-start(bf16[4,192,192]{2,1,0:T(8,128)(2,1)S(1)} %pad_maximum_fusion), channel_id=1, source_target_pairs={{0,1},{1,2},{2,3},{3,4},{4,5},{5,6},{6,7},{7,0},{8,9},{9,10},{10,1... | collective-permute-start | bytes 884744 | tf_op jit(solution)/shard_map/ppermute | solution.py:43
  23.3 6.4 %reshape_squeeze.3 = bf16[192,4,8,192]{3,2,1,0:T(8,128)(2,1)} reshape(bf16[1,192,6144]{2,1,0:T(8,128)(2,1)} %param.6) | data formatting | bytes 4718592 | tf_op jit(solution)/shard_map/reshape;squeeze | solution.py:113
  29.8 8.6 %collective-permute-start.4 = (bf16[4,192,192]{2,1,0:T(8,128)(2,1)S(1)}, bf16[4,192,192]{2,1,0:T(8,128)(2,1)S(1)}, u32[]{:S(2)}, u32[]{:S(2)}) collective-permute-start(bf16[4,192,192]{2,1,0:T(8,128)(2,1)S(1)} %pad_maximum_fusion), channel_id=1, source_target_pairs={{0,7},{1,0},{2,1},{3,2},{4,3},{5,4},{6,5},{7,6},{8,15},{9,8},{10,9... | collective-permute-start | bytes 884744 | tf_op jit(solution)/shard_map/ppermute | solution.py:43
  43.7 5.3 %collective-permute-start.6 = (bf16[4,192,192]{2,1,0:T(8,128)(2,1)S(1)}, bf16[4,192,192]{2,1,0:T(8,128)(2,1)S(1)}, u32[]{:S(2)}, u32[]{:S(2)}) collective-permute-start(bf16[4,192,192]{2,1,0:T(8,128)(2,1)S(1)} %collective-permute-done.4), channel_id=1, source_target_pairs={{0,7},{1,0},{2,1},{3,2},{4,3},{5,4},{6,5},{7,6},{8,15},{9,8},{10,9... | collective-permute-start | bytes 884744 | tf_op jit(solution)/shard_map/ppermute | solution.py:43
  53.8 5.0 %collective-permute-start.8 = (bf16[4,192,192]{2,1,0:T(8,128)(2,1)S(1)}, bf16[4,192,192]{2,1,0:T(8,128)(2,1)S(1)}, u32[]{:S(2)}, u32[]{:S(2)}) collective-permute-start(bf16[4,192,192]{2,1,0:T(8,128)(2,1)S(1)} %collective-permute-done.6), channel_id=1, source_target_pairs={{0,7},{1,0},{2,1},{3,2},{4,3},{5,4},{6,5},{7,6},{8,15},{9,8},{10,9... | collective-permute-start | bytes 884744 | tf_op jit(solution)/shard_map/ppermute | solution.py:43
  63.5 5.0 %collective-permute-done.9 = bf16[4,192,192]{2,1,0:T(8,128)(2,1)S(1)} collective-permute-done((bf16[4,192,192]{2,1,0:T(8,128)(2,1)S(1)}, bf16[4,192,192]{2,1,0:T(8,128)(2,1)S(1)}, u32[]{:S(2)}, u32[]{:S(2)}) %collective-permute-start.9) | collective-permute-done | bytes 294944 | tf_op jit(solution)/shard_map/ppermute | solution.py:43
  75.5 8.4 %collective-permute-start.10 = (bf16[6144,192]{0,1:T(8,128)(2,1)}, bf16[6144,192]{0,1:T(8,128)(2,1)}, u32[]{:S(2)}, u32[]{:S(2)}) collective-permute-start(bf16[6144,192]{0,1:T(8,128)(2,1)} %copy.32), channel_id=1, source_target_pairs={{0,128},{128,0},{256,384},{384,256},{1,129},{129,1},{257,385},{385... | collective-permute-start | bytes 7077896 | tf_op jit(solution)/shard_map/ppermute | solution.py:23
  91.1 12.9 %all_gather.13 = bf16[768,640]{1,0:T(8,128)(2,1)S(1)} all-gather(bf16[192,640]{1,0:T(8,128)(2,1)S(1)} %pad_maximum_fusion.2), channel_id=1, replica_groups=mesh['dp'=4,'seq'=4,'fsdp'=32] {'seq'}, dimensions={0}, use_global_device_ids=true | all-gather | bytes 1228800 | tf_op jit(solution)/shard_map/all_gather | solution.py:137
  108.5 4.1 %convert_bitcast_fusion = bf16[8,4,192,192]{2,3,0,1:T(8,128)(2,1)} fusion(bf16[192,4,8,192]{3,2,1,0:T(8,128)(2,1)S(1)} %copy-done.1, pred[]{:T(512)S(6)} %eq.41, bf16[192,128]{1,0:T(8,128)(2,1)S(1)} %convolution_convert_fusion.1, bf16[192,128]{1,0:T(8,128)(2,1)S(1)} %convolution_convert_fusion.2, bf16[192,128]{1,0:T(8,128)(2,1)S(1)} %convolution_convert_fusion), kind=kOutput, calls=%fused_computation.8 | convolution fusion | flops 454496256 | bytes 4866049 | tf_op jit(solution)/shard_map/pyzd,pc->zydc/dot_general | solution.py:172
  112.7 4.2 %collective-permute-start.11 = (bf16[8,4,192,192]{2,3,0,1:T(8,128)(2,1)}, bf16[8,4,192,192]{2,3,0,1:T(8,128)(2,1)}, u32[]{:S(2)}, u32[]{:S(2)}) collective-permute-start(bf16[8,4,192,192]{2,3,0,1:T(8,128)(2,1)} %convert_bitcast_fusion), channel_id=1, source_target_pairs={{0,128},{128,0},{256,384},{384,256},{1,129},{129,1},{257,385},{385... | collective-permute-start | bytes 7077896 | tf_op jit(solution)/shard_map/ppermute | solution.py:23
  127.3 4.0 %fusion = bf16[192,6144]{1,0:T(8,128)(2,1)} fusion(f32[192,6144]{1,0:T(8,128)S(1)} %fusion.64, bf16[6144,192]{0,1:T(8,128)(2,1)} %collective-permute-done.10, pred[]{:T(512)S(6)} %eq.41, bf16[192,128]{1,0:T(8,128)(2,1)S(1)} %convolution_convert_fusion.1, bf16[192,128]{1,0:T(8,128)(2,1)S(1)} %convolution_convert_fusion.2, ...), kind=kOutput, calls=%fused_computation.3 | convolution fusion | flops 455675904 | bytes 9584641 | tf_op jit(solution)/shard_map/dot_general | solution.py:16
  131.3 4.5 %collective-permute-start.16 = (bf16[4,192,192]{1,2,0:T(8,128)(2,1)S(1)}, bf16[4,192,192]{1,2,0:T(8,128)(2,1)S(1)}, u32[]{:S(2)}, u32[]{:S(2)}) collective-permute-start(bf16[4,192,192]{1,2,0:T(8,128)(2,1)S(1)} %get-tuple-element.22), channel_id=1, source_target_pairs={{0,7},{1,0},{2,1},{3,2},{4,3},{5,4},{6,5},{7,6},{8,15},{9,8},{10,9... | collective-permute-start | bytes 884744 | tf_op jit(solution)/shard_map/ppermute | solution.py:43
  143.6 7.9 %collective-permute-done.13 = bf16[4,192,192]{1,2,0:T(8,128)(2,1)S(1)} collective-permute-done((bf16[4,192,192]{1,2,0:T(8,128)(2,1)S(1)}, bf16[4,192,192]{1,2,0:T(8,128)(2,1)S(1)}, u32[]{:S(2)}, u32[]{:S(2)}) %collective-permute-start.13) | collective-permute-done | bytes 294944 | tf_op jit(solution)/shard_map/ppermute | solution.py:43
  154.9 4.6 %collective-permute-start.17 = (bf16[4,192,192]{1,2,0:T(8,128)(2,1)S(1)}, bf16[4,192,192]{1,2,0:T(8,128)(2,1)S(1)}, u32[]{:S(2)}, u32[]{:S(2)}) collective-permute-start(bf16[4,192,192]{1,2,0:T(8,128)(2,1)S(1)} %get-tuple-element.21), channel_id=1, source_target_pairs={{0,7},{1,0},{2,1},{3,2},{4,3},{5,4},{6,5},{7,6},{8,15},{9,8},{10,9... | collective-permute-start | bytes 884744 | tf_op jit(solution)/shard_map/ppermute | solution.py:43
  159.6 5.0 %collective-permute-done.14 = bf16[4,192,192]{1,2,0:T(8,128)(2,1)S(1)} collective-permute-done((bf16[4,192,192]{1,2,0:T(8,128)(2,1)S(1)}, bf16[4,192,192]{1,2,0:T(8,128)(2,1)S(1)}, u32[]{:S(2)}, u32[]{:S(2)}) %collective-permute-start.14) | collective-permute-done | bytes 294944 | tf_op jit(solution)/shard_map/ppermute | solution.py:43
  169.0 5.3 %collective-permute-start.18 = (bf16[4,192,192]{1,2,0:T(8,128)(2,1)S(1)}, bf16[4,192,192]{1,2,0:T(8,128)(2,1)S(1)}, u32[]{:S(2)}, u32[]{:S(2)}) collective-permute-start(bf16[4,192,192]{1,2,0:T(8,128)(2,1)S(1)} %get-tuple-element.19), channel_id=1, source_target_pairs={{0,7},{1,0},{2,1},{3,2},{4,3},{5,4},{6,5},{7,6},{8,15},{9,8},{10,9... | collective-permute-start | bytes 884744 | tf_op jit(solution)/shard_map/ppermute | solution.py:43
  174.4 4.1 %collective-permute-done.15 = bf16[4,192,192]{1,2,0:T(8,128)(2,1)S(1)} collective-permute-done((bf16[4,192,192]{1,2,0:T(8,128)(2,1)S(1)}, bf16[4,192,192]{1,2,0:T(8,128)(2,1)S(1)}, u32[]{:S(2)}, u32[]{:S(2)}) %collective-permute-start.15) | collective-permute-done | bytes 294944 | tf_op jit(solution)/shard_map/ppermute | solution.py:43
  180.7 4.4 %collective-permute-start.19 = (bf16[192,192]{0,1:T(8,128)(2,1)S(1)}, bf16[192,192]{0,1:T(8,128)(2,1)S(1)}, u32[]{:S(2)}, u32[]{:S(2)}) collective-permute-start(bf16[192,192]{0,1:T(8,128)(2,1)S(1)} %get-tuple-element.26), channel_id=1, source_target_pairs={{0,8},{1,9},{2,10},{3,11},{4,12},{5,13},{6,14},{7,15},{8,16},{9,17... | collective-permute-start | bytes 221192 | tf_op jit(solution)/shard_map/ppermute | solution.py:43
  189.2 6.9 %collective-permute-start.20 = (bf16[192,192]{0,1:T(8,128)(2,1)S(1)}, bf16[192,192]{0,1:T(8,128)(2,1)S(1)}, u32[]{:S(2)}, u32[]{:S(2)}) collective-permute-start(bf16[192,192]{0,1:T(8,128)(2,1)S(1)} %fusion.39), channel_id=1, source_target_pairs={{0,8},{1,9},{2,10},{3,11},{4,12},{5,13},{6,14},{7,15},{8,16},{9,17... | collective-permute-start | bytes 221192 | tf_op jit(solution)/shard_map/ppermute | solution.py:43
  198.5 11.5 %all-gather = f32[768,192]{1,0:T(8,128)S(1)} all-gather(f32[192,192]{1,0:T(8,128)S(1)} %copy.40), channel_id=2, replica_groups=mesh['dp'=4,'seq'=4,'fsdp'=32] {'seq'}, dimensions={0}, use_global_device_ids=true | all-gather | bytes 737280 | tf_op jit(solution)/shard_map/all_gather | solution.py:180
  210.0 19.9 %all_gather.16 = f32[4,192,192]{2,1,0:T(8,128)S(1)} all-gather(f32[1,192,192]{2,1,0:T(8,128)S(1)} %fusion.38), channel_id=1, replica_groups=mesh['dp'=4,'seq'=4,'fsdp'=32] {'dp'}, dimensions={0}, use_global_device_ids=true | all-gather | bytes 737280 | tf_op jit(solution)/shard_map/all_gather | solution.py:184
  (91 shorter events, 74.1 us)
Async XLA Ops:
  1.6 10.1 %collective-permute-start = (bf16[192,192]{1,0:T(8,128)(2,1)S(1)}, bf16[192,192]{1,0:T(8,128)(2,1)S(1)}, u32[]{:S(2)}, u32[]{:S(2)}) collective-permute-start(bf16[192,192]{1,0:T(8,128)(2,1)S(1)} %constant_dynamic-slice_fusion), channel_id=1, source_target_pairs={{0,8},{1,9},{2,10},{3,11},{4,12},{5,13},{6,14},{7,15},{8,16},{9,17... | collective-permute-start | bytes 221192 | tf_op jit(solution)/shard_map/ppermute | solution.py:43
  6.7 9.9 %collective-permute-start.1 = (bf16[192,192]{1,0:T(8,128)(2,1)S(1)}, bf16[192,192]{1,0:T(8,128)(2,1)S(1)}, u32[]{:S(2)}, u32[]{:S(2)}) collective-permute-start(bf16[192,192]{1,0:T(8,128)(2,1)S(1)} %constant_dynamic-slice_fusion), channel_id=1, source_target_pairs={{0,24},{1,25},{2,26},{3,27},{4,28},{5,29},{6,30},{7,31},{8,0},{9,1... | collective-permute-start | bytes 221192 | tf_op jit(solution)/shard_map/ppermute | solution.py:43
  11.7 7.5 %collective-permute-start.2 = (bf16[192,192]{1,0:T(8,128)(2,1)S(1)}, bf16[192,192]{1,0:T(8,128)(2,1)S(1)}, u32[]{:S(2)}, u32[]{:S(2)}) collective-permute-start(bf16[192,192]{1,0:T(8,128)(2,1)S(1)} %collective-permute-done), channel_id=1, source_target_pairs={{0,8},{1,9},{2,10},{3,11},{4,12},{5,13},{6,14},{7,15},{8,16},{9,17... | collective-permute-start | bytes 221192 | tf_op jit(solution)/shard_map/ppermute | solution.py:43
  19.4 19.1 %collective-permute-start.3 = (bf16[4,192,192]{2,1,0:T(8,128)(2,1)S(1)}, bf16[4,192,192]{2,1,0:T(8,128)(2,1)S(1)}, u32[]{:S(2)}, u32[]{:S(2)}) collective-permute-start(bf16[4,192,192]{2,1,0:T(8,128)(2,1)S(1)} %pad_maximum_fusion), channel_id=1, source_target_pairs={{0,1},{1,2},{2,3},{3,4},{4,5},{5,6},{6,7},{7,0},{8,9},{9,10},{10,1... | collective-permute-start | bytes 884744 | tf_op jit(solution)/shard_map/ppermute | solution.py:43
  29.8 14.0 %collective-permute-start.4 = (bf16[4,192,192]{2,1,0:T(8,128)(2,1)S(1)}, bf16[4,192,192]{2,1,0:T(8,128)(2,1)S(1)}, u32[]{:S(2)}, u32[]{:S(2)}) collective-permute-start(bf16[4,192,192]{2,1,0:T(8,128)(2,1)S(1)} %pad_maximum_fusion), channel_id=1, source_target_pairs={{0,7},{1,0},{2,1},{3,2},{4,3},{5,4},{6,5},{7,6},{8,15},{9,8},{10,9... | collective-permute-start | bytes 884744 | tf_op jit(solution)/shard_map/ppermute | solution.py:43
  38.4 10.7 %collective-permute-start.5 = (bf16[4,192,192]{2,1,0:T(8,128)(2,1)S(1)}, bf16[4,192,192]{2,1,0:T(8,128)(2,1)S(1)}, u32[]{:S(2)}, u32[]{:S(2)}) collective-permute-start(bf16[4,192,192]{2,1,0:T(8,128)(2,1)S(1)} %collective-permute-done.3), channel_id=1, source_target_pairs={{0,1},{1,2},{2,3},{3,4},{4,5},{5,6},{6,7},{7,0},{8,9},{9,10},{10,1... | collective-permute-start | bytes 884744 | tf_op jit(solution)/shard_map/ppermute | solution.py:43
  43.7 10.0 %collective-permute-start.6 = (bf16[4,192,192]{2,1,0:T(8,128)(2,1)S(1)}, bf16[4,192,192]{2,1,0:T(8,128)(2,1)S(1)}, u32[]{:S(2)}, u32[]{:S(2)}) collective-permute-start(bf16[4,192,192]{2,1,0:T(8,128)(2,1)S(1)} %collective-permute-done.4), channel_id=1, source_target_pairs={{0,7},{1,0},{2,1},{3,2},{4,3},{5,4},{6,5},{7,6},{8,15},{9,8},{10,9... | collective-permute-start | bytes 884744 | tf_op jit(solution)/shard_map/ppermute | solution.py:43
  49.1 9.7 %collective-permute-start.7 = (bf16[4,192,192]{2,1,0:T(8,128)(2,1)S(1)}, bf16[4,192,192]{2,1,0:T(8,128)(2,1)S(1)}, u32[]{:S(2)}, u32[]{:S(2)}) collective-permute-start(bf16[4,192,192]{2,1,0:T(8,128)(2,1)S(1)} %collective-permute-done.5), channel_id=1, source_target_pairs={{0,1},{1,2},{2,3},{3,4},{4,5},{5,6},{6,7},{7,0},{8,9},{9,10},{10,1... | collective-permute-start | bytes 884744 | tf_op jit(solution)/shard_map/ppermute | solution.py:43
  53.8 9.7 %collective-permute-start.8 = (bf16[4,192,192]{2,1,0:T(8,128)(2,1)S(1)}, bf16[4,192,192]{2,1,0:T(8,128)(2,1)S(1)}, u32[]{:S(2)}, u32[]{:S(2)}) collective-permute-start(bf16[4,192,192]{2,1,0:T(8,128)(2,1)S(1)} %collective-permute-done.6), channel_id=1, source_target_pairs={{0,7},{1,0},{2,1},{3,2},{4,3},{5,4},{6,5},{7,6},{8,15},{9,8},{10,9... | collective-permute-start | bytes 884744 | tf_op jit(solution)/shard_map/ppermute | solution.py:43
  58.8 9.7 %collective-permute-start.9 = (bf16[4,192,192]{2,1,0:T(8,128)(2,1)S(1)}, bf16[4,192,192]{2,1,0:T(8,128)(2,1)S(1)}, u32[]{:S(2)}, u32[]{:S(2)}) collective-permute-start(bf16[4,192,192]{2,1,0:T(8,128)(2,1)S(1)} %collective-permute-done.7), channel_id=1, source_target_pairs={{0,1},{1,2},{2,3},{3,4},{4,5},{5,6},{6,7},{7,0},{8,9},{9,10},{10,1... | collective-permute-start | bytes 884744 | tf_op jit(solution)/shard_map/ppermute | solution.py:43
  72.9 11.0 %copy-start.7 = (s32[1,192]{1,0:T(1,128)S(1)}, s32[1,192]{1,0:T(1,128)}, u32[]{:S(2)}) copy-start(s32[1,192]{1,0:T(1,128)} %param.7) | copy-start | bytes 2308
  75.5 12.9 %collective-permute-start.10 = (bf16[6144,192]{0,1:T(8,128)(2,1)}, bf16[6144,192]{0,1:T(8,128)(2,1)}, u32[]{:S(2)}, u32[]{:S(2)}) collective-permute-start(bf16[6144,192]{0,1:T(8,128)(2,1)} %copy.32), channel_id=1, source_target_pairs={{0,128},{128,0},{256,384},{384,256},{1,129},{129,1},{257,385},{385... | collective-permute-start | bytes 7077896 | tf_op jit(solution)/shard_map/ppermute | solution.py:23
  112.7 9.6 %collective-permute-start.11 = (bf16[8,4,192,192]{2,3,0,1:T(8,128)(2,1)}, bf16[8,4,192,192]{2,3,0,1:T(8,128)(2,1)}, u32[]{:S(2)}, u32[]{:S(2)}) collective-permute-start(bf16[8,4,192,192]{2,3,0,1:T(8,128)(2,1)} %convert_bitcast_fusion), channel_id=1, source_target_pairs={{0,128},{128,0},{256,384},{384,256},{1,129},{129,1},{257,385},{385... | collective-permute-start | bytes 7077896 | tf_op jit(solution)/shard_map/ppermute | solution.py:23
  125.3 13.5 %copy-start.3 = (f32[8,4,192,192]{2,3,0,1:T(8,128)}, f32[8,4,192,192]{2,3,0,1:T(8,128)S(1)}, u32[]{:S(2)}) copy-start(f32[8,4,192,192]{2,3,0,1:T(8,128)S(1)} %convert_add_fusion) | copy-start | bytes 14155780
  125.4 13.4 %collective-permute-start.12 = (bf16[4,192,192]{1,2,0:T(8,128)(2,1)S(1)}, bf16[4,192,192]{1,2,0:T(8,128)(2,1)S(1)}, u32[]{:S(2)}, u32[]{:S(2)}) collective-permute-start(bf16[4,192,192]{1,2,0:T(8,128)(2,1)S(1)} %get-tuple-element.23), channel_id=1, source_target_pairs={{0,1},{1,2},{2,3},{3,4},{4,5},{5,6},{6,7},{7,0},{8,9},{9,10},{10,1... | collective-permute-start | bytes 884744 | tf_op jit(solution)/shard_map/ppermute | solution.py:43
  131.3 12.3 %collective-permute-start.16 = (bf16[4,192,192]{1,2,0:T(8,128)(2,1)S(1)}, bf16[4,192,192]{1,2,0:T(8,128)(2,1)S(1)}, u32[]{:S(2)}, u32[]{:S(2)}) collective-permute-start(bf16[4,192,192]{1,2,0:T(8,128)(2,1)S(1)} %get-tuple-element.22), channel_id=1, source_target_pairs={{0,7},{1,0},{2,1},{3,2},{4,3},{5,4},{6,5},{7,6},{8,15},{9,8},{10,9... | collective-permute-start | bytes 884744 | tf_op jit(solution)/shard_map/ppermute | solution.py:43
  138.9 12.5 %collective-permute-start.13 = (bf16[4,192,192]{1,2,0:T(8,128)(2,1)S(1)}, bf16[4,192,192]{1,2,0:T(8,128)(2,1)S(1)}, u32[]{:S(2)}, u32[]{:S(2)}) collective-permute-start(bf16[4,192,192]{1,2,0:T(8,128)(2,1)S(1)} %fusion.28), channel_id=1, source_target_pairs={{0,1},{1,2},{2,3},{3,4},{4,5},{5,6},{6,7},{7,0},{8,9},{9,10},{10,1... | collective-permute-start | bytes 884744 | tf_op jit(solution)/shard_map/ppermute | solution.py:43
  153.0 11.6 %collective-permute-start.14 = (bf16[4,192,192]{1,2,0:T(8,128)(2,1)S(1)}, bf16[4,192,192]{1,2,0:T(8,128)(2,1)S(1)}, u32[]{:S(2)}, u32[]{:S(2)}) collective-permute-start(bf16[4,192,192]{1,2,0:T(8,128)(2,1)S(1)} %get-tuple-element.20), channel_id=1, source_target_pairs={{0,1},{1,2},{2,3},{3,4},{4,5},{5,6},{6,7},{7,0},{8,9},{9,10},{10,1... | collective-permute-start | bytes 884744 | tf_op jit(solution)/shard_map/ppermute | solution.py:43
  154.9 10.6 %collective-permute-start.17 = (bf16[4,192,192]{1,2,0:T(8,128)(2,1)S(1)}, bf16[4,192,192]{1,2,0:T(8,128)(2,1)S(1)}, u32[]{:S(2)}, u32[]{:S(2)}) collective-permute-start(bf16[4,192,192]{1,2,0:T(8,128)(2,1)S(1)} %get-tuple-element.21), channel_id=1, source_target_pairs={{0,7},{1,0},{2,1},{3,2},{4,3},{5,4},{6,5},{7,6},{8,15},{9,8},{10,9... | collective-permute-start | bytes 884744 | tf_op jit(solution)/shard_map/ppermute | solution.py:43
  167.1 11.4 %collective-permute-start.15 = (bf16[4,192,192]{1,2,0:T(8,128)(2,1)S(1)}, bf16[4,192,192]{1,2,0:T(8,128)(2,1)S(1)}, u32[]{:S(2)}, u32[]{:S(2)}) collective-permute-start(bf16[4,192,192]{1,2,0:T(8,128)(2,1)S(1)} %get-tuple-element.18), channel_id=1, source_target_pairs={{0,1},{1,2},{2,3},{3,4},{4,5},{5,6},{6,7},{7,0},{8,9},{9,10},{10,1... | collective-permute-start | bytes 884744 | tf_op jit(solution)/shard_map/ppermute | solution.py:43
  169.0 10.4 %collective-permute-start.18 = (bf16[4,192,192]{1,2,0:T(8,128)(2,1)S(1)}, bf16[4,192,192]{1,2,0:T(8,128)(2,1)S(1)}, u32[]{:S(2)}, u32[]{:S(2)}) collective-permute-start(bf16[4,192,192]{1,2,0:T(8,128)(2,1)S(1)} %get-tuple-element.19), channel_id=1, source_target_pairs={{0,7},{1,0},{2,1},{3,2},{4,3},{5,4},{6,5},{7,6},{8,15},{9,8},{10,9... | collective-permute-start | bytes 884744 | tf_op jit(solution)/shard_map/ppermute | solution.py:43
  180.7 8.5 %collective-permute-start.19 = (bf16[192,192]{0,1:T(8,128)(2,1)S(1)}, bf16[192,192]{0,1:T(8,128)(2,1)S(1)}, u32[]{:S(2)}, u32[]{:S(2)}) collective-permute-start(bf16[192,192]{0,1:T(8,128)(2,1)S(1)} %get-tuple-element.26), channel_id=1, source_target_pairs={{0,8},{1,9},{2,10},{3,11},{4,12},{5,13},{6,14},{7,15},{8,16},{9,17... | collective-permute-start | bytes 221192 | tf_op jit(solution)/shard_map/ppermute | solution.py:43
  185.1 11.1 %collective-permute-start.21 = (bf16[192,192]{0,1:T(8,128)(2,1)S(1)}, bf16[192,192]{0,1:T(8,128)(2,1)S(1)}, u32[]{:S(2)}, u32[]{:S(2)}) collective-permute-start(bf16[192,192]{0,1:T(8,128)(2,1)S(1)} %get-tuple-element.27), channel_id=1, source_target_pairs={{0,24},{1,25},{2,26},{3,27},{4,28},{5,29},{6,30},{7,31},{8,0},{9,1... | collective-permute-start | bytes 221192 | tf_op jit(solution)/shard_map/ppermute | solution.py:43
  189.2 9.1 %collective-permute-start.20 = (bf16[192,192]{0,1:T(8,128)(2,1)S(1)}, bf16[192,192]{0,1:T(8,128)(2,1)S(1)}, u32[]{:S(2)}, u32[]{:S(2)}) collective-permute-start(bf16[192,192]{0,1:T(8,128)(2,1)S(1)} %fusion.39), channel_id=1, source_target_pairs={{0,8},{1,9},{2,10},{3,11},{4,12},{5,13},{6,14},{7,15},{8,16},{9,17... | collective-permute-start | bytes 221192 | tf_op jit(solution)/shard_map/ppermute | solution.py:43
  (6 other events, 15.3 us)

commit v7 on v6

--- a/solution.py
+++ b/solution.py
@@ -43,22 +43,41 @@
         return lax.ppermute(x, self.axis, perm=pairs)
 
 
+def halves_axis(shape):
+    return 0 if shape[0] % 2 == 0 else 1
+
+
+def split_halves(x):
+    axis = halves_axis(x.shape)
+    size = x.shape[axis]
+    return (
+        lax.slice_in_dim(x, 0, size // 2, axis=axis),
+        lax.slice_in_dim(x, size // 2, size, axis=axis),
+        axis,
+    )
+
+
 def ring_gather(x, ring, beside=None):
     n = ring.size
-    got, slot = [x], {0: 0}
+    by_offset = {0: x}
     cw, ccw = x, x
-    for t in range(1, n):
-        if t % 2 == 1:
-            cw = ring.shift(cw, 1)
-            if t == 1 and beside is not None:
-                cw, beside = lax.optimization_barrier((cw, beside))
-            slot[(n - (t + 1) // 2) % n] = len(got)
-            got.append(cw)
-        else:
-            ccw = ring.shift(ccw, -1)
-            slot[t // 2] = len(got)
-            got.append(ccw)
-    return jnp.stack(got), [slot[k] for k in range(n)], beside
+    far = n // 2 if n % 2 == 0 else None
+    for t in range(1, (n - 1) // 2 + 1):
+        cw = ring.shift(cw, 1)
+        by_offset[n - t] = cw
+        ccw = ring.shift(ccw, -1)
+        if t == 1 and beside is not None:
+            ccw, beside = lax.optimization_barrier((ccw, beside))
+        by_offset[t] = ccw
+    if far is not None:
+        top, _, axis = split_halves(cw)
+        _, bottom, _ = split_halves(ccw)
+        top = ring.shift(top, 1)
+        bottom = ring.shift(bottom, -1)
+        if far == 1 and beside is not None:
+            bottom, beside = lax.optimization_barrier((bottom, beside))
+        by_offset[far] = jnp.concatenate([top, bottom], axis=axis)
+    return jnp.stack([by_offset[k] for k in range(n)]), beside
 
 
 def ring_reduce_scatter(blocks, ring, axis=0, beside=None):
@@ -68,26 +87,44 @@
     def pick(index):
         return lax.dynamic_index_in_dim(blocks, index % n, axis=axis, keepdims=False)
 
+    def send(value, step):
+        return ring.shift(value.astype(jnp.bfloat16), step)
+
     total = pick(me)
     if n == 1:
         return total, beside
-    up, down = n // 2, (n - 1) // 2
-    acc = pick(me + up)
-    for t in range(1, up + 1):
-        acc = ring.shift(acc.astype(jnp.bfloat16), 1)
-        if t == 1 and beside is not None:
+    h = n // 2
+    even = n % 2 == 0
+    results = []
+    for direction in (1, -1):
+        steps = h if (even or direction == 1) else (n - 1) // 2
+        if steps == 0:
+            continue
+        start = pick(me + direction * steps)
+        if even:
+            top, bottom, split = split_halves(start)
+            start = top if direction == 1 else bottom
+        acc = send(start, direction)
+        if direction == 1 and beside is not None:
             acc, beside = lax.optimization_barrier((acc, beside))
         acc = acc.astype(jnp.float32)
-        if t < up:
-            acc = acc + pick(me + up - t)
-    total = total + acc
-    if down:
-        acc = pick(me - down)
-        for t in range(1, down + 1):
-            acc = ring.shift(acc.astype(jnp.bfloat16), -1).astype(jnp.float32)
-            if t < down:
-                acc = acc + pick(me - down + t)
-        total = total + acc
+        for t in range(2, steps + 1):
+            own = pick(me + direction * (steps - t + 1))
+            if even and t == 2:
+                top, bottom, split = split_halves(own)
+                if direction == 1:
+                    own = jnp.concatenate([top + acc, bottom], axis=split)
+                else:
+                    own = jnp.concatenate([top, bottom + acc], axis=split)
+            else:
+                own = own + acc
+            acc = send(own, direction).astype(jnp.float32)
+        results.append(acc)
+    if even and h == 1:
+        total = total + jnp.concatenate(results, axis=halves_axis(total.shape))
+    else:
+        for r in results:
+            total = total + r
     return total, beside
 
 
@@ -109,15 +146,15 @@
     ring_x = Ring("seq", lax.axis_size("seq"), 1)
 
     w_mine = lax.dynamic_slice_in_dim(qkv_weight, core * half, half, axis=1)
-    stack_y, slot_y, _ = ring_gather(w_mine, ring_y)
+    stack_y, _ = ring_gather(w_mine, ring_y)
     blocked = features.reshape(features.shape[0], outer_fsdp, inner_fsdp, rows_w)
-    stack_zy, slot_z, blocked = ring_gather(stack_y, ring_z, beside=blocked)
+    stack_zy, blocked = ring_gather(stack_y, ring_z, beside=blocked)
     flat = stack_zy.reshape(-1, rows_w, half)
     me_y, me_z = ring_y.position(), ring_z.position()
     absolute = jnp.arange(n_fsdp, dtype=jnp.int32)
     rel_y = (absolute // inner_fsdp - me_y) % outer_fsdp
     rel_z = (absolute % inner_fsdp - me_z) % inner_fsdp
-    order = jnp.asarray(slot_z, jnp.int32)[rel_z] * outer_fsdp + jnp.asarray(slot_y, jnp.int32)[rel_y]
+    order = rel_z * outer_fsdp + rel_y
     w_mine_all = jnp.take(flat, order, axis=0, mode="clip").reshape(n_fsdp * rows_w, half)
     w_other_all = dp_partner(w_mine_all, 1)
 

time: 232 us -> 257 us (1.11)
  waiting for transfers between devices: 47.3 us -> 64.3 us
  starting transfers between devices: 90.7 us -> 99.9 us
    ppermute x20 -> x24, waiting for transfers between devices: 44.4 us -> 62.5 us  [shift(): return lax.ppermute(x, self.axis, perm=pairs)]
    ppermute x20 -> x24, starting transfers between devices: 78.1 us -> 88.2 us  [shift(): return lax.ppermute(x, self.axis, perm=pairs)]
  transfers between devices with their start and end apart: 22 -> 26, of which waited for: 18 -> 14; matrix products, arithmetic and copies ran while one was open for 8% -> 7% of each run, Pallas kernels for 0% -> 0%
where the time goes in v7:
time: 257 us; the launch traced here: 255 us
  starting transfers between devices  99.9 us (39%)
  waiting for transfers between devices  64.3 us (25%)
  blocking collectives  43.6 us (17%)
  matrix products  19.5 us (8%)
  local copies, waits for them, and re-layouts  16.2 us (6%)
  other arithmetic  10.2 us (4%)
    ppermute x24, starting transfers between devices, shift(): return lax.ppermute(x, self.axis, perm=pairs)  88.2 us
    ppermute x24, waiting for transfers between devices, shift(): return lax.ppermute(x, self.axis, perm=pairs)  62.5 us
    all_gather x1, blocking collectives, shards(): by_dp = lax.all_gather(over_seq, 'dp', axis=0, tiled=False)  19.1 us
    all_gather x1, blocking collectives, shards(): packed_all = lax.all_gather(packed, 'seq', axis=0, tiled=True)  12.9 us
    ppermute x2, starting transfers between devices, dp_partner(): return lax.ppermute(x, 'dp', perm=pairs)  11.7 us
    all_gather x1, blocking collectives, shards(): by_seq = lax.all_gather(over_fsdp, 'seq', axis=0, tiled=False)  11.5 us
    another operation x1, local copies, waits for them, and re-layouts, shards(): features.reshape(features.shape[0], outer_fsdp, inner_fsdp, rows_w)  6.44 us
    dot_general x4, matrix products, contract_last(): lax.dot_general(left, right, (((1,), (1,)), ((), ())), preferred_element_...  6.43 us
  transfers between devices with their start and end apart: 26, of which 14 were waited for; matrix products, arithmetic and copies ran while one was open for 7% of the time, Pallas kernels for 0%

profile of v7, /device:TPU:1, one launch (start us, length us, event | category | flops | bytes accessed | tf_op | source)
XLA Modules:
  0.0 255.3 jit_solution(333865111886374578)
XLA Ops:
  1.6 6.7 %collective-permute-start = (bf16[192,192]{1,0:T(8,128)(2,1)S(1)}, bf16[192,192]{1,0:T(8,128)(2,1)S(1)}, u32[]{:S(2)}, u32[]{:S(2)}) collective-permute-start(bf16[192,192]{1,0:T(8,128)(2,1)S(1)} %constant_dynamic-slice_fusion), channel_id=1, source_target_pairs={{0,24},{1,25},{2,26},{3,27},{4,28},{5,29},{6,30},{7,31},{8,0},{9,1... | collective-permute-start | bytes 221192 | tf_op jit(solution)/shard_map/ppermute | solution.py:43
  12.9 6.2 %collective-permute-start.3 = (bf16[96,192]{1,0:T(8,128)(2,1)S(1)}, bf16[96,192]{1,0:T(8,128)(2,1)S(1)}, u32[]{:S(2)}, u32[]{:S(2)}) collective-permute-start(bf16[96,192]{1,0:T(8,128)(2,1)S(1)} %slice.177), channel_id=1, source_target_pairs={{0,24},{1,25},{2,26},{3,27},{4,28},{5,29},{6,30},{7,31},{8,0},{9,1... | collective-permute-start | bytes 110600 | tf_op jit(solution)/shard_map/ppermute | solution.py:43
  21.1 5.2 %collective-permute-done.2 = bf16[96,192]{1,0:T(8,128)(2,1)S(1)} collective-permute-done((bf16[96,192]{1,0:T(8,128)(2,1)S(1)}, bf16[96,192]{1,0:T(8,128)(2,1)S(1)}, u32[]{:S(2)}, u32[]{:S(2)}) %collective-permute-start.2) | collective-permute-done | bytes 36896 | tf_op jit(solution)/shard_map/ppermute | solution.py:43
  26.4 10.6 %collective-permute-start.4 = (bf16[4,192,192]{2,1,0:T(8,128)(2,1)S(1)}, bf16[4,192,192]{2,1,0:T(8,128)(2,1)S(1)}, u32[]{:S(2)}, u32[]{:S(2)}) collective-permute-start(bf16[4,192,192]{2,1,0:T(8,128)(2,1)S(1)} %pad_maximum_fusion), channel_id=1, source_target_pairs={{0,7},{1,0},{2,1},{3,2},{4,3},{5,4},{6,5},{7,6},{8,15},{9,8},{10,9... | collective-permute-start | bytes 884744 | tf_op jit(solution)/shard_map/ppermute | solution.py:43
  39.0 6.4 %reshape_squeeze.3 = bf16[192,4,8,192]{3,2,1,0:T(8,128)(2,1)} reshape(bf16[1,192,6144]{2,1,0:T(8,128)(2,1)} %param.4) | data formatting | bytes 4718592 | tf_op jit(solution)/shard_map/reshape;squeeze | solution.py:150
  45.5 4.6 %collective-permute-start.5 = (bf16[4,192,192]{2,1,0:T(8,128)(2,1)S(1)}, bf16[4,192,192]{2,1,0:T(8,128)(2,1)S(1)}, u32[]{:S(2)}, u32[]{:S(2)}) collective-permute-start(bf16[4,192,192]{2,1,0:T(8,128)(2,1)S(1)} %collective-permute-done.4), channel_id=1, source_target_pairs={{0,7},{1,0},{2,1},{3,2},{4,3},{5,4},{6,5},{7,6},{8,15},{9,8},{10,9... | collective-permute-start | bytes 884744 | tf_op jit(solution)/shard_map/ppermute | solution.py:43
  52.1 9.0 %collective-permute-done.8 = bf16[4,192,192]{2,1,0:T(8,128)(2,1)S(1)} collective-permute-done((bf16[4,192,192]{2,1,0:T(8,128)(2,1)S(1)}, bf16[4,192,192]{2,1,0:T(8,128)(2,1)S(1)}, u32[]{:S(2)}, u32[]{:S(2)}) %collective-permute-start.8) | collective-permute-done | bytes 294944 | tf_op jit(solution)/shard_map/ppermute | solution.py:43
  63.0 4.6 %collective-permute-start.6 = (bf16[4,192,192]{2,1,0:T(8,128)(2,1)S(1)}, bf16[4,192,192]{2,1,0:T(8,128)(2,1)S(1)}, u32[]{:S(2)}, u32[]{:S(2)}) collective-permute-start(bf16[4,192,192]{2,1,0:T(8,128)(2,1)S(1)} %collective-permute-done.5), channel_id=1, source_target_pairs={{0,7},{1,0},{2,1},{3,2},{4,3},{5,4},{6,5},{7,6},{8,15},{9,8},{10,9... | collective-permute-start | bytes 884744 | tf_op jit(solution)/shard_map/ppermute | solution.py:43
  73.2 4.6 %collective-permute-start.11 = (bf16[2,192,192]{2,1,0:T(8,128)(2,1)S(1)}, bf16[2,192,192]{2,1,0:T(8,128)(2,1)S(1)}, u32[]{:S(2)}, u32[]{:S(2)}) collective-permute-start(bf16[2,192,192]{2,1,0:T(8,128)(2,1)S(1)} %slice.179), channel_id=1, source_target_pairs={{0,7},{1,0},{2,1},{3,2},{4,3},{5,4},{6,5},{7,6},{8,15},{9,8},{10,9... | collective-permute-start | bytes 442376 | tf_op jit(solution)/shard_map/ppermute | solution.py:43
  87.5 7.5 %collective-permute-start.12 = (bf16[6144,192]{0,1:T(8,128)(2,1)}, bf16[6144,192]{0,1:T(8,128)(2,1)}, u32[]{:S(2)}, u32[]{:S(2)}) collective-permute-start(bf16[6144,192]{0,1:T(8,128)(2,1)} %copy.36), channel_id=1, source_target_pairs={{0,128},{128,0},{256,384},{384,256},{1,129},{129,1},{257,385},{385... | collective-permute-start | bytes 7077896 | tf_op jit(solution)/shard_map/ppermute | solution.py:23
  102.2 12.9 %all_gather.13 = bf16[768,640]{1,0:T(8,128)(2,1)S(1)} all-gather(bf16[192,640]{1,0:T(8,128)(2,1)S(1)} %pad_maximum_fusion.4), channel_id=1, replica_groups=mesh['dp'=4,'seq'=4,'fsdp'=32] {'seq'}, dimensions={0}, use_global_device_ids=true | all-gather | bytes 1228800 | tf_op jit(solution)/shard_map/all_gather | solution.py:174
  123.5 4.2 %collective-permute-start.13 = (bf16[8,4,192,192]{2,3,0,1:T(8,128)(2,1)}, bf16[8,4,192,192]{2,3,0,1:T(8,128)(2,1)}, u32[]{:S(2)}, u32[]{:S(2)}) collective-permute-start(bf16[8,4,192,192]{2,3,0,1:T(8,128)(2,1)} %convert_bitcast_fusion), channel_id=1, source_target_pairs={{0,128},{128,0},{256,384},{384,256},{1,129},{129,1},{257,385},{385... | collective-permute-start | bytes 7077896 | tf_op jit(solution)/shard_map/ppermute | solution.py:23
  139.1 5.3 %collective-permute-start.18 = (bf16[2,192,192]{1,2,0:T(8,128)(2,1)S(1)}, bf16[2,192,192]{1,2,0:T(8,128)(2,1)S(1)}, u32[]{:S(2)}, u32[]{:S(2)}) collective-permute-start(bf16[2,192,192]{1,2,0:T(8,128)(2,1)S(1)} %fusion.41), channel_id=1, source_target_pairs={{0,7},{1,0},{2,1},{3,2},{4,3},{5,4},{6,5},{7,6},{8,15},{9,8},{10,9... | collective-permute-start | bytes 442376 | tf_op jit(solution)/shard_map/ppermute | solution.py:43
  146.6 7.2 %collective-permute-done.14 = bf16[2,192,192]{1,2,0:T(8,128)(2,1)S(1)} collective-permute-done((bf16[2,192,192]{1,2,0:T(8,128)(2,1)S(1)}, bf16[2,192,192]{1,2,0:T(8,128)(2,1)S(1)}, u32[]{:S(2)}, u32[]{:S(2)}) %collective-permute-start.14) | collective-permute-done | bytes 147488 | tf_op jit(solution)/shard_map/ppermute | solution.py:43
  156.0 4.6 %collective-permute-start.19 = (bf16[4,192,192]{1,2,0:T(8,128)(2,1)S(1)}, bf16[4,192,192]{1,2,0:T(8,128)(2,1)S(1)}, u32[]{:S(2)}, u32[]{:S(2)}) collective-permute-start(bf16[4,192,192]{1,2,0:T(8,128)(2,1)S(1)} %pad_maximum_fusion.2), channel_id=1, source_target_pairs={{0,7},{1,0},{2,1},{3,2},{4,3},{5,4},{6,5},{7,6},{8,15},{9,8},{10,9... | collective-permute-start | bytes 884744 | tf_op jit(solution)/shard_map/ppermute | solution.py:43
  160.6 6.0 %collective-permute-done.15 = bf16[4,192,192]{1,2,0:T(8,128)(2,1)S(1)} collective-permute-done((bf16[4,192,192]{1,2,0:T(8,128)(2,1)S(1)}, bf16[4,192,192]{1,2,0:T(8,128)(2,1)S(1)}, u32[]{:S(2)}, u32[]{:S(2)}) %collective-permute-start.15) | collective-permute-done | bytes 294944 | tf_op jit(solution)/shard_map/ppermute | solution.py:43
  168.6 9.7 %collective-permute-done.16 = bf16[4,192,192]{1,2,0:T(8,128)(2,1)S(1)} collective-permute-done((bf16[4,192,192]{1,2,0:T(8,128)(2,1)S(1)}, bf16[4,192,192]{1,2,0:T(8,128)(2,1)S(1)}, u32[]{:S(2)}, u32[]{:S(2)}) %collective-permute-start.16) | collective-permute-done | bytes 294944 | tf_op jit(solution)/shard_map/ppermute | solution.py:43
  185.2 4.2 %collective-permute-done.20 = bf16[4,192,192]{1,2,0:T(8,128)(2,1)S(1)} collective-permute-done((bf16[4,192,192]{1,2,0:T(8,128)(2,1)S(1)}, bf16[4,192,192]{1,2,0:T(8,128)(2,1)S(1)}, u32[]{:S(2)}, u32[]{:S(2)}) %collective-permute-start.20) | collective-permute-done | bytes 294944 | tf_op jit(solution)/shard_map/ppermute | solution.py:43
  194.2 5.0 %collective-permute-done.21 = bf16[4,192,192]{1,2,0:T(8,128)(2,1)S(1)} collective-permute-done((bf16[4,192,192]{1,2,0:T(8,128)(2,1)S(1)}, bf16[4,192,192]{1,2,0:T(8,128)(2,1)S(1)}, u32[]{:S(2)}, u32[]{:S(2)}) %collective-permute-start.21) | collective-permute-done | bytes 294944 | tf_op jit(solution)/shard_map/ppermute | solution.py:43
  202.5 5.5 %collective-permute-start.24 = (bf16[96,192]{0,1:T(8,128)(2,1)S(1)}, bf16[96,192]{0,1:T(8,128)(2,1)S(1)}, u32[]{:S(2)}, u32[]{:S(2)}) collective-permute-start(bf16[96,192]{0,1:T(8,128)(2,1)S(1)} %get-tuple-element.27), channel_id=1, source_target_pairs={{0,24},{1,25},{2,26},{3,27},{4,28},{5,29},{6,30},{7,31},{8,0},{9,1... | collective-permute-start | bytes 110600 | tf_op jit(solution)/shard_map/ppermute | solution.py:43
  209.3 5.8 %collective-permute-start.25 = (bf16[192,192]{0,1:T(8,128)(2,1)S(1)}, bf16[192,192]{0,1:T(8,128)(2,1)S(1)}, u32[]{:S(2)}, u32[]{:S(2)}) collective-permute-start(bf16[192,192]{0,1:T(8,128)(2,1)S(1)} %pad_maximum_fusion.8), channel_id=1, source_target_pairs={{0,24},{1,25},{2,26},{3,27},{4,28},{5,29},{6,30},{7,31},{8,0},{9,1... | collective-permute-start | bytes 221192 | tf_op jit(solution)/shard_map/ppermute | solution.py:43
  217.2 6.4 %collective-permute-done.23 = bf16[192,192]{0,1:T(8,128)(2,1)S(1)} collective-permute-done((bf16[192,192]{0,1:T(8,128)(2,1)S(1)}, bf16[192,192]{0,1:T(8,128)(2,1)S(1)}, u32[]{:S(2)}, u32[]{:S(2)}) %collective-permute-start.23) | collective-permute-done | bytes 73760 | tf_op jit(solution)/shard_map/ppermute | solution.py:43
  223.7 11.5 %all-gather = f32[768,192]{1,0:T(8,128)S(1)} all-gather(f32[192,192]{1,0:T(8,128)S(1)} %copy.46), channel_id=2, replica_groups=mesh['dp'=4,'seq'=4,'fsdp'=32] {'seq'}, dimensions={0}, use_global_device_ids=true | all-gather | bytes 737280 | tf_op jit(solution)/shard_map/all_gather | solution.py:217
  235.3 19.1 %all_gather.16 = f32[4,192,192]{2,1,0:T(8,128)S(1)} all-gather(f32[1,192,192]{2,1,0:T(8,128)S(1)} %fusion.44), channel_id=1, replica_groups=mesh['dp'=4,'seq'=4,'fsdp'=32] {'dp'}, dimensions={0}, use_global_device_ids=true | all-gather | bytes 737280 | tf_op jit(solution)/shard_map/all_gather | solution.py:221
  (112 shorter events, 80.8 us)
Async XLA Ops:
  1.6 11.2 %collective-permute-start = (bf16[192,192]{1,0:T(8,128)(2,1)S(1)}, bf16[192,192]{1,0:T(8,128)(2,1)S(1)}, u32[]{:S(2)}, u32[]{:S(2)}) collective-permute-start(bf16[192,192]{1,0:T(8,128)(2,1)S(1)} %constant_dynamic-slice_fusion), channel_id=1, source_target_pairs={{0,24},{1,25},{2,26},{3,27},{4,28},{5,29},{6,30},{7,31},{8,0},{9,1... | collective-permute-start | bytes 221192 | tf_op jit(solution)/shard_map/ppermute | solution.py:43
  8.4 10.7 %collective-permute-start.1 = (bf16[192,192]{1,0:T(8,128)(2,1)S(1)}, bf16[192,192]{1,0:T(8,128)(2,1)S(1)}, u32[]{:S(2)}, u32[]{:S(2)}) collective-permute-start(bf16[192,192]{1,0:T(8,128)(2,1)S(1)} %constant_dynamic-slice_fusion), channel_id=1, source_target_pairs={{0,8},{1,9},{2,10},{3,11},{4,12},{5,13},{6,14},{7,15},{8,16},{9,17... | collective-permute-start | bytes 221192 | tf_op jit(solution)/shard_map/ppermute | solution.py:43
  12.9 8.3 %collective-permute-start.3 = (bf16[96,192]{1,0:T(8,128)(2,1)S(1)}, bf16[96,192]{1,0:T(8,128)(2,1)S(1)}, u32[]{:S(2)}, u32[]{:S(2)}) collective-permute-start(bf16[96,192]{1,0:T(8,128)(2,1)S(1)} %slice.177), channel_id=1, source_target_pairs={{0,24},{1,25},{2,26},{3,27},{4,28},{5,29},{6,30},{7,31},{8,0},{9,1... | collective-permute-start | bytes 110600 | tf_op jit(solution)/shard_map/ppermute | solution.py:43
  19.1 7.2 %collective-permute-start.2 = (bf16[96,192]{1,0:T(8,128)(2,1)S(1)}, bf16[96,192]{1,0:T(8,128)(2,1)S(1)}, u32[]{:S(2)}, u32[]{:S(2)}) collective-permute-start(bf16[96,192]{1,0:T(8,128)(2,1)S(1)} %slice.176), channel_id=1, source_target_pairs={{0,8},{1,9},{2,10},{3,11},{4,12},{5,13},{6,14},{7,15},{8,16},{9,17... | collective-permute-start | bytes 110600 | tf_op jit(solution)/shard_map/ppermute | solution.py:43
  26.4 19.0 %collective-permute-start.4 = (bf16[4,192,192]{2,1,0:T(8,128)(2,1)S(1)}, bf16[4,192,192]{2,1,0:T(8,128)(2,1)S(1)}, u32[]{:S(2)}, u32[]{:S(2)}) collective-permute-start(bf16[4,192,192]{2,1,0:T(8,128)(2,1)S(1)} %pad_maximum_fusion), channel_id=1, source_target_pairs={{0,7},{1,0},{2,1},{3,2},{4,3},{5,4},{6,5},{7,6},{8,15},{9,8},{10,9... | collective-permute-start | bytes 884744 | tf_op jit(solution)/shard_map/ppermute | solution.py:43
  37.1 13.0 %collective-permute-start.7 = (bf16[4,192,192]{2,1,0:T(8,128)(2,1)S(1)}, bf16[4,192,192]{2,1,0:T(8,128)(2,1)S(1)}, u32[]{:S(2)}, u32[]{:S(2)}) collective-permute-start(bf16[4,192,192]{2,1,0:T(8,128)(2,1)S(1)} %pad_maximum_fusion), channel_id=1, source_target_pairs={{0,1},{1,2},{2,3},{3,4},{4,5},{5,6},{6,7},{7,0},{8,9},{9,10},{10,1... | collective-permute-start | bytes 884744 | tf_op jit(solution)/shard_map/ppermute | solution.py:43
  45.5 17.6 %collective-permute-start.5 = (bf16[4,192,192]{2,1,0:T(8,128)(2,1)S(1)}, bf16[4,192,192]{2,1,0:T(8,128)(2,1)S(1)}, u32[]{:S(2)}, u32[]{:S(2)}) collective-permute-start(bf16[4,192,192]{2,1,0:T(8,128)(2,1)S(1)} %collective-permute-done.4), channel_id=1, source_target_pairs={{0,7},{1,0},{2,1},{3,2},{4,3},{5,4},{6,5},{7,6},{8,15},{9,8},{10,9... | collective-permute-start | bytes 884744 | tf_op jit(solution)/shard_map/ppermute | solution.py:43
  50.0 11.1 %collective-permute-start.8 = (bf16[4,192,192]{2,1,0:T(8,128)(2,1)S(1)}, bf16[4,192,192]{2,1,0:T(8,128)(2,1)S(1)}, u32[]{:S(2)}, u32[]{:S(2)}) collective-permute-start(bf16[4,192,192]{2,1,0:T(8,128)(2,1)S(1)} %collective-permute-done.7), channel_id=1, source_target_pairs={{0,1},{1,2},{2,3},{3,4},{4,5},{5,6},{6,7},{7,0},{8,9},{9,10},{10,1... | collective-permute-start | bytes 884744 | tf_op jit(solution)/shard_map/ppermute | solution.py:43
  61.1 10.1 %collective-permute-start.9 = (bf16[4,192,192]{2,1,0:T(8,128)(2,1)S(1)}, bf16[4,192,192]{2,1,0:T(8,128)(2,1)S(1)}, u32[]{:S(2)}, u32[]{:S(2)}) collective-permute-start(bf16[4,192,192]{2,1,0:T(8,128)(2,1)S(1)} %collective-permute-done.8), channel_id=1, source_target_pairs={{0,1},{1,2},{2,3},{3,4},{4,5},{5,6},{6,7},{7,0},{8,9},{9,10},{10,1... | collective-permute-start | bytes 884744 | tf_op jit(solution)/shard_map/ppermute | solution.py:43
  63.0 10.2 %collective-permute-start.6 = (bf16[4,192,192]{2,1,0:T(8,128)(2,1)S(1)}, bf16[4,192,192]{2,1,0:T(8,128)(2,1)S(1)}, u32[]{:S(2)}, u32[]{:S(2)}) collective-permute-start(bf16[4,192,192]{2,1,0:T(8,128)(2,1)S(1)} %collective-permute-done.5), channel_id=1, source_target_pairs={{0,7},{1,0},{2,1},{3,2},{4,3},{5,4},{6,5},{7,6},{8,15},{9,8},{10,9... | collective-permute-start | bytes 884744 | tf_op jit(solution)/shard_map/ppermute | solution.py:43
  71.3 7.6 %collective-permute-start.10 = (bf16[2,192,192]{2,1,0:T(8,128)(2,1)S(1)}, bf16[2,192,192]{2,1,0:T(8,128)(2,1)S(1)}, u32[]{:S(2)}, u32[]{:S(2)}) collective-permute-start(bf16[2,192,192]{2,1,0:T(8,128)(2,1)S(1)} %slice.178), channel_id=1, source_target_pairs={{0,1},{1,2},{2,3},{3,4},{4,5},{5,6},{6,7},{7,0},{8,9},{9,10},{10,1... | collective-permute-start | bytes 442376 | tf_op jit(solution)/shard_map/ppermute | solution.py:43
  87.5 12.0 %collective-permute-start.12 = (bf16[6144,192]{0,1:T(8,128)(2,1)}, bf16[6144,192]{0,1:T(8,128)(2,1)}, u32[]{:S(2)}, u32[]{:S(2)}) collective-permute-start(bf16[6144,192]{0,1:T(8,128)(2,1)} %copy.36), channel_id=1, source_target_pairs={{0,128},{128,0},{256,384},{384,256},{1,129},{129,1},{257,385},{385... | collective-permute-start | bytes 7077896 | tf_op jit(solution)/shard_map/ppermute | solution.py:23
  123.5 12.5 %collective-permute-start.13 = (bf16[8,4,192,192]{2,3,0,1:T(8,128)(2,1)}, bf16[8,4,192,192]{2,3,0,1:T(8,128)(2,1)}, u32[]{:S(2)}, u32[]{:S(2)}) collective-permute-start(bf16[8,4,192,192]{2,3,0,1:T(8,128)(2,1)} %convert_bitcast_fusion), channel_id=1, source_target_pairs={{0,128},{128,0},{256,384},{384,256},{1,129},{129,1},{257,385},{385... | collective-permute-start | bytes 7077896 | tf_op jit(solution)/shard_map/ppermute | solution.py:23
  139.1 16.8 %collective-permute-start.18 = (bf16[2,192,192]{1,2,0:T(8,128)(2,1)S(1)}, bf16[2,192,192]{1,2,0:T(8,128)(2,1)S(1)}, u32[]{:S(2)}, u32[]{:S(2)}) collective-permute-start(bf16[2,192,192]{1,2,0:T(8,128)(2,1)S(1)} %fusion.41), channel_id=1, source_target_pairs={{0,7},{1,0},{2,1},{3,2},{4,3},{5,4},{6,5},{7,6},{8,15},{9,8},{10,9... | collective-permute-start | bytes 442376 | tf_op jit(solution)/shard_map/ppermute | solution.py:43
  144.5 9.3 %collective-permute-start.14 = (bf16[2,192,192]{1,2,0:T(8,128)(2,1)S(1)}, bf16[2,192,192]{1,2,0:T(8,128)(2,1)S(1)}, u32[]{:S(2)}, u32[]{:S(2)}) collective-permute-start(bf16[2,192,192]{1,2,0:T(8,128)(2,1)S(1)} %fusion.38), channel_id=1, source_target_pairs={{0,1},{1,2},{2,3},{3,4},{4,5},{5,6},{6,7},{7,0},{8,9},{9,10},{10,1... | collective-permute-start | bytes 442376 | tf_op jit(solution)/shard_map/ppermute | solution.py:43
  153.9 12.6 %collective-permute-start.15 = (bf16[4,192,192]{1,2,0:T(8,128)(2,1)S(1)}, bf16[4,192,192]{1,2,0:T(8,128)(2,1)S(1)}, u32[]{:S(2)}, u32[]{:S(2)}) collective-permute-start(bf16[4,192,192]{1,2,0:T(8,128)(2,1)S(1)} %pad_maximum_fusion.1), channel_id=1, source_target_pairs={{0,1},{1,2},{2,3},{3,4},{4,5},{5,6},{6,7},{7,0},{8,9},{9,10},{10,1... | collective-permute-start | bytes 884744 | tf_op jit(solution)/shard_map/ppermute | solution.py:43
  156.0 12.6 %collective-permute-start.19 = (bf16[4,192,192]{1,2,0:T(8,128)(2,1)S(1)}, bf16[4,192,192]{1,2,0:T(8,128)(2,1)S(1)}, u32[]{:S(2)}, u32[]{:S(2)}) collective-permute-start(bf16[4,192,192]{1,2,0:T(8,128)(2,1)S(1)} %pad_maximum_fusion.2), channel_id=1, source_target_pairs={{0,7},{1,0},{2,1},{3,2},{4,3},{5,4},{6,5},{7,6},{8,15},{9,8},{10,9... | collective-permute-start | bytes 884744 | tf_op jit(solution)/shard_map/ppermute | solution.py:43
  166.6 11.7 %collective-permute-start.16 = (bf16[4,192,192]{1,2,0:T(8,128)(2,1)S(1)}, bf16[4,192,192]{1,2,0:T(8,128)(2,1)S(1)}, u32[]{:S(2)}, u32[]{:S(2)}) collective-permute-start(bf16[4,192,192]{1,2,0:T(8,128)(2,1)S(1)} %fusion.26), channel_id=1, source_target_pairs={{0,1},{1,2},{2,3},{3,4},{4,5},{5,6},{6,7},{7,0},{8,9},{9,10},{10,1... | collective-permute-start | bytes 884744 | tf_op jit(solution)/shard_map/ppermute | solution.py:43
  179.9 9.6 %collective-permute-start.20 = (bf16[4,192,192]{1,2,0:T(8,128)(2,1)S(1)}, bf16[4,192,192]{1,2,0:T(8,128)(2,1)S(1)}, u32[]{:S(2)}, u32[]{:S(2)}) collective-permute-start(bf16[4,192,192]{1,2,0:T(8,128)(2,1)S(1)} %get-tuple-element.19), channel_id=1, source_target_pairs={{0,7},{1,0},{2,1},{3,2},{4,3},{5,4},{6,5},{7,6},{8,15},{9,8},{10,9... | collective-permute-start | bytes 884744 | tf_op jit(solution)/shard_map/ppermute | solution.py:43
  181.8 12.4 %collective-permute-start.17 = (bf16[4,192,192]{1,2,0:T(8,128)(2,1)S(1)}, bf16[4,192,192]{1,2,0:T(8,128)(2,1)S(1)}, u32[]{:S(2)}, u32[]{:S(2)}) collective-permute-start(bf16[4,192,192]{1,2,0:T(8,128)(2,1)S(1)} %get-tuple-element.18), channel_id=1, source_target_pairs={{0,1},{1,2},{2,3},{3,4},{4,5},{5,6},{6,7},{7,0},{8,9},{9,10},{10,1... | collective-permute-start | bytes 884744 | tf_op jit(solution)/shard_map/ppermute | solution.py:43
  190.7 8.5 %collective-permute-start.21 = (bf16[4,192,192]{1,2,0:T(8,128)(2,1)S(1)}, bf16[4,192,192]{1,2,0:T(8,128)(2,1)S(1)}, u32[]{:S(2)}, u32[]{:S(2)}) collective-permute-start(bf16[4,192,192]{1,2,0:T(8,128)(2,1)S(1)} %fusion.25), channel_id=1, source_target_pairs={{0,7},{1,0},{2,1},{3,2},{4,3},{5,4},{6,5},{7,6},{8,15},{9,8},{10,9... | collective-permute-start | bytes 884744 | tf_op jit(solution)/shard_map/ppermute | solution.py:43
  200.6 7.4 %collective-permute-start.22 = (bf16[96,192]{0,1:T(8,128)(2,1)S(1)}, bf16[96,192]{0,1:T(8,128)(2,1)S(1)}, u32[]{:S(2)}, u32[]{:S(2)}) collective-permute-start(bf16[96,192]{0,1:T(8,128)(2,1)S(1)} %get-tuple-element.26), channel_id=1, source_target_pairs={{0,8},{1,9},{2,10},{3,11},{4,12},{5,13},{6,14},{7,15},{8,16},{9,17... | collective-permute-start | bytes 110600 | tf_op jit(solution)/shard_map/ppermute | solution.py:43
  209.3 7.8 %collective-permute-start.25 = (bf16[192,192]{0,1:T(8,128)(2,1)S(1)}, bf16[192,192]{0,1:T(8,128)(2,1)S(1)}, u32[]{:S(2)}, u32[]{:S(2)}) collective-permute-start(bf16[192,192]{0,1:T(8,128)(2,1)S(1)} %pad_maximum_fusion.8), channel_id=1, source_target_pairs={{0,24},{1,25},{2,26},{3,27},{4,28},{5,29},{6,30},{7,31},{8,0},{9,1... | collective-permute-start | bytes 221192 | tf_op jit(solution)/shard_map/ppermute | solution.py:43
  215.2 8.3 %collective-permute-start.23 = (bf16[192,192]{0,1:T(8,128)(2,1)S(1)}, bf16[192,192]{0,1:T(8,128)(2,1)S(1)}, u32[]{:S(2)}, u32[]{:S(2)}) collective-permute-start(bf16[192,192]{0,1:T(8,128)(2,1)S(1)} %pad_maximum_fusion.7), channel_id=1, source_target_pairs={{0,8},{1,9},{2,10},{3,11},{4,12},{5,13},{6,14},{7,15},{8,16},{9,17... | collective-permute-start | bytes 221192 | tf_op jit(solution)/shard_map/ppermute | solution.py:43
  (10 other events, 66.8 us)

commit v8 on v6

--- a/solution.py
+++ b/solution.py
@@ -66,6 +66,11 @@
     me = ring.position()
 
     def pick(index):
+        if isinstance(blocks, tuple):
+            return sum(
+                lax.dynamic_index_in_dim(b, index % n, axis=axis, keepdims=False).astype(jnp.float32)
+                for b in blocks
+            )
         return lax.dynamic_index_in_dim(blocks, index % n, axis=axis, keepdims=False)
 
     total = pick(me)
@@ -173,7 +178,7 @@
     wg_from_partner = dp_partner(wg_other.astype(jnp.bfloat16), 1)
     wg_mine = jnp.einsum("pyzd,pc->zydc", blocked, g_mine, preferred_element_type=jnp.float32)
     wg_mine, wg_from_partner = lax.optimization_barrier((wg_mine, wg_from_partner))
-    blocks = wg_mine + wg_from_partner.astype(jnp.float32)
+    blocks = (wg_mine, wg_from_partner)
     over_z, input_grad = ring_reduce_scatter(blocks, ring_z, axis=0, beside=input_grad)
     over_fsdp, _ = ring_reduce_scatter(over_z, ring_y)
 

time: 232 us -> 241 us (1.039)
  waiting for transfers between devices: 47.3 us -> 56 us
  starting transfers between devices: 90.7 us -> 87.5 us
    ppermute x20, waiting for transfers between devices: 44.4 us -> 53 us  [shift(): return lax.ppermute(x, self.axis, perm=pairs)]
    convert_element_type x0 -> x2, other arithmetic: none -> 3.28 us  [ring_reduce_scatter(): acc = ring.shift(acc.astype(jnp.bfloat16), -1).astype(jnp.float32)]
    ppermute x20, starting transfers between devices: 78.1 us -> 75.1 us  [shift(): return lax.ppermute(x, self.axis, perm=pairs)]
    add x1 -> x0, other arithmetic: 3.03 us -> none  [shards(): blocks = wg_mine + wg_from_partner.astype(jnp.float32)]
  transfers between devices with their start and end apart: 22 -> 22, of which waited for: 18 -> 16; matrix products, arithmetic and copies ran while one was open for 8% -> 9% of each run, Pallas kernels for 0% -> 0%
where the time goes in v8:
time: 241 us; the launch traced here: 240 us
  starting transfers between devices  87.5 us (36%)
  waiting for transfers between devices  56 us (23%)
  blocking collectives  44.6 us (19%)
  matrix products  21.1 us (9%)
  local copies, waits for them, and re-layouts  17.5 us (7%)
  other arithmetic  11.6 us (5%)
    ppermute x20, starting transfers between devices, shift(): return lax.ppermute(x, self.axis, perm=pairs)  75.1 us
    ppermute x20, waiting for transfers between devices, shift(): return lax.ppermute(x, self.axis, perm=pairs)  53 us
    all_gather x1, blocking collectives, shards(): by_dp = lax.all_gather(over_seq, 'dp', axis=0, tiled=False)  20 us
    all_gather x1, blocking collectives, shards(): packed_all = lax.all_gather(packed, 'seq', axis=0, tiled=True)  13.1 us
    ppermute x2, starting transfers between devices, dp_partner(): return lax.ppermute(x, 'dp', perm=pairs)  12.4 us
    all_gather x1, blocking collectives, shards(): by_seq = lax.all_gather(over_fsdp, 'seq', axis=0, tiled=False)  11.5 us
    dot_general x4, matrix products, contract_last(): lax.dot_general(left, right, (((1,), (1,)), ((), ())), preferred_element_...  6.51 us
    another operation x1, local copies, waits for them, and re-layouts, shards(): features.reshape(features.shape[0], outer_fsdp, inner_fsdp, rows_w)  6.44 us
  transfers between devices with their start and end apart: 22, of which 16 were waited for; matrix products, arithmetic and copies ran while one was open for 9% of the time, Pallas kernels for 0%

profile of v8, /device:TPU:1, one launch (start us, length us, event | category | flops | bytes accessed | tf_op | source)
XLA Modules:
  0.0 239.8 jit_solution(2335149457085940866)
XLA Ops:
  1.6 5.0 %collective-permute-start = (bf16[192,192]{1,0:T(8,128)(2,1)S(1)}, bf16[192,192]{1,0:T(8,128)(2,1)S(1)}, u32[]{:S(2)}, u32[]{:S(2)}) collective-permute-start(bf16[192,192]{1,0:T(8,128)(2,1)S(1)} %constant_dynamic-slice_fusion), channel_id=1, source_target_pairs={{0,8},{1,9},{2,10},{3,11},{4,12},{5,13},{6,14},{7,15},{8,16},{9,17... | collective-permute-start | bytes 221192 | tf_op jit(solution)/shard_map/ppermute | solution.py:43
  6.7 3.6 %collective-permute-start.1 = (bf16[192,192]{1,0:T(8,128)(2,1)S(1)}, bf16[192,192]{1,0:T(8,128)(2,1)S(1)}, u32[]{:S(2)}, u32[]{:S(2)}) collective-permute-start(bf16[192,192]{1,0:T(8,128)(2,1)S(1)} %constant_dynamic-slice_fusion), channel_id=1, source_target_pairs={{0,24},{1,25},{2,26},{3,27},{4,28},{5,29},{6,30},{7,31},{8,0},{9,1... | collective-permute-start | bytes 221192 | tf_op jit(solution)/shard_map/ppermute | solution.py:43
  11.7 4.6 %collective-permute-start.2 = (bf16[192,192]{1,0:T(8,128)(2,1)S(1)}, bf16[192,192]{1,0:T(8,128)(2,1)S(1)}, u32[]{:S(2)}, u32[]{:S(2)}) collective-permute-start(bf16[192,192]{1,0:T(8,128)(2,1)S(1)} %collective-permute-done), channel_id=1, source_target_pairs={{0,8},{1,9},{2,10},{3,11},{4,12},{5,13},{6,14},{7,15},{8,16},{9,17... | collective-permute-start | bytes 221192 | tf_op jit(solution)/shard_map/ppermute | solution.py:43
  19.4 3.9 %collective-permute-start.3 = (bf16[4,192,192]{2,1,0:T(8,128)(2,1)S(1)}, bf16[4,192,192]{2,1,0:T(8,128)(2,1)S(1)}, u32[]{:S(2)}, u32[]{:S(2)}) collective-permute-start(bf16[4,192,192]{2,1,0:T(8,128)(2,1)S(1)} %pad_maximum_fusion), channel_id=1, source_target_pairs={{0,1},{1,2},{2,3},{3,4},{4,5},{5,6},{6,7},{7,0},{8,9},{9,10},{10,1... | collective-permute-start | bytes 884744 | tf_op jit(solution)/shard_map/ppermute | solution.py:43
  23.3 6.4 %reshape_squeeze.3 = bf16[192,4,8,192]{3,2,1,0:T(8,128)(2,1)} reshape(bf16[1,192,6144]{2,1,0:T(8,128)(2,1)} %param.6) | data formatting | bytes 4718592 | tf_op jit(solution)/shard_map/reshape;squeeze | solution.py:118
  29.8 8.6 %collective-permute-start.4 = (bf16[4,192,192]{2,1,0:T(8,128)(2,1)S(1)}, bf16[4,192,192]{2,1,0:T(8,128)(2,1)S(1)}, u32[]{:S(2)}, u32[]{:S(2)}) collective-permute-start(bf16[4,192,192]{2,1,0:T(8,128)(2,1)S(1)} %pad_maximum_fusion), channel_id=1, source_target_pairs={{0,7},{1,0},{2,1},{3,2},{4,3},{5,4},{6,5},{7,6},{8,15},{9,8},{10,9... | collective-permute-start | bytes 884744 | tf_op jit(solution)/shard_map/ppermute | solution.py:43
  43.7 5.3 %collective-permute-start.6 = (bf16[4,192,192]{2,1,0:T(8,128)(2,1)S(1)}, bf16[4,192,192]{2,1,0:T(8,128)(2,1)S(1)}, u32[]{:S(2)}, u32[]{:S(2)}) collective-permute-start(bf16[4,192,192]{2,1,0:T(8,128)(2,1)S(1)} %collective-permute-done.4), channel_id=1, source_target_pairs={{0,7},{1,0},{2,1},{3,2},{4,3},{5,4},{6,5},{7,6},{8,15},{9,8},{10,9... | collective-permute-start | bytes 884744 | tf_op jit(solution)/shard_map/ppermute | solution.py:43
  53.8 5.0 %collective-permute-start.8 = (bf16[4,192,192]{2,1,0:T(8,128)(2,1)S(1)}, bf16[4,192,192]{2,1,0:T(8,128)(2,1)S(1)}, u32[]{:S(2)}, u32[]{:S(2)}) collective-permute-start(bf16[4,192,192]{2,1,0:T(8,128)(2,1)S(1)} %collective-permute-done.6), channel_id=1, source_target_pairs={{0,7},{1,0},{2,1},{3,2},{4,3},{5,4},{6,5},{7,6},{8,15},{9,8},{10,9... | collective-permute-start | bytes 884744 | tf_op jit(solution)/shard_map/ppermute | solution.py:43
  63.5 5.0 %collective-permute-done.9 = bf16[4,192,192]{2,1,0:T(8,128)(2,1)S(1)} collective-permute-done((bf16[4,192,192]{2,1,0:T(8,128)(2,1)S(1)}, bf16[4,192,192]{2,1,0:T(8,128)(2,1)S(1)}, u32[]{:S(2)}, u32[]{:S(2)}) %collective-permute-start.9) | collective-permute-done | bytes 294944 | tf_op jit(solution)/shard_map/ppermute | solution.py:43
  75.5 8.4 %collective-permute-start.10 = (bf16[6144,192]{0,1:T(8,128)(2,1)}, bf16[6144,192]{0,1:T(8,128)(2,1)}, u32[]{:S(2)}, u32[]{:S(2)}) collective-permute-start(bf16[6144,192]{0,1:T(8,128)(2,1)} %copy.56), channel_id=1, source_target_pairs={{0,128},{128,0},{256,384},{384,256},{1,129},{129,1},{257,385},{385... | collective-permute-start | bytes 7077896 | tf_op jit(solution)/shard_map/ppermute | solution.py:23
  91.2 13.1 %all_gather.13 = bf16[768,640]{1,0:T(8,128)(2,1)S(1)} all-gather(bf16[192,640]{1,0:T(8,128)(2,1)S(1)} %pad_maximum_fusion.2), channel_id=1, replica_groups=mesh['dp'=4,'seq'=4,'fsdp'=32] {'seq'}, dimensions={0}, use_global_device_ids=true | all-gather | bytes 1228800 | tf_op jit(solution)/shard_map/all_gather | solution.py:142
  108.7 5.7 %convert_bitcast_fusion = bf16[8,4,192,192]{2,3,1,0:T(8,128)(2,1)} fusion(bf16[192,4,8,192]{3,2,1,0:T(8,128)(2,1)S(1)} %copy-done.1, pred[]{:T(512)S(6)} %eq.49, bf16[192,128]{1,0:T(8,128)(2,1)S(1)} %convolution_convert_fusion.1, bf16[192,128]{1,0:T(8,128)(2,1)S(1)} %convolution_convert_fusion.2, bf16[192,128]{1,0:T(8,128)(2,1)S(1)} %convolution_convert_fusion), kind=kOutput, calls=%fused_computation.11 | convolution fusion | flops 454496256 | bytes 4866049 | tf_op jit(solution)/shard_map/pyzd,pc->zydc/dot_general | solution.py:177
  114.4 4.0 %collective-permute-start.11 = (bf16[8,4,192,192]{2,3,1,0:T(8,128)(2,1)}, bf16[8,4,192,192]{2,3,1,0:T(8,128)(2,1)}, u32[]{:S(2)}, u32[]{:S(2)}) collective-permute-start(bf16[8,4,192,192]{2,3,1,0:T(8,128)(2,1)} %convert_bitcast_fusion), channel_id=1, source_target_pairs={{0,128},{128,0},{256,384},{384,256},{1,129},{129,1},{257,385},{385... | collective-permute-start | bytes 7077896 | tf_op jit(solution)/shard_map/ppermute | solution.py:23
  127.9 4.0 %fusion = bf16[192,6144]{1,0:T(8,128)(2,1)} fusion(f32[192,6144]{1,0:T(8,128)S(1)} %fusion.66, bf16[6144,192]{0,1:T(8,128)(2,1)} %collective-permute-done.10, pred[]{:T(512)S(6)} %eq.49, bf16[192,128]{1,0:T(8,128)(2,1)S(1)} %convolution_convert_fusion.1, bf16[192,128]{1,0:T(8,128)(2,1)S(1)} %convolution_convert_fusion.2, ...), kind=kOutput, calls=%fused_computation.3 | convolution fusion | flops 455675904 | bytes 9584641 | tf_op jit(solution)/shard_map/dot_general | solution.py:16
  131.9 7.6 %collective-permute-done.12 = bf16[4,192,192]{1,2,0:T(8,128)(2,1)S(1)} collective-permute-done((bf16[4,192,192]{1,2,0:T(8,128)(2,1)S(1)}, bf16[4,192,192]{1,2,0:T(8,128)(2,1)S(1)}, u32[]{:S(2)}, u32[]{:S(2)}) %collective-permute-start.12) | collective-permute-done | bytes 294944 | tf_op jit(solution)/shard_map/ppermute | solution.py:43
  142.5 4.6 %collective-permute-start.16 = (bf16[4,192,192]{1,2,0:T(8,128)(2,1)S(1)}, bf16[4,192,192]{1,2,0:T(8,128)(2,1)S(1)}, u32[]{:S(2)}, u32[]{:S(2)}) collective-permute-start(bf16[4,192,192]{1,2,0:T(8,128)(2,1)S(1)} %get-tuple-element.20), channel_id=1, source_target_pairs={{0,7},{1,0},{2,1},{3,2},{4,3},{5,4},{6,5},{7,6},{8,15},{9,8},{10,9... | collective-permute-start | bytes 884744 | tf_op jit(solution)/shard_map/ppermute | solution.py:43
  147.1 6.0 %collective-permute-done.13 = bf16[4,192,192]{1,2,0:T(8,128)(2,1)S(1)} collective-permute-done((bf16[4,192,192]{1,2,0:T(8,128)(2,1)S(1)}, bf16[4,192,192]{1,2,0:T(8,128)(2,1)S(1)}, u32[]{:S(2)}, u32[]{:S(2)}) %collective-permute-start.13) | collective-permute-done | bytes 294944 | tf_op jit(solution)/shard_map/ppermute | solution.py:43
  156.5 9.7 %collective-permute-done.14 = bf16[4,192,192]{1,2,0:T(8,128)(2,1)S(1)} collective-permute-done((bf16[4,192,192]{1,2,0:T(8,128)(2,1)S(1)}, bf16[4,192,192]{1,2,0:T(8,128)(2,1)S(1)}, u32[]{:S(2)}, u32[]{:S(2)}) %collective-permute-start.14) | collective-permute-done | bytes 294944 | tf_op jit(solution)/shard_map/ppermute | solution.py:43
  173.4 4.2 %collective-permute-done.17 = bf16[4,192,192]{1,2,0:T(8,128)(2,1)S(1)} collective-permute-done((bf16[4,192,192]{1,2,0:T(8,128)(2,1)S(1)}, bf16[4,192,192]{1,2,0:T(8,128)(2,1)S(1)}, u32[]{:S(2)}, u32[]{:S(2)}) %collective-permute-start.17) | collective-permute-done | bytes 294944 | tf_op jit(solution)/shard_map/ppermute | solution.py:43
  182.4 5.0 %collective-permute-done.18 = bf16[4,192,192]{1,2,0:T(8,128)(2,1)S(1)} collective-permute-done((bf16[4,192,192]{1,2,0:T(8,128)(2,1)S(1)}, bf16[4,192,192]{1,2,0:T(8,128)(2,1)S(1)}, u32[]{:S(2)}, u32[]{:S(2)}) %collective-permute-start.18) | collective-permute-done | bytes 294944 | tf_op jit(solution)/shard_map/ppermute | solution.py:43
  188.9 4.4 %collective-permute-start.19 = (bf16[192,192]{0,1:T(8,128)(2,1)S(1)}, bf16[192,192]{0,1:T(8,128)(2,1)S(1)}, u32[]{:S(2)}, u32[]{:S(2)}) collective-permute-start(bf16[192,192]{0,1:T(8,128)(2,1)S(1)} %get-tuple-element.24), channel_id=1, source_target_pairs={{0,8},{1,9},{2,10},{3,11},{4,12},{5,13},{6,14},{7,15},{8,16},{9,17... | collective-permute-start | bytes 221192 | tf_op jit(solution)/shard_map/ppermute | solution.py:43
  197.4 6.9 %collective-permute-start.20 = (bf16[192,192]{0,1:T(8,128)(2,1)S(1)}, bf16[192,192]{0,1:T(8,128)(2,1)S(1)}, u32[]{:S(2)}, u32[]{:S(2)}) collective-permute-start(bf16[192,192]{0,1:T(8,128)(2,1)S(1)} %fusion.41), channel_id=1, source_target_pairs={{0,8},{1,9},{2,10},{3,11},{4,12},{5,13},{6,14},{7,15},{8,16},{9,17... | collective-permute-start | bytes 221192 | tf_op jit(solution)/shard_map/ppermute | solution.py:43
  207.3 11.5 %all-gather = f32[768,192]{1,0:T(8,128)S(1)} all-gather(f32[192,192]{1,0:T(8,128)S(1)} %copy.72), channel_id=2, replica_groups=mesh['dp'=4,'seq'=4,'fsdp'=32] {'seq'}, dimensions={0}, use_global_device_ids=true | all-gather | bytes 737280 | tf_op jit(solution)/shard_map/all_gather | solution.py:185
  218.9 20.0 %all_gather.16 = f32[4,192,192]{2,1,0:T(8,128)S(1)} all-gather(f32[1,192,192]{2,1,0:T(8,128)S(1)} %fusion.40), channel_id=1, replica_groups=mesh['dp'=4,'seq'=4,'fsdp'=32] {'dp'}, dimensions={0}, use_global_device_ids=true | all-gather | bytes 737280 | tf_op jit(solution)/shard_map/all_gather | solution.py:189
  (91 shorter events, 75.8 us)
Async XLA Ops:
  1.6 10.1 %collective-permute-start = (bf16[192,192]{1,0:T(8,128)(2,1)S(1)}, bf16[192,192]{1,0:T(8,128)(2,1)S(1)}, u32[]{:S(2)}, u32[]{:S(2)}) collective-permute-start(bf16[192,192]{1,0:T(8,128)(2,1)S(1)} %constant_dynamic-slice_fusion), channel_id=1, source_target_pairs={{0,8},{1,9},{2,10},{3,11},{4,12},{5,13},{6,14},{7,15},{8,16},{9,17... | collective-permute-start | bytes 221192 | tf_op jit(solution)/shard_map/ppermute | solution.py:43
  6.7 9.9 %collective-permute-start.1 = (bf16[192,192]{1,0:T(8,128)(2,1)S(1)}, bf16[192,192]{1,0:T(8,128)(2,1)S(1)}, u32[]{:S(2)}, u32[]{:S(2)}) collective-permute-start(bf16[192,192]{1,0:T(8,128)(2,1)S(1)} %constant_dynamic-slice_fusion), channel_id=1, source_target_pairs={{0,24},{1,25},{2,26},{3,27},{4,28},{5,29},{6,30},{7,31},{8,0},{9,1... | collective-permute-start | bytes 221192 | tf_op jit(solution)/shard_map/ppermute | solution.py:43
  11.7 7.5 %collective-permute-start.2 = (bf16[192,192]{1,0:T(8,128)(2,1)S(1)}, bf16[192,192]{1,0:T(8,128)(2,1)S(1)}, u32[]{:S(2)}, u32[]{:S(2)}) collective-permute-start(bf16[192,192]{1,0:T(8,128)(2,1)S(1)} %collective-permute-done), channel_id=1, source_target_pairs={{0,8},{1,9},{2,10},{3,11},{4,12},{5,13},{6,14},{7,15},{8,16},{9,17... | collective-permute-start | bytes 221192 | tf_op jit(solution)/shard_map/ppermute | solution.py:43
  19.4 19.1 %collective-permute-start.3 = (bf16[4,192,192]{2,1,0:T(8,128)(2,1)S(1)}, bf16[4,192,192]{2,1,0:T(8,128)(2,1)S(1)}, u32[]{:S(2)}, u32[]{:S(2)}) collective-permute-start(bf16[4,192,192]{2,1,0:T(8,128)(2,1)S(1)} %pad_maximum_fusion), channel_id=1, source_target_pairs={{0,1},{1,2},{2,3},{3,4},{4,5},{5,6},{6,7},{7,0},{8,9},{9,10},{10,1... | collective-permute-start | bytes 884744 | tf_op jit(solution)/shard_map/ppermute | solution.py:43
  29.8 14.0 %collective-permute-start.4 = (bf16[4,192,192]{2,1,0:T(8,128)(2,1)S(1)}, bf16[4,192,192]{2,1,0:T(8,128)(2,1)S(1)}, u32[]{:S(2)}, u32[]{:S(2)}) collective-permute-start(bf16[4,192,192]{2,1,0:T(8,128)(2,1)S(1)} %pad_maximum_fusion), channel_id=1, source_target_pairs={{0,7},{1,0},{2,1},{3,2},{4,3},{5,4},{6,5},{7,6},{8,15},{9,8},{10,9... | collective-permute-start | bytes 884744 | tf_op jit(solution)/shard_map/ppermute | solution.py:43
  38.4 10.7 %collective-permute-start.5 = (bf16[4,192,192]{2,1,0:T(8,128)(2,1)S(1)}, bf16[4,192,192]{2,1,0:T(8,128)(2,1)S(1)}, u32[]{:S(2)}, u32[]{:S(2)}) collective-permute-start(bf16[4,192,192]{2,1,0:T(8,128)(2,1)S(1)} %collective-permute-done.3), channel_id=1, source_target_pairs={{0,1},{1,2},{2,3},{3,4},{4,5},{5,6},{6,7},{7,0},{8,9},{9,10},{10,1... | collective-permute-start | bytes 884744 | tf_op jit(solution)/shard_map/ppermute | solution.py:43
  43.7 10.0 %collective-permute-start.6 = (bf16[4,192,192]{2,1,0:T(8,128)(2,1)S(1)}, bf16[4,192,192]{2,1,0:T(8,128)(2,1)S(1)}, u32[]{:S(2)}, u32[]{:S(2)}) collective-permute-start(bf16[4,192,192]{2,1,0:T(8,128)(2,1)S(1)} %collective-permute-done.4), channel_id=1, source_target_pairs={{0,7},{1,0},{2,1},{3,2},{4,3},{5,4},{6,5},{7,6},{8,15},{9,8},{10,9... | collective-permute-start | bytes 884744 | tf_op jit(solution)/shard_map/ppermute | solution.py:43
  49.1 9.7 %collective-permute-start.7 = (bf16[4,192,192]{2,1,0:T(8,128)(2,1)S(1)}, bf16[4,192,192]{2,1,0:T(8,128)(2,1)S(1)}, u32[]{:S(2)}, u32[]{:S(2)}) collective-permute-start(bf16[4,192,192]{2,1,0:T(8,128)(2,1)S(1)} %collective-permute-done.5), channel_id=1, source_target_pairs={{0,1},{1,2},{2,3},{3,4},{4,5},{5,6},{6,7},{7,0},{8,9},{9,10},{10,1... | collective-permute-start | bytes 884744 | tf_op jit(solution)/shard_map/ppermute | solution.py:43
  53.8 9.7 %collective-permute-start.8 = (bf16[4,192,192]{2,1,0:T(8,128)(2,1)S(1)}, bf16[4,192,192]{2,1,0:T(8,128)(2,1)S(1)}, u32[]{:S(2)}, u32[]{:S(2)}) collective-permute-start(bf16[4,192,192]{2,1,0:T(8,128)(2,1)S(1)} %collective-permute-done.6), channel_id=1, source_target_pairs={{0,7},{1,0},{2,1},{3,2},{4,3},{5,4},{6,5},{7,6},{8,15},{9,8},{10,9... | collective-permute-start | bytes 884744 | tf_op jit(solution)/shard_map/ppermute | solution.py:43
  58.8 9.7 %collective-permute-start.9 = (bf16[4,192,192]{2,1,0:T(8,128)(2,1)S(1)}, bf16[4,192,192]{2,1,0:T(8,128)(2,1)S(1)}, u32[]{:S(2)}, u32[]{:S(2)}) collective-permute-start(bf16[4,192,192]{2,1,0:T(8,128)(2,1)S(1)} %collective-permute-done.7), channel_id=1, source_target_pairs={{0,1},{1,2},{2,3},{3,4},{4,5},{5,6},{6,7},{7,0},{8,9},{9,10},{10,1... | collective-permute-start | bytes 884744 | tf_op jit(solution)/shard_map/ppermute | solution.py:43
  72.9 11.0 %copy-start.7 = (s32[1,192]{1,0:T(1,128)S(1)}, s32[1,192]{1,0:T(1,128)}, u32[]{:S(2)}) copy-start(s32[1,192]{1,0:T(1,128)} %param.7) | copy-start | bytes 2308
  75.5 12.9 %collective-permute-start.10 = (bf16[6144,192]{0,1:T(8,128)(2,1)}, bf16[6144,192]{0,1:T(8,128)(2,1)}, u32[]{:S(2)}, u32[]{:S(2)}) collective-permute-start(bf16[6144,192]{0,1:T(8,128)(2,1)} %copy.56), channel_id=1, source_target_pairs={{0,128},{128,0},{256,384},{384,256},{1,129},{129,1},{257,385},{385... | collective-permute-start | bytes 7077896 | tf_op jit(solution)/shard_map/ppermute | solution.py:23
  114.4 9.6 %collective-permute-start.11 = (bf16[8,4,192,192]{2,3,1,0:T(8,128)(2,1)}, bf16[8,4,192,192]{2,3,1,0:T(8,128)(2,1)}, u32[]{:S(2)}, u32[]{:S(2)}) collective-permute-start(bf16[8,4,192,192]{2,3,1,0:T(8,128)(2,1)} %convert_bitcast_fusion), channel_id=1, source_target_pairs={{0,128},{128,0},{256,384},{384,256},{1,129},{129,1},{257,385},{385... | collective-permute-start | bytes 7077896 | tf_op jit(solution)/shard_map/ppermute | solution.py:23
  122.8 16.7 %copy-start.3 = (f32[8,4,192,192]{2,3,0,1:T(8,128)}, f32[8,4,192,192]{2,3,0,1:T(8,128)S(1)}, u32[]{:S(2)}) copy-start(f32[8,4,192,192]{2,3,0,1:T(8,128)S(1)} %fusion.5) | copy-start | bytes 14155780
  125.9 13.5 %collective-permute-start.12 = (bf16[4,192,192]{1,2,0:T(8,128)(2,1)S(1)}, bf16[4,192,192]{1,2,0:T(8,128)(2,1)S(1)}, u32[]{:S(2)}, u32[]{:S(2)}) collective-permute-start(bf16[4,192,192]{1,2,0:T(8,128)(2,1)S(1)} %get-tuple-element.21), channel_id=1, source_target_pairs={{0,1},{1,2},{2,3},{3,4},{4,5},{5,6},{6,7},{7,0},{8,9},{9,10},{10,1... | collective-permute-start | bytes 884744 | tf_op jit(solution)/shard_map/ppermute | solution.py:43
  140.6 12.6 %collective-permute-start.13 = (bf16[4,192,192]{1,2,0:T(8,128)(2,1)S(1)}, bf16[4,192,192]{1,2,0:T(8,128)(2,1)S(1)}, u32[]{:S(2)}, u32[]{:S(2)}) collective-permute-start(bf16[4,192,192]{1,2,0:T(8,128)(2,1)S(1)} %fusion.30), channel_id=1, source_target_pairs={{0,1},{1,2},{2,3},{3,4},{4,5},{5,6},{6,7},{7,0},{8,9},{9,10},{10,1... | collective-permute-start | bytes 884744 | tf_op jit(solution)/shard_map/ppermute | solution.py:43
  142.5 14.0 %collective-permute-start.16 = (bf16[4,192,192]{1,2,0:T(8,128)(2,1)S(1)}, bf16[4,192,192]{1,2,0:T(8,128)(2,1)S(1)}, u32[]{:S(2)}, u32[]{:S(2)}) collective-permute-start(bf16[4,192,192]{1,2,0:T(8,128)(2,1)S(1)} %get-tuple-element.20), channel_id=1, source_target_pairs={{0,7},{1,0},{2,1},{3,2},{4,3},{5,4},{6,5},{7,6},{8,15},{9,8},{10,9... | collective-permute-start | bytes 884744 | tf_op jit(solution)/shard_map/ppermute | solution.py:43
  154.5 11.6 %collective-permute-start.14 = (bf16[4,192,192]{1,2,0:T(8,128)(2,1)S(1)}, bf16[4,192,192]{1,2,0:T(8,128)(2,1)S(1)}, u32[]{:S(2)}, u32[]{:S(2)}) collective-permute-start(bf16[4,192,192]{1,2,0:T(8,128)(2,1)S(1)} %fusion.29), channel_id=1, source_target_pairs={{0,1},{1,2},{2,3},{3,4},{4,5},{5,6},{6,7},{7,0},{8,9},{9,10},{10,1... | collective-permute-start | bytes 884744 | tf_op jit(solution)/shard_map/ppermute | solution.py:43
  168.1 9.5 %collective-permute-start.17 = (bf16[4,192,192]{1,2,0:T(8,128)(2,1)S(1)}, bf16[4,192,192]{1,2,0:T(8,128)(2,1)S(1)}, u32[]{:S(2)}, u32[]{:S(2)}) collective-permute-start(bf16[4,192,192]{1,2,0:T(8,128)(2,1)S(1)} %get-tuple-element.19), channel_id=1, source_target_pairs={{0,7},{1,0},{2,1},{3,2},{4,3},{5,4},{6,5},{7,6},{8,15},{9,8},{10,9... | collective-permute-start | bytes 884744 | tf_op jit(solution)/shard_map/ppermute | solution.py:43
  170.0 12.4 %collective-permute-start.15 = (bf16[4,192,192]{1,2,0:T(8,128)(2,1)S(1)}, bf16[4,192,192]{1,2,0:T(8,128)(2,1)S(1)}, u32[]{:S(2)}, u32[]{:S(2)}) collective-permute-start(bf16[4,192,192]{1,2,0:T(8,128)(2,1)S(1)} %get-tuple-element.18), channel_id=1, source_target_pairs={{0,1},{1,2},{2,3},{3,4},{4,5},{5,6},{6,7},{7,0},{8,9},{9,10},{10,1... | collective-permute-start | bytes 884744 | tf_op jit(solution)/shard_map/ppermute | solution.py:43
  178.9 8.5 %collective-permute-start.18 = (bf16[4,192,192]{1,2,0:T(8,128)(2,1)S(1)}, bf16[4,192,192]{1,2,0:T(8,128)(2,1)S(1)}, u32[]{:S(2)}, u32[]{:S(2)}) collective-permute-start(bf16[4,192,192]{1,2,0:T(8,128)(2,1)S(1)} %fusion.26), channel_id=1, source_target_pairs={{0,7},{1,0},{2,1},{3,2},{4,3},{5,4},{6,5},{7,6},{8,15},{9,8},{10,9... | collective-permute-start | bytes 884744 | tf_op jit(solution)/shard_map/ppermute | solution.py:43
  188.9 8.5 %collective-permute-start.19 = (bf16[192,192]{0,1:T(8,128)(2,1)S(1)}, bf16[192,192]{0,1:T(8,128)(2,1)S(1)}, u32[]{:S(2)}, u32[]{:S(2)}) collective-permute-start(bf16[192,192]{0,1:T(8,128)(2,1)S(1)} %get-tuple-element.24), channel_id=1, source_target_pairs={{0,8},{1,9},{2,10},{3,11},{4,12},{5,13},{6,14},{7,15},{8,16},{9,17... | collective-permute-start | bytes 221192 | tf_op jit(solution)/shard_map/ppermute | solution.py:43
  193.3 11.1 %collective-permute-start.21 = (bf16[192,192]{0,1:T(8,128)(2,1)S(1)}, bf16[192,192]{0,1:T(8,128)(2,1)S(1)}, u32[]{:S(2)}, u32[]{:S(2)}) collective-permute-start(bf16[192,192]{0,1:T(8,128)(2,1)S(1)} %get-tuple-element.25), channel_id=1, source_target_pairs={{0,24},{1,25},{2,26},{3,27},{4,28},{5,29},{6,30},{7,31},{8,0},{9,1... | collective-permute-start | bytes 221192 | tf_op jit(solution)/shard_map/ppermute | solution.py:43
  197.4 9.7 %collective-permute-start.20 = (bf16[192,192]{0,1:T(8,128)(2,1)S(1)}, bf16[192,192]{0,1:T(8,128)(2,1)S(1)}, u32[]{:S(2)}, u32[]{:S(2)}) collective-permute-start(bf16[192,192]{0,1:T(8,128)(2,1)S(1)} %fusion.41), channel_id=1, source_target_pairs={{0,8},{1,9},{2,10},{3,11},{4,12},{5,13},{6,14},{7,15},{8,16},{9,17... | collective-permute-start | bytes 221192 | tf_op jit(solution)/shard_map/ppermute | solution.py:43
  (6 other events, 15.4 us)

commit v9 on v6

--- a/solution.py
+++ b/solution.py
@@ -102,22 +102,21 @@
     scale = width_head ** (-0.5)
     core = lax.axis_index("dp") % 2
     first = core == 0
-    n_fsdp = lax.axis_size("fsdp")
-    outer_fsdp = n_fsdp // inner_fsdp
-    ring_y = Ring("fsdp", outer_fsdp, inner_fsdp)
-    ring_z = Ring("fsdp", inner_fsdp, 1)
+    outer_fsdp = lax.axis_size("fh")
+    n_fsdp = outer_fsdp * inner_fsdp
+    ring_y = Ring("fh", outer_fsdp, 1)
+    ring_z = Ring("fz", inner_fsdp, 1)
     ring_x = Ring("seq", lax.axis_size("seq"), 1)
 
     w_mine = lax.dynamic_slice_in_dim(qkv_weight, core * half, half, axis=1)
-    stack_y, slot_y, _ = ring_gather(w_mine, ring_y)
+    stack_y = lax.all_gather(w_mine, "fh", axis=0, tiled=False)
     blocked = features.reshape(features.shape[0], outer_fsdp, inner_fsdp, rows_w)
     stack_zy, slot_z, blocked = ring_gather(stack_y, ring_z, beside=blocked)
     flat = stack_zy.reshape(-1, rows_w, half)
     me_y, me_z = ring_y.position(), ring_z.position()
     absolute = jnp.arange(n_fsdp, dtype=jnp.int32)
-    rel_y = (absolute // inner_fsdp - me_y) % outer_fsdp
     rel_z = (absolute % inner_fsdp - me_z) % inner_fsdp
-    order = jnp.asarray(slot_z, jnp.int32)[rel_z] * outer_fsdp + jnp.asarray(slot_y, jnp.int32)[rel_y]
+    order = jnp.asarray(slot_z, jnp.int32)[rel_z] * outer_fsdp + absolute // inner_fsdp
     w_mine_all = jnp.take(flat, order, axis=0, mode="clip").reshape(n_fsdp * rows_w, half)
     w_other_all = dp_partner(w_mine_all, 1)
 
@@ -205,16 +204,23 @@
 
 
 def solution(mesh):
+    inner = inner_ring_size(mesh)
+    sizes = dict(zip(mesh.axis_names, mesh.devices.shape))
+    split = jax.sharding.Mesh(
+        mesh.devices.reshape(sizes["dp"], sizes["seq"], sizes["fsdp"] // inner, inner),
+        ("dp", "seq", "fh", "fz"),
+    )
+    rows = ("dp", "fh", "fz")
     placed = (
-        P(("dp", "fsdp"), "seq", None),
-        P(("dp", "fsdp"), "seq"),
-        P("fsdp", None),
-        P(("dp", "fsdp"), "seq", None),
+        P(rows, "seq", None),
+        P(rows, "seq"),
+        P(("fh", "fz"), None),
+        P(rows, "seq", None),
     )
     return jax.shard_map(
-        functools.partial(shards, inner_fsdp=inner_ring_size(mesh)),
-        mesh=mesh,
+        functools.partial(shards, inner_fsdp=inner),
+        mesh=split,
         in_specs=placed,
-        out_specs=(P(("dp", "fsdp"), "seq", None), P("fsdp", None)),
+        out_specs=(P(rows, "seq", None), P(("fh", "fz"), None)),
         check_vma=False,
     )

time: 232 us -> 228 us (0.983)
  starting transfers between devices: 90.7 us -> 72.8 us
  blocking collectives: 44.4 us -> 58 us
  local copies, waits for them, and re-layouts: 17.5 us -> 20.4 us
    ppermute x20 -> x17, starting transfers between devices: 78.1 us -> 58.9 us  [shift(): return lax.ppermute(x, self.axis, perm=pairs)]
    all_gather x0 -> x1, blocking collectives: none -> 16.8 us  [shards(): stack_y = lax.all_gather(w_mine, 'fh', axis=0, tiled=False)]
    all_gather x1, blocking collectives: 19.9 us -> 16.8 us  [shards(): by_dp = lax.all_gather(over_seq, 'dp', axis=0, tiled=False)]
    unnamed x22 -> x23, local copies, waits for them, and re-layouts: 3.79 us -> 6.83 us
    ppermute x20 -> x17, waiting for transfers between devices: 44.4 us -> 42.1 us  [shift(): return lax.ppermute(x, self.axis, perm=pairs)]
  transfers between devices with their start and end apart: 22 -> 19, of which waited for: 18 -> 16; matrix products, arithmetic and copies ran while one was open for 8% -> 9% of each run, Pallas kernels for 0% -> 0%
where the time goes in v9:
time: 228 us; the launch traced here: 227 us
  starting transfers between devices  72.8 us (32%)
  blocking collectives  58 us (25%)
  waiting for transfers between devices  45 us (20%)
  local copies, waits for them, and re-layouts  20.4 us (9%)
  matrix products  19.5 us (9%)
  other arithmetic  9.77 us (4%)
    ppermute x17, starting transfers between devices, shift(): return lax.ppermute(x, self.axis, perm=pairs)  58.9 us
    ppermute x17, waiting for transfers between devices, shift(): return lax.ppermute(x, self.axis, perm=pairs)  42.1 us
    all_gather x1, blocking collectives, shards(): stack_y = lax.all_gather(w_mine, 'fh', axis=0, tiled=False)  16.8 us
    all_gather x1, blocking collectives, shards(): by_dp = lax.all_gather(over_seq, 'dp', axis=0, tiled=False)  16.8 us
    ppermute x2, starting transfers between devices, dp_partner(): return lax.ppermute(x, 'dp', perm=pairs)  13.8 us
    all_gather x1, blocking collectives, shards(): packed_all = lax.all_gather(packed, 'seq', axis=0, tiled=True)  12.9 us
    all_gather x1, blocking collectives, shards(): by_seq = lax.all_gather(over_fsdp, 'seq', axis=0, tiled=False)  11.5 us
    unnamed x23, local copies, waits for them, and re-layouts  6.83 us
  transfers between devices with their start and end apart: 19, of which 16 were waited for; matrix products, arithmetic and copies ran while one was open for 9% of the time, Pallas kernels for 0%

profile of v9, /device:TPU:1, one launch (start us, length us, event | category | flops | bytes accessed | tf_op | source)
XLA Modules:
  0.0 227.0 jit_solution(15358303081576632680)
XLA Ops:
  1.6 16.8 %all-gather = bf16[768,192]{1,0:T(8,128)(2,1)} all-gather(bf16[192,192]{1,0:T(8,128)(2,1)S(1)} %constant_dynamic-slice_fusion), channel_id=2, replica_groups=mesh['dp'=4,'seq'=4,'fh'=4,'fz'=8] {'fh'}, dimensions={0}, use_global_device_ids=true | all-gather | bytes 368640 | tf_op jit(solution)/shard_map/all_gather | solution.py:112
  18.5 3.4 %collective-permute-start = (bf16[4,192,192]{2,1,0:T(8,128)(2,1)}, bf16[4,192,192]{2,1,0:T(8,128)(2,1)}, u32[]{:S(2)}, u32[]{:S(2)}) collective-permute-start(bf16[4,192,192]{2,1,0:T(8,128)(2,1)} %bitcast.1), channel_id=1, source_target_pairs={{0,1},{1,2},{2,3},{3,4},{4,5},{5,6},{6,7},{7,0},{8,9},{9,10},{10,1... | collective-permute-start | bytes 884744 | tf_op jit(solution)/shard_map/ppermute | solution.py:43
  21.8 8.6 %collective-permute-start.1 = (bf16[4,192,192]{2,1,0:T(8,128)(2,1)}, bf16[4,192,192]{2,1,0:T(8,128)(2,1)}, u32[]{:S(2)}, u32[]{:S(2)}) collective-permute-start(bf16[4,192,192]{2,1,0:T(8,128)(2,1)} %bitcast.1), channel_id=1, source_target_pairs={{0,7},{1,0},{2,1},{3,2},{4,3},{5,4},{6,5},{7,6},{8,15},{9,8},{10,9... | collective-permute-start | bytes 884744 | tf_op jit(solution)/shard_map/ppermute | solution.py:43
  32.9 6.4 %reshape_squeeze.3 = bf16[192,4,8,192]{3,2,1,0:T(8,128)(2,1)} reshape(bf16[1,192,6144]{2,1,0:T(8,128)(2,1)} %param.5) | data formatting | bytes 4718592 | tf_op jit(solution)/shard_map/reshape;squeeze | solution.py:113
  42.3 4.6 %collective-permute-start.3 = (bf16[4,192,192]{2,1,0:T(8,128)(2,1)}, bf16[4,192,192]{2,1,0:T(8,128)(2,1)S(1)}, u32[]{:S(2)}, u32[]{:S(2)}) collective-permute-start(bf16[4,192,192]{2,1,0:T(8,128)(2,1)} %collective-permute-done.1), channel_id=1, source_target_pairs={{0,7},{1,0},{2,1},{3,2},{4,3},{5,4},{6,5},{7,6},{8,15},{9,8},{10,9... | collective-permute-start | bytes 884744 | tf_op jit(solution)/shard_map/ppermute | solution.py:43
  51.9 4.9 %collective-permute-start.5 = (bf16[4,192,192]{2,1,0:T(8,128)(2,1)S(1)}, bf16[4,192,192]{2,1,0:T(8,128)(2,1)S(1)}, u32[]{:S(2)}, u32[]{:S(2)}) collective-permute-start(bf16[4,192,192]{2,1,0:T(8,128)(2,1)S(1)} %collective-permute-done.3), channel_id=1, source_target_pairs={{0,7},{1,0},{2,1},{3,2},{4,3},{5,4},{6,5},{7,6},{8,15},{9,8},{10,9... | collective-permute-start | bytes 884744 | tf_op jit(solution)/shard_map/ppermute | solution.py:43
  61.5 7.7 %collective-permute-done.6 = bf16[4,192,192]{2,1,0:T(8,128)(2,1)S(1)} collective-permute-done((bf16[4,192,192]{2,1,0:T(8,128)(2,1)S(1)}, bf16[4,192,192]{2,1,0:T(8,128)(2,1)S(1)}, u32[]{:S(2)}, u32[]{:S(2)}) %collective-permute-start.6) | collective-permute-done | bytes 294944 | tf_op jit(solution)/shard_map/ppermute | solution.py:43
  76.2 9.7 %collective-permute-start.7 = (bf16[6144,192]{0,1:T(8,128)(2,1)}, bf16[6144,192]{0,1:T(8,128)(2,1)}, u32[]{:S(2)}, u32[]{:S(2)}) collective-permute-start(bf16[6144,192]{0,1:T(8,128)(2,1)} %copy.31), channel_id=1, source_target_pairs={{0,128},{128,0},{256,384},{384,256},{1,129},{129,1},{257,385},{385... | collective-permute-start | bytes 7077896 | tf_op jit(solution)/shard_map/ppermute | solution.py:23
  93.1 12.9 %all_gather.21 = bf16[768,640]{1,0:T(8,128)(2,1)S(1)} all-gather(bf16[192,640]{1,0:T(8,128)(2,1)S(1)} %pad_maximum_fusion.1), channel_id=1, replica_groups=mesh['dp'=4,'seq'=4,'fh'=4,'fz'=8] {'seq'}, dimensions={0}, use_global_device_ids=true | all-gather | bytes 1228800 | tf_op jit(solution)/shard_map/all_gather | solution.py:136
  110.5 4.1 %convert_bitcast_fusion = bf16[8,4,192,192]{2,3,0,1:T(8,128)(2,1)} fusion(bf16[192,4,8,192]{3,2,1,0:T(8,128)(2,1)S(1)} %copy-done.1, pred[]{:T(512)S(6)} %eq.39, bf16[192,128]{1,0:T(8,128)(2,1)S(1)} %convolution_convert_fusion.1, bf16[192,128]{1,0:T(8,128)(2,1)S(1)} %convolution_convert_fusion.2, bf16[192,128]{1,0:T(8,128)(2,1)S(1)} %convolution_convert_fusion), kind=kOutput, calls=%fused_computation.8 | convolution fusion | flops 454496256 | bytes 4866049 | tf_op jit(solution)/shard_map/pyzd,pc->zydc/dot_general | solution.py:171
  114.6 4.2 %collective-permute-start.8 = (bf16[8,4,192,192]{2,3,0,1:T(8,128)(2,1)}, bf16[8,4,192,192]{2,3,0,1:T(8,128)(2,1)}, u32[]{:S(2)}, u32[]{:S(2)}) collective-permute-start(bf16[8,4,192,192]{2,3,0,1:T(8,128)(2,1)} %convert_bitcast_fusion), channel_id=1, source_target_pairs={{0,128},{128,0},{256,384},{384,256},{1,129},{129,1},{257,385},{385... | collective-permute-start | bytes 7077896 | tf_op jit(solution)/shard_map/ppermute | solution.py:23
  124.2 3.0 %convert_add_fusion = f32[8,4,192,192]{2,3,0,1:T(8,128)S(1)} fusion(f32[8,4,192,192]{2,3,0,1:T(8,128)S(1)} %fusion.5, bf16[8,4,192,192]{2,3,0,1:T(8,128)(2,1)} %collective-permute-done.8), kind=kLoop, calls=%fused_computation.4 | loop fusion | flops 2359296 | bytes 11796480 | tf_op jit(solution)/shard_map/add | solution.py:175
  129.3 4.0 %fusion = bf16[192,6144]{1,0:T(8,128)(2,1)} fusion(f32[192,6144]{1,0:T(8,128)S(1)} %fusion.62, bf16[6144,192]{0,1:T(8,128)(2,1)} %collective-permute-done.7, pred[]{:T(512)S(6)} %eq.39, bf16[192,128]{1,0:T(8,128)(2,1)S(1)} %convolution_convert_fusion.1, bf16[192,128]{1,0:T(8,128)(2,1)S(1)} %convolution_convert_fusion.2, ...), kind=kOutput, calls=%fused_computation.3 | convolution fusion | flops 455675904 | bytes 9584641 | tf_op jit(solution)/shard_map/dot_general | solution.py:16
  133.2 4.5 %collective-permute-start.13 = (bf16[4,192,192]{1,2,0:T(8,128)(2,1)S(1)}, bf16[4,192,192]{1,2,0:T(8,128)(2,1)S(1)}, u32[]{:S(2)}, u32[]{:S(2)}) collective-permute-start(bf16[4,192,192]{1,2,0:T(8,128)(2,1)S(1)} %get-tuple-element.22), channel_id=1, source_target_pairs={{0,7},{1,0},{2,1},{3,2},{4,3},{5,4},{6,5},{7,6},{8,15},{9,8},{10,9... | collective-permute-start | bytes 884744 | tf_op jit(solution)/shard_map/ppermute | solution.py:43
  137.7 3.0 %collective-permute-done.9 = bf16[4,192,192]{1,2,0:T(8,128)(2,1)S(1)} collective-permute-done((bf16[4,192,192]{1,2,0:T(8,128)(2,1)S(1)}, bf16[4,192,192]{1,2,0:T(8,128)(2,1)S(1)}, u32[]{:S(2)}, u32[]{:S(2)}) %collective-permute-start.9) | collective-permute-done | bytes 294944 | tf_op jit(solution)/shard_map/ppermute | solution.py:43
  145.5 7.9 %collective-permute-done.10 = bf16[4,192,192]{1,2,0:T(8,128)(2,1)S(1)} collective-permute-done((bf16[4,192,192]{1,2,0:T(8,128)(2,1)S(1)}, bf16[4,192,192]{1,2,0:T(8,128)(2,1)S(1)}, u32[]{:S(2)}, u32[]{:S(2)}) %collective-permute-start.10) | collective-permute-done | bytes 294944 | tf_op jit(solution)/shard_map/ppermute | solution.py:43
  156.9 4.6 %collective-permute-start.14 = (bf16[4,192,192]{1,2,0:T(8,128)(2,1)S(1)}, bf16[4,192,192]{1,2,0:T(8,128)(2,1)S(1)}, u32[]{:S(2)}, u32[]{:S(2)}) collective-permute-start(bf16[4,192,192]{1,2,0:T(8,128)(2,1)S(1)} %get-tuple-element.21), channel_id=1, source_target_pairs={{0,7},{1,0},{2,1},{3,2},{4,3},{5,4},{6,5},{7,6},{8,15},{9,8},{10,9... | collective-permute-start | bytes 884744 | tf_op jit(solution)/shard_map/ppermute | solution.py:43
  161.5 5.0 %collective-permute-done.11 = bf16[4,192,192]{1,2,0:T(8,128)(2,1)S(1)} collective-permute-done((bf16[4,192,192]{1,2,0:T(8,128)(2,1)S(1)}, bf16[4,192,192]{1,2,0:T(8,128)(2,1)S(1)}, u32[]{:S(2)}, u32[]{:S(2)}) %collective-permute-start.11) | collective-permute-done | bytes 294944 | tf_op jit(solution)/shard_map/ppermute | solution.py:43
  170.9 5.3 %collective-permute-start.15 = (bf16[4,192,192]{1,2,0:T(8,128)(2,1)S(1)}, bf16[4,192,192]{1,2,0:T(8,128)(2,1)S(1)}, u32[]{:S(2)}, u32[]{:S(2)}) collective-permute-start(bf16[4,192,192]{1,2,0:T(8,128)(2,1)S(1)} %get-tuple-element.19), channel_id=1, source_target_pairs={{0,7},{1,0},{2,1},{3,2},{4,3},{5,4},{6,5},{7,6},{8,15},{9,8},{10,9... | collective-permute-start | bytes 884744 | tf_op jit(solution)/shard_map/ppermute | solution.py:43
  176.3 4.1 %collective-permute-done.12 = bf16[4,192,192]{1,2,0:T(8,128)(2,1)S(1)} collective-permute-done((bf16[4,192,192]{1,2,0:T(8,128)(2,1)S(1)}, bf16[4,192,192]{1,2,0:T(8,128)(2,1)S(1)}, u32[]{:S(2)}, u32[]{:S(2)}) %collective-permute-start.12) | collective-permute-done | bytes 294944 | tf_op jit(solution)/shard_map/ppermute | solution.py:43
  184.9 5.1 %collective-permute-start.18 = (bf16[192,192]{0,1:T(8,128)(2,1)S(1)}, bf16[192,192]{0,1:T(8,128)(2,1)S(1)}, u32[]{:S(2)}, u32[]{:S(2)}) collective-permute-start(bf16[192,192]{0,1:T(8,128)(2,1)S(1)} %get-tuple-element.27), channel_id=1, source_target_pairs={{0,24},{8,0},{16,8},{24,16},{1,25},{9,1},{17,9},{25,17},{2,26},{10... | collective-permute-start | bytes 221192 | tf_op jit(solution)/shard_map/ppermute | solution.py:43
  192.5 5.0 %collective-permute-done.17 = bf16[192,192]{0,1:T(8,128)(2,1)S(1)} collective-permute-done((bf16[192,192]{0,1:T(8,128)(2,1)S(1)}, bf16[192,192]{0,1:T(8,128)(2,1)S(1)}, u32[]{:S(2)}, u32[]{:S(2)}) %collective-permute-start.17) | collective-permute-done | bytes 73760 | tf_op jit(solution)/shard_map/ppermute | solution.py:43
  197.7 11.5 %all-gather.1 = f32[768,192]{1,0:T(8,128)S(1)} all-gather(f32[192,192]{1,0:T(8,128)S(1)} %copy.39), channel_id=3, replica_groups=mesh['dp'=4,'seq'=4,'fh'=4,'fz'=8] {'seq'}, dimensions={0}, use_global_device_ids=true | all-gather | bytes 737280 | tf_op jit(solution)/shard_map/all_gather | solution.py:179
  209.3 16.8 %all_gather.24 = f32[4,192,192]{2,1,0:T(8,128)S(1)} all-gather(f32[1,192,192]{2,1,0:T(8,128)S(1)} %fusion.38), channel_id=1, replica_groups=mesh['dp'=4,'seq'=4,'fh'=4,'fz'=8] {'dp'}, dimensions={0}, use_global_device_ids=true | all-gather | bytes 737280 | tf_op jit(solution)/shard_map/all_gather | solution.py:183
  (84 shorter events, 62.4 us)
Async XLA Ops:
  18.5 20.9 %collective-permute-start = (bf16[4,192,192]{2,1,0:T(8,128)(2,1)}, bf16[4,192,192]{2,1,0:T(8,128)(2,1)}, u32[]{:S(2)}, u32[]{:S(2)}) collective-permute-start(bf16[4,192,192]{2,1,0:T(8,128)(2,1)} %bitcast.1), channel_id=1, source_target_pairs={{0,1},{1,2},{2,3},{3,4},{4,5},{5,6},{6,7},{7,0},{8,9},{9,10},{10,1... | collective-permute-start | bytes 884744 | tf_op jit(solution)/shard_map/ppermute | solution.py:43
  21.8 20.5 %collective-permute-start.1 = (bf16[4,192,192]{2,1,0:T(8,128)(2,1)}, bf16[4,192,192]{2,1,0:T(8,128)(2,1)}, u32[]{:S(2)}, u32[]{:S(2)}) collective-permute-start(bf16[4,192,192]{2,1,0:T(8,128)(2,1)} %bitcast.1), channel_id=1, source_target_pairs={{0,7},{1,0},{2,1},{3,2},{4,3},{5,4},{6,5},{7,6},{8,15},{9,8},{10,9... | collective-permute-start | bytes 884744 | tf_op jit(solution)/shard_map/ppermute | solution.py:43
  39.3 9.9 %collective-permute-start.2 = (bf16[4,192,192]{2,1,0:T(8,128)(2,1)}, bf16[4,192,192]{2,1,0:T(8,128)(2,1)S(1)}, u32[]{:S(2)}, u32[]{:S(2)}) collective-permute-start(bf16[4,192,192]{2,1,0:T(8,128)(2,1)} %collective-permute-done), channel_id=1, source_target_pairs={{0,1},{1,2},{2,3},{3,4},{4,5},{5,6},{6,7},{7,0},{8,9},{9,10},{10,1... | collective-permute-start | bytes 884744 | tf_op jit(solution)/shard_map/ppermute | solution.py:43
  42.3 9.6 %collective-permute-start.3 = (bf16[4,192,192]{2,1,0:T(8,128)(2,1)}, bf16[4,192,192]{2,1,0:T(8,128)(2,1)S(1)}, u32[]{:S(2)}, u32[]{:S(2)}) collective-permute-start(bf16[4,192,192]{2,1,0:T(8,128)(2,1)} %collective-permute-done.1), channel_id=1, source_target_pairs={{0,7},{1,0},{2,1},{3,2},{4,3},{5,4},{6,5},{7,6},{8,15},{9,8},{10,9... | collective-permute-start | bytes 884744 | tf_op jit(solution)/shard_map/ppermute | solution.py:43
  49.3 9.7 %collective-permute-start.4 = (bf16[4,192,192]{2,1,0:T(8,128)(2,1)S(1)}, bf16[4,192,192]{2,1,0:T(8,128)(2,1)S(1)}, u32[]{:S(2)}, u32[]{:S(2)}) collective-permute-start(bf16[4,192,192]{2,1,0:T(8,128)(2,1)S(1)} %collective-permute-done.2), channel_id=1, source_target_pairs={{0,1},{1,2},{2,3},{3,4},{4,5},{5,6},{6,7},{7,0},{8,9},{9,10},{10,1... | collective-permute-start | bytes 884744 | tf_op jit(solution)/shard_map/ppermute | solution.py:43
  51.9 9.6 %collective-permute-start.5 = (bf16[4,192,192]{2,1,0:T(8,128)(2,1)S(1)}, bf16[4,192,192]{2,1,0:T(8,128)(2,1)S(1)}, u32[]{:S(2)}, u32[]{:S(2)}) collective-permute-start(bf16[4,192,192]{2,1,0:T(8,128)(2,1)S(1)} %collective-permute-done.3), channel_id=1, source_target_pairs={{0,7},{1,0},{2,1},{3,2},{4,3},{5,4},{6,5},{7,6},{8,15},{9,8},{10,9... | collective-permute-start | bytes 884744 | tf_op jit(solution)/shard_map/ppermute | solution.py:43
  59.0 10.2 %collective-permute-start.6 = (bf16[4,192,192]{2,1,0:T(8,128)(2,1)S(1)}, bf16[4,192,192]{2,1,0:T(8,128)(2,1)S(1)}, u32[]{:S(2)}, u32[]{:S(2)}) collective-permute-start(bf16[4,192,192]{2,1,0:T(8,128)(2,1)S(1)} %collective-permute-done.4), channel_id=1, source_target_pairs={{0,1},{1,2},{2,3},{3,4},{4,5},{5,6},{6,7},{7,0},{8,9},{9,10},{10,1... | collective-permute-start | bytes 884744 | tf_op jit(solution)/shard_map/ppermute | solution.py:43
  73.6 12.3 %copy-start.7 = (s32[1,192]{1,0:T(1,128)S(1)}, s32[1,192]{1,0:T(1,128)}, u32[]{:S(2)}) copy-start(s32[1,192]{1,0:T(1,128)} %param.6) | copy-start | bytes 2308
  76.2 14.2 %collective-permute-start.7 = (bf16[6144,192]{0,1:T(8,128)(2,1)}, bf16[6144,192]{0,1:T(8,128)(2,1)}, u32[]{:S(2)}, u32[]{:S(2)}) collective-permute-start(bf16[6144,192]{0,1:T(8,128)(2,1)} %copy.31), channel_id=1, source_target_pairs={{0,128},{128,0},{256,384},{384,256},{1,129},{129,1},{257,385},{385... | collective-permute-start | bytes 7077896 | tf_op jit(solution)/shard_map/ppermute | solution.py:23
  85.9 4.4 %copy-start.4 = (bf16[1,192,6144]{2,1,0:T(8,128)(2,1)S(1)}, bf16[1,192,6144]{2,1,0:T(8,128)(2,1)}, u32[]{:S(2)}) copy-start(bf16[1,192,6144]{2,1,0:T(8,128)(2,1)} %param.5) | copy-start | bytes 7077892
  88.5 4.5 %copy-start.6 = (bf16[1,192,128]{2,1,0:T(8,128)(2,1)S(1)}, bf16[1,192,128]{2,1,0:T(8,128)(2,1)}, u32[]{:S(2)}) copy-start(bf16[1,192,128]{2,1,0:T(8,128)(2,1)} %param.8) | copy-start | bytes 147460
  108.6 1.9 copy-start.1
  114.6 9.6 %collective-permute-start.8 = (bf16[8,4,192,192]{2,3,0,1:T(8,128)(2,1)}, bf16[8,4,192,192]{2,3,0,1:T(8,128)(2,1)}, u32[]{:S(2)}, u32[]{:S(2)}) collective-permute-start(bf16[8,4,192,192]{2,3,0,1:T(8,128)(2,1)} %convert_bitcast_fusion), channel_id=1, source_target_pairs={{0,128},{128,0},{256,384},{384,256},{1,129},{129,1},{257,385},{385... | collective-permute-start | bytes 7077896 | tf_op jit(solution)/shard_map/ppermute | solution.py:23
  127.2 13.5 %copy-start.3 = (f32[8,4,192,192]{2,3,0,1:T(8,128)}, f32[8,4,192,192]{2,3,0,1:T(8,128)S(1)}, u32[]{:S(2)}) copy-start(f32[8,4,192,192]{2,3,0,1:T(8,128)S(1)} %convert_add_fusion) | copy-start | bytes 14155780
  127.3 13.4 %collective-permute-start.9 = (bf16[4,192,192]{1,2,0:T(8,128)(2,1)S(1)}, bf16[4,192,192]{1,2,0:T(8,128)(2,1)S(1)}, u32[]{:S(2)}, u32[]{:S(2)}) collective-permute-start(bf16[4,192,192]{1,2,0:T(8,128)(2,1)S(1)} %get-tuple-element.23), channel_id=1, source_target_pairs={{0,1},{1,2},{2,3},{3,4},{4,5},{5,6},{6,7},{7,0},{8,9},{9,10},{10,1... | collective-permute-start | bytes 884744 | tf_op jit(solution)/shard_map/ppermute | solution.py:43
  133.2 12.3 %collective-permute-start.13 = (bf16[4,192,192]{1,2,0:T(8,128)(2,1)S(1)}, bf16[4,192,192]{1,2,0:T(8,128)(2,1)S(1)}, u32[]{:S(2)}, u32[]{:S(2)}) collective-permute-start(bf16[4,192,192]{1,2,0:T(8,128)(2,1)S(1)} %get-tuple-element.22), channel_id=1, source_target_pairs={{0,7},{1,0},{2,1},{3,2},{4,3},{5,4},{6,5},{7,6},{8,15},{9,8},{10,9... | collective-permute-start | bytes 884744 | tf_op jit(solution)/shard_map/ppermute | solution.py:43
  140.9 12.5 %collective-permute-start.10 = (bf16[4,192,192]{1,2,0:T(8,128)(2,1)S(1)}, bf16[4,192,192]{1,2,0:T(8,128)(2,1)S(1)}, u32[]{:S(2)}, u32[]{:S(2)}) collective-permute-start(bf16[4,192,192]{1,2,0:T(8,128)(2,1)S(1)} %fusion.28), channel_id=1, source_target_pairs={{0,1},{1,2},{2,3},{3,4},{4,5},{5,6},{6,7},{7,0},{8,9},{9,10},{10,1... | collective-permute-start | bytes 884744 | tf_op jit(solution)/shard_map/ppermute | solution.py:43
  154.9 11.6 %collective-permute-start.11 = (bf16[4,192,192]{1,2,0:T(8,128)(2,1)S(1)}, bf16[4,192,192]{1,2,0:T(8,128)(2,1)S(1)}, u32[]{:S(2)}, u32[]{:S(2)}) collective-permute-start(bf16[4,192,192]{1,2,0:T(8,128)(2,1)S(1)} %get-tuple-element.20), channel_id=1, source_target_pairs={{0,1},{1,2},{2,3},{3,4},{4,5},{5,6},{6,7},{7,0},{8,9},{9,10},{10,1... | collective-permute-start | bytes 884744 | tf_op jit(solution)/shard_map/ppermute | solution.py:43
  156.9 10.6 %collective-permute-start.14 = (bf16[4,192,192]{1,2,0:T(8,128)(2,1)S(1)}, bf16[4,192,192]{1,2,0:T(8,128)(2,1)S(1)}, u32[]{:S(2)}, u32[]{:S(2)}) collective-permute-start(bf16[4,192,192]{1,2,0:T(8,128)(2,1)S(1)} %get-tuple-element.21), channel_id=1, source_target_pairs={{0,7},{1,0},{2,1},{3,2},{4,3},{5,4},{6,5},{7,6},{8,15},{9,8},{10,9... | collective-permute-start | bytes 884744 | tf_op jit(solution)/shard_map/ppermute | solution.py:43
  169.0 11.4 %collective-permute-start.12 = (bf16[4,192,192]{1,2,0:T(8,128)(2,1)S(1)}, bf16[4,192,192]{1,2,0:T(8,128)(2,1)S(1)}, u32[]{:S(2)}, u32[]{:S(2)}) collective-permute-start(bf16[4,192,192]{1,2,0:T(8,128)(2,1)S(1)} %get-tuple-element.18), channel_id=1, source_target_pairs={{0,1},{1,2},{2,3},{3,4},{4,5},{5,6},{6,7},{7,0},{8,9},{9,10},{10,1... | collective-permute-start | bytes 884744 | tf_op jit(solution)/shard_map/ppermute | solution.py:43
  170.9 10.4 %collective-permute-start.15 = (bf16[4,192,192]{1,2,0:T(8,128)(2,1)S(1)}, bf16[4,192,192]{1,2,0:T(8,128)(2,1)S(1)}, u32[]{:S(2)}, u32[]{:S(2)}) collective-permute-start(bf16[4,192,192]{1,2,0:T(8,128)(2,1)S(1)} %get-tuple-element.19), channel_id=1, source_target_pairs={{0,7},{1,0},{2,1},{3,2},{4,3},{5,4},{6,5},{7,6},{8,15},{9,8},{10,9... | collective-permute-start | bytes 884744 | tf_op jit(solution)/shard_map/ppermute | solution.py:43
  182.6 7.5 %collective-permute-start.16 = (bf16[192,192]{0,1:T(8,128)(2,1)S(1)}, bf16[192,192]{0,1:T(8,128)(2,1)S(1)}, u32[]{:S(2)}, u32[]{:S(2)}) collective-permute-start(bf16[192,192]{0,1:T(8,128)(2,1)S(1)} %get-tuple-element.26), channel_id=1, source_target_pairs={{0,8},{8,16},{16,24},{24,0},{1,9},{9,17},{17,25},{25,1},{2,10},{10... | collective-permute-start | bytes 221192 | tf_op jit(solution)/shard_map/ppermute | solution.py:43
  184.9 7.6 %collective-permute-start.18 = (bf16[192,192]{0,1:T(8,128)(2,1)S(1)}, bf16[192,192]{0,1:T(8,128)(2,1)S(1)}, u32[]{:S(2)}, u32[]{:S(2)}) collective-permute-start(bf16[192,192]{0,1:T(8,128)(2,1)S(1)} %get-tuple-element.27), channel_id=1, source_target_pairs={{0,24},{8,0},{16,8},{24,16},{1,25},{9,1},{17,9},{25,17},{2,26},{10... | collective-permute-start | bytes 221192 | tf_op jit(solution)/shard_map/ppermute | solution.py:43
  190.1 7.5 %collective-permute-start.17 = (bf16[192,192]{0,1:T(8,128)(2,1)S(1)}, bf16[192,192]{0,1:T(8,128)(2,1)S(1)}, u32[]{:S(2)}, u32[]{:S(2)}) collective-permute-start(bf16[192,192]{0,1:T(8,128)(2,1)S(1)} %fusion.39), channel_id=1, source_target_pairs={{0,8},{8,16},{16,24},{24,0},{1,9},{9,17},{17,25},{25,1},{2,10},{10... | collective-permute-start | bytes 221192 | tf_op jit(solution)/shard_map/ppermute | solution.py:43
  (3 other events, 4.5 us)

commit v10 on v9

--- a/solution.py
+++ b/solution.py
@@ -47,10 +47,11 @@
     n = ring.size
     got, slot = [x], {0: 0}
     cw, ccw = x, x
+    last_cw = n - 1 if (n - 1) % 2 == 1 else n - 2
     for t in range(1, n):
         if t % 2 == 1:
             cw = ring.shift(cw, 1)
-            if t == 1 and beside is not None:
+            if t == last_cw and beside is not None:
                 cw, beside = lax.optimization_barrier((cw, beside))
             slot[(n - (t + 1) // 2) % n] = len(got)
             got.append(cw)
@@ -75,7 +76,7 @@
     acc = pick(me + up)
     for t in range(1, up + 1):
         acc = ring.shift(acc.astype(jnp.bfloat16), 1)
-        if t == 1 and beside is not None:
+        if t == up and beside is not None:
             acc, beside = lax.optimization_barrier((acc, beside))
         acc = acc.astype(jnp.float32)
         if t < up:

time: 228 us -> 235 us (1.031)
  local copies, waits for them, and re-layouts: 20.4 us -> 23.3 us
    convert_element_type x0 -> x2, other arithmetic: none -> 3.38 us  [ring_reduce_scatter(): acc = ring.shift(acc.astype(jnp.bfloat16), -1).astype(jnp.float32)]
    unnamed x23 -> x21, local copies, waits for them, and re-layouts: 6.83 us -> 8.79 us
  transfers between devices with their start and end apart: 19 -> 19, of which waited for: 16 -> 15; matrix products, arithmetic and copies ran while one was open for 9% -> 11% of each run, Pallas kernels for 0% -> 0%
where the time goes in v10:
time: 235 us; the launch traced here: 233 us
  starting transfers between devices  72.8 us (31%)
  blocking collectives  58 us (25%)
  waiting for transfers between devices  44.3 us (19%)
  local copies, waits for them, and re-layouts  23.3 us (10%)
  matrix products  21.5 us (9%)
  other arithmetic  12 us (5%)
    ppermute x17, starting transfers between devices, shift(): return lax.ppermute(x, self.axis, perm=pairs)  59 us
    ppermute x17, waiting for transfers between devices, shift(): return lax.ppermute(x, self.axis, perm=pairs)  41.4 us
    all_gather x1, blocking collectives, shards(): stack_y = lax.all_gather(w_mine, 'fh', axis=0, tiled=False)  16.8 us
    all_gather x1, blocking collectives, shards(): by_dp = lax.all_gather(over_seq, 'dp', axis=0, tiled=False)  16.8 us
    ppermute x2, starting transfers between devices, dp_partner(): return lax.ppermute(x, 'dp', perm=pairs)  13.8 us
    all_gather x1, blocking collectives, shards(): packed_all = lax.all_gather(packed, 'seq', axis=0, tiled=True)  12.9 us
    all_gather x1, blocking collectives, shards(): by_seq = lax.all_gather(over_fsdp, 'seq', axis=0, tiled=False)  11.5 us
    unnamed x21, local copies, waits for them, and re-layouts  8.79 us
  transfers between devices with their start and end apart: 19, of which 15 were waited for; matrix products, arithmetic and copies ran while one was open for 11% of the time, Pallas kernels for 0%

profile of v10, /device:TPU:1, one launch (start us, length us, event | category | flops | bytes accessed | tf_op | source)
XLA Modules:
  0.0 233.3 jit_solution(5037031333657859631)
XLA Ops:
  1.6 16.8 %all-gather = bf16[768,192]{1,0:T(8,128)(2,1)} all-gather(bf16[192,192]{1,0:T(8,128)(2,1)S(1)} %constant_dynamic-slice_fusion), channel_id=2, replica_groups=mesh['dp'=4,'seq'=4,'fh'=4,'fz'=8] {'fh'}, dimensions={0}, use_global_device_ids=true | all-gather | bytes 368640 | tf_op jit(solution)/shard_map/all_gather | solution.py:113
  18.5 3.4 %collective-permute-start = (bf16[4,192,192]{2,1,0:T(8,128)(2,1)}, bf16[4,192,192]{2,1,0:T(8,128)(2,1)}, u32[]{:S(2)}, u32[]{:S(2)}) collective-permute-start(bf16[4,192,192]{2,1,0:T(8,128)(2,1)} %bitcast.1), channel_id=1, source_target_pairs={{0,1},{1,2},{2,3},{3,4},{4,5},{5,6},{6,7},{7,0},{8,9},{9,10},{10,1... | collective-permute-start | bytes 884744 | tf_op jit(solution)/shard_map/ppermute | solution.py:43
  21.8 8.6 %collective-permute-start.1 = (bf16[4,192,192]{2,1,0:T(8,128)(2,1)}, bf16[4,192,192]{2,1,0:T(8,128)(2,1)}, u32[]{:S(2)}, u32[]{:S(2)}) collective-permute-start(bf16[4,192,192]{2,1,0:T(8,128)(2,1)} %bitcast.1), channel_id=1, source_target_pairs={{0,7},{1,0},{2,1},{3,2},{4,3},{5,4},{6,5},{7,6},{8,15},{9,8},{10,9... | collective-permute-start | bytes 884744 | tf_op jit(solution)/shard_map/ppermute | solution.py:43
  32.9 6.4 %reshape_squeeze.3 = bf16[192,4,8,192]{3,2,1,0:T(8,128)(2,1)} reshape(bf16[1,192,6144]{2,1,0:T(8,128)(2,1)} %param.5) | data formatting | bytes 4718592 | tf_op jit(solution)/shard_map/reshape;squeeze | solution.py:114
  42.3 4.6 %collective-permute-start.3 = (bf16[4,192,192]{2,1,0:T(8,128)(2,1)}, bf16[4,192,192]{2,1,0:T(8,128)(2,1)S(1)}, u32[]{:S(2)}, u32[]{:S(2)}) collective-permute-start(bf16[4,192,192]{2,1,0:T(8,128)(2,1)} %collective-permute-done.1), channel_id=1, source_target_pairs={{0,7},{1,0},{2,1},{3,2},{4,3},{5,4},{6,5},{7,6},{8,15},{9,8},{10,9... | collective-permute-start | bytes 884744 | tf_op jit(solution)/shard_map/ppermute | solution.py:43
  51.9 4.9 %collective-permute-start.5 = (bf16[4,192,192]{2,1,0:T(8,128)(2,1)S(1)}, bf16[4,192,192]{2,1,0:T(8,128)(2,1)S(1)}, u32[]{:S(2)}, u32[]{:S(2)}) collective-permute-start(bf16[4,192,192]{2,1,0:T(8,128)(2,1)S(1)} %collective-permute-done.3), channel_id=1, source_target_pairs={{0,7},{1,0},{2,1},{3,2},{4,3},{5,4},{6,5},{7,6},{8,15},{9,8},{10,9... | collective-permute-start | bytes 884744 | tf_op jit(solution)/shard_map/ppermute | solution.py:43
  61.5 7.7 %collective-permute-done.6 = bf16[4,192,192]{2,1,0:T(8,128)(2,1)S(1)} collective-permute-done((bf16[4,192,192]{2,1,0:T(8,128)(2,1)S(1)}, bf16[4,192,192]{2,1,0:T(8,128)(2,1)S(1)}, u32[]{:S(2)}, u32[]{:S(2)}) %collective-permute-start.6) | collective-permute-done | bytes 294944 | tf_op jit(solution)/shard_map/ppermute | solution.py:43
  76.2 9.7 %collective-permute-start.7 = (bf16[6144,192]{0,1:T(8,128)(2,1)}, bf16[6144,192]{0,1:T(8,128)(2,1)}, u32[]{:S(2)}, u32[]{:S(2)}) collective-permute-start(bf16[6144,192]{0,1:T(8,128)(2,1)} %copy.31), channel_id=1, source_target_pairs={{0,128},{128,0},{256,384},{384,256},{1,129},{129,1},{257,385},{385... | collective-permute-start | bytes 7077896 | tf_op jit(solution)/shard_map/ppermute | solution.py:23
  93.1 12.9 %all_gather.21 = bf16[768,640]{1,0:T(8,128)(2,1)S(1)} all-gather(bf16[192,640]{1,0:T(8,128)(2,1)S(1)} %pad_maximum_fusion.1), channel_id=1, replica_groups=mesh['dp'=4,'seq'=4,'fh'=4,'fz'=8] {'seq'}, dimensions={0}, use_global_device_ids=true | all-gather | bytes 1228800 | tf_op jit(solution)/shard_map/all_gather | solution.py:137
  110.5 4.1 %convert_bitcast_fusion = bf16[8,4,192,192]{2,3,0,1:T(8,128)(2,1)} fusion(bf16[192,4,8,192]{3,2,1,0:T(8,128)(2,1)S(1)} %copy-done.1, pred[]{:T(512)S(6)} %eq.39, bf16[192,128]{1,0:T(8,128)(2,1)S(1)} %convolution_convert_fusion.1, bf16[192,128]{1,0:T(8,128)(2,1)S(1)} %convolution_convert_fusion.2, bf16[192,128]{1,0:T(8,128)(2,1)S(1)} %convolution_convert_fusion), kind=kOutput, calls=%fused_computation.8 | convolution fusion | flops 454496256 | bytes 4866049 | tf_op jit(solution)/shard_map/pyzd,pc->zydc/dot_general | solution.py:172
  114.6 4.2 %collective-permute-start.8 = (bf16[8,4,192,192]{2,3,0,1:T(8,128)(2,1)}, bf16[8,4,192,192]{2,3,0,1:T(8,128)(2,1)}, u32[]{:S(2)}, u32[]{:S(2)}) collective-permute-start(bf16[8,4,192,192]{2,3,0,1:T(8,128)(2,1)} %convert_bitcast_fusion), channel_id=1, source_target_pairs={{0,128},{128,0},{256,384},{384,256},{1,129},{129,1},{257,385},{385... | collective-permute-start | bytes 7077896 | tf_op jit(solution)/shard_map/ppermute | solution.py:23
  118.8 4.3 %fusion.5 = f32[8,4,192,192]{2,3,0,1:T(8,128)S(1)} fusion(bf16[192,4,8,192]{3,2,1,0:T(8,128)(2,1)} %reshape_squeeze.3, pred[]{:T(512)S(6)} %eq.39, bf16[192,128]{1,0:T(8,128)(2,1)S(1)} %convolution_convert_fusion.1, bf16[192,128]{1,0:T(8,128)(2,1)S(1)} %convolution_convert_fusion.2, bf16[192,128]{1,0:T(8,128)(2,1)S(1)} %convolution_convert_fusion), kind=kOutput, calls=%fused_computation.13 | convolution fusion | flops 453316608 | bytes 7225345 | tf_op jit(solution)/shard_map/pyzd,pc->zydc/dot_general | solution.py:174
  124.2 3.0 %convert_add_fusion = f32[8,4,192,192]{2,3,0,1:T(8,128)S(1)} fusion(f32[8,4,192,192]{2,3,0,1:T(8,128)S(1)} %fusion.5, bf16[8,4,192,192]{2,3,0,1:T(8,128)(2,1)} %collective-permute-done.8), kind=kLoop, calls=%fused_computation.4 | loop fusion | flops 2359296 | bytes 11796480 | tf_op jit(solution)/shard_map/add | solution.py:176
  132.8 4.6 %collective-permute-start.13 = (bf16[4,192,192]{1,2,0:T(8,128)(2,1)}, bf16[4,192,192]{1,2,0:T(8,128)(2,1)}, u32[]{:S(2)}, u32[]{:S(2)}) collective-permute-start(bf16[4,192,192]{1,2,0:T(8,128)(2,1)} %get-tuple-element.22), channel_id=1, source_target_pairs={{0,7},{1,0},{2,1},{3,2},{4,3},{5,4},{6,5},{7,6},{8,15},{9,8},{10,9... | collective-permute-start | bytes 884744 | tf_op jit(solution)/shard_map/ppermute | solution.py:43
  137.4 7.2 %collective-permute-done.9 = bf16[4,192,192]{1,2,0:T(8,128)(2,1)} collective-permute-done((bf16[4,192,192]{1,2,0:T(8,128)(2,1)}, bf16[4,192,192]{1,2,0:T(8,128)(2,1)}, u32[]{:S(2)}, u32[]{:S(2)}) %collective-permute-start.9) | collective-permute-done | bytes 294944 | tf_op jit(solution)/shard_map/ppermute | solution.py:43
  148.7 10.7 %collective-permute-done.10 = bf16[4,192,192]{1,2,0:T(8,128)(2,1)} collective-permute-done((bf16[4,192,192]{1,2,0:T(8,128)(2,1)}, bf16[4,192,192]{1,2,0:T(8,128)(2,1)}, u32[]{:S(2)}, u32[]{:S(2)}) %collective-permute-start.10) | collective-permute-done | bytes 294944 | tf_op jit(solution)/shard_map/ppermute | solution.py:43
  163.2 4.6 %collective-permute-start.14 = (bf16[4,192,192]{1,2,0:T(8,128)(2,1)S(1)}, bf16[4,192,192]{1,2,0:T(8,128)(2,1)S(1)}, u32[]{:S(2)}, u32[]{:S(2)}) collective-permute-start(bf16[4,192,192]{1,2,0:T(8,128)(2,1)S(1)} %get-tuple-element.20), channel_id=1, source_target_pairs={{0,7},{1,0},{2,1},{3,2},{4,3},{5,4},{6,5},{7,6},{8,15},{9,8},{10,9... | collective-permute-start | bytes 884744 | tf_op jit(solution)/shard_map/ppermute | solution.py:43
  168.9 3.9 %collective-permute-done.11 = bf16[4,192,192]{1,2,0:T(8,128)(2,1)S(1)} collective-permute-done((bf16[4,192,192]{1,2,0:T(8,128)(2,1)S(1)}, bf16[4,192,192]{1,2,0:T(8,128)(2,1)S(1)}, u32[]{:S(2)}, u32[]{:S(2)}) %collective-permute-start.11) | collective-permute-done | bytes 294944 | tf_op jit(solution)/shard_map/ppermute | solution.py:43
  177.3 5.3 %collective-permute-start.15 = (bf16[4,192,192]{1,2,0:T(8,128)(2,1)S(1)}, bf16[4,192,192]{1,2,0:T(8,128)(2,1)S(1)}, u32[]{:S(2)}, u32[]{:S(2)}) collective-permute-start(bf16[4,192,192]{1,2,0:T(8,128)(2,1)S(1)} %get-tuple-element.18), channel_id=1, source_target_pairs={{0,7},{1,0},{2,1},{3,2},{4,3},{5,4},{6,5},{7,6},{8,15},{9,8},{10,9... | collective-permute-start | bytes 884744 | tf_op jit(solution)/shard_map/ppermute | solution.py:43
  182.6 4.0 %fusion = bf16[192,6144]{1,0:T(8,128)(2,1)} fusion(f32[192,6144]{1,0:T(8,128)S(1)} %fusion.62, bf16[6144,192]{0,1:T(8,128)(2,1)} %collective-permute-done.7, pred[]{:T(512)S(6)} %eq.39, bf16[192,128]{1,0:T(8,128)(2,1)S(1)} %convolution_convert_fusion.1, bf16[192,128]{1,0:T(8,128)(2,1)S(1)} %convolution_convert_fusion.2, ...), kind=kOutput, calls=%fused_computation.3 | convolution fusion | flops 455675904 | bytes 9584641 | tf_op jit(solution)/shard_map/dot_general | solution.py:16
  191.3 5.1 %collective-permute-start.18 = (bf16[192,192]{0,1:T(8,128)(2,1)S(1)}, bf16[192,192]{0,1:T(8,128)(2,1)S(1)}, u32[]{:S(2)}, u32[]{:S(2)}) collective-permute-start(bf16[192,192]{0,1:T(8,128)(2,1)S(1)} %get-tuple-element.27), channel_id=1, source_target_pairs={{0,24},{8,0},{16,8},{24,16},{1,25},{9,1},{17,9},{25,17},{2,26},{10... | collective-permute-start | bytes 221192 | tf_op jit(solution)/shard_map/ppermute | solution.py:43
  198.9 5.0 %collective-permute-done.17 = bf16[192,192]{0,1:T(8,128)(2,1)S(1)} collective-permute-done((bf16[192,192]{0,1:T(8,128)(2,1)S(1)}, bf16[192,192]{0,1:T(8,128)(2,1)S(1)}, u32[]{:S(2)}, u32[]{:S(2)}) %collective-permute-start.17) | collective-permute-done | bytes 73760 | tf_op jit(solution)/shard_map/ppermute | solution.py:43
  204.1 11.5 %all-gather.1 = f32[768,192]{1,0:T(8,128)S(1)} all-gather(f32[192,192]{1,0:T(8,128)S(1)} %copy.39), channel_id=3, replica_groups=mesh['dp'=4,'seq'=4,'fh'=4,'fz'=8] {'seq'}, dimensions={0}, use_global_device_ids=true | all-gather | bytes 737280 | tf_op jit(solution)/shard_map/all_gather | solution.py:180
  215.6 16.8 %all_gather.24 = f32[4,192,192]{2,1,0:T(8,128)S(1)} all-gather(f32[1,192,192]{2,1,0:T(8,128)S(1)} %fusion.38), channel_id=1, replica_groups=mesh['dp'=4,'seq'=4,'fh'=4,'fz'=8] {'dp'}, dimensions={0}, use_global_device_ids=true | all-gather | bytes 737280 | tf_op jit(solution)/shard_map/all_gather | solution.py:184
  (82 shorter events, 62.6 us)
Async XLA Ops:
  18.5 20.9 %collective-permute-start = (bf16[4,192,192]{2,1,0:T(8,128)(2,1)}, bf16[4,192,192]{2,1,0:T(8,128)(2,1)}, u32[]{:S(2)}, u32[]{:S(2)}) collective-permute-start(bf16[4,192,192]{2,1,0:T(8,128)(2,1)} %bitcast.1), channel_id=1, source_target_pairs={{0,1},{1,2},{2,3},{3,4},{4,5},{5,6},{6,7},{7,0},{8,9},{9,10},{10,1... | collective-permute-start | bytes 884744 | tf_op jit(solution)/shard_map/ppermute | solution.py:43
  21.8 20.5 %collective-permute-start.1 = (bf16[4,192,192]{2,1,0:T(8,128)(2,1)}, bf16[4,192,192]{2,1,0:T(8,128)(2,1)}, u32[]{:S(2)}, u32[]{:S(2)}) collective-permute-start(bf16[4,192,192]{2,1,0:T(8,128)(2,1)} %bitcast.1), channel_id=1, source_target_pairs={{0,7},{1,0},{2,1},{3,2},{4,3},{5,4},{6,5},{7,6},{8,15},{9,8},{10,9... | collective-permute-start | bytes 884744 | tf_op jit(solution)/shard_map/ppermute | solution.py:43
  39.3 9.9 %collective-permute-start.2 = (bf16[4,192,192]{2,1,0:T(8,128)(2,1)}, bf16[4,192,192]{2,1,0:T(8,128)(2,1)S(1)}, u32[]{:S(2)}, u32[]{:S(2)}) collective-permute-start(bf16[4,192,192]{2,1,0:T(8,128)(2,1)} %collective-permute-done), channel_id=1, source_target_pairs={{0,1},{1,2},{2,3},{3,4},{4,5},{5,6},{6,7},{7,0},{8,9},{9,10},{10,1... | collective-permute-start | bytes 884744 | tf_op jit(solution)/shard_map/ppermute | solution.py:43
  42.3 9.6 %collective-permute-start.3 = (bf16[4,192,192]{2,1,0:T(8,128)(2,1)}, bf16[4,192,192]{2,1,0:T(8,128)(2,1)S(1)}, u32[]{:S(2)}, u32[]{:S(2)}) collective-permute-start(bf16[4,192,192]{2,1,0:T(8,128)(2,1)} %collective-permute-done.1), channel_id=1, source_target_pairs={{0,7},{1,0},{2,1},{3,2},{4,3},{5,4},{6,5},{7,6},{8,15},{9,8},{10,9... | collective-permute-start | bytes 884744 | tf_op jit(solution)/shard_map/ppermute | solution.py:43
  49.3 9.7 %collective-permute-start.4 = (bf16[4,192,192]{2,1,0:T(8,128)(2,1)S(1)}, bf16[4,192,192]{2,1,0:T(8,128)(2,1)S(1)}, u32[]{:S(2)}, u32[]{:S(2)}) collective-permute-start(bf16[4,192,192]{2,1,0:T(8,128)(2,1)S(1)} %collective-permute-done.2), channel_id=1, source_target_pairs={{0,1},{1,2},{2,3},{3,4},{4,5},{5,6},{6,7},{7,0},{8,9},{9,10},{10,1... | collective-permute-start | bytes 884744 | tf_op jit(solution)/shard_map/ppermute | solution.py:43
  51.9 9.6 %collective-permute-start.5 = (bf16[4,192,192]{2,1,0:T(8,128)(2,1)S(1)}, bf16[4,192,192]{2,1,0:T(8,128)(2,1)S(1)}, u32[]{:S(2)}, u32[]{:S(2)}) collective-permute-start(bf16[4,192,192]{2,1,0:T(8,128)(2,1)S(1)} %collective-permute-done.3), channel_id=1, source_target_pairs={{0,7},{1,0},{2,1},{3,2},{4,3},{5,4},{6,5},{7,6},{8,15},{9,8},{10,9... | collective-permute-start | bytes 884744 | tf_op jit(solution)/shard_map/ppermute | solution.py:43
  59.0 10.2 %collective-permute-start.6 = (bf16[4,192,192]{2,1,0:T(8,128)(2,1)S(1)}, bf16[4,192,192]{2,1,0:T(8,128)(2,1)S(1)}, u32[]{:S(2)}, u32[]{:S(2)}) collective-permute-start(bf16[4,192,192]{2,1,0:T(8,128)(2,1)S(1)} %collective-permute-done.4), channel_id=1, source_target_pairs={{0,1},{1,2},{2,3},{3,4},{4,5},{5,6},{6,7},{7,0},{8,9},{9,10},{10,1... | collective-permute-start | bytes 884744 | tf_op jit(solution)/shard_map/ppermute | solution.py:43
  73.6 12.3 %copy-start.6 = (s32[1,192]{1,0:T(1,128)S(1)}, s32[1,192]{1,0:T(1,128)}, u32[]{:S(2)}) copy-start(s32[1,192]{1,0:T(1,128)} %param.6) | copy-start | bytes 2308
  76.2 14.2 %collective-permute-start.7 = (bf16[6144,192]{0,1:T(8,128)(2,1)}, bf16[6144,192]{0,1:T(8,128)(2,1)}, u32[]{:S(2)}, u32[]{:S(2)}) collective-permute-start(bf16[6144,192]{0,1:T(8,128)(2,1)} %copy.31), channel_id=1, source_target_pairs={{0,128},{128,0},{256,384},{384,256},{1,129},{129,1},{257,385},{385... | collective-permute-start | bytes 7077896 | tf_op jit(solution)/shard_map/ppermute | solution.py:23
  85.9 4.4 %copy-start.3 = (bf16[1,192,6144]{2,1,0:T(8,128)(2,1)S(1)}, bf16[1,192,6144]{2,1,0:T(8,128)(2,1)}, u32[]{:S(2)}) copy-start(bf16[1,192,6144]{2,1,0:T(8,128)(2,1)} %param.5) | copy-start | bytes 7077892
  88.5 4.5 %copy-start.5 = (bf16[1,192,128]{2,1,0:T(8,128)(2,1)S(1)}, bf16[1,192,128]{2,1,0:T(8,128)(2,1)}, u32[]{:S(2)}) copy-start(bf16[1,192,128]{2,1,0:T(8,128)(2,1)} %param.8) | copy-start | bytes 147460
  108.6 1.9 copy-start.1
  114.6 9.6 %collective-permute-start.8 = (bf16[8,4,192,192]{2,3,0,1:T(8,128)(2,1)}, bf16[8,4,192,192]{2,3,0,1:T(8,128)(2,1)}, u32[]{:S(2)}, u32[]{:S(2)}) collective-permute-start(bf16[8,4,192,192]{2,3,0,1:T(8,128)(2,1)} %convert_bitcast_fusion), channel_id=1, source_target_pairs={{0,128},{128,0},{256,384},{384,256},{1,129},{129,1},{257,385},{385... | collective-permute-start | bytes 7077896 | tf_op jit(solution)/shard_map/ppermute | solution.py:23
  127.2 2.7 %copy-start.2 = (f32[8,4,192,192]{2,3,0,1:T(8,128)}, f32[8,4,192,192]{2,3,0,1:T(8,128)S(1)}, u32[]{:S(2)}) copy-start(f32[8,4,192,192]{2,3,0,1:T(8,128)S(1)} %convert_add_fusion) | copy-start | bytes 14155780
  130.9 13.7 %collective-permute-start.9 = (bf16[4,192,192]{1,2,0:T(8,128)(2,1)}, bf16[4,192,192]{1,2,0:T(8,128)(2,1)}, u32[]{:S(2)}, u32[]{:S(2)}) collective-permute-start(bf16[4,192,192]{1,2,0:T(8,128)(2,1)} %get-tuple-element.23), channel_id=1, source_target_pairs={{0,1},{1,2},{2,3},{3,4},{4,5},{5,6},{6,7},{7,0},{8,9},{9,10},{10,1... | collective-permute-start | bytes 884744 | tf_op jit(solution)/shard_map/ppermute | solution.py:43
  132.8 15.9 %collective-permute-start.13 = (bf16[4,192,192]{1,2,0:T(8,128)(2,1)}, bf16[4,192,192]{1,2,0:T(8,128)(2,1)}, u32[]{:S(2)}, u32[]{:S(2)}) collective-permute-start(bf16[4,192,192]{1,2,0:T(8,128)(2,1)} %get-tuple-element.22), channel_id=1, source_target_pairs={{0,7},{1,0},{2,1},{3,2},{4,3},{5,4},{6,5},{7,6},{8,15},{9,8},{10,9... | collective-permute-start | bytes 884744 | tf_op jit(solution)/shard_map/ppermute | solution.py:43
  146.7 12.8 %collective-permute-start.10 = (bf16[4,192,192]{1,2,0:T(8,128)(2,1)}, bf16[4,192,192]{1,2,0:T(8,128)(2,1)}, u32[]{:S(2)}, u32[]{:S(2)}) collective-permute-start(bf16[4,192,192]{1,2,0:T(8,128)(2,1)} %fusion.29), channel_id=1, source_target_pairs={{0,1},{1,2},{2,3},{3,4},{4,5},{5,6},{6,7},{7,0},{8,9},{9,10},{10,1... | collective-permute-start | bytes 884744 | tf_op jit(solution)/shard_map/ppermute | solution.py:43
  161.3 11.6 %collective-permute-start.11 = (bf16[4,192,192]{1,2,0:T(8,128)(2,1)S(1)}, bf16[4,192,192]{1,2,0:T(8,128)(2,1)S(1)}, u32[]{:S(2)}, u32[]{:S(2)}) collective-permute-start(bf16[4,192,192]{1,2,0:T(8,128)(2,1)S(1)} %get-tuple-element.21), channel_id=1, source_target_pairs={{0,1},{1,2},{2,3},{3,4},{4,5},{5,6},{6,7},{7,0},{8,9},{9,10},{10,1... | collective-permute-start | bytes 884744 | tf_op jit(solution)/shard_map/ppermute | solution.py:43
  163.2 10.6 %collective-permute-start.14 = (bf16[4,192,192]{1,2,0:T(8,128)(2,1)S(1)}, bf16[4,192,192]{1,2,0:T(8,128)(2,1)S(1)}, u32[]{:S(2)}, u32[]{:S(2)}) collective-permute-start(bf16[4,192,192]{1,2,0:T(8,128)(2,1)S(1)} %get-tuple-element.20), channel_id=1, source_target_pairs={{0,7},{1,0},{2,1},{3,2},{4,3},{5,4},{6,5},{7,6},{8,15},{9,8},{10,9... | collective-permute-start | bytes 884744 | tf_op jit(solution)/shard_map/ppermute | solution.py:43
  175.4 11.4 %collective-permute-start.12 = (bf16[4,192,192]{1,2,0:T(8,128)(2,1)S(1)}, bf16[4,192,192]{1,2,0:T(8,128)(2,1)S(1)}, u32[]{:S(2)}, u32[]{:S(2)}) collective-permute-start(bf16[4,192,192]{1,2,0:T(8,128)(2,1)S(1)} %get-tuple-element.19), channel_id=1, source_target_pairs={{0,1},{1,2},{2,3},{3,4},{4,5},{5,6},{6,7},{7,0},{8,9},{9,10},{10,1... | collective-permute-start | bytes 884744 | tf_op jit(solution)/shard_map/ppermute | solution.py:43
  177.3 10.4 %collective-permute-start.15 = (bf16[4,192,192]{1,2,0:T(8,128)(2,1)S(1)}, bf16[4,192,192]{1,2,0:T(8,128)(2,1)S(1)}, u32[]{:S(2)}, u32[]{:S(2)}) collective-permute-start(bf16[4,192,192]{1,2,0:T(8,128)(2,1)S(1)} %get-tuple-element.18), channel_id=1, source_target_pairs={{0,7},{1,0},{2,1},{3,2},{4,3},{5,4},{6,5},{7,6},{8,15},{9,8},{10,9... | collective-permute-start | bytes 884744 | tf_op jit(solution)/shard_map/ppermute | solution.py:43
  189.0 7.5 %collective-permute-start.16 = (bf16[192,192]{0,1:T(8,128)(2,1)S(1)}, bf16[192,192]{0,1:T(8,128)(2,1)S(1)}, u32[]{:S(2)}, u32[]{:S(2)}) collective-permute-start(bf16[192,192]{0,1:T(8,128)(2,1)S(1)} %get-tuple-element.26), channel_id=1, source_target_pairs={{0,8},{8,16},{16,24},{24,0},{1,9},{9,17},{17,25},{25,1},{2,10},{10... | collective-permute-start | bytes 221192 | tf_op jit(solution)/shard_map/ppermute | solution.py:43
  191.3 7.6 %collective-permute-start.18 = (bf16[192,192]{0,1:T(8,128)(2,1)S(1)}, bf16[192,192]{0,1:T(8,128)(2,1)S(1)}, u32[]{:S(2)}, u32[]{:S(2)}) collective-permute-start(bf16[192,192]{0,1:T(8,128)(2,1)S(1)} %get-tuple-element.27), channel_id=1, source_target_pairs={{0,24},{8,0},{16,8},{24,16},{1,25},{9,1},{17,9},{25,17},{2,26},{10... | collective-permute-start | bytes 221192 | tf_op jit(solution)/shard_map/ppermute | solution.py:43
  196.5 7.5 %collective-permute-start.17 = (bf16[192,192]{0,1:T(8,128)(2,1)S(1)}, bf16[192,192]{0,1:T(8,128)(2,1)S(1)}, u32[]{:S(2)}, u32[]{:S(2)}) collective-permute-start(bf16[192,192]{0,1:T(8,128)(2,1)S(1)} %fusion.39), channel_id=1, source_target_pairs={{0,8},{8,16},{16,24},{24,0},{1,9},{9,17},{17,25},{25,1},{2,10},{10... | collective-permute-start | bytes 221192 | tf_op jit(solution)/shard_map/ppermute | solution.py:43
  (2 other events, 2.6 us)

commit v11 on v9

--- a/solution.py
+++ b/solution.py
@@ -43,21 +43,31 @@
         return lax.ppermute(x, self.axis, perm=pairs)
 
 
-def ring_gather(x, ring, beside=None):
+def ring_gather(x, ring, beside=None, late=None):
     n = ring.size
     got, slot = [x], {0: 0}
     cw, ccw = x, x
+    last_cw = n - 1 if (n - 1) % 2 == 1 else n - 2
+    last_ccw = n - 1 if (n - 1) % 2 == 0 else n - 2
     for t in range(1, n):
         if t % 2 == 1:
             cw = ring.shift(cw, 1)
             if t == 1 and beside is not None:
                 cw, beside = lax.optimization_barrier((cw, beside))
+            if t == last_cw and late is not None:
+                cw, late = lax.optimization_barrier((cw, late))
             slot[(n - (t + 1) // 2) % n] = len(got)
             got.append(cw)
         else:
             ccw = ring.shift(ccw, -1)
+            if t == last_ccw and late is not None:
+                value, make = late
+                ccw, value = lax.optimization_barrier((ccw, value))
+                late = make(value)
             slot[t // 2] = len(got)
             got.append(ccw)
+    if late is not None:
+        return jnp.stack(got), [slot[k] for k in range(n)], late
     return jnp.stack(got), [slot[k] for k in range(n)], beside
 
 
@@ -110,8 +120,8 @@
 
     w_mine = lax.dynamic_slice_in_dim(qkv_weight, core * half, half, axis=1)
     stack_y = lax.all_gather(w_mine, "fh", axis=0, tiled=False)
-    blocked = features.reshape(features.shape[0], outer_fsdp, inner_fsdp, rows_w)
-    stack_zy, slot_z, blocked = ring_gather(stack_y, ring_z, beside=blocked)
+    relayout = lambda f: f.reshape(f.shape[0], outer_fsdp, inner_fsdp, rows_w)
+    stack_zy, slot_z, blocked = ring_gather(stack_y, ring_z, late=(features, relayout))
     flat = stack_zy.reshape(-1, rows_w, half)
     me_y, me_z = ring_y.position(), ring_z.position()
     absolute = jnp.arange(n_fsdp, dtype=jnp.int32)

time: 228 us -> 224 us (0.982)
  waiting for transfers between devices: 45 us -> 39.3 us
  local copies, waits for them, and re-layouts: 20.4 us -> 23.1 us
    ppermute x17, waiting for transfers between devices: 42.1 us -> 36.4 us  [shift(): return lax.ppermute(x, self.axis, perm=pairs)]
    another operation x2 -> x1, local copies, waits for them, and re-layouts: 6.47 us -> 1.79 us  [ring_gather(): return (jnp.stack(got), [slot[k] for k in range(n)], late)]
    reshape x0 -> x1, local copies, waits for them, and re-layouts: none -> 4.52 us  [shards(): relayout = lambda f: f.reshape(f.shape[0], outer_fsdp, inner_fsdp, rows_w)]
    unnamed x23, local copies, waits for them, and re-layouts: 6.83 us -> 9.47 us
  transfers between devices with their start and end apart: 19 -> 19, of which waited for: 16 -> 16; matrix products, arithmetic and copies ran while one was open for 9% -> 11% of each run, Pallas kernels for 0% -> 0%
where the time goes in v11:
time: 224 us; the launch traced here: 223 us
  starting transfers between devices  73.1 us (33%)
  blocking collectives  56.4 us (25%)
  waiting for transfers between devices  39.3 us (18%)
  local copies, waits for them, and re-layouts  23.1 us (10%)
  matrix products  19.5 us (9%)
  other arithmetic  9.77 us (4%)
    ppermute x17, starting transfers between devices, shift(): return lax.ppermute(x, self.axis, perm=pairs)  58.5 us
    ppermute x17, waiting for transfers between devices, shift(): return lax.ppermute(x, self.axis, perm=pairs)  36.4 us
    all_gather x1, blocking collectives, shards(): stack_y = lax.all_gather(w_mine, 'fh', axis=0, tiled=False)  16.3 us
    all_gather x1, blocking collectives, shards(): by_dp = lax.all_gather(over_seq, 'dp', axis=0, tiled=False)  16 us
    ppermute x2, starting transfers between devices, dp_partner(): return lax.ppermute(x, 'dp', perm=pairs)  14.6 us
    all_gather x1, blocking collectives, shards(): packed_all = lax.all_gather(packed, 'seq', axis=0, tiled=True)  12.9 us
    all_gather x1, blocking collectives, shards(): by_seq = lax.all_gather(over_fsdp, 'seq', axis=0, tiled=False)  11.2 us
    unnamed x23, local copies, waits for them, and re-layouts  9.47 us
  transfers between devices with their start and end apart: 19, of which 16 were waited for; matrix products, arithmetic and copies ran while one was open for 11% of the time, Pallas kernels for 0%

profile of v11, /device:TPU:1, one launch (start us, length us, event | category | flops | bytes accessed | tf_op | source)
XLA Modules:
  0.0 222.6 jit_solution(9267431359710863556)
XLA Ops:
  1.6 16.3 %all-gather = bf16[768,192]{1,0:T(8,128)(2,1)S(1)} all-gather(bf16[192,192]{1,0:T(8,128)(2,1)S(1)} %constant_dynamic-slice_fusion), channel_id=2, replica_groups=mesh['dp'=4,'seq'=4,'fh'=4,'fz'=8] {'fh'}, dimensions={0}, use_global_device_ids=true | all-gather | bytes 368640 | tf_op jit(solution)/shard_map/all_gather | solution.py:122
  17.9 3.2 %collective-permute-start = (bf16[4,192,192]{2,1,0:T(8,128)(2,1)S(1)}, bf16[4,192,192]{2,1,0:T(8,128)(2,1)}, u32[]{:S(2)}, u32[]{:S(2)}) collective-permute-start(bf16[4,192,192]{2,1,0:T(8,128)(2,1)S(1)} %bitcast.108), channel_id=1, source_target_pairs={{0,1},{1,2},{2,3},{3,4},{4,5},{5,6},{6,7},{7,0},{8,9},{9,10},{10,1... | collective-permute-start | bytes 884744 | tf_op jit(solution)/shard_map/ppermute | solution.py:43
  21.2 8.6 %collective-permute-start.1 = (bf16[4,192,192]{2,1,0:T(8,128)(2,1)S(1)}, bf16[4,192,192]{2,1,0:T(8,128)(2,1)S(1)}, u32[]{:S(2)}, u32[]{:S(2)}) collective-permute-start(bf16[4,192,192]{2,1,0:T(8,128)(2,1)S(1)} %bitcast.109), channel_id=1, source_target_pairs={{0,7},{1,0},{2,1},{3,2},{4,3},{5,4},{6,5},{7,6},{8,15},{9,8},{10,9... | collective-permute-start | bytes 884744 | tf_op jit(solution)/shard_map/ppermute | solution.py:43
  36.8 4.6 %collective-permute-start.3 = (bf16[4,192,192]{2,1,0:T(8,128)(2,1)S(1)}, bf16[4,192,192]{2,1,0:T(8,128)(2,1)S(1)}, u32[]{:S(2)}, u32[]{:S(2)}) collective-permute-start(bf16[4,192,192]{2,1,0:T(8,128)(2,1)S(1)} %collective-permute-done.1), channel_id=1, source_target_pairs={{0,7},{1,0},{2,1},{3,2},{4,3},{5,4},{6,5},{7,6},{8,15},{9,8},{10,9... | collective-permute-start | bytes 884744 | tf_op jit(solution)/shard_map/ppermute | solution.py:43
  46.0 5.0 %collective-permute-start.5 = (bf16[4,192,192]{2,1,0:T(8,128)(2,1)S(1)}, bf16[4,192,192]{2,1,0:T(8,128)(2,1)S(1)}, u32[]{:S(2)}, u32[]{:S(2)}) collective-permute-start(bf16[4,192,192]{2,1,0:T(8,128)(2,1)S(1)} %collective-permute-done.3), channel_id=1, source_target_pairs={{0,7},{1,0},{2,1},{3,2},{4,3},{5,4},{6,5},{7,6},{8,15},{9,8},{10,9... | collective-permute-start | bytes 884744 | tf_op jit(solution)/shard_map/ppermute | solution.py:43
  56.8 4.5 %reshape.141 = bf16[192,4,8,192]{3,2,1,0:T(8,128)(2,1)} reshape(bf16[192,6144]{1,0:T(8,128)(2,1)S(1)} %bitcast.105) | data formatting | bytes 4718592 | tf_op jit(solution)/shard_map/reshape | solution.py:123
  71.1 10.5 %collective-permute-start.7 = (bf16[6144,192]{0,1:T(8,128)(2,1)}, bf16[6144,192]{0,1:T(8,128)(2,1)}, u32[]{:S(2)}, u32[]{:S(2)}) collective-permute-start(bf16[6144,192]{0,1:T(8,128)(2,1)} %copy.31), channel_id=1, source_target_pairs={{0,128},{128,0},{256,384},{384,256},{1,129},{129,1},{257,385},{385... | collective-permute-start | bytes 7077896 | tf_op jit(solution)/shard_map/ppermute | solution.py:23
  88.8 12.9 %all_gather.21 = bf16[768,640]{1,0:T(8,128)(2,1)S(1)} all-gather(bf16[192,640]{1,0:T(8,128)(2,1)S(1)} %pad_maximum_fusion.1), channel_id=1, replica_groups=mesh['dp'=4,'seq'=4,'fh'=4,'fz'=8] {'seq'}, dimensions={0}, use_global_device_ids=true | all-gather | bytes 1228800 | tf_op jit(solution)/shard_map/all_gather | solution.py:146
  106.2 4.1 %convert_bitcast_fusion = bf16[8,4,192,192]{2,3,0,1:T(8,128)(2,1)} fusion(bf16[192,4,8,192]{3,2,1,0:T(8,128)(2,1)S(1)} %copy-done.1, pred[]{:T(512)S(6)} %eq.39, bf16[192,128]{1,0:T(8,128)(2,1)S(1)} %convolution_convert_fusion.1, bf16[192,128]{1,0:T(8,128)(2,1)S(1)} %convolution_convert_fusion.2, bf16[192,128]{1,0:T(8,128)(2,1)S(1)} %convolution_convert_fusion), kind=kOutput, calls=%fused_computation.8 | convolution fusion | flops 454496256 | bytes 4866049 | tf_op jit(solution)/shard_map/pyzd,pc->zydc/dot_general | solution.py:181
  110.3 4.2 %collective-permute-start.8 = (bf16[8,4,192,192]{2,3,0,1:T(8,128)(2,1)}, bf16[8,4,192,192]{2,3,0,1:T(8,128)(2,1)}, u32[]{:S(2)}, u32[]{:S(2)}) collective-permute-start(bf16[8,4,192,192]{2,3,0,1:T(8,128)(2,1)} %convert_bitcast_fusion), channel_id=1, source_target_pairs={{0,128},{128,0},{256,384},{384,256},{1,129},{129,1},{257,385},{385... | collective-permute-start | bytes 7077896 | tf_op jit(solution)/shard_map/ppermute | solution.py:23
  119.9 3.0 %convert_add_fusion = f32[8,4,192,192]{2,3,0,1:T(8,128)S(1)} fusion(f32[8,4,192,192]{2,3,0,1:T(8,128)S(1)} %fusion.5, bf16[8,4,192,192]{2,3,0,1:T(8,128)(2,1)} %collective-permute-done.8), kind=kLoop, calls=%fused_computation.4 | loop fusion | flops 2359296 | bytes 11796480 | tf_op jit(solution)/shard_map/add | solution.py:185
  124.9 4.0 %fusion = bf16[192,6144]{1,0:T(8,128)(2,1)} fusion(f32[192,6144]{1,0:T(8,128)S(1)} %fusion.54, bf16[6144,192]{0,1:T(8,128)(2,1)} %collective-permute-done.7, pred[]{:T(512)S(6)} %eq.39, bf16[192,128]{1,0:T(8,128)(2,1)S(1)} %convolution_convert_fusion.1, bf16[192,128]{1,0:T(8,128)(2,1)S(1)} %convolution_convert_fusion.2, ...), kind=kOutput, calls=%fused_computation.3 | convolution fusion | flops 455675904 | bytes 9584641 | tf_op jit(solution)/shard_map/dot_general | solution.py:16
  128.9 4.5 %collective-permute-start.13 = (bf16[4,192,192]{1,2,0:T(8,128)(2,1)S(1)}, bf16[4,192,192]{1,2,0:T(8,128)(2,1)S(1)}, u32[]{:S(2)}, u32[]{:S(2)}) collective-permute-start(bf16[4,192,192]{1,2,0:T(8,128)(2,1)S(1)} %get-tuple-element.26), channel_id=1, source_target_pairs={{0,7},{1,0},{2,1},{3,2},{4,3},{5,4},{6,5},{7,6},{8,15},{9,8},{10,9... | collective-permute-start | bytes 884744 | tf_op jit(solution)/shard_map/ppermute | solution.py:43
  133.4 3.0 %collective-permute-done.9 = bf16[4,192,192]{1,2,0:T(8,128)(2,1)S(1)} collective-permute-done((bf16[4,192,192]{1,2,0:T(8,128)(2,1)S(1)}, bf16[4,192,192]{1,2,0:T(8,128)(2,1)S(1)}, u32[]{:S(2)}, u32[]{:S(2)}) %collective-permute-start.9) | collective-permute-done | bytes 294944 | tf_op jit(solution)/shard_map/ppermute | solution.py:43
  138.5 2.7 %collective-permute-done.13 = bf16[4,192,192]{1,2,0:T(8,128)(2,1)S(1)} collective-permute-done((bf16[4,192,192]{1,2,0:T(8,128)(2,1)S(1)}, bf16[4,192,192]{1,2,0:T(8,128)(2,1)S(1)}, u32[]{:S(2)}, u32[]{:S(2)}) %collective-permute-start.13) | collective-permute-done | bytes 294944 | tf_op jit(solution)/shard_map/ppermute | solution.py:43
  141.2 7.9 %collective-permute-done.10 = bf16[4,192,192]{1,2,0:T(8,128)(2,1)S(1)} collective-permute-done((bf16[4,192,192]{1,2,0:T(8,128)(2,1)S(1)}, bf16[4,192,192]{1,2,0:T(8,128)(2,1)S(1)}, u32[]{:S(2)}, u32[]{:S(2)}) %collective-permute-start.10) | collective-permute-done | bytes 294944 | tf_op jit(solution)/shard_map/ppermute | solution.py:43
  152.5 4.6 %collective-permute-start.14 = (bf16[4,192,192]{1,2,0:T(8,128)(2,1)S(1)}, bf16[4,192,192]{1,2,0:T(8,128)(2,1)S(1)}, u32[]{:S(2)}, u32[]{:S(2)}) collective-permute-start(bf16[4,192,192]{1,2,0:T(8,128)(2,1)S(1)} %get-tuple-element.25), channel_id=1, source_target_pairs={{0,7},{1,0},{2,1},{3,2},{4,3},{5,4},{6,5},{7,6},{8,15},{9,8},{10,9... | collective-permute-start | bytes 884744 | tf_op jit(solution)/shard_map/ppermute | solution.py:43
  157.2 5.0 %collective-permute-done.11 = bf16[4,192,192]{1,2,0:T(8,128)(2,1)S(1)} collective-permute-done((bf16[4,192,192]{1,2,0:T(8,128)(2,1)S(1)}, bf16[4,192,192]{1,2,0:T(8,128)(2,1)S(1)}, u32[]{:S(2)}, u32[]{:S(2)}) %collective-permute-start.11) | collective-permute-done | bytes 294944 | tf_op jit(solution)/shard_map/ppermute | solution.py:43
  166.6 5.3 %collective-permute-start.15 = (bf16[4,192,192]{1,2,0:T(8,128)(2,1)S(1)}, bf16[4,192,192]{1,2,0:T(8,128)(2,1)S(1)}, u32[]{:S(2)}, u32[]{:S(2)}) collective-permute-start(bf16[4,192,192]{1,2,0:T(8,128)(2,1)S(1)} %get-tuple-element.23), channel_id=1, source_target_pairs={{0,7},{1,0},{2,1},{3,2},{4,3},{5,4},{6,5},{7,6},{8,15},{9,8},{10,9... | collective-permute-start | bytes 884744 | tf_op jit(solution)/shard_map/ppermute | solution.py:43
  172.0 4.1 %collective-permute-done.12 = bf16[4,192,192]{1,2,0:T(8,128)(2,1)S(1)} collective-permute-done((bf16[4,192,192]{1,2,0:T(8,128)(2,1)S(1)}, bf16[4,192,192]{1,2,0:T(8,128)(2,1)S(1)}, u32[]{:S(2)}, u32[]{:S(2)}) %collective-permute-start.12) | collective-permute-done | bytes 294944 | tf_op jit(solution)/shard_map/ppermute | solution.py:43
  180.5 5.5 %collective-permute-start.18 = (bf16[192,192]{0,1:T(8,128)(2,1)S(1)}, bf16[192,192]{0,1:T(8,128)(2,1)S(1)}, u32[]{:S(2)}, u32[]{:S(2)}) collective-permute-start(bf16[192,192]{0,1:T(8,128)(2,1)S(1)} %get-tuple-element.31), channel_id=1, source_target_pairs={{0,24},{8,0},{16,8},{24,16},{1,25},{9,1},{17,9},{25,17},{2,26},{10... | collective-permute-start | bytes 221192 | tf_op jit(solution)/shard_map/ppermute | solution.py:43
  188.8 5.5 %collective-permute-done.17 = bf16[192,192]{0,1:T(8,128)(2,1)S(1)} collective-permute-done((bf16[192,192]{0,1:T(8,128)(2,1)S(1)}, bf16[192,192]{0,1:T(8,128)(2,1)S(1)}, u32[]{:S(2)}, u32[]{:S(2)}) %collective-permute-start.17) | collective-permute-done | bytes 73760 | tf_op jit(solution)/shard_map/ppermute | solution.py:43
  194.4 11.2 %all-gather.1 = f32[768,192]{1,0:T(8,128)S(1)} all-gather(f32[192,192]{1,0:T(8,128)S(1)} %copy.39), channel_id=3, replica_groups=mesh['dp'=4,'seq'=4,'fh'=4,'fz'=8] {'seq'}, dimensions={0}, use_global_device_ids=true | all-gather | bytes 737280 | tf_op jit(solution)/shard_map/all_gather | solution.py:189
  205.7 16.0 %all_gather.24 = f32[4,192,192]{2,1,0:T(8,128)S(1)} all-gather(f32[1,192,192]{2,1,0:T(8,128)S(1)} %fusion.28), channel_id=1, replica_groups=mesh['dp'=4,'seq'=4,'fh'=4,'fz'=8] {'dp'}, dimensions={0}, use_global_device_ids=true | all-gather | bytes 737280 | tf_op jit(solution)/shard_map/all_gather | solution.py:193
  (84 shorter events, 65.1 us)
Async XLA Ops:
  17.9 15.2 %collective-permute-start = (bf16[4,192,192]{2,1,0:T(8,128)(2,1)S(1)}, bf16[4,192,192]{2,1,0:T(8,128)(2,1)}, u32[]{:S(2)}, u32[]{:S(2)}) collective-permute-start(bf16[4,192,192]{2,1,0:T(8,128)(2,1)S(1)} %bitcast.108), channel_id=1, source_target_pairs={{0,1},{1,2},{2,3},{3,4},{4,5},{5,6},{6,7},{7,0},{8,9},{9,10},{10,1... | collective-permute-start | bytes 884744 | tf_op jit(solution)/shard_map/ppermute | solution.py:43
  21.2 15.6 %collective-permute-start.1 = (bf16[4,192,192]{2,1,0:T(8,128)(2,1)S(1)}, bf16[4,192,192]{2,1,0:T(8,128)(2,1)S(1)}, u32[]{:S(2)}, u32[]{:S(2)}) collective-permute-start(bf16[4,192,192]{2,1,0:T(8,128)(2,1)S(1)} %bitcast.109), channel_id=1, source_target_pairs={{0,7},{1,0},{2,1},{3,2},{4,3},{5,4},{6,5},{7,6},{8,15},{9,8},{10,9... | collective-permute-start | bytes 884744 | tf_op jit(solution)/shard_map/ppermute | solution.py:43
  30.6 26.2 %copy-start.4 = (bf16[1,192,6144]{2,1,0:T(8,128)(2,1)S(1)}, bf16[1,192,6144]{2,1,0:T(8,128)(2,1)}, u32[]{:S(2)}) copy-start(bf16[1,192,6144]{2,1,0:T(8,128)(2,1)} %param.5) | copy-start | bytes 7077892
  33.1 9.9 %collective-permute-start.2 = (bf16[4,192,192]{2,1,0:T(8,128)(2,1)}, bf16[4,192,192]{2,1,0:T(8,128)(2,1)S(1)}, u32[]{:S(2)}, u32[]{:S(2)}) collective-permute-start(bf16[4,192,192]{2,1,0:T(8,128)(2,1)} %collective-permute-done), channel_id=1, source_target_pairs={{0,1},{1,2},{2,3},{3,4},{4,5},{5,6},{6,7},{7,0},{8,9},{9,10},{10,1... | collective-permute-start | bytes 884744 | tf_op jit(solution)/shard_map/ppermute | solution.py:43
  36.8 9.3 %collective-permute-start.3 = (bf16[4,192,192]{2,1,0:T(8,128)(2,1)S(1)}, bf16[4,192,192]{2,1,0:T(8,128)(2,1)S(1)}, u32[]{:S(2)}, u32[]{:S(2)}) collective-permute-start(bf16[4,192,192]{2,1,0:T(8,128)(2,1)S(1)} %collective-permute-done.1), channel_id=1, source_target_pairs={{0,7},{1,0},{2,1},{3,2},{4,3},{5,4},{6,5},{7,6},{8,15},{9,8},{10,9... | collective-permute-start | bytes 884744 | tf_op jit(solution)/shard_map/ppermute | solution.py:43
  43.0 10.0 %collective-permute-start.4 = (bf16[4,192,192]{2,1,0:T(8,128)(2,1)S(1)}, bf16[4,192,192]{2,1,0:T(8,128)(2,1)}, u32[]{:S(2)}, u32[]{:S(2)}) collective-permute-start(bf16[4,192,192]{2,1,0:T(8,128)(2,1)S(1)} %collective-permute-done.2), channel_id=1, source_target_pairs={{0,1},{1,2},{2,3},{3,4},{4,5},{5,6},{6,7},{7,0},{8,9},{9,10},{10,1... | collective-permute-start | bytes 884744 | tf_op jit(solution)/shard_map/ppermute | solution.py:43
  46.0 10.7 %collective-permute-start.5 = (bf16[4,192,192]{2,1,0:T(8,128)(2,1)S(1)}, bf16[4,192,192]{2,1,0:T(8,128)(2,1)S(1)}, u32[]{:S(2)}, u32[]{:S(2)}) collective-permute-start(bf16[4,192,192]{2,1,0:T(8,128)(2,1)S(1)} %collective-permute-done.3), channel_id=1, source_target_pairs={{0,7},{1,0},{2,1},{3,2},{4,3},{5,4},{6,5},{7,6},{8,15},{9,8},{10,9... | collective-permute-start | bytes 884744 | tf_op jit(solution)/shard_map/ppermute | solution.py:43
  53.0 11.0 %collective-permute-start.6 = (bf16[4,192,192]{2,1,0:T(8,128)(2,1)}, bf16[4,192,192]{2,1,0:T(8,128)(2,1)}, u32[]{:S(2)}, u32[]{:S(2)}) collective-permute-start(bf16[4,192,192]{2,1,0:T(8,128)(2,1)} %collective-permute-done.4), channel_id=1, source_target_pairs={{0,1},{1,2},{2,3},{3,4},{4,5},{5,6},{6,7},{7,0},{8,9},{9,10},{10,1... | collective-permute-start | bytes 884744 | tf_op jit(solution)/shard_map/ppermute | solution.py:43
  68.5 13.1 %copy-start.7 = (s32[1,192]{1,0:T(1,128)S(1)}, s32[1,192]{1,0:T(1,128)}, u32[]{:S(2)}) copy-start(s32[1,192]{1,0:T(1,128)} %param.6) | copy-start | bytes 2308
  71.1 14.9 %collective-permute-start.7 = (bf16[6144,192]{0,1:T(8,128)(2,1)}, bf16[6144,192]{0,1:T(8,128)(2,1)}, u32[]{:S(2)}, u32[]{:S(2)}) collective-permute-start(bf16[6144,192]{0,1:T(8,128)(2,1)} %copy.31), channel_id=1, source_target_pairs={{0,128},{128,0},{256,384},{384,256},{1,129},{129,1},{257,385},{385... | collective-permute-start | bytes 7077896 | tf_op jit(solution)/shard_map/ppermute | solution.py:23
  81.6 4.4 %copy-start.5 = (bf16[1,192,6144]{2,1,0:T(8,128)(2,1)S(1)}, bf16[1,192,6144]{2,1,0:T(8,128)(2,1)}, u32[]{:S(2)}) copy-start(bf16[1,192,6144]{2,1,0:T(8,128)(2,1)} %param.5) | copy-start | bytes 7077892
  84.2 4.5 %copy-start.6 = (bf16[1,192,128]{2,1,0:T(8,128)(2,1)S(1)}, bf16[1,192,128]{2,1,0:T(8,128)(2,1)}, u32[]{:S(2)}) copy-start(bf16[1,192,128]{2,1,0:T(8,128)(2,1)} %param.8) | copy-start | bytes 147460
  110.3 9.6 %collective-permute-start.8 = (bf16[8,4,192,192]{2,3,0,1:T(8,128)(2,1)}, bf16[8,4,192,192]{2,3,0,1:T(8,128)(2,1)}, u32[]{:S(2)}, u32[]{:S(2)}) collective-permute-start(bf16[8,4,192,192]{2,3,0,1:T(8,128)(2,1)} %convert_bitcast_fusion), channel_id=1, source_target_pairs={{0,128},{128,0},{256,384},{384,256},{1,129},{129,1},{257,385},{385... | collective-permute-start | bytes 7077896 | tf_op jit(solution)/shard_map/ppermute | solution.py:23
  122.9 13.5 %copy-start.3 = (f32[8,4,192,192]{2,3,0,1:T(8,128)}, f32[8,4,192,192]{2,3,0,1:T(8,128)S(1)}, u32[]{:S(2)}) copy-start(f32[8,4,192,192]{2,3,0,1:T(8,128)S(1)} %convert_add_fusion) | copy-start | bytes 14155780
  123.0 13.4 %collective-permute-start.9 = (bf16[4,192,192]{1,2,0:T(8,128)(2,1)S(1)}, bf16[4,192,192]{1,2,0:T(8,128)(2,1)S(1)}, u32[]{:S(2)}, u32[]{:S(2)}) collective-permute-start(bf16[4,192,192]{1,2,0:T(8,128)(2,1)S(1)} %get-tuple-element.27), channel_id=1, source_target_pairs={{0,1},{1,2},{2,3},{3,4},{4,5},{5,6},{6,7},{7,0},{8,9},{9,10},{10,1... | collective-permute-start | bytes 884744 | tf_op jit(solution)/shard_map/ppermute | solution.py:43
  128.9 12.3 %collective-permute-start.13 = (bf16[4,192,192]{1,2,0:T(8,128)(2,1)S(1)}, bf16[4,192,192]{1,2,0:T(8,128)(2,1)S(1)}, u32[]{:S(2)}, u32[]{:S(2)}) collective-permute-start(bf16[4,192,192]{1,2,0:T(8,128)(2,1)S(1)} %get-tuple-element.26), channel_id=1, source_target_pairs={{0,7},{1,0},{2,1},{3,2},{4,3},{5,4},{6,5},{7,6},{8,15},{9,8},{10,9... | collective-permute-start | bytes 884744 | tf_op jit(solution)/shard_map/ppermute | solution.py:43
  136.6 12.5 %collective-permute-start.10 = (bf16[4,192,192]{1,2,0:T(8,128)(2,1)S(1)}, bf16[4,192,192]{1,2,0:T(8,128)(2,1)S(1)}, u32[]{:S(2)}, u32[]{:S(2)}) collective-permute-start(bf16[4,192,192]{1,2,0:T(8,128)(2,1)S(1)} %fusion.18), channel_id=1, source_target_pairs={{0,1},{1,2},{2,3},{3,4},{4,5},{5,6},{6,7},{7,0},{8,9},{9,10},{10,1... | collective-permute-start | bytes 884744 | tf_op jit(solution)/shard_map/ppermute | solution.py:43
  150.6 11.6 %collective-permute-start.11 = (bf16[4,192,192]{1,2,0:T(8,128)(2,1)S(1)}, bf16[4,192,192]{1,2,0:T(8,128)(2,1)S(1)}, u32[]{:S(2)}, u32[]{:S(2)}) collective-permute-start(bf16[4,192,192]{1,2,0:T(8,128)(2,1)S(1)} %get-tuple-element.24), channel_id=1, source_target_pairs={{0,1},{1,2},{2,3},{3,4},{4,5},{5,6},{6,7},{7,0},{8,9},{9,10},{10,1... | collective-permute-start | bytes 884744 | tf_op jit(solution)/shard_map/ppermute | solution.py:43
  152.5 10.6 %collective-permute-start.14 = (bf16[4,192,192]{1,2,0:T(8,128)(2,1)S(1)}, bf16[4,192,192]{1,2,0:T(8,128)(2,1)S(1)}, u32[]{:S(2)}, u32[]{:S(2)}) collective-permute-start(bf16[4,192,192]{1,2,0:T(8,128)(2,1)S(1)} %get-tuple-element.25), channel_id=1, source_target_pairs={{0,7},{1,0},{2,1},{3,2},{4,3},{5,4},{6,5},{7,6},{8,15},{9,8},{10,9... | collective-permute-start | bytes 884744 | tf_op jit(solution)/shard_map/ppermute | solution.py:43
  164.7 11.4 %collective-permute-start.12 = (bf16[4,192,192]{1,2,0:T(8,128)(2,1)S(1)}, bf16[4,192,192]{1,2,0:T(8,128)(2,1)S(1)}, u32[]{:S(2)}, u32[]{:S(2)}) collective-permute-start(bf16[4,192,192]{1,2,0:T(8,128)(2,1)S(1)} %get-tuple-element.22), channel_id=1, source_target_pairs={{0,1},{1,2},{2,3},{3,4},{4,5},{5,6},{6,7},{7,0},{8,9},{9,10},{10,1... | collective-permute-start | bytes 884744 | tf_op jit(solution)/shard_map/ppermute | solution.py:43
  166.6 10.7 %collective-permute-start.15 = (bf16[4,192,192]{1,2,0:T(8,128)(2,1)S(1)}, bf16[4,192,192]{1,2,0:T(8,128)(2,1)S(1)}, u32[]{:S(2)}, u32[]{:S(2)}) collective-permute-start(bf16[4,192,192]{1,2,0:T(8,128)(2,1)S(1)} %get-tuple-element.23), channel_id=1, source_target_pairs={{0,7},{1,0},{2,1},{3,2},{4,3},{5,4},{6,5},{7,6},{8,15},{9,8},{10,9... | collective-permute-start | bytes 884744 | tf_op jit(solution)/shard_map/ppermute | solution.py:43
  178.6 8.2 %collective-permute-start.16 = (bf16[192,192]{0,1:T(8,128)(2,1)S(1)}, bf16[192,192]{0,1:T(8,128)(2,1)S(1)}, u32[]{:S(2)}, u32[]{:S(2)}) collective-permute-start(bf16[192,192]{0,1:T(8,128)(2,1)S(1)} %get-tuple-element.30), channel_id=1, source_target_pairs={{0,8},{8,16},{16,24},{24,0},{1,9},{9,17},{17,25},{25,1},{2,10},{10... | collective-permute-start | bytes 221192 | tf_op jit(solution)/shard_map/ppermute | solution.py:43
  180.5 8.2 %collective-permute-start.18 = (bf16[192,192]{0,1:T(8,128)(2,1)S(1)}, bf16[192,192]{0,1:T(8,128)(2,1)S(1)}, u32[]{:S(2)}, u32[]{:S(2)}) collective-permute-start(bf16[192,192]{0,1:T(8,128)(2,1)S(1)} %get-tuple-element.31), channel_id=1, source_target_pairs={{0,24},{8,0},{16,8},{24,16},{1,25},{9,1},{17,9},{25,17},{2,26},{10... | collective-permute-start | bytes 221192 | tf_op jit(solution)/shard_map/ppermute | solution.py:43
  186.8 7.5 %collective-permute-start.17 = (bf16[192,192]{0,1:T(8,128)(2,1)S(1)}, bf16[192,192]{0,1:T(8,128)(2,1)S(1)}, u32[]{:S(2)}, u32[]{:S(2)}) collective-permute-start(bf16[192,192]{0,1:T(8,128)(2,1)S(1)} %fusion.29), channel_id=1, source_target_pairs={{0,8},{8,16},{16,24},{24,0},{1,9},{9,17},{17,25},{25,1},{2,10},{10... | collective-permute-start | bytes 221192 | tf_op jit(solution)/shard_map/ppermute | solution.py:43
  (3 other events, 4.7 us)

commit v12 on v11

--- a/solution.py
+++ b/solution.py
@@ -80,24 +80,31 @@
 
     total = pick(me)
     if n == 1:
-        return total, beside
+        return total, (None if beside is None else beside[1](beside[0]))
     up, down = n // 2, (n - 1) // 2
-    acc = pick(me + up)
+    cw = pick(me + up)
+    ccw = pick(me - down) if down else None
     for t in range(1, up + 1):
-        acc = ring.shift(acc.astype(jnp.bfloat16), 1)
-        if t == 1 and beside is not None:
-            acc, beside = lax.optimization_barrier((acc, beside))
-        acc = acc.astype(jnp.float32)
+        cw = ring.shift(cw.astype(jnp.bfloat16), 1)
+        if t == up and beside is not None and not callable(beside[1]):
+            cw, beside = lax.optimization_barrier((cw, beside))
+        cw = cw.astype(jnp.float32)
         if t < up:
-            acc = acc + pick(me + up - t)
-    total = total + acc
+            cw = cw + pick(me + up - t)
+        if t <= down:
+            ccw = ring.shift(ccw.astype(jnp.bfloat16), -1)
+            if t == down and beside is not None:
+                value, make = beside
+                ccw, value = lax.optimization_barrier((ccw, value))
+                beside = (make(value), None)
+            ccw = ccw.astype(jnp.float32)
+            if t < down:
+                ccw = ccw + pick(me - down + t)
+    total = total + cw
     if down:
-        acc = pick(me - down)
-        for t in range(1, down + 1):
-            acc = ring.shift(acc.astype(jnp.bfloat16), -1).astype(jnp.float32)
-            if t < down:
-                acc = acc + pick(me - down + t)
-        total = total + acc
+        total = total + ccw
+    if beside is not None:
+        beside = beside[0] if beside[1] is None else beside[1](beside[0])
     return total, beside
 
 
@@ -174,16 +181,18 @@
     g_mine = jnp.where(first, g_lo, g_hi)
     g_other = jnp.where(first, g_hi, g_lo)
 
-    input_grad = (
-        contract_last(g_mine, w_mine_all) + contract_last(g_other, w_other_all)
-    ).astype(jnp.bfloat16)
+    def finish_input(parts):
+        gm, go, wm, wo = parts
+        return (contract_last(gm, wm) + contract_last(go, wo)).astype(jnp.bfloat16)
+
+    input_parts = (g_mine, g_other, w_mine_all, w_other_all)
 
     wg_other = jnp.einsum("pyzd,pc->zydc", blocked, g_other, preferred_element_type=jnp.float32)
     wg_from_partner = dp_partner(wg_other.astype(jnp.bfloat16), 1)
     wg_mine = jnp.einsum("pyzd,pc->zydc", blocked, g_mine, preferred_element_type=jnp.float32)
     wg_mine, wg_from_partner = lax.optimization_barrier((wg_mine, wg_from_partner))
     blocks = wg_mine + wg_from_partner.astype(jnp.float32)
-    over_z, input_grad = ring_reduce_scatter(blocks, ring_z, axis=0, beside=input_grad)
+    over_z, input_grad = ring_reduce_scatter(blocks, ring_z, axis=0, beside=(input_parts, finish_input))
     over_fsdp, _ = ring_reduce_scatter(over_z, ring_y)
 
     by_seq = lax.all_gather(over_fsdp, "seq", axis=0, tiled=False)

time: 224 us -> 237 us (1.058)
  other arithmetic: 9.77 us -> 14.2 us
  waiting for transfers between devices: 39.3 us -> 42.4 us
  local copies, waits for them, and re-layouts: 23.1 us -> 25.8 us
    convert_element_type x4, other arithmetic: 3.22 us -> 7.42 us  [the longest x2 5.33 us: ring_reduce_scatter(): ccw = ring.shift(ccw.astype(jnp.bfloat16), -1)]
    ppermute x17, waiting for transfers between devices: 36.4 us -> 39.5 us  [shift(): return lax.ppermute(x, self.axis, perm=pairs)]
    unnamed x23 -> x21, local copies, waits for them, and re-layouts: 9.47 us -> 11.3 us
  transfers between devices with their start and end apart: 19 -> 19, of which waited for: 16 -> 14; matrix products, arithmetic and copies ran while one was open for 11% -> 12% of each run, Pallas kernels for 0% -> 0%
where the time goes in v12:
time: 237 us; the launch traced here: 235 us
  starting transfers between devices  73.2 us (31%)
  blocking collectives  57.3 us (24%)
  waiting for transfers between devices  42.4 us (18%)
  local copies, waits for them, and re-layouts  25.8 us (11%)
  matrix products  21.2 us (9%)
  other arithmetic  14.2 us (6%)
    ppermute x17, starting transfers between devices, shift(): return lax.ppermute(x, self.axis, perm=pairs)  58.5 us
    ppermute x17, waiting for transfers between devices, shift(): return lax.ppermute(x, self.axis, perm=pairs)  39.5 us
    all_gather x1, blocking collectives, shards(): by_dp = lax.all_gather(over_seq, 'dp', axis=0, tiled=False)  16.8 us
    all_gather x1, blocking collectives, shards(): stack_y = lax.all_gather(w_mine, 'fh', axis=0, tiled=False)  16.3 us
    ppermute x2, starting transfers between devices, dp_partner(): return lax.ppermute(x, 'dp', perm=pairs)  14.6 us
    all_gather x1, blocking collectives, shards(): packed_all = lax.all_gather(packed, 'seq', axis=0, tiled=True)  12.9 us
    all_gather x1, blocking collectives, shards(): by_seq = lax.all_gather(over_fsdp, 'seq', axis=0, tiled=False)  11.3 us
    unnamed x21, local copies, waits for them, and re-layouts  11.3 us
  transfers between devices with their start and end apart: 19, of which 14 were waited for; matrix products, arithmetic and copies ran while one was open for 12% of the time, Pallas kernels for 0%

profile of v12, /device:TPU:1, one launch (start us, length us, event | category | flops | bytes accessed | tf_op | source)
XLA Modules:
  0.0 235.4 jit_solution(11998606874481788807)
XLA Ops:
  1.6 16.3 %all-gather = bf16[768,192]{1,0:T(8,128)(2,1)S(1)} all-gather(bf16[192,192]{1,0:T(8,128)(2,1)S(1)} %constant_dynamic-slice_fusion), channel_id=2, replica_groups=mesh['dp'=4,'seq'=4,'fh'=4,'fz'=8] {'fh'}, dimensions={0}, use_global_device_ids=true | all-gather | bytes 368640 | tf_op jit(solution)/shard_map/all_gather | solution.py:129
  17.9 3.2 %collective-permute-start = (bf16[4,192,192]{2,1,0:T(8,128)(2,1)S(1)}, bf16[4,192,192]{2,1,0:T(8,128)(2,1)}, u32[]{:S(2)}, u32[]{:S(2)}) collective-permute-start(bf16[4,192,192]{2,1,0:T(8,128)(2,1)S(1)} %bitcast.110), channel_id=1, source_target_pairs={{0,1},{1,2},{2,3},{3,4},{4,5},{5,6},{6,7},{7,0},{8,9},{9,10},{10,1... | collective-permute-start | bytes 884744 | tf_op jit(solution)/shard_map/ppermute | solution.py:43
  21.2 8.6 %collective-permute-start.1 = (bf16[4,192,192]{2,1,0:T(8,128)(2,1)S(1)}, bf16[4,192,192]{2,1,0:T(8,128)(2,1)S(1)}, u32[]{:S(2)}, u32[]{:S(2)}) collective-permute-start(bf16[4,192,192]{2,1,0:T(8,128)(2,1)S(1)} %bitcast.111), channel_id=1, source_target_pairs={{0,7},{1,0},{2,1},{3,2},{4,3},{5,4},{6,5},{7,6},{8,15},{9,8},{10,9... | collective-permute-start | bytes 884744 | tf_op jit(solution)/shard_map/ppermute | solution.py:43
  36.8 4.6 %collective-permute-start.3 = (bf16[4,192,192]{2,1,0:T(8,128)(2,1)S(1)}, bf16[4,192,192]{2,1,0:T(8,128)(2,1)S(1)}, u32[]{:S(2)}, u32[]{:S(2)}) collective-permute-start(bf16[4,192,192]{2,1,0:T(8,128)(2,1)S(1)} %collective-permute-done.1), channel_id=1, source_target_pairs={{0,7},{1,0},{2,1},{3,2},{4,3},{5,4},{6,5},{7,6},{8,15},{9,8},{10,9... | collective-permute-start | bytes 884744 | tf_op jit(solution)/shard_map/ppermute | solution.py:43
  46.0 5.0 %collective-permute-start.5 = (bf16[4,192,192]{2,1,0:T(8,128)(2,1)S(1)}, bf16[4,192,192]{2,1,0:T(8,128)(2,1)S(1)}, u32[]{:S(2)}, u32[]{:S(2)}) collective-permute-start(bf16[4,192,192]{2,1,0:T(8,128)(2,1)S(1)} %collective-permute-done.3), channel_id=1, source_target_pairs={{0,7},{1,0},{2,1},{3,2},{4,3},{5,4},{6,5},{7,6},{8,15},{9,8},{10,9... | collective-permute-start | bytes 884744 | tf_op jit(solution)/shard_map/ppermute | solution.py:43
  56.8 4.5 %reshape.141 = bf16[192,4,8,192]{3,2,1,0:T(8,128)(2,1)} reshape(bf16[192,6144]{1,0:T(8,128)(2,1)S(1)} %bitcast.107) | data formatting | bytes 4718592 | tf_op jit(solution)/shard_map/reshape | solution.py:130
  71.1 10.5 %collective-permute-start.7 = (bf16[6144,192]{0,1:T(8,128)(2,1)}, bf16[6144,192]{0,1:T(8,128)(2,1)}, u32[]{:S(2)}, u32[]{:S(2)}) collective-permute-start(bf16[6144,192]{0,1:T(8,128)(2,1)} %copy.31), channel_id=1, source_target_pairs={{0,128},{128,0},{256,384},{384,256},{1,129},{129,1},{257,385},{385... | collective-permute-start | bytes 7077896 | tf_op jit(solution)/shard_map/ppermute | solution.py:23
  88.8 12.9 %all_gather.21 = bf16[768,640]{1,0:T(8,128)(2,1)S(1)} all-gather(bf16[192,640]{1,0:T(8,128)(2,1)S(1)} %pad_maximum_fusion.1), channel_id=1, replica_groups=mesh['dp'=4,'seq'=4,'fh'=4,'fz'=8] {'seq'}, dimensions={0}, use_global_device_ids=true | all-gather | bytes 1228800 | tf_op jit(solution)/shard_map/all_gather | solution.py:153
  106.2 4.1 %convert_bitcast_fusion = bf16[8,4,192,192]{2,3,0,1:T(8,128)(2,1)} fusion(bf16[192,4,8,192]{3,2,1,0:T(8,128)(2,1)S(1)} %copy-done.1, bf16[192,192]{1,0:T(8,128)(2,1)S(1)} %get-tuple-element.23), kind=kOutput, calls=%fused_computation.8 | convolution fusion | flops 454164480 | bytes 4792320 | tf_op jit(solution)/shard_map/pyzd,pc->zydc/dot_general | solution.py:190
  110.2 4.2 %collective-permute-start.8 = (bf16[8,4,192,192]{2,3,0,1:T(8,128)(2,1)}, bf16[8,4,192,192]{2,3,0,1:T(8,128)(2,1)}, u32[]{:S(2)}, u32[]{:S(2)}) collective-permute-start(bf16[8,4,192,192]{2,3,0,1:T(8,128)(2,1)} %convert_bitcast_fusion), channel_id=1, source_target_pairs={{0,128},{128,0},{256,384},{384,256},{1,129},{129,1},{257,385},{385... | collective-permute-start | bytes 7077896 | tf_op jit(solution)/shard_map/ppermute | solution.py:23
  114.4 4.2 %fusion.5 = f32[8,4,192,192]{2,3,0,1:T(8,128)S(1)} fusion(bf16[192,4,8,192]{3,2,1,0:T(8,128)(2,1)} %reshape.141, bf16[192,192]{1,0:T(8,128)(2,1)S(1)} %get-tuple-element.21), kind=kOutput, calls=%fused_computation.13 | convolution fusion | flops 452984832 | bytes 7151616 | tf_op jit(solution)/shard_map/pyzd,pc->zydc/dot_general | solution.py:192
  119.8 3.0 %convert_add_fusion = f32[8,4,192,192]{2,3,0,1:T(8,128)S(1)} fusion(f32[8,4,192,192]{2,3,0,1:T(8,128)S(1)} %fusion.5, bf16[8,4,192,192]{2,3,0,1:T(8,128)(2,1)} %collective-permute-done.8), kind=kLoop, calls=%fused_computation.4 | loop fusion | flops 2359296 | bytes 11796480 | tf_op jit(solution)/shard_map/add | solution.py:194
  128.4 4.6 %collective-permute-start.13 = (bf16[4,192,192]{1,2,0:T(8,128)(2,1)}, bf16[4,192,192]{1,2,0:T(8,128)(2,1)}, u32[]{:S(2)}, u32[]{:S(2)}) collective-permute-start(bf16[4,192,192]{1,2,0:T(8,128)(2,1)} %get-tuple-element.36), channel_id=1, source_target_pairs={{0,7},{1,0},{2,1},{3,2},{4,3},{5,4},{6,5},{7,6},{8,15},{9,8},{10,9... | collective-permute-start | bytes 884744 | tf_op jit(solution)/shard_map/ppermute | solution.py:43
  133.0 7.2 %collective-permute-done.9 = bf16[4,192,192]{1,2,0:T(8,128)(2,1)} collective-permute-done((bf16[4,192,192]{1,2,0:T(8,128)(2,1)}, bf16[4,192,192]{1,2,0:T(8,128)(2,1)}, u32[]{:S(2)}, u32[]{:S(2)}) %collective-permute-start.9) | collective-permute-done | bytes 294944 | tf_op jit(solution)/shard_map/ppermute | solution.py:43
  144.3 10.8 %collective-permute-done.10 = bf16[4,192,192]{1,2,0:T(8,128)(2,1)} collective-permute-done((bf16[4,192,192]{1,2,0:T(8,128)(2,1)}, bf16[4,192,192]{1,2,0:T(8,128)(2,1)}, u32[]{:S(2)}, u32[]{:S(2)}) %collective-permute-start.10) | collective-permute-done | bytes 294944 | tf_op jit(solution)/shard_map/ppermute | solution.py:43
  159.7 4.6 %collective-permute-start.14 = (bf16[4,192,192]{1,2,0:T(8,128)(2,1)}, bf16[4,192,192]{1,2,0:T(8,128)(2,1)}, u32[]{:S(2)}, u32[]{:S(2)}) collective-permute-start(bf16[4,192,192]{1,2,0:T(8,128)(2,1)} %get-tuple-element.34), channel_id=1, source_target_pairs={{0,7},{1,0},{2,1},{3,2},{4,3},{5,4},{6,5},{7,6},{8,15},{9,8},{10,9... | collective-permute-start | bytes 884744 | tf_op jit(solution)/shard_map/ppermute | solution.py:43
  164.3 5.4 %collective-permute-done.11 = bf16[4,192,192]{1,2,0:T(8,128)(2,1)} collective-permute-done((bf16[4,192,192]{1,2,0:T(8,128)(2,1)}, bf16[4,192,192]{1,2,0:T(8,128)(2,1)}, u32[]{:S(2)}, u32[]{:S(2)}) %collective-permute-start.11) | collective-permute-done | bytes 294944 | tf_op jit(solution)/shard_map/ppermute | solution.py:43
  170.6 2.7 %fusion.15 = (bf16[4,192,192]{1,2,0:T(8,128)(2,1)}, bf16[4,192,192]{1,2,0:T(8,128)(2,1)}) fusion(f32[8,4,192,192]{2,3,0,1:T(8,128)} %copy-done.2, s32[]{:T(128)S(6)} %select_n.226, bf16[4,192,192]{1,2,0:T(8,128)(2,1)} %collective-permute-done.14, s32[]{:T(128)S(6)} %select_n.220, bf16[4,192,192]{1,2,0:T(8,128)(2,1)} %collective-permute-done.11), kind=kLoop, calls=%fused_computation.29 | loop fusion | flops 884736 | bytes 2359304 | tf_op jit(solution)/shard_map/convert_element_type | solution.py:95
  173.2 5.3 %collective-permute-start.15 = (bf16[4,192,192]{1,2,0:T(8,128)(2,1)}, bf16[4,192,192]{1,2,0:T(8,128)(2,1)}, u32[]{:S(2)}, u32[]{:S(2)}) collective-permute-start(bf16[4,192,192]{1,2,0:T(8,128)(2,1)} %get-tuple-element.32), channel_id=1, source_target_pairs={{0,7},{1,0},{2,1},{3,2},{4,3},{5,4},{6,5},{7,6},{8,15},{9,8},{10,9... | collective-permute-start | bytes 884744 | tf_op jit(solution)/shard_map/ppermute | solution.py:43
  180.6 3.4 %collective-permute-done.15 = bf16[4,192,192]{1,2,0:T(8,128)(2,1)} collective-permute-done((bf16[4,192,192]{1,2,0:T(8,128)(2,1)}, bf16[4,192,192]{1,2,0:T(8,128)(2,1)}, u32[]{:S(2)}, u32[]{:S(2)}) %collective-permute-start.15) | collective-permute-done | bytes 294944 | tf_op jit(solution)/shard_map/ppermute | solution.py:43
  192.5 5.3 %collective-permute-start.18 = (bf16[192,192]{0,1:T(8,128)(2,1)S(1)}, bf16[192,192]{0,1:T(8,128)(2,1)S(1)}, u32[]{:S(2)}, u32[]{:S(2)}) collective-permute-start(bf16[192,192]{0,1:T(8,128)(2,1)S(1)} %get-tuple-element.41), channel_id=1, source_target_pairs={{0,24},{8,0},{16,8},{24,16},{1,25},{9,1},{17,9},{25,17},{2,26},{10... | collective-permute-start | bytes 221192 | tf_op jit(solution)/shard_map/ppermute | solution.py:43
  200.6 5.6 %collective-permute-done.17 = bf16[192,192]{0,1:T(8,128)(2,1)S(1)} collective-permute-done((bf16[192,192]{0,1:T(8,128)(2,1)S(1)}, bf16[192,192]{0,1:T(8,128)(2,1)S(1)}, u32[]{:S(2)}, u32[]{:S(2)}) %collective-permute-start.17) | collective-permute-done | bytes 73760 | tf_op jit(solution)/shard_map/ppermute | solution.py:43
  206.4 11.3 %all-gather.1 = f32[768,192]{1,0:T(8,128)S(1)} all-gather(f32[192,192]{1,0:T(8,128)S(1)} %copy.39), channel_id=3, replica_groups=mesh['dp'=4,'seq'=4,'fh'=4,'fz'=8] {'seq'}, dimensions={0}, use_global_device_ids=true | all-gather | bytes 737280 | tf_op jit(solution)/shard_map/all_gather | solution.py:198
  217.8 16.8 %all_gather.24 = f32[4,192,192]{2,1,0:T(8,128)S(1)} all-gather(f32[1,192,192]{2,1,0:T(8,128)S(1)} %fusion.28), channel_id=1, replica_groups=mesh['dp'=4,'seq'=4,'fh'=4,'fz'=8] {'dp'}, dimensions={0}, use_global_device_ids=true | all-gather | bytes 737280 | tf_op jit(solution)/shard_map/all_gather | solution.py:202
  (83 shorter events, 70.1 us)
Async XLA Ops:
  17.9 15.2 %collective-permute-start = (bf16[4,192,192]{2,1,0:T(8,128)(2,1)S(1)}, bf16[4,192,192]{2,1,0:T(8,128)(2,1)}, u32[]{:S(2)}, u32[]{:S(2)}) collective-permute-start(bf16[4,192,192]{2,1,0:T(8,128)(2,1)S(1)} %bitcast.110), channel_id=1, source_target_pairs={{0,1},{1,2},{2,3},{3,4},{4,5},{5,6},{6,7},{7,0},{8,9},{9,10},{10,1... | collective-permute-start | bytes 884744 | tf_op jit(solution)/shard_map/ppermute | solution.py:43
  21.2 15.6 %collective-permute-start.1 = (bf16[4,192,192]{2,1,0:T(8,128)(2,1)S(1)}, bf16[4,192,192]{2,1,0:T(8,128)(2,1)S(1)}, u32[]{:S(2)}, u32[]{:S(2)}) collective-permute-start(bf16[4,192,192]{2,1,0:T(8,128)(2,1)S(1)} %bitcast.111), channel_id=1, source_target_pairs={{0,7},{1,0},{2,1},{3,2},{4,3},{5,4},{6,5},{7,6},{8,15},{9,8},{10,9... | collective-permute-start | bytes 884744 | tf_op jit(solution)/shard_map/ppermute | solution.py:43
  30.6 26.2 %copy-start.3 = (bf16[1,192,6144]{2,1,0:T(8,128)(2,1)S(1)}, bf16[1,192,6144]{2,1,0:T(8,128)(2,1)}, u32[]{:S(2)}) copy-start(bf16[1,192,6144]{2,1,0:T(8,128)(2,1)} %param.5) | copy-start | bytes 7077892
  33.1 9.9 %collective-permute-start.2 = (bf16[4,192,192]{2,1,0:T(8,128)(2,1)}, bf16[4,192,192]{2,1,0:T(8,128)(2,1)S(1)}, u32[]{:S(2)}, u32[]{:S(2)}) collective-permute-start(bf16[4,192,192]{2,1,0:T(8,128)(2,1)} %collective-permute-done), channel_id=1, source_target_pairs={{0,1},{1,2},{2,3},{3,4},{4,5},{5,6},{6,7},{7,0},{8,9},{9,10},{10,1... | collective-permute-start | bytes 884744 | tf_op jit(solution)/shard_map/ppermute | solution.py:43
  36.8 9.3 %collective-permute-start.3 = (bf16[4,192,192]{2,1,0:T(8,128)(2,1)S(1)}, bf16[4,192,192]{2,1,0:T(8,128)(2,1)S(1)}, u32[]{:S(2)}, u32[]{:S(2)}) collective-permute-start(bf16[4,192,192]{2,1,0:T(8,128)(2,1)S(1)} %collective-permute-done.1), channel_id=1, source_target_pairs={{0,7},{1,0},{2,1},{3,2},{4,3},{5,4},{6,5},{7,6},{8,15},{9,8},{10,9... | collective-permute-start | bytes 884744 | tf_op jit(solution)/shard_map/ppermute | solution.py:43
  43.0 10.0 %collective-permute-start.4 = (bf16[4,192,192]{2,1,0:T(8,128)(2,1)S(1)}, bf16[4,192,192]{2,1,0:T(8,128)(2,1)}, u32[]{:S(2)}, u32[]{:S(2)}) collective-permute-start(bf16[4,192,192]{2,1,0:T(8,128)(2,1)S(1)} %collective-permute-done.2), channel_id=1, source_target_pairs={{0,1},{1,2},{2,3},{3,4},{4,5},{5,6},{6,7},{7,0},{8,9},{9,10},{10,1... | collective-permute-start | bytes 884744 | tf_op jit(solution)/shard_map/ppermute | solution.py:43
  46.0 10.7 %collective-permute-start.5 = (bf16[4,192,192]{2,1,0:T(8,128)(2,1)S(1)}, bf16[4,192,192]{2,1,0:T(8,128)(2,1)S(1)}, u32[]{:S(2)}, u32[]{:S(2)}) collective-permute-start(bf16[4,192,192]{2,1,0:T(8,128)(2,1)S(1)} %collective-permute-done.3), channel_id=1, source_target_pairs={{0,7},{1,0},{2,1},{3,2},{4,3},{5,4},{6,5},{7,6},{8,15},{9,8},{10,9... | collective-permute-start | bytes 884744 | tf_op jit(solution)/shard_map/ppermute | solution.py:43
  53.0 11.0 %collective-permute-start.6 = (bf16[4,192,192]{2,1,0:T(8,128)(2,1)}, bf16[4,192,192]{2,1,0:T(8,128)(2,1)}, u32[]{:S(2)}, u32[]{:S(2)}) collective-permute-start(bf16[4,192,192]{2,1,0:T(8,128)(2,1)} %collective-permute-done.4), channel_id=1, source_target_pairs={{0,1},{1,2},{2,3},{3,4},{4,5},{5,6},{6,7},{7,0},{8,9},{9,10},{10,1... | collective-permute-start | bytes 884744 | tf_op jit(solution)/shard_map/ppermute | solution.py:43
  68.5 13.1 %copy-start.6 = (s32[1,192]{1,0:T(1,128)S(1)}, s32[1,192]{1,0:T(1,128)}, u32[]{:S(2)}) copy-start(s32[1,192]{1,0:T(1,128)} %param.6) | copy-start | bytes 2308
  71.1 14.9 %collective-permute-start.7 = (bf16[6144,192]{0,1:T(8,128)(2,1)}, bf16[6144,192]{0,1:T(8,128)(2,1)}, u32[]{:S(2)}, u32[]{:S(2)}) collective-permute-start(bf16[6144,192]{0,1:T(8,128)(2,1)} %copy.31), channel_id=1, source_target_pairs={{0,128},{128,0},{256,384},{384,256},{1,129},{129,1},{257,385},{385... | collective-permute-start | bytes 7077896 | tf_op jit(solution)/shard_map/ppermute | solution.py:23
  81.6 4.4 %copy-start.4 = (bf16[1,192,6144]{2,1,0:T(8,128)(2,1)S(1)}, bf16[1,192,6144]{2,1,0:T(8,128)(2,1)}, u32[]{:S(2)}) copy-start(bf16[1,192,6144]{2,1,0:T(8,128)(2,1)} %param.5) | copy-start | bytes 7077892
  84.2 4.5 %copy-start.5 = (bf16[1,192,128]{2,1,0:T(8,128)(2,1)S(1)}, bf16[1,192,128]{2,1,0:T(8,128)(2,1)}, u32[]{:S(2)}) copy-start(bf16[1,192,128]{2,1,0:T(8,128)(2,1)} %param.8) | copy-start | bytes 147460
  110.2 9.6 %collective-permute-start.8 = (bf16[8,4,192,192]{2,3,0,1:T(8,128)(2,1)}, bf16[8,4,192,192]{2,3,0,1:T(8,128)(2,1)}, u32[]{:S(2)}, u32[]{:S(2)}) collective-permute-start(bf16[8,4,192,192]{2,3,0,1:T(8,128)(2,1)} %convert_bitcast_fusion), channel_id=1, source_target_pairs={{0,128},{128,0},{256,384},{384,256},{1,129},{129,1},{257,385},{385... | collective-permute-start | bytes 7077896 | tf_op jit(solution)/shard_map/ppermute | solution.py:23
  122.9 2.7 %copy-start.2 = (f32[8,4,192,192]{2,3,0,1:T(8,128)}, f32[8,4,192,192]{2,3,0,1:T(8,128)S(1)}, u32[]{:S(2)}) copy-start(f32[8,4,192,192]{2,3,0,1:T(8,128)S(1)} %convert_add_fusion) | copy-start | bytes 14155780
  126.5 13.7 %collective-permute-start.9 = (bf16[4,192,192]{1,2,0:T(8,128)(2,1)}, bf16[4,192,192]{1,2,0:T(8,128)(2,1)}, u32[]{:S(2)}, u32[]{:S(2)}) collective-permute-start(bf16[4,192,192]{1,2,0:T(8,128)(2,1)} %get-tuple-element.37), channel_id=1, source_target_pairs={{0,1},{1,2},{2,3},{3,4},{4,5},{5,6},{6,7},{7,0},{8,9},{9,10},{10,1... | collective-permute-start | bytes 884744 | tf_op jit(solution)/shard_map/ppermute | solution.py:43
  128.4 15.8 %collective-permute-start.13 = (bf16[4,192,192]{1,2,0:T(8,128)(2,1)}, bf16[4,192,192]{1,2,0:T(8,128)(2,1)}, u32[]{:S(2)}, u32[]{:S(2)}) collective-permute-start(bf16[4,192,192]{1,2,0:T(8,128)(2,1)} %get-tuple-element.36), channel_id=1, source_target_pairs={{0,7},{1,0},{2,1},{3,2},{4,3},{5,4},{6,5},{7,6},{8,15},{9,8},{10,9... | collective-permute-start | bytes 884744 | tf_op jit(solution)/shard_map/ppermute | solution.py:43
  142.3 12.8 %collective-permute-start.10 = (bf16[4,192,192]{1,2,0:T(8,128)(2,1)}, bf16[4,192,192]{1,2,0:T(8,128)(2,1)}, u32[]{:S(2)}, u32[]{:S(2)}) collective-permute-start(bf16[4,192,192]{1,2,0:T(8,128)(2,1)} %fusion.19), channel_id=1, source_target_pairs={{0,1},{1,2},{2,3},{3,4},{4,5},{5,6},{6,7},{7,0},{8,9},{9,10},{10,1... | collective-permute-start | bytes 884744 | tf_op jit(solution)/shard_map/ppermute | solution.py:43
  157.8 11.9 %collective-permute-start.11 = (bf16[4,192,192]{1,2,0:T(8,128)(2,1)}, bf16[4,192,192]{1,2,0:T(8,128)(2,1)}, u32[]{:S(2)}, u32[]{:S(2)}) collective-permute-start(bf16[4,192,192]{1,2,0:T(8,128)(2,1)} %get-tuple-element.35), channel_id=1, source_target_pairs={{0,1},{1,2},{2,3},{3,4},{4,5},{5,6},{6,7},{7,0},{8,9},{9,10},{10,1... | collective-permute-start | bytes 884744 | tf_op jit(solution)/shard_map/ppermute | solution.py:43
  159.7 10.9 %collective-permute-start.14 = (bf16[4,192,192]{1,2,0:T(8,128)(2,1)}, bf16[4,192,192]{1,2,0:T(8,128)(2,1)}, u32[]{:S(2)}, u32[]{:S(2)}) collective-permute-start(bf16[4,192,192]{1,2,0:T(8,128)(2,1)} %get-tuple-element.34), channel_id=1, source_target_pairs={{0,7},{1,0},{2,1},{3,2},{4,3},{5,4},{6,5},{7,6},{8,15},{9,8},{10,9... | collective-permute-start | bytes 884744 | tf_op jit(solution)/shard_map/ppermute | solution.py:43
  173.2 10.7 %collective-permute-start.15 = (bf16[4,192,192]{1,2,0:T(8,128)(2,1)}, bf16[4,192,192]{1,2,0:T(8,128)(2,1)}, u32[]{:S(2)}, u32[]{:S(2)}) collective-permute-start(bf16[4,192,192]{1,2,0:T(8,128)(2,1)} %get-tuple-element.32), channel_id=1, source_target_pairs={{0,7},{1,0},{2,1},{3,2},{4,3},{5,4},{6,5},{7,6},{8,15},{9,8},{10,9... | collective-permute-start | bytes 884744 | tf_op jit(solution)/shard_map/ppermute | solution.py:43
  178.6 10.3 %collective-permute-start.12 = (bf16[4,192,192]{1,2,0:T(8,128)(2,1)}, bf16[4,192,192]{1,2,0:T(8,128)(2,1)S(1)}, u32[]{:S(2)}, u32[]{:S(2)}) collective-permute-start(bf16[4,192,192]{1,2,0:T(8,128)(2,1)} %get-tuple-element.33), channel_id=1, source_target_pairs={{0,1},{1,2},{2,3},{3,4},{4,5},{5,6},{6,7},{7,0},{8,9},{9,10},{10,1... | collective-permute-start | bytes 884744 | tf_op jit(solution)/shard_map/ppermute | solution.py:43
  190.4 8.2 %collective-permute-start.16 = (bf16[192,192]{0,1:T(8,128)(2,1)S(1)}, bf16[192,192]{0,1:T(8,128)(2,1)S(1)}, u32[]{:S(2)}, u32[]{:S(2)}) collective-permute-start(bf16[192,192]{0,1:T(8,128)(2,1)S(1)} %get-tuple-element.40), channel_id=1, source_target_pairs={{0,8},{8,16},{16,24},{24,0},{1,9},{9,17},{17,25},{25,1},{2,10},{10... | collective-permute-start | bytes 221192 | tf_op jit(solution)/shard_map/ppermute | solution.py:43
  192.5 8.1 %collective-permute-start.18 = (bf16[192,192]{0,1:T(8,128)(2,1)S(1)}, bf16[192,192]{0,1:T(8,128)(2,1)S(1)}, u32[]{:S(2)}, u32[]{:S(2)}) collective-permute-start(bf16[192,192]{0,1:T(8,128)(2,1)S(1)} %get-tuple-element.41), channel_id=1, source_target_pairs={{0,24},{8,0},{16,8},{24,16},{1,25},{9,1},{17,9},{25,17},{2,26},{10... | collective-permute-start | bytes 221192 | tf_op jit(solution)/shard_map/ppermute | solution.py:43
  198.7 7.6 %collective-permute-start.17 = (bf16[192,192]{0,1:T(8,128)(2,1)S(1)}, bf16[192,192]{0,1:T(8,128)(2,1)S(1)}, u32[]{:S(2)}, u32[]{:S(2)}) collective-permute-start(bf16[192,192]{0,1:T(8,128)(2,1)S(1)} %fusion.29), channel_id=1, source_target_pairs={{0,8},{8,16},{16,24},{24,0},{1,9},{9,17},{17,25},{25,1},{2,10},{10... | collective-permute-start | bytes 221192 | tf_op jit(solution)/shard_map/ppermute | solution.py:43
  (2 other events, 2.8 us)

commit v13 on v11

--- a/solution.py
+++ b/solution.py
@@ -85,8 +85,6 @@
     acc = pick(me + up)
     for t in range(1, up + 1):
         acc = ring.shift(acc.astype(jnp.bfloat16), 1)
-        if t == 1 and beside is not None:
-            acc, beside = lax.optimization_barrier((acc, beside))
         acc = acc.astype(jnp.float32)
         if t < up:
             acc = acc + pick(me + up - t)
@@ -94,7 +92,14 @@
     if down:
         acc = pick(me - down)
         for t in range(1, down + 1):
-            acc = ring.shift(acc.astype(jnp.bfloat16), -1).astype(jnp.float32)
+            acc = ring.shift(acc.astype(jnp.bfloat16), -1)
+            if t == 1 and beside is not None and down > 1:
+                value, make = beside
+                acc, value = lax.optimization_barrier((acc, value))
+                beside = make(value)
+            if t == 2 and beside is not None:
+                acc, beside = lax.optimization_barrier((acc, beside))
+            acc = acc.astype(jnp.float32)
             if t < down:
                 acc = acc + pick(me - down + t)
         total = total + acc
@@ -174,16 +179,20 @@
     g_mine = jnp.where(first, g_lo, g_hi)
     g_other = jnp.where(first, g_hi, g_lo)
 
-    input_grad = (
-        contract_last(g_mine, w_mine_all) + contract_last(g_other, w_other_all)
-    ).astype(jnp.bfloat16)
+    def finish_input(parts):
+        gm, go, wm, wo = parts
+        return (contract_last(gm, wm) + contract_last(go, wo)).astype(jnp.bfloat16)
+
+    input_parts = (g_mine, g_other, w_mine_all, w_other_all)
 
     wg_other = jnp.einsum("pyzd,pc->zydc", blocked, g_other, preferred_element_type=jnp.float32)
     wg_from_partner = dp_partner(wg_other.astype(jnp.bfloat16), 1)
     wg_mine = jnp.einsum("pyzd,pc->zydc", blocked, g_mine, preferred_element_type=jnp.float32)
     wg_mine, wg_from_partner = lax.optimization_barrier((wg_mine, wg_from_partner))
     blocks = wg_mine + wg_from_partner.astype(jnp.float32)
-    over_z, input_grad = ring_reduce_scatter(blocks, ring_z, axis=0, beside=input_grad)
+    over_z, input_grad = ring_reduce_scatter(blocks, ring_z, axis=0, beside=(input_parts, finish_input))
+    if isinstance(input_grad, tuple):
+        input_grad = input_grad[1](input_grad[0])
     over_fsdp, _ = ring_reduce_scatter(over_z, ring_y)
 
     by_seq = lax.all_gather(over_fsdp, "seq", axis=0, tiled=False)

time: 224 us -> 230 us (1.027)
  waiting for transfers between devices: 39.3 us -> 43.2 us
  local copies, waits for them, and re-layouts: 23.1 us -> 25.8 us
  starting transfers between devices: 73.1 us -> 70.4 us
    ppermute x17, waiting for transfers between devices: 36.4 us -> 40.2 us  [shift(): return lax.ppermute(x, self.axis, perm=pairs)]
    ppermute x17, starting transfers between devices: 58.5 us -> 55.8 us  [shift(): return lax.ppermute(x, self.axis, perm=pairs)]
where the time goes in v13:
time: 230 us; the launch traced here: 229 us
  starting transfers between devices  70.4 us (31%)
  blocking collectives  57.4 us (25%)
  waiting for transfers between devices  43.2 us (19%)
  local copies, waits for them, and re-layouts  25.8 us (11%)
  matrix products  21.3 us (9%)
  other arithmetic  9.44 us (4%)
    ppermute x17, starting transfers between devices, shift(): return lax.ppermute(x, self.axis, perm=pairs)  55.8 us
    ppermute x17, waiting for transfers between devices, shift(): return lax.ppermute(x, self.axis, perm=pairs)  40.2 us
    all_gather x1, blocking collectives, shards(): by_dp = lax.all_gather(over_seq, 'dp', axis=0, tiled=False)  16.8 us
    all_gather x1, blocking collectives, shards(): stack_y = lax.all_gather(w_mine, 'fh', axis=0, tiled=False)  16.3 us
    ppermute x2, starting transfers between devices, dp_partner(): return lax.ppermute(x, 'dp', perm=pairs)  14.6 us
    all_gather x1, blocking collectives, shards(): packed_all = lax.all_gather(packed, 'seq', axis=0, tiled=True)  12.9 us
    all_gather x1, blocking collectives, shards(): by_seq = lax.all_gather(over_fsdp, 'seq', axis=0, tiled=False)  11.4 us
    unnamed x23, local copies, waits for them, and re-layouts  11.3 us
  transfers between devices with their start and end apart: 19, of which 16 were waited for; matrix products, arithmetic and copies ran while one was open for 11% of the time, Pallas kernels for 0%

profile of v13, /device:TPU:1, one launch (start us, length us, event | category | flops | bytes accessed | tf_op | source)
XLA Modules:
  0.0 228.8 jit_solution(12445366043428283810)
XLA Ops:
  1.6 16.3 %all-gather = bf16[768,192]{1,0:T(8,128)(2,1)S(1)} all-gather(bf16[192,192]{1,0:T(8,128)(2,1)S(1)} %constant_dynamic-slice_fusion), channel_id=2, replica_groups=mesh['dp'=4,'seq'=4,'fh'=4,'fz'=8] {'fh'}, dimensions={0}, use_global_device_ids=true | all-gather | bytes 368640 | tf_op jit(solution)/shard_map/all_gather | solution.py:127
  17.9 3.2 %collective-permute-start = (bf16[4,192,192]{2,1,0:T(8,128)(2,1)S(1)}, bf16[4,192,192]{2,1,0:T(8,128)(2,1)}, u32[]{:S(2)}, u32[]{:S(2)}) collective-permute-start(bf16[4,192,192]{2,1,0:T(8,128)(2,1)S(1)} %bitcast.110), channel_id=1, source_target_pairs={{0,1},{1,2},{2,3},{3,4},{4,5},{5,6},{6,7},{7,0},{8,9},{9,10},{10,1... | collective-permute-start | bytes 884744 | tf_op jit(solution)/shard_map/ppermute | solution.py:43
  21.2 8.6 %collective-permute-start.1 = (bf16[4,192,192]{2,1,0:T(8,128)(2,1)S(1)}, bf16[4,192,192]{2,1,0:T(8,128)(2,1)S(1)}, u32[]{:S(2)}, u32[]{:S(2)}) collective-permute-start(bf16[4,192,192]{2,1,0:T(8,128)(2,1)S(1)} %bitcast.111), channel_id=1, source_target_pairs={{0,7},{1,0},{2,1},{3,2},{4,3},{5,4},{6,5},{7,6},{8,15},{9,8},{10,9... | collective-permute-start | bytes 884744 | tf_op jit(solution)/shard_map/ppermute | solution.py:43
  36.8 4.6 %collective-permute-start.3 = (bf16[4,192,192]{2,1,0:T(8,128)(2,1)S(1)}, bf16[4,192,192]{2,1,0:T(8,128)(2,1)S(1)}, u32[]{:S(2)}, u32[]{:S(2)}) collective-permute-start(bf16[4,192,192]{2,1,0:T(8,128)(2,1)S(1)} %collective-permute-done.1), channel_id=1, source_target_pairs={{0,7},{1,0},{2,1},{3,2},{4,3},{5,4},{6,5},{7,6},{8,15},{9,8},{10,9... | collective-permute-start | bytes 884744 | tf_op jit(solution)/shard_map/ppermute | solution.py:43
  46.0 5.0 %collective-permute-start.5 = (bf16[4,192,192]{2,1,0:T(8,128)(2,1)S(1)}, bf16[4,192,192]{2,1,0:T(8,128)(2,1)S(1)}, u32[]{:S(2)}, u32[]{:S(2)}) collective-permute-start(bf16[4,192,192]{2,1,0:T(8,128)(2,1)S(1)} %collective-permute-done.3), channel_id=1, source_target_pairs={{0,7},{1,0},{2,1},{3,2},{4,3},{5,4},{6,5},{7,6},{8,15},{9,8},{10,9... | collective-permute-start | bytes 884744 | tf_op jit(solution)/shard_map/ppermute | solution.py:43
  56.8 4.5 %reshape.141 = bf16[192,4,8,192]{3,2,1,0:T(8,128)(2,1)} reshape(bf16[192,6144]{1,0:T(8,128)(2,1)S(1)} %bitcast.107) | data formatting | bytes 4718592 | tf_op jit(solution)/shard_map/reshape | solution.py:128
  71.1 10.5 %collective-permute-start.7 = (bf16[6144,192]{0,1:T(8,128)(2,1)}, bf16[6144,192]{0,1:T(8,128)(2,1)}, u32[]{:S(2)}, u32[]{:S(2)}) collective-permute-start(bf16[6144,192]{0,1:T(8,128)(2,1)} %copy.31), channel_id=1, source_target_pairs={{0,128},{128,0},{256,384},{384,256},{1,129},{129,1},{257,385},{385... | collective-permute-start | bytes 7077896 | tf_op jit(solution)/shard_map/ppermute | solution.py:23
  88.8 12.9 %all_gather.21 = bf16[768,640]{1,0:T(8,128)(2,1)S(1)} all-gather(bf16[192,640]{1,0:T(8,128)(2,1)S(1)} %pad_maximum_fusion.1), channel_id=1, replica_groups=mesh['dp'=4,'seq'=4,'fh'=4,'fz'=8] {'seq'}, dimensions={0}, use_global_device_ids=true | all-gather | bytes 1228800 | tf_op jit(solution)/shard_map/all_gather | solution.py:151
  106.2 4.1 %convert_bitcast_fusion = bf16[8,4,192,192]{2,3,0,1:T(8,128)(2,1)} fusion(bf16[192,4,8,192]{3,2,1,0:T(8,128)(2,1)S(1)} %copy-done.1, bf16[192,192]{1,0:T(8,128)(2,1)S(1)} %get-tuple-element.24), kind=kOutput, calls=%fused_computation.8 | convolution fusion | flops 454164480 | bytes 4792320 | tf_op jit(solution)/shard_map/pyzd,pc->zydc/dot_general | solution.py:188
  110.2 4.2 %collective-permute-start.8 = (bf16[8,4,192,192]{2,3,0,1:T(8,128)(2,1)}, bf16[8,4,192,192]{2,3,0,1:T(8,128)(2,1)}, u32[]{:S(2)}, u32[]{:S(2)}) collective-permute-start(bf16[8,4,192,192]{2,3,0,1:T(8,128)(2,1)} %convert_bitcast_fusion), channel_id=1, source_target_pairs={{0,128},{128,0},{256,384},{384,256},{1,129},{129,1},{257,385},{385... | collective-permute-start | bytes 7077896 | tf_op jit(solution)/shard_map/ppermute | solution.py:23
  114.5 4.2 %fusion.5 = f32[8,4,192,192]{2,3,0,1:T(8,128)S(1)} fusion(bf16[192,4,8,192]{3,2,1,0:T(8,128)(2,1)} %reshape.141, bf16[192,192]{1,0:T(8,128)(2,1)S(1)} %get-tuple-element.22), kind=kOutput, calls=%fused_computation.13 | convolution fusion | flops 452984832 | bytes 7151616 | tf_op jit(solution)/shard_map/pyzd,pc->zydc/dot_general | solution.py:190
  119.8 3.0 %convert_add_fusion = f32[8,4,192,192]{2,3,0,1:T(8,128)S(1)} fusion(f32[8,4,192,192]{2,3,0,1:T(8,128)S(1)} %fusion.5, bf16[8,4,192,192]{2,3,0,1:T(8,128)(2,1)} %collective-permute-done.8), kind=kLoop, calls=%fused_computation.4 | loop fusion | flops 2359296 | bytes 11796480 | tf_op jit(solution)/shard_map/add | solution.py:192
  126.5 2.8 %collective-permute-start.9 = (bf16[4,192,192]{1,2,0:T(8,128)(2,1)}, bf16[4,192,192]{1,2,0:T(8,128)(2,1)}, u32[]{:S(2)}, u32[]{:S(2)}) collective-permute-start(bf16[4,192,192]{1,2,0:T(8,128)(2,1)} %get-tuple-element.37), channel_id=1, source_target_pairs={{0,7},{1,0},{2,1},{3,2},{4,3},{5,4},{6,5},{7,6},{8,15},{9,8},{10,9... | collective-permute-start | bytes 884744 | tf_op jit(solution)/shard_map/ppermute | solution.py:43
  131.9 7.1 %collective-permute-done.9 = bf16[4,192,192]{1,2,0:T(8,128)(2,1)} collective-permute-done((bf16[4,192,192]{1,2,0:T(8,128)(2,1)}, bf16[4,192,192]{1,2,0:T(8,128)(2,1)}, u32[]{:S(2)}, u32[]{:S(2)}) %collective-permute-start.9) | collective-permute-done | bytes 294944 | tf_op jit(solution)/shard_map/ppermute | solution.py:43
  139.1 3.7 %collective-permute-done.11 = bf16[4,192,192]{1,2,0:T(8,128)(2,1)} collective-permute-done((bf16[4,192,192]{1,2,0:T(8,128)(2,1)}, bf16[4,192,192]{1,2,0:T(8,128)(2,1)}, u32[]{:S(2)}, u32[]{:S(2)}) %collective-permute-start.11) | collective-permute-done | bytes 294944 | tf_op jit(solution)/shard_map/ppermute | solution.py:43
  148.9 7.7 %collective-permute-done.12 = bf16[4,192,192]{1,2,0:T(8,128)(2,1)S(1)} collective-permute-done((bf16[4,192,192]{1,2,0:T(8,128)(2,1)S(1)}, bf16[4,192,192]{1,2,0:T(8,128)(2,1)S(1)}, u32[]{:S(2)}, u32[]{:S(2)}) %collective-permute-start.12) | collective-permute-done | bytes 294944 | tf_op jit(solution)/shard_map/ppermute | solution.py:43
  159.7 3.4 %collective-permute-start.13 = (bf16[4,192,192]{1,2,0:T(8,128)(2,1)S(1)}, bf16[4,192,192]{1,2,0:T(8,128)(2,1)S(1)}, u32[]{:S(2)}, u32[]{:S(2)}) collective-permute-start(bf16[4,192,192]{1,2,0:T(8,128)(2,1)S(1)} %get-tuple-element.34), channel_id=1, source_target_pairs={{0,1},{1,2},{2,3},{3,4},{4,5},{5,6},{6,7},{7,0},{8,9},{9,10},{10,1... | collective-permute-start | bytes 884744 | tf_op jit(solution)/shard_map/ppermute | solution.py:43
  167.9 3.1 %collective-permute-done.13 = bf16[4,192,192]{1,2,0:T(8,128)(2,1)S(1)} collective-permute-done((bf16[4,192,192]{1,2,0:T(8,128)(2,1)S(1)}, bf16[4,192,192]{1,2,0:T(8,128)(2,1)S(1)}, u32[]{:S(2)}, u32[]{:S(2)}) %collective-permute-start.13) | collective-permute-done | bytes 294944 | tf_op jit(solution)/shard_map/ppermute | solution.py:43
  173.1 4.6 %collective-permute-start.15 = (bf16[4,192,192]{1,2,0:T(8,128)(2,1)S(1)}, bf16[4,192,192]{1,2,0:T(8,128)(2,1)S(1)}, u32[]{:S(2)}, u32[]{:S(2)}) collective-permute-start(bf16[4,192,192]{1,2,0:T(8,128)(2,1)S(1)} %get-tuple-element.33), channel_id=1, source_target_pairs={{0,7},{1,0},{2,1},{3,2},{4,3},{5,4},{6,5},{7,6},{8,15},{9,8},{10,9... | collective-permute-start | bytes 884744 | tf_op jit(solution)/shard_map/ppermute | solution.py:43
  177.8 3.8 %collective-permute-done.14 = bf16[4,192,192]{1,2,0:T(8,128)(2,1)S(1)} collective-permute-done((bf16[4,192,192]{1,2,0:T(8,128)(2,1)S(1)}, bf16[4,192,192]{1,2,0:T(8,128)(2,1)S(1)}, u32[]{:S(2)}, u32[]{:S(2)}) %collective-permute-start.14) | collective-permute-done | bytes 294944 | tf_op jit(solution)/shard_map/ppermute | solution.py:43
  185.7 5.4 %collective-permute-start.18 = (bf16[192,192]{0,1:T(8,128)(2,1)S(1)}, bf16[192,192]{0,1:T(8,128)(2,1)S(1)}, u32[]{:S(2)}, u32[]{:S(2)}) collective-permute-start(bf16[192,192]{0,1:T(8,128)(2,1)S(1)} %get-tuple-element.41), channel_id=1, source_target_pairs={{0,24},{8,0},{16,8},{24,16},{1,25},{9,1},{17,9},{25,17},{2,26},{10... | collective-permute-start | bytes 221192 | tf_op jit(solution)/shard_map/ppermute | solution.py:43
  193.9 5.6 %collective-permute-done.17 = bf16[192,192]{0,1:T(8,128)(2,1)S(1)} collective-permute-done((bf16[192,192]{0,1:T(8,128)(2,1)S(1)}, bf16[192,192]{0,1:T(8,128)(2,1)S(1)}, u32[]{:S(2)}, u32[]{:S(2)}) %collective-permute-start.17) | collective-permute-done | bytes 73760 | tf_op jit(solution)/shard_map/ppermute | solution.py:43
  199.7 11.4 %all-gather.1 = f32[768,192]{1,0:T(8,128)S(1)} all-gather(f32[192,192]{1,0:T(8,128)S(1)} %copy.39), channel_id=3, replica_groups=mesh['dp'=4,'seq'=4,'fh'=4,'fz'=8] {'seq'}, dimensions={0}, use_global_device_ids=true | all-gather | bytes 737280 | tf_op jit(solution)/shard_map/all_gather | solution.py:198
  211.2 16.8 %all_gather.24 = f32[4,192,192]{2,1,0:T(8,128)S(1)} all-gather(f32[1,192,192]{2,1,0:T(8,128)S(1)} %fusion.28), channel_id=1, replica_groups=mesh['dp'=4,'seq'=4,'fh'=4,'fz'=8] {'dp'}, dimensions={0}, use_global_device_ids=true | all-gather | bytes 737280 | tf_op jit(solution)/shard_map/all_gather | solution.py:202
  (85 shorter events, 70.9 us)
Async XLA Ops:
  17.9 15.2 %collective-permute-start = (bf16[4,192,192]{2,1,0:T(8,128)(2,1)S(1)}, bf16[4,192,192]{2,1,0:T(8,128)(2,1)}, u32[]{:S(2)}, u32[]{:S(2)}) collective-permute-start(bf16[4,192,192]{2,1,0:T(8,128)(2,1)S(1)} %bitcast.110), channel_id=1, source_target_pairs={{0,1},{1,2},{2,3},{3,4},{4,5},{5,6},{6,7},{7,0},{8,9},{9,10},{10,1... | collective-permute-start | bytes 884744 | tf_op jit(solution)/shard_map/ppermute | solution.py:43
  21.2 15.6 %collective-permute-start.1 = (bf16[4,192,192]{2,1,0:T(8,128)(2,1)S(1)}, bf16[4,192,192]{2,1,0:T(8,128)(2,1)S(1)}, u32[]{:S(2)}, u32[]{:S(2)}) collective-permute-start(bf16[4,192,192]{2,1,0:T(8,128)(2,1)S(1)} %bitcast.111), channel_id=1, source_target_pairs={{0,7},{1,0},{2,1},{3,2},{4,3},{5,4},{6,5},{7,6},{8,15},{9,8},{10,9... | collective-permute-start | bytes 884744 | tf_op jit(solution)/shard_map/ppermute | solution.py:43
  30.6 26.2 %copy-start.4 = (bf16[1,192,6144]{2,1,0:T(8,128)(2,1)S(1)}, bf16[1,192,6144]{2,1,0:T(8,128)(2,1)}, u32[]{:S(2)}) copy-start(bf16[1,192,6144]{2,1,0:T(8,128)(2,1)} %param.5) | copy-start | bytes 7077892
  33.1 9.9 %collective-permute-start.2 = (bf16[4,192,192]{2,1,0:T(8,128)(2,1)}, bf16[4,192,192]{2,1,0:T(8,128)(2,1)S(1)}, u32[]{:S(2)}, u32[]{:S(2)}) collective-permute-start(bf16[4,192,192]{2,1,0:T(8,128)(2,1)} %collective-permute-done), channel_id=1, source_target_pairs={{0,1},{1,2},{2,3},{3,4},{4,5},{5,6},{6,7},{7,0},{8,9},{9,10},{10,1... | collective-permute-start | bytes 884744 | tf_op jit(solution)/shard_map/ppermute | solution.py:43
  36.8 9.3 %collective-permute-start.3 = (bf16[4,192,192]{2,1,0:T(8,128)(2,1)S(1)}, bf16[4,192,192]{2,1,0:T(8,128)(2,1)S(1)}, u32[]{:S(2)}, u32[]{:S(2)}) collective-permute-start(bf16[4,192,192]{2,1,0:T(8,128)(2,1)S(1)} %collective-permute-done.1), channel_id=1, source_target_pairs={{0,7},{1,0},{2,1},{3,2},{4,3},{5,4},{6,5},{7,6},{8,15},{9,8},{10,9... | collective-permute-start | bytes 884744 | tf_op jit(solution)/shard_map/ppermute | solution.py:43
  43.0 10.0 %collective-permute-start.4 = (bf16[4,192,192]{2,1,0:T(8,128)(2,1)S(1)}, bf16[4,192,192]{2,1,0:T(8,128)(2,1)}, u32[]{:S(2)}, u32[]{:S(2)}) collective-permute-start(bf16[4,192,192]{2,1,0:T(8,128)(2,1)S(1)} %collective-permute-done.2), channel_id=1, source_target_pairs={{0,1},{1,2},{2,3},{3,4},{4,5},{5,6},{6,7},{7,0},{8,9},{9,10},{10,1... | collective-permute-start | bytes 884744 | tf_op jit(solution)/shard_map/ppermute | solution.py:43
  46.0 10.7 %collective-permute-start.5 = (bf16[4,192,192]{2,1,0:T(8,128)(2,1)S(1)}, bf16[4,192,192]{2,1,0:T(8,128)(2,1)S(1)}, u32[]{:S(2)}, u32[]{:S(2)}) collective-permute-start(bf16[4,192,192]{2,1,0:T(8,128)(2,1)S(1)} %collective-permute-done.3), channel_id=1, source_target_pairs={{0,7},{1,0},{2,1},{3,2},{4,3},{5,4},{6,5},{7,6},{8,15},{9,8},{10,9... | collective-permute-start | bytes 884744 | tf_op jit(solution)/shard_map/ppermute | solution.py:43
  53.0 11.0 %collective-permute-start.6 = (bf16[4,192,192]{2,1,0:T(8,128)(2,1)}, bf16[4,192,192]{2,1,0:T(8,128)(2,1)}, u32[]{:S(2)}, u32[]{:S(2)}) collective-permute-start(bf16[4,192,192]{2,1,0:T(8,128)(2,1)} %collective-permute-done.4), channel_id=1, source_target_pairs={{0,1},{1,2},{2,3},{3,4},{4,5},{5,6},{6,7},{7,0},{8,9},{9,10},{10,1... | collective-permute-start | bytes 884744 | tf_op jit(solution)/shard_map/ppermute | solution.py:43
  68.5 13.1 %copy-start.7 = (s32[1,192]{1,0:T(1,128)S(1)}, s32[1,192]{1,0:T(1,128)}, u32[]{:S(2)}) copy-start(s32[1,192]{1,0:T(1,128)} %param.6) | copy-start | bytes 2308
  71.1 14.9 %collective-permute-start.7 = (bf16[6144,192]{0,1:T(8,128)(2,1)}, bf16[6144,192]{0,1:T(8,128)(2,1)}, u32[]{:S(2)}, u32[]{:S(2)}) collective-permute-start(bf16[6144,192]{0,1:T(8,128)(2,1)} %copy.31), channel_id=1, source_target_pairs={{0,128},{128,0},{256,384},{384,256},{1,129},{129,1},{257,385},{385... | collective-permute-start | bytes 7077896 | tf_op jit(solution)/shard_map/ppermute | solution.py:23
  81.6 4.4 %copy-start.5 = (bf16[1,192,6144]{2,1,0:T(8,128)(2,1)S(1)}, bf16[1,192,6144]{2,1,0:T(8,128)(2,1)}, u32[]{:S(2)}) copy-start(bf16[1,192,6144]{2,1,0:T(8,128)(2,1)} %param.5) | copy-start | bytes 7077892
  84.2 4.5 %copy-start.6 = (bf16[1,192,128]{2,1,0:T(8,128)(2,1)S(1)}, bf16[1,192,128]{2,1,0:T(8,128)(2,1)}, u32[]{:S(2)}) copy-start(bf16[1,192,128]{2,1,0:T(8,128)(2,1)} %param.8) | copy-start | bytes 147460
  110.2 9.6 %collective-permute-start.8 = (bf16[8,4,192,192]{2,3,0,1:T(8,128)(2,1)}, bf16[8,4,192,192]{2,3,0,1:T(8,128)(2,1)}, u32[]{:S(2)}, u32[]{:S(2)}) collective-permute-start(bf16[8,4,192,192]{2,3,0,1:T(8,128)(2,1)} %convert_bitcast_fusion), channel_id=1, source_target_pairs={{0,128},{128,0},{256,384},{384,256},{1,129},{129,1},{257,385},{385... | collective-permute-start | bytes 7077896 | tf_op jit(solution)/shard_map/ppermute | solution.py:23
  126.5 12.5 %collective-permute-start.9 = (bf16[4,192,192]{1,2,0:T(8,128)(2,1)}, bf16[4,192,192]{1,2,0:T(8,128)(2,1)}, u32[]{:S(2)}, u32[]{:S(2)}) collective-permute-start(bf16[4,192,192]{1,2,0:T(8,128)(2,1)} %get-tuple-element.37), channel_id=1, source_target_pairs={{0,7},{1,0},{2,1},{3,2},{4,3},{5,4},{6,5},{7,6},{8,15},{9,8},{10,9... | collective-permute-start | bytes 884744 | tf_op jit(solution)/shard_map/ppermute | solution.py:43
  129.4 13.4 %collective-permute-start.11 = (bf16[4,192,192]{1,2,0:T(8,128)(2,1)}, bf16[4,192,192]{1,2,0:T(8,128)(2,1)}, u32[]{:S(2)}, u32[]{:S(2)}) collective-permute-start(bf16[4,192,192]{1,2,0:T(8,128)(2,1)} %get-tuple-element.36), channel_id=1, source_target_pairs={{0,1},{1,2},{2,3},{3,4},{4,5},{5,6},{6,7},{7,0},{8,9},{9,10},{10,1... | collective-permute-start | bytes 884744 | tf_op jit(solution)/shard_map/ppermute | solution.py:43
  144.1 12.5 %copy-start.3 = (f32[8,4,192,192]{2,3,0,1:T(8,128)S(1)}, f32[8,4,192,192]{2,3,0,1:T(8,128)}, u32[]{:S(2)}) copy-start(f32[8,4,192,192]{2,3,0,1:T(8,128)} %copy-done.2) | copy-start | bytes 14155780
  144.1 12.5 %collective-permute-start.12 = (bf16[4,192,192]{1,2,0:T(8,128)(2,1)S(1)}, bf16[4,192,192]{1,2,0:T(8,128)(2,1)S(1)}, u32[]{:S(2)}, u32[]{:S(2)}) collective-permute-start(bf16[4,192,192]{1,2,0:T(8,128)(2,1)S(1)} %fusion.17), channel_id=1, source_target_pairs={{0,1},{1,2},{2,3},{3,4},{4,5},{5,6},{6,7},{7,0},{8,9},{9,10},{10,1... | collective-permute-start | bytes 884744 | tf_op jit(solution)/shard_map/ppermute | solution.py:43
  157.8 10.1 %collective-permute-start.10 = (bf16[4,192,192]{1,2,0:T(8,128)(2,1)S(1)}, bf16[4,192,192]{1,2,0:T(8,128)(2,1)S(1)}, u32[]{:S(2)}, u32[]{:S(2)}) collective-permute-start(bf16[4,192,192]{1,2,0:T(8,128)(2,1)S(1)} %get-tuple-element.35), channel_id=1, source_target_pairs={{0,7},{1,0},{2,1},{3,2},{4,3},{5,4},{6,5},{7,6},{8,15},{9,8},{10,9... | collective-permute-start | bytes 884744 | tf_op jit(solution)/shard_map/ppermute | solution.py:43
  159.7 11.3 %collective-permute-start.13 = (bf16[4,192,192]{1,2,0:T(8,128)(2,1)S(1)}, bf16[4,192,192]{1,2,0:T(8,128)(2,1)S(1)}, u32[]{:S(2)}, u32[]{:S(2)}) collective-permute-start(bf16[4,192,192]{1,2,0:T(8,128)(2,1)S(1)} %get-tuple-element.34), channel_id=1, source_target_pairs={{0,1},{1,2},{2,3},{3,4},{4,5},{5,6},{6,7},{7,0},{8,9},{9,10},{10,1... | collective-permute-start | bytes 884744 | tf_op jit(solution)/shard_map/ppermute | solution.py:43
  171.2 10.3 %collective-permute-start.14 = (bf16[4,192,192]{1,2,0:T(8,128)(2,1)S(1)}, bf16[4,192,192]{1,2,0:T(8,128)(2,1)S(1)}, u32[]{:S(2)}, u32[]{:S(2)}) collective-permute-start(bf16[4,192,192]{1,2,0:T(8,128)(2,1)S(1)} %get-tuple-element.32), channel_id=1, source_target_pairs={{0,1},{1,2},{2,3},{3,4},{4,5},{5,6},{6,7},{7,0},{8,9},{9,10},{10,1... | collective-permute-start | bytes 884744 | tf_op jit(solution)/shard_map/ppermute | solution.py:43
  173.1 9.3 %collective-permute-start.15 = (bf16[4,192,192]{1,2,0:T(8,128)(2,1)S(1)}, bf16[4,192,192]{1,2,0:T(8,128)(2,1)S(1)}, u32[]{:S(2)}, u32[]{:S(2)}) collective-permute-start(bf16[4,192,192]{1,2,0:T(8,128)(2,1)S(1)} %get-tuple-element.33), channel_id=1, source_target_pairs={{0,7},{1,0},{2,1},{3,2},{4,3},{5,4},{6,5},{7,6},{8,15},{9,8},{10,9... | collective-permute-start | bytes 884744 | tf_op jit(solution)/shard_map/ppermute | solution.py:43
  183.7 8.2 %collective-permute-start.16 = (bf16[192,192]{0,1:T(8,128)(2,1)S(1)}, bf16[192,192]{0,1:T(8,128)(2,1)S(1)}, u32[]{:S(2)}, u32[]{:S(2)}) collective-permute-start(bf16[192,192]{0,1:T(8,128)(2,1)S(1)} %get-tuple-element.40), channel_id=1, source_target_pairs={{0,8},{8,16},{16,24},{24,0},{1,9},{9,17},{17,25},{25,1},{2,10},{10... | collective-permute-start | bytes 221192 | tf_op jit(solution)/shard_map/ppermute | solution.py:43
  185.7 8.2 %collective-permute-start.18 = (bf16[192,192]{0,1:T(8,128)(2,1)S(1)}, bf16[192,192]{0,1:T(8,128)(2,1)S(1)}, u32[]{:S(2)}, u32[]{:S(2)}) collective-permute-start(bf16[192,192]{0,1:T(8,128)(2,1)S(1)} %get-tuple-element.41), channel_id=1, source_target_pairs={{0,24},{8,0},{16,8},{24,16},{1,25},{9,1},{17,9},{25,17},{2,26},{10... | collective-permute-start | bytes 221192 | tf_op jit(solution)/shard_map/ppermute | solution.py:43
  192.0 7.6 %collective-permute-start.17 = (bf16[192,192]{0,1:T(8,128)(2,1)S(1)}, bf16[192,192]{0,1:T(8,128)(2,1)S(1)}, u32[]{:S(2)}, u32[]{:S(2)}) collective-permute-start(bf16[192,192]{0,1:T(8,128)(2,1)S(1)} %fusion.29), channel_id=1, source_target_pairs={{0,8},{8,16},{16,24},{24,0},{1,9},{9,17},{17,25},{25,1},{2,10},{10... | collective-permute-start | bytes 221192 | tf_op jit(solution)/shard_map/ppermute | solution.py:43
  (3 other events, 5.5 us)
